TPU v7x, 512 devices: a whole 4x4x16 slice. The times are simulated.
512 devices in a mesh: seq: 64 (over x, z), head: 8 (over y, core).
Axes of the slice: x: 4, y: 4, z: 16, core: 2. Of those that a mesh axis runs over, the one named last changes fastest.
Arguments:
- queries: bfloat16 [32768, 8192], P(('seq', 'head')), may hold values from -9 to 9
- keys: bfloat16 [32768, 1024], P(('seq', 'head')), may hold values from -9 to 9
- values: bfloat16 [32768, 1024], P(('seq', 'head')), may hold values from -6 to 6
- prefix_keys: bfloat16 [131072, 1024], P('seq', 'head'), may hold values from -6 to 6
- prefix_values: bfloat16 [131072, 1024], P('seq', 'head'), may hold values from -6 to 6
- roles: int32 [64], P('head'), may hold values from 0 to 1, as said below
- columns: int32 [64, 6], P('head'), may hold values from 0 to 2015, as said below
- col_count: int32 [64], P('head'), may hold values from 1 to 6, as said below
- diagonals: int32 [64, 4], P('head'), may hold values from 0 to 7, as said below
Outputs:
- attended: bfloat16 [32768, 8192], P('seq', 'head')
Inputs may be any that keep to these rules, and one draw needn't show every extreme that they name: `roles`: 1 marks a retrieval head, 0 a passing head; at most 4 retrieval heads share one key-value head, and some key-value head has exactly 4. `columns`: prefix block indices, blocks of 64 cache rows, distinct within a head. `col_count`: some retrieval head uses all 6 of its column blocks. `diagonals`: distinct within a head; the first offset of every head is 0.
All inputs are finite; a program needn't handle non-finite values.
Results may differ from a plain program's by a relative error of at most 0.0049.
Values may be sent and summed in bfloat16 or wider, within the bound.
No kernel may reach another device: no remote copies, remote signals or barrier semaphores. Data moves between devices by JAX's collectives and lax.ppermute only.
A program may use at most 64 MiB of HBM per device.

v0:
```python
import math

import jax
import jax.numpy as jnp
from jax import lax
from jax.sharding import PartitionSpec as P

QUERY_HEADS = 64
KEY_VALUE_HEADS = 8
HEAD_SIZE = 128
SINK = 128
WIN = 512
BLK = 64
VB = 6
NSL = 4


def shifted(block, axis, distance):
    devices = range(lax.axis_size(axis))
    route = [((i - distance) % len(devices), i) for i in devices]
    return lax.ppermute(block, axis, route)


def broadcast(block, axis, source):
    block = jnp.where(lax.axis_index(axis) == source, block, jnp.zeros_like(block))
    return lax.psum(block, axis)


def masked_softmax(score_matrix, allowed):
    row_max = jnp.max(jnp.where(allowed, score_matrix, -jnp.inf), axis=-1, keepdims=True)
    expo = jnp.where(allowed, jnp.exp(score_matrix - row_max), 0.0)
    total = jnp.sum(expo, axis=-1, keepdims=True)
    return (expo / total).astype(jnp.bfloat16)


def stream_head(q_head, sink_k, sink_v, comb_k, comb_v):
    rows_here = q_head.shape[0]
    scaling = 1.0 / math.sqrt(HEAD_SIZE)
    offset_grid = jnp.arange(2 * WIN)[None, :] - jnp.arange(WIN)[:, None]
    band_ok = (offset_grid >= 1) & (offset_grid <= WIN)
    allowed = jnp.concatenate([jnp.ones((WIN, SINK), dtype=jnp.bool_), band_ok], 1)

    def one_block(which):
        keys_here = jnp.concatenate([sink_k, comb_k], 0)
        vals_here = jnp.concatenate([sink_v, comb_v], 0)
        score_matrix = jnp.dot(q_head, keys_here.T, preferred_element_type=jnp.float32) * scaling
        probs = masked_softmax(score_matrix, allowed)
        return jnp.dot(probs, vals_here, preferred_element_type=jnp.float32)

    final_output = lax.map(one_block, jnp.arange(rows_here // WIN, dtype=jnp.int32))
    return final_output.reshape(rows_here, HEAD_SIZE)


def retrieve_slot(q_head, vert_k, vert_v, count_used, offsets_d, comb_k, comb_v):
    rows_here = q_head.shape[0]
    qblocks = rows_here // BLK
    scaling = 1.0 / math.sqrt(HEAD_SIZE)
    key_blocks = comb_k.reshape(-1, BLK, HEAD_SIZE)
    val_blocks = comb_v.reshape(-1, BLK, HEAD_SIZE)
    picks = jnp.arange(qblocks)[:, None] + WIN // BLK - offsets_d[None, :]
    slash_k = key_blocks[picks].reshape(qblocks, NSL * BLK, HEAD_SIZE)
    slash_v = val_blocks[picks].reshape(qblocks, NSL * BLK, HEAD_SIZE)
    q_blocks = q_head.reshape(qblocks, BLK, HEAD_SIZE)
    vert_scores = jnp.dot(q_head, vert_k.T, preferred_element_type=jnp.float32) * scaling
    vert_scores = vert_scores.reshape(qblocks, BLK, VB * BLK)
    slash_scores = (
        jnp.einsum("nqd,nkd->nqk", q_blocks, slash_k, preferred_element_type=jnp.float32) * scaling
    )
    vert_ok = jnp.arange(VB * BLK) // BLK < count_used
    within = jnp.arange(BLK)[None, :] <= jnp.arange(BLK)[:, None]
    slash_ok = (offsets_d[:, None, None] > 0) | within[None, :, :]
    slash_ok = jnp.transpose(slash_ok, (1, 0, 2)).reshape(BLK, NSL * BLK)
    allowed = jnp.concatenate([jnp.broadcast_to(vert_ok[None, :], (BLK, VB * BLK)), slash_ok], 1)
    score_matrix = jnp.concatenate([vert_scores, slash_scores], -1)
    probs = masked_softmax(score_matrix, allowed[None, :, :])
    vert_part = jnp.dot(
        probs[:, :, : VB * BLK].reshape(rows_here, VB * BLK),
        vert_v,
        preferred_element_type=jnp.float32,
    )
    slash_part = jnp.einsum(
        "nqk,nkd->nqd", probs[:, :, VB * BLK :], slash_v, preferred_element_type=jnp.float32
    )
    return vert_part + slash_part.reshape(rows_here, HEAD_SIZE)


def shards(queries, keys, values, prefix_keys, prefix_values, roles, columns, col_count, diagonals):
    q_local, k_local, v_local = (
        lax.all_to_all(queries, "head", split_axis=1, concat_axis=0, tiled=True),
        lax.all_to_all(keys, "head", split_axis=1, concat_axis=0, tiled=True),
        lax.all_to_all(values, "head", split_axis=1, concat_axis=0, tiled=True),
    )
    rows_here = q_local.shape[0]
    kv_count = k_local.shape[1] // HEAD_SIZE
    group_share = QUERY_HEADS // KEY_VALUE_HEADS
    seq_devices = lax.axis_size("seq")
    my_seq = lax.axis_index("seq")
    cache_rows = prefix_keys.shape[0]
    tail_own = jnp.concatenate([k_local, v_local], 1)
    tail_cache = jnp.concatenate(
        [prefix_keys[cache_rows - WIN :], prefix_values[cache_rows - WIN :]], 1
    )
    outgoing = jnp.where(my_seq == seq_devices - 1, tail_cache, tail_own)
    previous = shifted(outgoing, "seq", 1)
    sink = broadcast(jnp.concatenate([prefix_keys[:SINK], prefix_values[:SINK]], 1), "seq", 0)
    head_roles = roles.reshape(kv_count, group_share)
    slot_heads = jnp.arange(group_share, dtype=jnp.int32)[None, :]
    slot_count = slot_heads.shape[1]
    local_heads = slot_heads + (jnp.arange(kv_count, dtype=jnp.int32) * group_share)[:, None]
    cols_used = columns[local_heads]
    count_used = col_count[local_heads]
    diag_used = diagonals[local_heads]
    blocks_dev = cache_rows // BLK
    owner = cols_used // blocks_dev
    local_block = cols_used - owner * blocks_dev
    grouped = jnp.stack(
        [
            prefix_keys.reshape(cache_rows, kv_count, HEAD_SIZE),
            prefix_values.reshape(cache_rows, kv_count, HEAD_SIZE),
        ],
        2,
    )
    grouped = jnp.transpose(
        grouped.reshape(blocks_dev, BLK, kv_count, 2, HEAD_SIZE), (2, 0, 1, 3, 4)
    )
    pieces = grouped[jnp.arange(kv_count)[:, None, None], local_block]
    mine = (owner == my_seq)[:, :, :, None, None, None]
    terms = jnp.where(mine, pieces.astype(jnp.float32), 0.0)
    vertical = lax.psum(terms, "seq").astype(jnp.bfloat16)
    v_low = kv_count * HEAD_SIZE
    comb_k = jnp.concatenate([previous[:, 0:HEAD_SIZE], k_local], 0)
    comb_v = jnp.concatenate([previous[:, v_low : v_low + HEAD_SIZE], v_local], 0)
    sink_k = sink[:, 0:HEAD_SIZE]
    sink_v = sink[:, v_low : v_low + HEAD_SIZE]

    def stream_one(head_index):
        q_head = lax.dynamic_slice_in_dim(q_local, head_index * HEAD_SIZE, HEAD_SIZE, 1)
        return stream_head(q_head, sink_k, sink_v, comb_k, comb_v)

    passed = lax.map(stream_one, jnp.arange(group_share, dtype=jnp.int32))

    def retrieve_one(slot_index):
        head_index = slot_heads[0, slot_index]
        q_head = lax.dynamic_slice_in_dim(q_local, head_index * HEAD_SIZE, HEAD_SIZE, 1)
        vert_k = vertical[0, slot_index, :, :, 0, :].reshape(VB * BLK, HEAD_SIZE)
        vert_v = vertical[0, slot_index, :, :, 1, :].reshape(VB * BLK, HEAD_SIZE)
        return retrieve_slot(
            q_head,
            vert_k,
            vert_v,
            count_used[0, slot_index],
            diag_used[0, slot_index],
            comb_k,
            comb_v,
        )

    retrieved = lax.map(retrieve_one, jnp.arange(slot_count, dtype=jnp.int32))
    is_retrieval = head_roles[0] == 1
    merged = jnp.where(is_retrieval[:, None, None], retrieved, passed)
    outputs = (
        jnp.transpose(merged, (1, 0, 2))
        .reshape(rows_here, group_share * HEAD_SIZE)
        .astype(jnp.bfloat16)
    )
    return outputs


def solution(mesh):
    placed = (
        P(("seq", "head"), None),
        P(("seq", "head"), None),
        P(("seq", "head"), None),
        P("seq", "head"),
        P("seq", "head"),
        P("head"),
        P("head", None),
        P("head"),
        P("head", None),
    )
    return jax.shard_map(
        shards, mesh=mesh, in_specs=placed, out_specs=P("seq", "head"), check_vma=False
    )
```

profile of v0, /device:TPU:1, one launch (start us, length us, event | category | flops | bytes accessed | tf_op | source)
XLA Modules:
  0.0 517.2 jit_solution(2549630586442925470)
XLA Ops:
  6.5 0.9 copy-done
  8.1 10.2 %all-to-all-start.1 = ((bf16[64,8,128]{2,0,1:T(8,128)(2,1)}), bf16[64,8,128]{2,0,1:T(8,128)(2,1)S(1)}, u32[]{:S(2)}, u32[]{:S(2)}) async-start(bf16[64,8,128]{2,0,1:T(8,128)(2,1)} %copy_bitcast_fusion.3), calls=%async_computation.1 | async-start | bytes 262144 | tf_op jit(solution)/shard_map/all_to_all | solution.py:90
  18.3 0.8 slice.40
  19.0 0.8 slice.41
  20.5 1.2 gather_fusion.4
  22.0 1.3 pad_maximum_fusion.2
  23.3 2.0 gather_fusion.5
  25.3 1.7 copy_select_fusion
  27.7 4.8 all-to-all-start.2
  32.6 264.5 %all-reduce.6 = bf16[1,8,6,64,2,128]{5,3,2,4,1,0:T(8,128)(2,1)} all-reduce(f32[1,8,6,64,2,128]{5,3,2,4,1,0:T(8,128)S(1)} %copy_select_fusion), channel_id=1, replica_groups=mesh['seq'=64,'head'=8] {'seq'}, use_global_device_ids=true, to_apply=%region_0.1 | all-reduce | flops 786432 | bytes 4718592 | tf_op jit(solution)/shard_map/psum | solution.py:129
  297.0 0.9 slice.36
  298.0 0.9 slice.37
  298.9 2.3 copy.40
  301.2 58.0 %all-to-all-start = ((bf16[64,8,1024]{2,0,1:T(8,128)(2,1)}), bf16[64,8,1024]{2,0,1:T(8,128)(2,1)}, u32[]{:S(2)}, u32[]{:S(2)}) async-start(bf16[64,8,1024]{2,0,1:T(8,128)(2,1)} %bitcast.95), calls=%async_computation | async-start | bytes 2097152 | tf_op jit(solution)/shard_map/all_to_all | solution.py:89
  359.3 1.9 collective-permute-start
  362.6 0.8 fusion.48
  363.3 9.1 %collective-permute-done = bf16[512,256]{1,0:T(8,128)(2,1)S(1)} collective-permute-done((bf16[512,256]{1,0:T(8,128)(2,1)S(1)}, bf16[512,256]{1,0:T(8,128)(2,1)S(1)}, u32[]{:S(2)}, u32[]{:S(2)}) %collective-permute-start) | collective-permute-done | bytes 262176 | tf_op jit(solution)/shard_map/ppermute | solution.py:21
  372.6 1.9 all-to-all-done
  374.4 1.1 broadcast.366.clone
  375.5 96.2 %while.28 = (s32[]{:T(128)}, bf16[8,512,128]{2,1,0:T(8,128)(2,1)}, s32[8]{0:T(128)S(1)}, s32[1,8]{1,0:T(1,128)S(1)}, s32[1,8,4]{2,1,0:T(8,128)S(1)}, /*index=5*/...) while((s32[]{:T(128)}, bf16[8,512,128]{2,1,0:T(8,128)(2,1)}, ...), condition=%wide.region_4.5_spmd, body=%wide.region_1.4_spmd.sunk | while | flops 170853520 | bytes 12587642 | solution.py:157
  380.7 0.9 constant_dynamic-slice_fusion.10
  382.7 1.0 constant_dynamic-slice_fusion.11
  384.0 0.7 fusion.87
  386.6 0.9 fusion.90
  392.7 0.9 constant_dynamic-slice_fusion.10
  394.8 1.0 constant_dynamic-slice_fusion.11
  396.0 0.7 fusion.87
  398.6 0.9 fusion.90
  404.7 0.9 constant_dynamic-slice_fusion.10
  406.8 1.0 constant_dynamic-slice_fusion.11
  410.7 0.9 fusion.90
  416.7 0.9 constant_dynamic-slice_fusion.10
  418.8 1.0 constant_dynamic-slice_fusion.11
  422.7 0.9 fusion.90
  428.8 0.9 constant_dynamic-slice_fusion.10
  430.8 1.0 constant_dynamic-slice_fusion.11
  434.7 0.9 fusion.90
  440.8 0.9 constant_dynamic-slice_fusion.10
  442.9 1.0 constant_dynamic-slice_fusion.11
  446.7 0.9 fusion.90
  452.8 0.9 constant_dynamic-slice_fusion.10
  454.9 1.0 constant_dynamic-slice_fusion.11
  458.8 0.9 fusion.90
  464.8 0.9 constant_dynamic-slice_fusion.10
  466.9 1.0 constant_dynamic-slice_fusion.11
  470.8 0.9 fusion.90
  471.9 37.1 %while.29 = (s32[]{:T(128)}, bf16[8,512,128]{2,1,0:T(8,128)(2,1)S(1)}, s32[8]{0:T(128)S(1)}, bf16[512,1024]{1,0:T(8,128)(2,1)}, bf16[1152,128]{1,0:T(8,128)(2,1)...) while((s32[]{:T(128)}, bf16[8,512,128]{2,1,0:T(8,128)(2,1)S(1)}, ...), condition=%wide.region_9.10_spmd, body=%wide.region_6.9_spmd.sunk | while | flops 309984256 | bytes 10168487 | solution.py:140
  473.5 1.5 select_reduce_fusion.3
  475.7 0.8 fusion.95
  478.1 1.5 select_reduce_fusion.3
  480.3 0.8 fusion.95
  482.7 1.5 select_reduce_fusion.3
  485.0 0.8 fusion.95
  487.4 1.5 select_reduce_fusion.3
  489.6 0.8 fusion.95
  492.0 1.5 select_reduce_fusion.3
  494.3 0.8 fusion.95
  496.7 1.5 select_reduce_fusion.3
  498.9 0.8 fusion.95
  501.3 1.5 select_reduce_fusion.3
  503.5 0.8 fusion.95
  505.9 1.5 select_reduce_fusion.3
  508.2 0.8 fusion.95
  509.0 1.3 copy_bitcast_fusion
  (254 shorter events, 57.4 us)
Async XLA Ops:
  6.5 0.9 copy-start
  8.1 19.6 %all-to-all-start.1 = ((bf16[64,8,128]{2,0,1:T(8,128)(2,1)}), bf16[64,8,128]{2,0,1:T(8,128)(2,1)S(1)}, u32[]{:S(2)}, u32[]{:S(2)}) async-start(bf16[64,8,128]{2,0,1:T(8,128)(2,1)} %copy_bitcast_fusion.3), calls=%async_computation.1 | async-start | bytes 262144 | tf_op jit(solution)/shard_map/all_to_all | solution.py:90
  18.3 344.3 %all-reduce.5.cloned.1.call-start = ((), (), s32[]{:S(2)}) async-start(), calls=%async_computation.3 | async-start | bytes 131072 | tf_op jit(solution)/shard_map/psum | solution.py:26
  25.3 1.7 copy-start.3
  27.7 273.5 %all-to-all-start.2 = ((bf16[64,8,128]{2,0,1:T(8,128)(2,1)}), bf16[64,8,128]{2,0,1:T(8,128)(2,1)S(1)}, u32[]{:S(2)}, u32[]{:S(2)}) async-start(bf16[64,8,128]{2,0,1:T(8,128)(2,1)} %copy_bitcast_fusion.2), calls=%async_computation.2 | async-start | bytes 262144 | tf_op jit(solution)/shard_map/all_to_all | solution.py:91
  298.9 62.3 %copy-start.5 = (s32[8]{0:T(128)S(1)}, s32[8]{0:T(128)}, u32[]{:S(2)}) copy-start(s32[8]{0:T(128)} %param.18) | copy-start | bytes 100
  298.9 62.4 %copy-start.4 = (s32[8,4]{0,1:T(4,128)S(1)}, s32[8,4]{0,1:T(4,128)}, u32[]{:S(2)}) copy-start(s32[8,4]{0,1:T(4,128)} %param.21) | copy-start | bytes 388
  298.9 63.0 %copy-start.1 = (s32[8]{0:T(128)S(1)}, s32[8]{0:T(128)}, u32[]{:S(2)}) copy-start(s32[8]{0:T(128)} %param.20) | copy-start | bytes 100
  301.2 73.2 %all-to-all-start = ((bf16[64,8,1024]{2,0,1:T(8,128)(2,1)}), bf16[64,8,1024]{2,0,1:T(8,128)(2,1)}, u32[]{:S(2)}, u32[]{:S(2)}) async-start(bf16[64,8,1024]{2,0,1:T(8,128)(2,1)} %bitcast.95), calls=%async_computation | async-start | bytes 2097152 | tf_op jit(solution)/shard_map/all_to_all | solution.py:89
  359.3 13.2 %collective-permute-start = (bf16[512,256]{1,0:T(8,128)(2,1)S(1)}, bf16[512,256]{1,0:T(8,128)(2,1)S(1)}, u32[]{:S(2)}, u32[]{:S(2)}) collective-permute-start(bf16[512,256]{1,0:T(8,128)(2,1)S(1)} %maximum_select_fusion), channel_id=1, source_target_pairs={{504,0},{0,8},{8,16},{16,24},{24,32},{32,40},{40,48},{48,56},{56,6... | collective-permute-start | bytes 786440 | tf_op jit(solution)/shard_map/ppermute | solution.py:21
  471.9 37.1 %copy-start.2 = (bf16[8,512,128]{2,1,0:T(8,128)(2,1)S(1)}, bf16[8,512,128]{2,1,0:T(8,128)(2,1)}, u32[]{:S(2)}) copy-start(bf16[8,512,128]{2,1,0:T(8,128)(2,1)} %get-tuple-element.245) | copy-start | bytes 3145732
Sparse Core Ops, SparseCore 0:
  22.5 247.7 all-reduce.4
where the time goes:
time: 519 us; the launch traced here: 517 us
  blocking collectives  264 us (51%)
  starting transfers between devices  74.9 us (14%)
  local copies, waits for them, and re-layouts  54.3 us (10%)
  loops' own time  37.2 us (7%)
  matrix products  32.6 us (6%)
  other arithmetic  29.2 us (6%)
  between operations  13.6 us (3%)
  waiting for transfers between devices  11 us (2%)
    psum x1, blocking collectives, shards(): vertical = lax.psum(terms, 'seq').astype(jnp.bfloat16)  264 us
    all_to_all x1, starting transfers between devices, shards(): lax.all_to_all(queries, 'head', split_axis=1, concat_axis=0, tiled=True)  58 us
    another operation x1, loops' own time, shards(): retrieved = lax.map(retrieve_one, jnp.arange(slot_count, dtype=jnp.int32))  31.3 us
    dot_general x8, matrix products, one_block(): jnp.dot(q_head, keys_here.T, preferred_element_type=jnp.float32) * scaling  12.4 us
    dynamic_slice x16, local copies, waits for them, and re-layouts, shards(): passed = lax.map(stream_one, jnp.arange(group_share, dtype=jnp.int32))  10.7 us
  transfers between devices with their start and end apart: 5, of which 2 were waited for; matrix products, arithmetic and copies ran while one was open for 3% of the time, Pallas kernels for 0%

commit v1 on v0

v1 whole, which is shorter than its diff:
```python
import functools
import math

import jax
import jax.numpy as jnp
from jax import lax
from jax.experimental import pallas as pl
from jax.experimental.pallas import tpu as pltpu
from jax.sharding import PartitionSpec as P

QUERY_HEADS = 64
KEY_VALUE_HEADS = 8
HEAD_SIZE = 128
SINK = 128
WIN = 512
BLK = 64
VB = 6
NSL = 4
MAX_RETRIEVERS = 4


def shifted(block, axis, distance):
    devices = range(lax.axis_size(axis))
    route = [((i - distance) % len(devices), i) for i in devices]
    return lax.ppermute(block, axis, route)


def attend_kernel(roles_ref, slot_ref, count_ref, diag_ref,
                  q_ref, prev_ref, own_ref, vk_ref, vv_ref, sk_ref, sv_ref, o_ref):
    h = pl.program_id(0)
    rows = q_ref.shape[0]
    scaling = 1.0 / math.sqrt(HEAD_SIZE)
    q = q_ref[...]
    dims = (((1,), (1,)), ((), ()))

    def scores(keys):
        return lax.dot_general(q, keys, dims, preferred_element_type=jnp.float32) * scaling

    s_prev = scores(prev_ref[0])
    s_own = scores(own_ref[0])
    row = lax.broadcasted_iota(jnp.int32, (rows, rows), 0)
    col = lax.broadcasted_iota(jnp.int32, (rows, rows), 1)

    def finish(s_side, ok_side, v_side, ok_prev, ok_own):
        neg = -jnp.inf
        m_side = jnp.max(jnp.where(ok_side, s_side, neg), axis=1, keepdims=True)
        m_prev = jnp.max(jnp.where(ok_prev, s_prev, neg), axis=1, keepdims=True)
        m_own = jnp.max(jnp.where(ok_own, s_own, neg), axis=1, keepdims=True)
        m = jnp.maximum(jnp.maximum(m_side, m_prev), m_own)
        e_side = jnp.where(ok_side, jnp.exp(s_side - m), 0.0)
        e_prev = jnp.where(ok_prev, jnp.exp(s_prev - m), 0.0)
        e_own = jnp.where(ok_own, jnp.exp(s_own - m), 0.0)
        total = (jnp.sum(e_side, axis=1, keepdims=True)
                 + jnp.sum(e_prev, axis=1, keepdims=True)
                 + jnp.sum(e_own, axis=1, keepdims=True))
        p_side = (e_side / total).astype(jnp.bfloat16)
        p_prev = (e_prev / total).astype(jnp.bfloat16)
        p_own = (e_own / total).astype(jnp.bfloat16)
        out = jnp.dot(p_side, v_side, preferred_element_type=jnp.float32)
        out = out + jnp.dot(p_prev, prev_ref[1], preferred_element_type=jnp.float32)
        out = out + jnp.dot(p_own, own_ref[1], preferred_element_type=jnp.float32)
        o_ref[...] = out.astype(o_ref.dtype)

    @pl.when(roles_ref[h] != 1)
    def _():
        s_side = scores(sk_ref[...])
        ok_side = jnp.ones(s_side.shape, jnp.bool_)
        finish(s_side, ok_side, sv_ref[...], col > row, col <= row)

    @pl.when(roles_ref[h] == 1)
    def _():
        s_side = scores(vk_ref[...])
        side_col = lax.broadcasted_iota(jnp.int32, s_side.shape, 1)
        ok_side = side_col // BLK < count_ref[h]
        rel_prev = row // BLK + rows // BLK - col // BLK
        rel_own = row // BLK - col // BLK
        ok_prev = jnp.zeros((rows, rows), jnp.bool_)
        ok_own = jnp.zeros((rows, rows), jnp.bool_)
        for d in range(NSL):
            off = diag_ref[h * NSL + d]
            ok_prev = ok_prev | (rel_prev == off)
            ok_own = ok_own | ((rel_own == off) & ((off > 0) | (col <= row)))
        finish(s_side, ok_side, vv_ref[...], ok_prev, ok_own)


def attend(roles_l, slot_l, count_l, diag_l, q_local, prev_kv, own_kv, side):
    rows = q_local.shape[0]
    heads = q_local.shape[1] // HEAD_SIZE
    vrows = VB * BLK
    sink_block = MAX_RETRIEVERS * vrows // SINK
    grid_spec = pltpu.PrefetchScalarGridSpec(
        num_scalar_prefetch=4,
        grid=(heads,),
        in_specs=[
            pl.BlockSpec((rows, HEAD_SIZE), lambda h, *_: (0, h)),
            pl.BlockSpec((2, rows, HEAD_SIZE), lambda h, *_: (0, 0, 0)),
            pl.BlockSpec((2, rows, HEAD_SIZE), lambda h, *_: (0, 0, 0)),
            pl.BlockSpec((None, vrows, HEAD_SIZE), lambda h, r, s, *_: (0, s[h], 0)),
            pl.BlockSpec((None, vrows, HEAD_SIZE), lambda h, r, s, *_: (1, s[h], 0)),
            pl.BlockSpec((None, SINK, HEAD_SIZE), lambda h, *_: (0, sink_block, 0)),
            pl.BlockSpec((None, SINK, HEAD_SIZE), lambda h, *_: (1, sink_block, 0)),
        ],
        out_specs=pl.BlockSpec((rows, HEAD_SIZE), lambda h, *_: (0, h)),
    )
    return pl.pallas_call(
        attend_kernel,
        grid_spec=grid_spec,
        out_shape=jax.ShapeDtypeStruct(q_local.shape, jnp.bfloat16),
    )(roles_l, slot_l, count_l, diag_l, q_local, prev_kv, own_kv, side, side, side, side)


def shards(queries, keys, values, prefix_keys, prefix_values, roles, columns, col_count, diagonals):
    seq_devices = lax.axis_size("seq")
    my_seq = lax.axis_index("seq")
    cache_rows = prefix_keys.shape[0]
    blocks_dev = cache_rows // BLK
    heads = roles.shape[0]

    is_ret = roles == 1
    slot = jnp.cumsum(is_ret.astype(jnp.int32)) - 1
    match = is_ret[None, :] & (slot[None, :] == jnp.arange(MAX_RETRIEVERS, dtype=jnp.int32)[:, None])
    head_of_slot = jnp.argmax(match, axis=1)
    cols_s = columns[head_of_slot]
    owner = cols_s // blocks_dev
    local_block = cols_s - owner * blocks_dev
    mine = (owner == my_seq)[:, :, None, None]
    kv_blocks = jnp.stack([prefix_keys, prefix_values], 0).reshape(2, blocks_dev, BLK, HEAD_SIZE)
    pieces = kv_blocks[:, local_block]
    pieces = jnp.where(mine[None], pieces, jnp.zeros_like(pieces))
    pieces = pieces.reshape(2, MAX_RETRIEVERS * VB * BLK, HEAD_SIZE)
    sink = jnp.stack([prefix_keys[:SINK], prefix_values[:SINK]], 0)
    sink = jnp.where(my_seq == 0, sink, jnp.zeros_like(sink))
    side = lax.psum(jnp.concatenate([pieces, sink], 1), "seq")

    q_local = lax.all_to_all(queries, "head", split_axis=1, concat_axis=0, tiled=True)
    kv = jnp.stack([keys, values], 0)
    kv_local = lax.all_to_all(kv, "head", split_axis=2, concat_axis=1, tiled=True)
    tail_cache = jnp.stack([prefix_keys[cache_rows - WIN:], prefix_values[cache_rows - WIN:]], 0)
    outgoing = jnp.where(my_seq == seq_devices - 1, tail_cache, kv_local)
    prev_kv = shifted(outgoing, "seq", 1)

    slot_l = jnp.where(is_ret, slot, 0).astype(jnp.int32)
    return attend(
        roles.astype(jnp.int32),
        slot_l,
        col_count.astype(jnp.int32),
        diagonals.reshape(heads * NSL).astype(jnp.int32),
        q_local,
        prev_kv,
        kv_local,
        side,
    )


def solution(mesh):
    placed = (
        P(("seq", "head"), None),
        P(("seq", "head"), None),
        P(("seq", "head"), None),
        P("seq", "head"),
        P("seq", "head"),
        P("head"),
        P("head", None),
        P("head"),
        P("head", None),
    )
    return jax.shard_map(
        shards, mesh=mesh, in_specs=placed, out_specs=P("seq", "head"), check_vma=False
    )
```

time: 519 us -> 333 us (0.64)
  the two profiles are of different devices: /device:TPU:1 before, /device:TPU:6 now
where the time goes in v1:
time: 333 us; the launch traced here: 332 us
  waiting for transfers between devices  274 us (82%)
  Pallas kernels  21.4 us (6%)
  between operations  13.6 us (4%)
  starting transfers between devices  11.9 us (4%)
  local copies, waits for them, and re-layouts  7.14 us (2%)
  other arithmetic  3.85 us (1%)
    psum x1, waiting for transfers between devices, shards(): side = lax.psum(jnp.concatenate([pieces, sink], 1), 'seq')  258 us
    pallas_call x1, Pallas kernels, attend(): pl.pallas_call(attend_kernel, grid_spec=grid_spec, out_shape=jax.ShapeDty...  21.4 us
    ppermute x1, waiting for transfers between devices, shifted(): return lax.ppermute(block, axis, route)  13.3 us
  transfers between devices with their start and end apart: 4, of which 3 were waited for; matrix products, arithmetic and copies ran while one was open for 2% of the time, Pallas kernels for 0%

profile of v1, /device:TPU:6, one launch (start us, length us, event | category | flops | bytes accessed | tf_op | source)
XLA Modules:
  0.0 332.1 jit_solution(5196278766450320241)
XLA Ops:
  6.5 0.0 copy-start
  6.5 1.0 pad_maximum_fusion.2
  7.5 0.0 copy-start.8
  7.6 0.0 copy-start.3
  7.6 0.4 copy.31
  8.0 1.1 reshape.140
  9.1 4.5 %all-to-all-start.1 = ((bf16[8,2,8192]{2,1,0:T(2,128)(2,1)}), bf16[8,2,8192]{2,1,0:T(2,128)(2,1)S(1)}, u32[]{:S(2)}, u32[]{:S(2)}) async-start(bf16[8,2,8192]{2,1,0:T(2,128)(2,1)} %reshape.140), calls=%async_computation.1 | async-start | bytes 524288 | tf_op jit(solution)/shard_map/all_to_all | solution.py:137
  13.5 0.0 copy-done.8
  13.6 0.2 reduce-window.7
  13.7 0.6 iota_reduce_fusion
  14.4 0.0 copy-done
  14.4 0.6 gather_fusion
  15.0 0.1 reshape.132
  15.1 0.1 broadcast_in_dim.31
  15.2 0.1 broadcast_in_dim.32
  15.3 0.0 copy-done.3
  15.3 0.0 copy-start.4
  15.3 0.0 copy-start.5
  15.3 1.1 copy.36
  16.3 0.1 copy-done.4
  16.4 0.4 copy-done.5
  16.8 0.1 pad_maximum_fusion
  16.9 0.7 gather_fusion.1
  17.6 0.1 copy.33
  17.7 0.3 bitcast_select_fusion
  18.0 3.0 all-to-all-done.1
  21.1 3.6 %all-to-all-start = ((bf16[64,8,1024]{2,0,1:T(8,128)(2,1)}), bf16[64,8,1024]{2,0,1:T(8,128)(2,1)S(1)}, u32[]{:S(2)}, u32[]{:S(2)}) async-start(bf16[64,8,1024]{2,0,1:T(8,128)(2,1)} %bitcast.60), calls=%async_computation | async-start | bytes 2097152 | tf_op jit(solution)/shard_map/all_to_all | solution.py:135
  24.6 0.0 all-reduce.2.cloned.1.call-start
  24.7 1.0 pad_maximum_fusion.1
  25.7 0.0 all-reduce.2.cloned.1.call-update
  25.7 0.0 copy-start.7
  25.7 0.3 reshape.141
  26.1 0.4 copy.32
  26.5 0.0 copy-start.2
  26.5 0.1 maximum_select_fusion
  26.6 3.8 %collective-permute-start = (bf16[2,512,128]{2,1,0:T(8,128)(2,1)S(1)}, bf16[2,512,128]{2,1,0:T(8,128)(2,1)S(1)}, u32[]{:S(2)}, u32[]{:S(2)}) collective-permute-start(bf16[2,512,128]{2,1,0:T(8,128)(2,1)S(1)} %maximum_select_fusion), channel_id=1, source_target_pairs={{504,0},{0,8},{8,16},{16,24},{24,32},{32,40},{40,48},{48,56},{56,6... | collective-permute-start | bytes 786440 | tf_op jit(solution)/shard_map/ppermute | solution.py:25
  30.4 0.0 copy-done.7
  30.4 0.1 copy.29
  30.5 0.7 reshape.120.diag_ref
  31.2 0.6 broadcast_select_fusion.slot_ref
  31.7 13.3 %collective-permute-done.prev_ref = bf16[2,512,128]{2,1,0:T(8,128)(2,1)S(1)} collective-permute-done((bf16[2,512,128]{2,1,0:T(8,128)(2,1)S(1)}, bf16[2,512,128]{2,1,0:T(8,128)(2,1)S(1)}, u32[]{:S(2)}, u32[]{:S(2)}) %collective-permute-start) | collective-permute-done | bytes 262176 | tf_op jit(solution)/shard_map/ppermute | solution.py:25
  45.1 0.0 copy-start.6
  45.1 257.8 %all-reduce.2.cloned.1.call-done.vk_ref.vv_ref.sk_ref.sv_ref = bf16[2,1664,128]{2,1,0:T(8,128)(2,1)} async-done(((bf16[2,1664,128]{2,1,0:T(8,128)(2,1)}), bf16[2,1664,128]{2,1,0:T(8,128)(2,1)}) %all-reduce.2.cloned.1.call-update) | async-done | bytes 851984 | tf_op jit(solution)/shard_map/psum | solution.py:133
  302.9 0.0 all-to-all-done
  302.9 0.0 copy-start.1
  302.9 0.0 copy-done.2
  302.9 0.0 copy-done.6
  302.9 1.0 copy-done.1
  303.8 21.4 %shard_map.91 = bf16[512,1024]{1,0:T(8,128)(2,1)} custom-call(s32[8]{0:T(128)} %roles_ref.1, s32[8]{0:T(128)} %broadcast_select_fusion.slot_ref, s32[8]{0:T(128)} %count_ref.1, s32[32]{0:T(128)} %reshape.120.diag_ref, bf16[512,1024]{1,0:T(8,128)(2,1)} %bitcast.61, bf16[2,512,128]{2,1,0:T(8,128)(2,1)} %copy-done.6, bf16[2,512,128]{2,1,0:T(8,128)(2,1)} %bitcast.62, ...), custom_call_target="tpu_custom_call" | custom-call | tf_op jit(solution)/shard_map/pallas_call | solution.py:105
  (10 shorter events, 0.1 us)
Async XLA Ops:
  6.5 7.9 %copy-start = (s32[8,6]{1,0:T(8,128)S(1)}, s32[8,6]{1,0:T(8,128)}, u32[]{:S(2)}) copy-start(s32[8,6]{1,0:T(8,128)} %param.15) | copy-start | bytes 580
  7.5 6.0 %copy-start.8 = (s32[8]{0:T(128)S(1)}, s32[8]{0:T(128)}, u32[]{:S(2)}) copy-start(s32[8]{0:T(128)} %roles_ref.1) | copy-start | bytes 100
  7.6 7.7 %copy-start.3 = (bf16[64,8192]{1,0:T(8,128)(2,1)S(1)}, bf16[64,8192]{1,0:T(8,128)(2,1)}, u32[]{:S(2)}) copy-start(bf16[64,8192]{1,0:T(8,128)(2,1)} %param.9) | copy-start | bytes 3145732
  9.1 12.0 %all-to-all-start.1 = ((bf16[8,2,8192]{2,1,0:T(2,128)(2,1)}), bf16[8,2,8192]{2,1,0:T(2,128)(2,1)S(1)}, u32[]{:S(2)}, u32[]{:S(2)}) async-start(bf16[8,2,8192]{2,1,0:T(2,128)(2,1)} %reshape.140), calls=%async_computation.1 | async-start | bytes 524288 | tf_op jit(solution)/shard_map/all_to_all | solution.py:137
  15.3 1.1 copy-start.4
  15.3 1.6 copy-start.5
  21.1 281.8 %all-to-all-start = ((bf16[64,8,1024]{2,0,1:T(8,128)(2,1)}), bf16[64,8,1024]{2,0,1:T(8,128)(2,1)S(1)}, u32[]{:S(2)}, u32[]{:S(2)}) async-start(bf16[64,8,1024]{2,0,1:T(8,128)(2,1)} %bitcast.60), calls=%async_computation | async-start | bytes 2097152 | tf_op jit(solution)/shard_map/all_to_all | solution.py:135
  24.6 278.2 %all-reduce.2.cloned.1.call-start = ((), (), s32[]{:S(2)}) async-start(), calls=%async_computation.2 | async-start | bytes 1703936 | tf_op jit(solution)/shard_map/psum | solution.py:133
  25.7 4.7 %copy-start.7 = (s32[8,4]{0,1:T(4,128)S(1)}, s32[8,4]{0,1:T(4,128)}, u32[]{:S(2)}) copy-start(s32[8,4]{0,1:T(4,128)} %param.17) | copy-start | bytes 388
  26.5 276.4 %copy-start.2 = (bf16[2,64,8,128]{3,1,2,0:T(8,128)(2,1)}, bf16[2,64,8,128]{3,1,2,0:T(8,128)(2,1)S(1)}, u32[]{:S(2)}) copy-start(bf16[2,64,8,128]{3,1,2,0:T(8,128)(2,1)S(1)} %copy.32) | copy-start | bytes 786436
  26.6 18.5 %collective-permute-start = (bf16[2,512,128]{2,1,0:T(8,128)(2,1)S(1)}, bf16[2,512,128]{2,1,0:T(8,128)(2,1)S(1)}, u32[]{:S(2)}, u32[]{:S(2)}) collective-permute-start(bf16[2,512,128]{2,1,0:T(8,128)(2,1)S(1)} %maximum_select_fusion), channel_id=1, source_target_pairs={{504,0},{0,8},{8,16},{16,24},{24,32},{32,40},{40,48},{48,56},{56,6... | collective-permute-start | bytes 786440 | tf_op jit(solution)/shard_map/ppermute | solution.py:25
  45.1 257.8 %copy-start.6 = (bf16[2,512,128]{2,1,0:T(8,128)(2,1)}, bf16[2,512,128]{2,1,0:T(8,128)(2,1)S(1)}, u32[]{:S(2)}) copy-start(bf16[2,512,128]{2,1,0:T(8,128)(2,1)S(1)} %collective-permute-done.prev_ref) | copy-start | bytes 786436
  302.9 1.0 copy-start.1
Sparse Core Ops, SparseCore 0:
  28.9 273.9 all-reduce.1

commit v2 on v1

--- a/solution.py
+++ b/solution.py
@@ -109,6 +109,14 @@
     )(roles_l, slot_l, count_l, diag_l, q_local, prev_kv, own_kv, side, side, side, side)
 
 
+def sum_over_seq(block, seq_devices):
+    flat = block.reshape(seq_devices, -1)
+    mine = lax.all_to_all(flat, "seq", 0, 0, tiled=True)
+    total = jnp.sum(mine.astype(jnp.float32), 0, keepdims=True).astype(block.dtype)
+    every = lax.all_to_all(jnp.broadcast_to(total, flat.shape), "seq", 0, 0, tiled=True)
+    return every.reshape(block.shape)
+
+
 def shards(queries, keys, values, prefix_keys, prefix_values, roles, columns, col_count, diagonals):
     seq_devices = lax.axis_size("seq")
     my_seq = lax.axis_index("seq")
@@ -130,7 +138,7 @@
     pieces = pieces.reshape(2, MAX_RETRIEVERS * VB * BLK, HEAD_SIZE)
     sink = jnp.stack([prefix_keys[:SINK], prefix_values[:SINK]], 0)
     sink = jnp.where(my_seq == 0, sink, jnp.zeros_like(sink))
-    side = lax.psum(jnp.concatenate([pieces, sink], 1), "seq")
+    side = sum_over_seq(jnp.concatenate([pieces, sink], 1), seq_devices)
 
     q_local = lax.all_to_all(queries, "head", split_axis=1, concat_axis=0, tiled=True)
     kv = jnp.stack([keys, values], 0)

time: 333 us -> 196 us (0.59)
  the two profiles are of different devices: /device:TPU:6 before, /device:TPU:14 now
where the time goes in v2:
time: 196 us; the launch traced here: 195 us
  waiting for transfers between devices  88.9 us (45%)
  starting transfers between devices  38.6 us (20%)
  other arithmetic  23.9 us (12%)
  local copies, waits for them, and re-layouts  22.2 us (11%)
  Pallas kernels  21.4 us (11%)
    all_to_all x1, waiting for transfers between devices, sum_over_seq(): lax.all_to_all(jnp.broadcast_to(total, flat.shape), 'seq', 0, 0, tiled=True)  44.8 us
    all_to_all x1, waiting for transfers between devices, sum_over_seq(): mine = lax.all_to_all(flat, 'seq', 0, 0, tiled=True)  44 us
    pallas_call x1, Pallas kernels, attend(): pl.pallas_call(attend_kernel, grid_spec=grid_spec, out_shape=jax.ShapeDty...  21.4 us
    all_to_all x1, starting transfers between devices, sum_over_seq(): mine = lax.all_to_all(flat, 'seq', 0, 0, tiled=True)  18.8 us
    unnamed x27, local copies, waits for them, and re-layouts  11.6 us
    all_to_all x1, starting transfers between devices, sum_over_seq(): lax.all_to_all(jnp.broadcast_to(total, flat.shape), 'seq', 0, 0, tiled=True)  6.75 us
    all_to_all x1, other arithmetic, sum_over_seq(): lax.all_to_all(jnp.broadcast_to(total, flat.shape), 'seq', 0, 0, tiled=True)  6.27 us
    broadcast_in_dim x1, other arithmetic, sum_over_seq(): jnp.broadcast_to(total, flat.shape)  6.05 us
  transfers between devices with their start and end apart: 5, of which 2 were waited for; matrix products, arithmetic and copies ran while one was open for 16% of the time, Pallas kernels for 0%

profile of v2, /device:TPU:14, one launch (start us, length us, event | category | flops | bytes accessed | tf_op | source)
XLA Modules:
  0.0 195.2 jit_solution(9340225186379363263)
XLA Ops:
  0.0 0.0 copy-start
  0.0 0.7 broadcast_compare_fusion
  0.7 0.2 reduce-window.7
  0.9 0.6 iota_reduce_fusion
  1.5 0.0 copy-done
  1.5 0.6 gather_fusion
  2.1 0.1 broadcast_in_dim.37
  2.2 0.1 broadcast_in_dim.38
  2.3 0.1 reshape.151
  2.4 0.8 slice_bitcast_fusion.2
  3.2 1.3 pad_maximum_fusion
  4.5 0.7 gather_fusion.1
  5.2 0.1 copy.37
  5.2 0.3 bitcast_select_fusion
  5.5 0.1 pad_maximum_fusion.1
  5.6 0.4 all_to_all.48
  6.0 0.6 broadcast.169
  6.6 6.0 %reduce.22 = bf16[64,6656]{1,0:T(8,128)(2,1)S(1)} reduce(bf16[64,1,6656]{2,1,0:T(2,128)(2,1)S(1)} %all_to_all.48, bf16[]{:T(256)} %broadcast.169), dimensions={1}, to_apply=%all_to_all.48.reduce_sub_computation | reduce | bytes 1703938 | tf_op jit(solution)/shard_map/all_to_all | solution.py:114
  12.7 0.0 copy-start.6
  12.7 0.0 copy-start.7
  12.7 1.1 reshape.162
  13.8 18.8 %all-to-all-start.2 = ((bf16[64,2,3328]{2,1,0:T(2,128)(2,1)}), bf16[64,2,3328]{2,1,0:T(2,128)(2,1)S(1)}, u32[]{:S(2)}, u32[]{:S(2)}) async-start(bf16[64,2,3328]{2,1,0:T(2,128)(2,1)} %reshape.162), calls=%async_computation.2 | async-start | bytes 1703936 | tf_op jit(solution)/shard_map/all_to_all | solution.py:114
  32.6 0.0 copy-done.6
  32.6 0.0 copy-done.7
  32.6 0.4 copy.35
  33.0 1.1 reshape.160
  34.1 44.0 %all-to-all-done.2 = bf16[64,2,3328]{2,1,0:T(2,128)(2,1)S(1)} async-done(((bf16[64,2,3328]{2,1,0:T(2,128)(2,1)}), bf16[64,2,3328]{2,1,0:T(2,128)(2,1)S(1)}, u32[]{:S(2)}, u32[]{:S(2)}) %all-to-all-start.2) | async-done | bytes 852000 | tf_op jit(solution)/shard_map/all_to_all | solution.py:114
  78.2 4.9 %all-to-all-start.1 = ((bf16[8,2,8192]{2,1,0:T(2,128)(2,1)}), bf16[8,2,8192]{2,1,0:T(2,128)(2,1)S(1)}, u32[]{:S(2)}, u32[]{:S(2)}) async-start(bf16[8,2,8192]{2,1,0:T(2,128)(2,1)} %reshape.160), calls=%async_computation.1 | async-start | bytes 524288 | tf_op jit(solution)/shard_map/all_to_all | solution.py:145
  83.1 0.7 reshape.163
  83.8 1.6 reduce_sum.12
  85.4 0.9 broadcast_in_dim.42
  86.3 6.0 %reduce.23 = bf16[64,6656]{1,0:T(8,128)(2,1)S(1)} reduce(bf16[64,1,6656]{2,1,0:T(2,128)(2,1)S(1)} %broadcast_in_dim.42, bf16[]{:T(256)} %broadcast.169), dimensions={1}, to_apply=%broadcast_in_dim.42.reduce_sub_computation | reduce | bytes 1703938 | tf_op jit(solution)/shard_map/broadcast_in_dim | solution.py:116
  92.3 1.1 reshape.164
  93.4 0.0 copy-start.4
  93.4 0.0 all-to-all-done.1
  93.4 6.7 %all-to-all-start.3 = ((bf16[64,2,3328]{2,1,0:T(2,128)(2,1)}), bf16[64,2,3328]{2,1,0:T(2,128)(2,1)S(1)}, u32[]{:S(2)}, u32[]{:S(2)}) async-start(bf16[64,2,3328]{2,1,0:T(2,128)(2,1)} %reshape.164), calls=%async_computation.3 | async-start | bytes 1703936 | tf_op jit(solution)/shard_map/all_to_all | solution.py:116
  100.2 0.0 copy-done.4
  100.2 1.1 copy.41
  101.3 44.8 %all-to-all-done.3 = bf16[64,2,3328]{2,1,0:T(2,128)(2,1)S(1)} async-done(((bf16[64,2,3328]{2,1,0:T(2,128)(2,1)}), bf16[64,2,3328]{2,1,0:T(2,128)(2,1)S(1)}, u32[]{:S(2)}, u32[]{:S(2)}) %all-to-all-start.3) | async-done | bytes 852000 | tf_op jit(solution)/shard_map/all_to_all | solution.py:116
  146.1 0.0 copy-start.2
  146.1 0.9 copy-done.2
  147.0 4.8 %all-to-all-start = ((bf16[64,8,1024]{2,0,1:T(8,128)(2,1)}), bf16[64,8,1024]{2,0,1:T(8,128)(2,1)S(1)}, u32[]{:S(2)}, u32[]{:S(2)}) async-start(bf16[64,8,1024]{2,0,1:T(8,128)(2,1)} %bitcast.59), calls=%async_computation | async-start | bytes 2097152 | tf_op jit(solution)/shard_map/all_to_all | solution.py:143
  151.8 0.0 copy-start.8
  151.8 1.0 slice_bitcast_fusion
  152.8 0.3 reshape.161
  153.2 0.4 copy.36
  153.6 0.0 copy-start.3
  153.6 0.1 maximum_select_fusion
  153.7 3.3 %collective-permute-start = (bf16[2,512,128]{2,1,0:T(8,128)(2,1)S(1)}, bf16[2,512,128]{2,1,0:T(8,128)(2,1)S(1)}, u32[]{:S(2)}, u32[]{:S(2)}) collective-permute-start(bf16[2,512,128]{2,1,0:T(8,128)(2,1)S(1)} %maximum_select_fusion), channel_id=1, source_target_pairs={{504,0},{0,8},{8,16},{16,24},{24,32},{32,40},{40,48},{48,56},{56,6... | collective-permute-start | bytes 786440 | tf_op jit(solution)/shard_map/ppermute | solution.py:25
  157.0 0.0 copy-done.8
  157.0 0.1 copy.33
  157.1 0.6 reshape.138.diag_ref
  157.7 0.0 copy-done.9
  157.7 0.6 broadcast_select_fusion.slot_ref
  158.2 5.2 %reshape.165 = bf16[64,1,6656]{2,1,0:T(2,128)(2,1)S(1)} reshape(bf16[64,2,3328]{2,1,0:T(2,128)(2,1)} %copy-done.2) | data formatting | bytes 1703936
  163.5 6.3 %reduce.20 = bf16[64,6656]{1,0:T(8,128)(2,1)} reduce(bf16[64,1,6656]{2,1,0:T(2,128)(2,1)S(1)} %reshape.165, bf16[]{:T(256)} %constant.49), dimensions={1}, to_apply=%all_to_all.47.reduce_sub_computation | reduce | bytes 1703938 | tf_op jit(solution)/shard_map/all_to_all | solution.py:116
  169.7 0.0 copy-done.3
  169.7 2.9 %reshape.139.vk_ref.vv_ref.sk_ref.sv_ref = bf16[2,1664,128]{2,1,0:T(8,128)(2,1)} reshape(bf16[64,6656]{1,0:T(8,128)(2,1)} %reduce.20) | data formatting | bytes 1703936 | tf_op jit(solution)/shard_map/reshape | solution.py:117
  172.7 0.0 collective-permute-done.prev_ref
  172.7 0.0 all-to-all-done
  172.7 0.0 copy-start.1
  172.7 0.7 copy-done.5
  173.4 0.4 copy-done.1
  173.8 21.4 %shard_map.91 = bf16[512,1024]{1,0:T(8,128)(2,1)} custom-call(s32[8]{0:T(128)} %roles_ref.1, s32[8]{0:T(128)} %broadcast_select_fusion.slot_ref, s32[8]{0:T(128)} %count_ref.1, s32[32]{0:T(128)} %reshape.138.diag_ref, bf16[512,1024]{1,0:T(8,128)(2,1)} %bitcast.60, bf16[2,512,128]{2,1,0:T(8,128)(2,1)} %copy-done.5, bf16[2,512,128]{2,1,0:T(8,128)(2,1)} %bitcast.62, ...), custom_call_target="tpu_custom_call" | custom-call | tf_op jit(solution)/shard_map/pallas_call | solution.py:105
  (10 shorter events, 0.1 us)
Async XLA Ops:
  0.0 1.5 copy-start
  12.7 19.9 %copy-start.6 = (bf16[64,1024]{1,0:T(8,128)(2,1)S(1)}, bf16[64,1024]{1,0:T(8,128)(2,1)}, u32[]{:S(2)}) copy-start(bf16[64,1024]{1,0:T(8,128)(2,1)} %param.11) | copy-start | bytes 393220
  12.7 19.9 %copy-start.7 = (bf16[64,1024]{1,0:T(8,128)(2,1)S(1)}, bf16[64,1024]{1,0:T(8,128)(2,1)}, u32[]{:S(2)}) copy-start(bf16[64,1024]{1,0:T(8,128)(2,1)} %param.10) | copy-start | bytes 393220
  13.8 64.4 %all-to-all-start.2 = ((bf16[64,2,3328]{2,1,0:T(2,128)(2,1)}), bf16[64,2,3328]{2,1,0:T(2,128)(2,1)S(1)}, u32[]{:S(2)}, u32[]{:S(2)}) async-start(bf16[64,2,3328]{2,1,0:T(2,128)(2,1)} %reshape.162), calls=%async_computation.2 | async-start | bytes 1703936 | tf_op jit(solution)/shard_map/all_to_all | solution.py:114
  78.2 15.3 %all-to-all-start.1 = ((bf16[8,2,8192]{2,1,0:T(2,128)(2,1)}), bf16[8,2,8192]{2,1,0:T(2,128)(2,1)S(1)}, u32[]{:S(2)}, u32[]{:S(2)}) async-start(bf16[8,2,8192]{2,1,0:T(2,128)(2,1)} %reshape.160), calls=%async_computation.1 | async-start | bytes 524288 | tf_op jit(solution)/shard_map/all_to_all | solution.py:145
  93.4 6.8 %copy-start.4 = (bf16[64,8192]{1,0:T(8,128)(2,1)S(1)}, bf16[64,8192]{1,0:T(8,128)(2,1)}, u32[]{:S(2)}) copy-start(bf16[64,8192]{1,0:T(8,128)(2,1)} %param.9) | copy-start | bytes 3145732
  93.4 52.6 %all-to-all-start.3 = ((bf16[64,2,3328]{2,1,0:T(2,128)(2,1)}), bf16[64,2,3328]{2,1,0:T(2,128)(2,1)S(1)}, u32[]{:S(2)}, u32[]{:S(2)}) async-start(bf16[64,2,3328]{2,1,0:T(2,128)(2,1)} %reshape.164), calls=%async_computation.3 | async-start | bytes 1703936 | tf_op jit(solution)/shard_map/all_to_all | solution.py:116
  146.1 0.9 copy-start.2
  147.0 25.7 %all-to-all-start = ((bf16[64,8,1024]{2,0,1:T(8,128)(2,1)}), bf16[64,8,1024]{2,0,1:T(8,128)(2,1)S(1)}, u32[]{:S(2)}, u32[]{:S(2)}) async-start(bf16[64,8,1024]{2,0,1:T(8,128)(2,1)} %bitcast.59), calls=%async_computation | async-start | bytes 2097152 | tf_op jit(solution)/shard_map/all_to_all | solution.py:143
  151.8 5.2 %copy-start.8 = (s32[8,4]{0,1:T(4,128)S(1)}, s32[8,4]{0,1:T(4,128)}, u32[]{:S(2)}) copy-start(s32[8,4]{0,1:T(4,128)} %param.17) | copy-start | bytes 388
  151.8 5.8 %copy-start.9 = (s32[8]{0:T(128)S(1)}, s32[8]{0:T(128)}, u32[]{:S(2)}) copy-start(s32[8]{0:T(128)} %roles_ref.1) | copy-start | bytes 100
  153.6 16.1 %copy-start.3 = (bf16[2,64,8,128]{3,1,2,0:T(8,128)(2,1)}, bf16[2,64,8,128]{3,1,2,0:T(8,128)(2,1)S(1)}, u32[]{:S(2)}) copy-start(bf16[2,64,8,128]{3,1,2,0:T(8,128)(2,1)S(1)} %copy.36) | copy-start | bytes 786436
  153.7 19.0 %collective-permute-start = (bf16[2,512,128]{2,1,0:T(8,128)(2,1)S(1)}, bf16[2,512,128]{2,1,0:T(8,128)(2,1)S(1)}, u32[]{:S(2)}, u32[]{:S(2)}) collective-permute-start(bf16[2,512,128]{2,1,0:T(8,128)(2,1)S(1)} %maximum_select_fusion), channel_id=1, source_target_pairs={{504,0},{0,8},{8,16},{16,24},{24,32},{32,40},{40,48},{48,56},{56,6... | collective-permute-start | bytes 786440 | tf_op jit(solution)/shard_map/ppermute | solution.py:25
  172.7 0.7 copy-start.5
  172.7 1.1 copy-start.1

commit v3 on v2

--- a/solution.py
+++ b/solution.py
@@ -110,7 +110,7 @@
 
 
 def sum_over_seq(block, seq_devices):
-    flat = block.reshape(seq_devices, -1)
+    flat = block.reshape(seq_devices, -1, block.shape[-1])
     mine = lax.all_to_all(flat, "seq", 0, 0, tiled=True)
     total = jnp.sum(mine.astype(jnp.float32), 0, keepdims=True).astype(block.dtype)
     every = lax.all_to_all(jnp.broadcast_to(total, flat.shape), "seq", 0, 0, tiled=True)
@@ -138,14 +138,16 @@
     pieces = pieces.reshape(2, MAX_RETRIEVERS * VB * BLK, HEAD_SIZE)
     sink = jnp.stack([prefix_keys[:SINK], prefix_values[:SINK]], 0)
     sink = jnp.where(my_seq == 0, sink, jnp.zeros_like(sink))
-    side = sum_over_seq(jnp.concatenate([pieces, sink], 1), seq_devices)
+    both = jnp.concatenate([pieces, sink], 1)
 
-    q_local = lax.all_to_all(queries, "head", split_axis=1, concat_axis=0, tiled=True)
     kv = jnp.stack([keys, values], 0)
     kv_local = lax.all_to_all(kv, "head", split_axis=2, concat_axis=1, tiled=True)
     tail_cache = jnp.stack([prefix_keys[cache_rows - WIN:], prefix_values[cache_rows - WIN:]], 0)
     outgoing = jnp.where(my_seq == seq_devices - 1, tail_cache, kv_local)
     prev_kv = shifted(outgoing, "seq", 1)
+    both, kv_local = lax.optimization_barrier((both, kv_local))
+    side = sum_over_seq(both, seq_devices)
+    q_local = lax.all_to_all(queries, "head", split_axis=1, concat_axis=0, tiled=True)
 
     slot_l = jnp.where(is_ret, slot, 0).astype(jnp.int32)
     return attend(

time: 196 us -> 181 us (0.923)
  the two profiles are of different devices: /device:TPU:14 before, /device:TPU:6 now
where the time goes in v3:
time: 181 us; the launch traced here: 178 us
  blocking collectives  66.4 us (37%)
  waiting for transfers between devices  61.7 us (34%)
  Pallas kernels  19.9 us (11%)
  starting transfers between devices  18.2 us (10%)
  local copies, waits for them, and re-layouts  8.91 us (5%)
  other arithmetic  3.14 us (2%)
    all_to_all x1, blocking collectives, sum_over_seq(): mine = lax.all_to_all(flat, 'seq', 0, 0, tiled=True)  66.4 us
    all_to_all x1, waiting for transfers between devices, sum_over_seq(): lax.all_to_all(jnp.broadcast_to(total, flat.shape), 'seq', 0, 0, tiled=True)  47 us
    pallas_call x1, Pallas kernels, attend(): pl.pallas_call(attend_kernel, grid_spec=grid_spec, out_shape=jax.ShapeDty...  19.9 us
    ppermute x1, waiting for transfers between devices, shifted(): return lax.ppermute(block, axis, route)  7 us
    all_to_all x1, starting transfers between devices, sum_over_seq(): lax.all_to_all(jnp.broadcast_to(total, flat.shape), 'seq', 0, 0, tiled=True)  6.94 us
    all_to_all x1, waiting for transfers between devices, shards(): lax.all_to_all(kv, 'head', split_axis=2, concat_axis=1, tiled=True)  4.48 us
    all_to_all x1, starting transfers between devices, shards(): lax.all_to_all(kv, 'head', split_axis=2, concat_axis=1, tiled=True)  4.47 us
  transfers between devices with their start and end apart: 4, of which 4 were waited for; matrix products, arithmetic and copies ran while one was open for 4% of the time, Pallas kernels for 0%

profile of v3, /device:TPU:6, one launch (start us, length us, event | category | flops | bytes accessed | tf_op | source)
XLA Modules:
  0.0 178.5 jit_solution(2888533429462912325)
XLA Ops:
  0.0 0.0 copy-start
  0.0 1.0 pad_maximum_fusion.2
  1.0 0.0 copy-start.8
  1.0 0.0 copy-start.4
  1.0 0.0 copy-start.5
  1.0 0.4 copy.33
  1.5 1.1 reshape.152
  2.6 4.5 %all-to-all-start.1 = ((bf16[8,2,8192]{2,1,0:T(2,128)(2,1)}), bf16[8,2,8192]{2,1,0:T(2,128)(2,1)S(1)}, u32[]{:S(2)}, u32[]{:S(2)}) async-start(bf16[8,2,8192]{2,1,0:T(2,128)(2,1)} %reshape.152), calls=%async_computation.1 | async-start | bytes 524288 | tf_op jit(solution)/shard_map/all_to_all | solution.py:144
  7.0 0.0 copy-done.8
  7.0 0.2 reduce-window.7
  7.2 0.7 iota_reduce_fusion
  7.9 0.0 copy-done
  8.0 0.6 gather_fusion
  8.6 0.1 reshape.144
  8.6 0.1 broadcast_in_dim.37
  8.7 0.1 broadcast_in_dim.38
  8.8 0.0 copy-done.4
  8.8 0.0 copy-done.5
  8.8 0.1 pad_maximum_fusion
  8.9 0.7 gather_fusion.1
  9.6 0.1 copy.35
  9.7 0.3 bitcast_select_fusion
  10.0 0.1 pad_maximum_fusion.1
  10.1 4.5 %all-to-all-done.1 = bf16[8,2,8192]{2,1,0:T(2,128)(2,1)S(1)} async-done(((bf16[8,2,8192]{2,1,0:T(2,128)(2,1)}), bf16[8,2,8192]{2,1,0:T(2,128)(2,1)S(1)}, u32[]{:S(2)}, u32[]{:S(2)}) %all-to-all-start.1) | async-done | bytes 262176 | tf_op jit(solution)/shard_map/all_to_all | solution.py:144
  14.6 0.3 reshape.153
  14.9 0.4 copy.34
  15.3 0.0 copy-start.2
  15.3 0.1 reshape.131
  15.5 66.4 %all_to_all.47 = bf16[64,52,128]{2,1,0:T(8,128)(2,1)S(1)} all-to-all(bf16[64,52,128]{2,1,0:T(8,128)(2,1)S(1)} %reshape.131), channel_id=1, replica_groups=mesh['seq'=64,'head'=8] {'seq'}, dimensions={0} | all-to-all | bytes 1703936 | tf_op jit(solution)/shard_map/all_to_all | solution.py:114
  81.9 0.2 reduce_sum.12
  82.1 1.0 broadcast_in_dim.42
  83.1 0.0 copy-start.3
  83.1 6.9 %all-to-all-start.3 = ((bf16[64,52,128]{2,1,0:T(8,128)(2,1)}), bf16[64,52,128]{2,1,0:T(8,128)(2,1)S(1)}, u32[]{:S(2)}, u32[]{:S(2)}) async-start(bf16[64,52,128]{2,1,0:T(8,128)(2,1)} %broadcast_in_dim.42), calls=%async_computation.3 | async-start | bytes 1835008 | tf_op jit(solution)/shard_map/all_to_all | solution.py:116
  90.1 0.0 copy-done.3
  90.1 1.1 copy.38
  91.2 47.0 %all-to-all-done.3 = bf16[64,52,128]{2,1,0:T(8,128)(2,1)S(1)} async-done(((bf16[64,52,128]{2,1,0:T(8,128)(2,1)}), bf16[64,52,128]{2,1,0:T(8,128)(2,1)S(1)}, u32[]{:S(2)}, u32[]{:S(2)}) %all-to-all-start.3) | async-done | bytes 852000 | tf_op jit(solution)/shard_map/all_to_all | solution.py:116
  138.2 3.6 %all-to-all-start = ((bf16[64,8,1024]{2,0,1:T(8,128)(2,1)}), bf16[64,8,1024]{2,0,1:T(8,128)(2,1)S(1)}, u32[]{:S(2)}, u32[]{:S(2)}) async-start(bf16[64,8,1024]{2,0,1:T(8,128)(2,1)} %bitcast.59), calls=%async_computation | async-start | bytes 2097152 | tf_op jit(solution)/shard_map/all_to_all | solution.py:150
  141.7 0.0 copy-start.7
  141.8 0.0 copy-done.2
  141.8 0.1 maximum_select_fusion
  141.9 3.2 %collective-permute-start = (bf16[2,512,128]{2,1,0:T(8,128)(2,1)S(1)}, bf16[2,512,128]{2,1,0:T(8,128)(2,1)S(1)}, u32[]{:S(2)}, u32[]{:S(2)}) collective-permute-start(bf16[2,512,128]{2,1,0:T(8,128)(2,1)S(1)} %maximum_select_fusion), channel_id=1, source_target_pairs={{504,0},{0,8},{8,16},{16,24},{24,32},{32,40},{40,48},{48,56},{56,6... | collective-permute-start | bytes 786440 | tf_op jit(solution)/shard_map/ppermute | solution.py:25
  145.1 0.0 copy-done.7
  145.1 0.1 copy.31
  145.2 0.6 reshape.130.diag_ref
  145.8 0.5 broadcast_select_fusion.slot_ref
  146.4 1.1 reshape.132.vk_ref.vv_ref.sk_ref.sv_ref
  147.5 7.0 %collective-permute-done.prev_ref = bf16[2,512,128]{2,1,0:T(8,128)(2,1)S(1)} collective-permute-done((bf16[2,512,128]{2,1,0:T(8,128)(2,1)S(1)}, bf16[2,512,128]{2,1,0:T(8,128)(2,1)S(1)}, u32[]{:S(2)}, u32[]{:S(2)}) %collective-permute-start) | collective-permute-done | bytes 262176 | tf_op jit(solution)/shard_map/ppermute | solution.py:25
  154.5 0.0 copy-start.6
  154.5 3.2 %all-to-all-done = bf16[64,8,1024]{2,0,1:T(8,128)(2,1)S(1)} async-done(((bf16[64,8,1024]{2,0,1:T(8,128)(2,1)}), bf16[64,8,1024]{2,0,1:T(8,128)(2,1)S(1)}, u32[]{:S(2)}, u32[]{:S(2)}) %all-to-all-start) | async-done | bytes 1048608 | tf_op jit(solution)/shard_map/all_to_all | solution.py:150
  157.6 0.0 copy-start.1
  157.6 0.0 copy-done.6
  157.6 1.0 copy-done.1
  158.6 19.9 %shard_map.91 = bf16[512,1024]{1,0:T(8,128)(2,1)} custom-call(s32[8]{0:T(128)} %roles_ref.1, s32[8]{0:T(128)} %broadcast_select_fusion.slot_ref, s32[8]{0:T(128)} %count_ref.1, s32[32]{0:T(128)} %reshape.130.diag_ref, bf16[512,1024]{1,0:T(8,128)(2,1)} %bitcast.60, bf16[2,512,128]{2,1,0:T(8,128)(2,1)} %copy-done.6, bf16[2,512,128]{2,1,0:T(8,128)(2,1)} %bitcast.62, ...), custom_call_target="tpu_custom_call" | custom-call | tf_op jit(solution)/shard_map/pallas_call | solution.py:105
  (10 shorter events, 0.1 us)
Async XLA Ops:
  0.0 8.0 %copy-start = (s32[8,6]{1,0:T(8,128)S(1)}, s32[8,6]{1,0:T(8,128)}, u32[]{:S(2)}) copy-start(s32[8,6]{1,0:T(8,128)} %param.15) | copy-start | bytes 580
  1.0 6.0 %copy-start.8 = (s32[8]{0:T(128)S(1)}, s32[8]{0:T(128)}, u32[]{:S(2)}) copy-start(s32[8]{0:T(128)} %roles_ref.1) | copy-start | bytes 100
  1.0 7.8 %copy-start.4 = (bf16[2048,128]{1,0:T(8,128)(2,1)S(1)}, bf16[2048,128]{1,0:T(8,128)(2,1)}, u32[]{:S(2)}) copy-start(bf16[2048,128]{1,0:T(8,128)(2,1)} %param.13) | copy-start | bytes 1572868
  1.0 7.8 %copy-start.5 = (bf16[2048,128]{1,0:T(8,128)(2,1)S(1)}, bf16[2048,128]{1,0:T(8,128)(2,1)}, u32[]{:S(2)}) copy-start(bf16[2048,128]{1,0:T(8,128)(2,1)} %param.12) | copy-start | bytes 1572868
  2.6 12.0 %all-to-all-start.1 = ((bf16[8,2,8192]{2,1,0:T(2,128)(2,1)}), bf16[8,2,8192]{2,1,0:T(2,128)(2,1)S(1)}, u32[]{:S(2)}, u32[]{:S(2)}) async-start(bf16[8,2,8192]{2,1,0:T(2,128)(2,1)} %reshape.152), calls=%async_computation.1 | async-start | bytes 524288 | tf_op jit(solution)/shard_map/all_to_all | solution.py:144
  15.3 126.5 %copy-start.2 = (bf16[2,64,8,128]{3,1,2,0:T(8,128)(2,1)}, bf16[2,64,8,128]{3,1,2,0:T(8,128)(2,1)S(1)}, u32[]{:S(2)}) copy-start(bf16[2,64,8,128]{3,1,2,0:T(8,128)(2,1)S(1)} %copy.34) | copy-start | bytes 786436
  83.1 7.0 %copy-start.3 = (bf16[64,8192]{1,0:T(8,128)(2,1)S(1)}, bf16[64,8192]{1,0:T(8,128)(2,1)}, u32[]{:S(2)}) copy-start(bf16[64,8192]{1,0:T(8,128)(2,1)} %param.9) | copy-start | bytes 3145732
  83.1 55.0 %all-to-all-start.3 = ((bf16[64,52,128]{2,1,0:T(8,128)(2,1)}), bf16[64,52,128]{2,1,0:T(8,128)(2,1)S(1)}, u32[]{:S(2)}, u32[]{:S(2)}) async-start(bf16[64,52,128]{2,1,0:T(8,128)(2,1)} %broadcast_in_dim.42), calls=%async_computation.3 | async-start | bytes 1835008 | tf_op jit(solution)/shard_map/all_to_all | solution.py:116
  138.2 19.5 %all-to-all-start = ((bf16[64,8,1024]{2,0,1:T(8,128)(2,1)}), bf16[64,8,1024]{2,0,1:T(8,128)(2,1)S(1)}, u32[]{:S(2)}, u32[]{:S(2)}) async-start(bf16[64,8,1024]{2,0,1:T(8,128)(2,1)} %bitcast.59), calls=%async_computation | async-start | bytes 2097152 | tf_op jit(solution)/shard_map/all_to_all | solution.py:150
  141.7 3.4 %copy-start.7 = (s32[8,4]{0,1:T(4,128)S(1)}, s32[8,4]{0,1:T(4,128)}, u32[]{:S(2)}) copy-start(s32[8,4]{0,1:T(4,128)} %param.17) | copy-start | bytes 388
  141.9 12.6 %collective-permute-start = (bf16[2,512,128]{2,1,0:T(8,128)(2,1)S(1)}, bf16[2,512,128]{2,1,0:T(8,128)(2,1)S(1)}, u32[]{:S(2)}, u32[]{:S(2)}) collective-permute-start(bf16[2,512,128]{2,1,0:T(8,128)(2,1)S(1)} %maximum_select_fusion), channel_id=1, source_target_pairs={{504,0},{0,8},{8,16},{16,24},{24,32},{32,40},{40,48},{48,56},{56,6... | collective-permute-start | bytes 786440 | tf_op jit(solution)/shard_map/ppermute | solution.py:25
  154.5 3.2 %copy-start.6 = (bf16[2,512,128]{2,1,0:T(8,128)(2,1)}, bf16[2,512,128]{2,1,0:T(8,128)(2,1)S(1)}, u32[]{:S(2)}) copy-start(bf16[2,512,128]{2,1,0:T(8,128)(2,1)S(1)} %collective-permute-done.prev_ref) | copy-start | bytes 786436
  157.6 1.0 copy-start.1

commit v4 on v3

--- a/solution.py
+++ b/solution.py
@@ -109,12 +109,15 @@
     )(roles_l, slot_l, count_l, diag_l, q_local, prev_kv, own_kv, side, side, side, side)
 
 
-def sum_over_seq(block, seq_devices):
+def scatter_sum(block, seq_devices):
     flat = block.reshape(seq_devices, -1, block.shape[-1])
     mine = lax.all_to_all(flat, "seq", 0, 0, tiled=True)
-    total = jnp.sum(mine.astype(jnp.float32), 0, keepdims=True).astype(block.dtype)
-    every = lax.all_to_all(jnp.broadcast_to(total, flat.shape), "seq", 0, 0, tiled=True)
-    return every.reshape(block.shape)
+    return jnp.sum(mine.astype(jnp.float32), 0, keepdims=True).astype(block.dtype)
+
+
+def gather_sums(total, shape, seq_devices):
+    every = lax.all_to_all(jnp.broadcast_to(total, (seq_devices,) + total.shape[1:]), "seq", 0, 0, tiled=True)
+    return every.reshape(shape)
 
 
 def shards(queries, keys, values, prefix_keys, prefix_values, roles, columns, col_count, diagonals):
@@ -145,9 +148,10 @@
     tail_cache = jnp.stack([prefix_keys[cache_rows - WIN:], prefix_values[cache_rows - WIN:]], 0)
     outgoing = jnp.where(my_seq == seq_devices - 1, tail_cache, kv_local)
     prev_kv = shifted(outgoing, "seq", 1)
-    both, kv_local = lax.optimization_barrier((both, kv_local))
-    side = sum_over_seq(both, seq_devices)
     q_local = lax.all_to_all(queries, "head", split_axis=1, concat_axis=0, tiled=True)
+    total = scatter_sum(both, seq_devices)
+    total, prev_kv, q_local = lax.optimization_barrier((total, prev_kv, q_local))
+    side = gather_sums(total, both.shape, seq_devices)
 
     slot_l = jnp.where(is_ret, slot, 0).astype(jnp.int32)
     return attend(

time: 181 us -> 176 us (0.972)
  blocking collectives: 66.4 us -> 0 us
  waiting for transfers between devices: 61.7 us -> 108 us
  starting transfers between devices: 18.2 us -> 36.9 us
  Pallas kernels: 19.9 us -> 15.2 us
    all_to_all x1 -> x0, blocking collectives: 66.4 us -> none  [sum_over_seq(): mine = lax.all_to_all(flat, 'seq', 0, 0, tiled=True)]
    all_to_all x1 -> x2, waiting for transfers between devices: 47 us -> 93.5 us  [the longest x1 46.8 us: scatter_sum(): mine = lax.all_to_all(flat, 'seq', 0, 0, tiled=True)]
    all_to_all x1 -> x2, starting transfers between devices: 6.94 us -> 25.6 us  [the longest x1 18.8 us: scatter_sum(): mine = lax.all_to_all(flat, 'seq', 0, 0, tiled=True)]
    pallas_call x1, Pallas kernels: 19.9 us -> 15.2 us  [attend(): pl.pallas_call(attend_kernel, grid_spec=grid_spec, out_shape=jax.ShapeDty...]
    ppermute x1, waiting for transfers between devices: 7 us -> 9.13 us  [shifted(): return lax.ppermute(block, axis, route)]
  transfers between devices with their start and end apart: 4 -> 5, of which waited for: 4 -> 5; matrix products, arithmetic and copies ran while one was open for 4% -> 4% of each run, Pallas kernels for 0% -> 0%
where the time goes in v4:
time: 176 us; the launch traced here: 173 us
  waiting for transfers between devices  108 us (61%)
  starting transfers between devices  36.9 us (21%)
  Pallas kernels  15.2 us (9%)
  local copies, waits for them, and re-layouts  9.08 us (5%)
  other arithmetic  3.16 us (2%)
    all_to_all x1, waiting for transfers between devices, scatter_sum(): mine = lax.all_to_all(flat, 'seq', 0, 0, tiled=True)  46.8 us
    all_to_all x1, waiting for transfers between devices, gather_sums(): lax.all_to_all(jnp.broadcast_to(total, (seq_devices,) + total.shape[1:]),...  46.7 us
    all_to_all x1, starting transfers between devices, scatter_sum(): mine = lax.all_to_all(flat, 'seq', 0, 0, tiled=True)  18.8 us
    pallas_call x1, Pallas kernels, attend(): pl.pallas_call(attend_kernel, grid_spec=grid_spec, out_shape=jax.ShapeDty...  15.2 us
    ppermute x1, waiting for transfers between devices, shifted(): return lax.ppermute(block, axis, route)  9.13 us
    all_to_all x1, starting transfers between devices, gather_sums(): lax.all_to_all(jnp.broadcast_to(total, (seq_devices,) + total.shape[1:]),...  6.81 us
    all_to_all x1, starting transfers between devices, shards(): lax.all_to_all(kv, 'head', split_axis=2, concat_axis=1, tiled=True)  4.47 us
    all_to_all x1, starting transfers between devices, shards(): lax.all_to_all(queries, 'head', split_axis=1, concat_axis=0, tiled=True)  3.56 us
  transfers between devices with their start and end apart: 5, of which 5 were waited for; matrix products, arithmetic and copies ran while one was open for 4% of the time, Pallas kernels for 0%

profile of v4, /device:TPU:6, one launch (start us, length us, event | category | flops | bytes accessed | tf_op | source)
XLA Modules:
  0.0 173.1 jit_solution(12003439237509799293)
XLA Ops:
  0.0 0.0 copy-start
  0.0 1.0 pad_maximum_fusion.2
  1.0 0.0 copy-start.8
  1.0 0.0 copy-start.4
  1.0 0.0 copy-start.5
  1.0 0.4 copy.33
  1.5 1.1 reshape.157
  2.6 4.5 %all-to-all-start.1 = ((bf16[8,2,8192]{2,1,0:T(2,128)(2,1)}), bf16[8,2,8192]{2,1,0:T(2,128)(2,1)S(1)}, u32[]{:S(2)}, u32[]{:S(2)}) async-start(bf16[8,2,8192]{2,1,0:T(2,128)(2,1)} %reshape.157), calls=%async_computation.1 | async-start | bytes 524288 | tf_op jit(solution)/shard_map/all_to_all | solution.py:147
  7.0 0.0 copy-done.8
  7.0 0.2 reduce-window.7
  7.2 0.6 iota_reduce_fusion
  7.9 0.0 copy-done
  7.9 0.6 gather_fusion
  8.5 0.1 broadcast_in_dim.39
  8.6 0.1 broadcast_in_dim.40
  8.7 0.1 reshape.149
  8.8 0.0 copy-done.4
  8.8 0.0 copy-done.5
  8.8 0.1 pad_maximum_fusion
  8.9 0.7 gather_fusion.1
  9.6 0.1 copy.32
  9.7 0.3 bitcast_select_fusion
  10.0 0.1 pad_maximum_fusion.1
  10.0 1.1 reshape.136
  11.1 0.0 copy-start.3
  11.1 3.5 %all-to-all-done.1 = bf16[8,2,8192]{2,1,0:T(2,128)(2,1)S(1)} async-done(((bf16[8,2,8192]{2,1,0:T(2,128)(2,1)}), bf16[8,2,8192]{2,1,0:T(2,128)(2,1)S(1)}, u32[]{:S(2)}, u32[]{:S(2)}) %all-to-all-start.1) | async-done | bytes 262176 | tf_op jit(solution)/shard_map/all_to_all | solution.py:147
  14.6 18.8 %all-to-all-start = ((bf16[64,52,128]{2,1,0:T(8,128)(2,1)}), bf16[64,52,128]{2,1,0:T(8,128)(2,1)S(1)}, u32[]{:S(2)}, u32[]{:S(2)}) async-start(bf16[64,52,128]{2,1,0:T(8,128)(2,1)} %reshape.136), calls=%async_computation | async-start | bytes 1835008 | tf_op jit(solution)/shard_map/all_to_all | solution.py:114
  33.4 0.0 copy-done.3
  33.4 1.1 copy.38
  34.4 46.8 %all-to-all-done = bf16[64,52,128]{2,1,0:T(8,128)(2,1)S(1)} async-done(((bf16[64,52,128]{2,1,0:T(8,128)(2,1)}), bf16[64,52,128]{2,1,0:T(8,128)(2,1)S(1)}, u32[]{:S(2)}, u32[]{:S(2)}) %all-to-all-start) | async-done | bytes 852000 | tf_op jit(solution)/shard_map/all_to_all | solution.py:114
  81.2 3.6 %all-to-all-start.2 = ((bf16[64,8,1024]{2,0,1:T(8,128)(2,1)}), bf16[64,8,1024]{2,0,1:T(8,128)(2,1)S(1)}, u32[]{:S(2)}, u32[]{:S(2)}) async-start(bf16[64,8,1024]{2,0,1:T(8,128)(2,1)} %bitcast.61), calls=%async_computation.2 | async-start | bytes 2097152 | tf_op jit(solution)/shard_map/all_to_all | solution.py:151
  84.8 0.3 reshape.158
  85.2 0.4 copy.34
  85.6 0.0 copy-start.2
  85.6 0.1 maximum_select_fusion
  85.7 3.3 %collective-permute-start = (bf16[2,512,128]{2,1,0:T(8,128)(2,1)S(1)}, bf16[2,512,128]{2,1,0:T(8,128)(2,1)S(1)}, u32[]{:S(2)}, u32[]{:S(2)}) collective-permute-start(bf16[2,512,128]{2,1,0:T(8,128)(2,1)S(1)} %maximum_select_fusion), channel_id=1, source_target_pairs={{504,0},{0,8},{8,16},{16,24},{24,32},{32,40},{40,48},{48,56},{56,6... | collective-permute-start | bytes 786440 | tf_op jit(solution)/shard_map/ppermute | solution.py:25
  89.0 0.2 reduce_sum.12
  89.1 9.1 %collective-permute-done.prev_ref = bf16[2,512,128]{2,1,0:T(8,128)(2,1)S(1)} collective-permute-done((bf16[2,512,128]{2,1,0:T(8,128)(2,1)S(1)}, bf16[2,512,128]{2,1,0:T(8,128)(2,1)S(1)}, u32[]{:S(2)}, u32[]{:S(2)}) %collective-permute-start) | collective-permute-done | bytes 262176 | tf_op jit(solution)/shard_map/ppermute | solution.py:25
  98.3 0.0 copy-start.6
  98.3 2.4 %all-to-all-done.2 = bf16[64,8,1024]{2,0,1:T(8,128)(2,1)S(1)} async-done(((bf16[64,8,1024]{2,0,1:T(8,128)(2,1)}), bf16[64,8,1024]{2,0,1:T(8,128)(2,1)S(1)}, u32[]{:S(2)}, u32[]{:S(2)}) %all-to-all-start.2) | async-done | bytes 1048608 | tf_op jit(solution)/shard_map/all_to_all | solution.py:151
  100.7 0.0 copy-start.1
  100.7 1.2 broadcast_in_dim.45
  101.8 0.0 copy-done.2
  101.8 0.0 copy-start.7
  101.8 0.0 copy-done.6
  101.8 0.1 copy-done.1
  101.9 6.8 %all-to-all-start.3 = ((bf16[64,52,128]{2,1,0:T(8,128)(2,1)}), bf16[64,52,128]{2,1,0:T(8,128)(2,1)S(1)}, u32[]{:S(2)}, u32[]{:S(2)}) async-start(bf16[64,52,128]{2,1,0:T(8,128)(2,1)} %broadcast_in_dim.45), calls=%async_computation.3 | async-start | bytes 1835008 | tf_op jit(solution)/shard_map/all_to_all | solution.py:119
  108.8 0.0 copy-done.7
  108.8 0.1 copy.31
  108.8 0.6 reshape.135.diag_ref
  109.5 0.6 broadcast_select_fusion.slot_ref
  110.1 46.7 %all-to-all-done.3 = bf16[64,52,128]{2,1,0:T(8,128)(2,1)S(1)} async-done(((bf16[64,52,128]{2,1,0:T(8,128)(2,1)}), bf16[64,52,128]{2,1,0:T(8,128)(2,1)S(1)}, u32[]{:S(2)}, u32[]{:S(2)}) %all-to-all-start.3) | async-done | bytes 852000 | tf_op jit(solution)/shard_map/all_to_all | solution.py:119
  156.8 1.1 reshape.137.vk_ref.vv_ref.sk_ref.sv_ref
  157.9 15.2 %shard_map.91 = bf16[512,1024]{1,0:T(8,128)(2,1)} custom-call(s32[8]{0:T(128)} %roles_ref.1, s32[8]{0:T(128)} %broadcast_select_fusion.slot_ref, s32[8]{0:T(128)} %count_ref.1, s32[32]{0:T(128)} %reshape.135.diag_ref, bf16[512,1024]{1,0:T(8,128)(2,1)} %bitcast.62, bf16[2,512,128]{2,1,0:T(8,128)(2,1)} %copy-done.6, bf16[2,512,128]{2,1,0:T(8,128)(2,1)} %bitcast.64, ...), custom_call_target="tpu_custom_call" | custom-call | tf_op jit(solution)/shard_map/pallas_call | solution.py:105
  (10 shorter events, 0.1 us)
Async XLA Ops:
  0.0 7.9 %copy-start = (s32[8,6]{1,0:T(8,128)S(1)}, s32[8,6]{1,0:T(8,128)}, u32[]{:S(2)}) copy-start(s32[8,6]{1,0:T(8,128)} %param.15) | copy-start | bytes 580
  1.0 6.0 %copy-start.8 = (s32[8]{0:T(128)S(1)}, s32[8]{0:T(128)}, u32[]{:S(2)}) copy-start(s32[8]{0:T(128)} %roles_ref.1) | copy-start | bytes 100
  1.0 7.7 %copy-start.4 = (bf16[2048,128]{1,0:T(8,128)(2,1)S(1)}, bf16[2048,128]{1,0:T(8,128)(2,1)}, u32[]{:S(2)}) copy-start(bf16[2048,128]{1,0:T(8,128)(2,1)} %param.13) | copy-start | bytes 1572868
  1.0 7.7 %copy-start.5 = (bf16[2048,128]{1,0:T(8,128)(2,1)S(1)}, bf16[2048,128]{1,0:T(8,128)(2,1)}, u32[]{:S(2)}) copy-start(bf16[2048,128]{1,0:T(8,128)(2,1)} %param.12) | copy-start | bytes 1572868
  2.6 12.0 %all-to-all-start.1 = ((bf16[8,2,8192]{2,1,0:T(2,128)(2,1)}), bf16[8,2,8192]{2,1,0:T(2,128)(2,1)S(1)}, u32[]{:S(2)}, u32[]{:S(2)}) async-start(bf16[8,2,8192]{2,1,0:T(2,128)(2,1)} %reshape.157), calls=%async_computation.1 | async-start | bytes 524288 | tf_op jit(solution)/shard_map/all_to_all | solution.py:147
  11.1 22.3 %copy-start.3 = (bf16[64,8192]{1,0:T(8,128)(2,1)S(1)}, bf16[64,8192]{1,0:T(8,128)(2,1)}, u32[]{:S(2)}) copy-start(bf16[64,8192]{1,0:T(8,128)(2,1)} %param.9) | copy-start | bytes 3145732
  14.6 66.6 %all-to-all-start = ((bf16[64,52,128]{2,1,0:T(8,128)(2,1)}), bf16[64,52,128]{2,1,0:T(8,128)(2,1)S(1)}, u32[]{:S(2)}, u32[]{:S(2)}) async-start(bf16[64,52,128]{2,1,0:T(8,128)(2,1)} %reshape.136), calls=%async_computation | async-start | bytes 1835008 | tf_op jit(solution)/shard_map/all_to_all | solution.py:114
  81.2 19.5 %all-to-all-start.2 = ((bf16[64,8,1024]{2,0,1:T(8,128)(2,1)}), bf16[64,8,1024]{2,0,1:T(8,128)(2,1)S(1)}, u32[]{:S(2)}, u32[]{:S(2)}) async-start(bf16[64,8,1024]{2,0,1:T(8,128)(2,1)} %bitcast.61), calls=%async_computation.2 | async-start | bytes 2097152 | tf_op jit(solution)/shard_map/all_to_all | solution.py:151
  85.6 16.2 %copy-start.2 = (bf16[2,64,8,128]{3,1,2,0:T(8,128)(2,1)}, bf16[2,64,8,128]{3,1,2,0:T(8,128)(2,1)S(1)}, u32[]{:S(2)}) copy-start(bf16[2,64,8,128]{3,1,2,0:T(8,128)(2,1)S(1)} %copy.34) | copy-start | bytes 786436
  85.7 12.6 %collective-permute-start = (bf16[2,512,128]{2,1,0:T(8,128)(2,1)S(1)}, bf16[2,512,128]{2,1,0:T(8,128)(2,1)S(1)}, u32[]{:S(2)}, u32[]{:S(2)}) collective-permute-start(bf16[2,512,128]{2,1,0:T(8,128)(2,1)S(1)} %maximum_select_fusion), channel_id=1, source_target_pairs={{504,0},{0,8},{8,16},{16,24},{24,32},{32,40},{40,48},{48,56},{56,6... | collective-permute-start | bytes 786440 | tf_op jit(solution)/shard_map/ppermute | solution.py:25
  98.3 3.6 %copy-start.6 = (bf16[2,512,128]{2,1,0:T(8,128)(2,1)}, bf16[2,512,128]{2,1,0:T(8,128)(2,1)S(1)}, u32[]{:S(2)}) copy-start(bf16[2,512,128]{2,1,0:T(8,128)(2,1)S(1)} %collective-permute-done.prev_ref) | copy-start | bytes 786436
  100.7 1.3 copy-start.1
  101.8 6.9 %copy-start.7 = (s32[8,4]{0,1:T(4,128)S(1)}, s32[8,4]{0,1:T(4,128)}, u32[]{:S(2)}) copy-start(s32[8,4]{0,1:T(4,128)} %param.17) | copy-start | bytes 388
  101.9 54.9 %all-to-all-start.3 = ((bf16[64,52,128]{2,1,0:T(8,128)(2,1)}), bf16[64,52,128]{2,1,0:T(8,128)(2,1)S(1)}, u32[]{:S(2)}, u32[]{:S(2)}) async-start(bf16[64,52,128]{2,1,0:T(8,128)(2,1)} %broadcast_in_dim.45), calls=%async_computation.3 | async-start | bytes 1835008 | tf_op jit(solution)/shard_map/all_to_all | solution.py:119

commit v5 on v4

--- a/solution.py
+++ b/solution.py
@@ -147,10 +147,11 @@
     kv_local = lax.all_to_all(kv, "head", split_axis=2, concat_axis=1, tiled=True)
     tail_cache = jnp.stack([prefix_keys[cache_rows - WIN:], prefix_values[cache_rows - WIN:]], 0)
     outgoing = jnp.where(my_seq == seq_devices - 1, tail_cache, kv_local)
+    q_local = lax.all_to_all(queries, "head", split_axis=1, concat_axis=0, tiled=True)
+    both, q_local = lax.optimization_barrier((both, q_local))
+    total = scatter_sum(both, seq_devices)
+    total, outgoing = lax.optimization_barrier((total, outgoing))
     prev_kv = shifted(outgoing, "seq", 1)
-    q_local = lax.all_to_all(queries, "head", split_axis=1, concat_axis=0, tiled=True)
-    total = scatter_sum(both, seq_devices)
-    total, prev_kv, q_local = lax.optimization_barrier((total, prev_kv, q_local))
     side = gather_sums(total, both.shape, seq_devices)
 
     slot_l = jnp.where(is_ret, slot, 0).astype(jnp.int32)

time: 176 us -> 180 us (1.023)
  local copies, waits for them, and re-layouts: 9.08 us -> 13.3 us
  Pallas kernels: 15.2 us -> 18.3 us
    ppermute x1, waiting for transfers between devices: 9.13 us -> 0.01 us  [shifted(): return lax.ppermute(block, axis, route)]
    all_to_all x1, waiting for transfers between devices: 2.4 us -> 9.87 us  [shards(): lax.all_to_all(queries, 'head', split_axis=1, concat_axis=0, tiled=True)]
    pallas_call x1, Pallas kernels: 15.2 us -> 18.3 us  [attend(): pl.pallas_call(attend_kernel, grid_spec=grid_spec, out_shape=jax.ShapeDty...]
    all_to_all x1, waiting for transfers between devices: 3.45 us -> 6.31 us  [shards(): lax.all_to_all(kv, 'head', split_axis=2, concat_axis=1, tiled=True)]
    all_to_all x1, waiting for transfers between devices: 46.7 us -> 44.3 us  [gather_sums(): lax.all_to_all(jnp.broadcast_to(total, (seq_devices,) + total.shape[1:]),...]
  transfers between devices with their start and end apart: 5 -> 5, of which waited for: 5 -> 4; matrix products, arithmetic and copies ran while one was open for 4% -> 6% of each run, Pallas kernels for 0% -> 0%
where the time goes in v5:
time: 180 us; the launch traced here: 178 us
  waiting for transfers between devices  107 us (59%)
  starting transfers between devices  37.1 us (21%)
  Pallas kernels  18.3 us (10%)
  local copies, waits for them, and re-layouts  13.3 us (7%)
  other arithmetic  2.1 us (1%)
    all_to_all x1, waiting for transfers between devices, scatter_sum(): mine = lax.all_to_all(flat, 'seq', 0, 0, tiled=True)  46.1 us
    all_to_all x1, waiting for transfers between devices, gather_sums(): lax.all_to_all(jnp.broadcast_to(total, (seq_devices,) + total.shape[1:]),...  44.3 us
    all_to_all x1, starting transfers between devices, scatter_sum(): mine = lax.all_to_all(flat, 'seq', 0, 0, tiled=True)  18.8 us
    pallas_call x1, Pallas kernels, attend(): pl.pallas_call(attend_kernel, grid_spec=grid_spec, out_shape=jax.ShapeDty...  18.3 us
    all_to_all x1, waiting for transfers between devices, shards(): lax.all_to_all(queries, 'head', split_axis=1, concat_axis=0, tiled=True)  9.87 us
    all_to_all x1, starting transfers between devices, gather_sums(): lax.all_to_all(jnp.broadcast_to(total, (seq_devices,) + total.shape[1:]),...  6.94 us
    all_to_all x1, waiting for transfers between devices, shards(): lax.all_to_all(kv, 'head', split_axis=2, concat_axis=1, tiled=True)  6.31 us
    all_to_all x1, starting transfers between devices, shards(): lax.all_to_all(queries, 'head', split_axis=1, concat_axis=0, tiled=True)  4.6 us
  transfers between devices with their start and end apart: 5, of which 4 were waited for; matrix products, arithmetic and copies ran while one was open for 6% of the time, Pallas kernels for 0%

profile of v5, /device:TPU:6, one launch (start us, length us, event | category | flops | bytes accessed | tf_op | source)
XLA Modules:
  0.0 177.6 jit_solution(16993361549445725279)
XLA Ops:
  0.0 0.0 copy-start
  0.0 2.3 %copy.38 = bf16[8,8,8,1024]{3,2,0,1:T(8,128)(2,1)} copy(bf16[8,8,8,1024]{3,2,1,0:T(8,128)(2,1)} %bitcast.67) | data formatting | bytes 2097152 | tf_op jit(solution)/shard_map/all_to_all | solution.py:150
  2.3 0.0 copy-start.9
  2.3 0.0 copy-start.3
  2.3 0.0 copy-start.4
  2.3 4.6 %all-to-all-start = ((bf16[64,8,1024]{2,0,1:T(8,128)(2,1)}), bf16[64,8,1024]{2,0,1:T(8,128)(2,1)S(1)}, u32[]{:S(2)}, u32[]{:S(2)}) async-start(bf16[64,8,1024]{2,0,1:T(8,128)(2,1)} %bitcast.61), calls=%async_computation | async-start | bytes 2097152 | tf_op jit(solution)/shard_map/all_to_all | solution.py:150
  6.9 0.0 copy-done.9
  6.9 0.2 reduce-window.7
  7.1 0.6 iota_reduce_fusion
  7.8 0.0 copy-done
  7.8 0.6 gather_fusion
  8.4 0.1 broadcast_in_dim.39
  8.4 0.1 broadcast_in_dim.40
  8.5 0.1 reshape.149
  8.6 0.0 copy-done.3
  8.6 0.0 copy-done.4
  8.6 0.1 pad_maximum_fusion
  8.7 0.7 gather_fusion.1
  9.5 0.0 copy-start.6
  9.5 0.0 copy-start.7
  9.5 0.1 copy.32
  9.5 0.8 copy-done.6
  10.4 0.1 copy-done.7
  10.5 0.4 copy.34
  10.9 1.1 reshape.157
  12.0 0.8 slice_bitcast_fusion.2
  12.7 0.3 bitcast_select_fusion
  13.0 9.9 %all-to-all-done = bf16[64,8,1024]{2,0,1:T(8,128)(2,1)S(1)} async-done(((bf16[64,8,1024]{2,0,1:T(8,128)(2,1)}), bf16[64,8,1024]{2,0,1:T(8,128)(2,1)S(1)}, u32[]{:S(2)}, u32[]{:S(2)}) %all-to-all-start) | async-done | bytes 1048608 | tf_op jit(solution)/shard_map/all_to_all | solution.py:150
  22.9 0.0 copy-start.1
  22.9 3.4 %all-to-all-start.2 = ((bf16[8,2,8192]{2,1,0:T(2,128)(2,1)}), bf16[8,2,8192]{2,1,0:T(2,128)(2,1)S(1)}, u32[]{:S(2)}, u32[]{:S(2)}) async-start(bf16[8,2,8192]{2,1,0:T(2,128)(2,1)} %reshape.157), calls=%async_computation.2 | async-start | bytes 524288 | tf_op jit(solution)/shard_map/all_to_all | solution.py:147
  26.3 0.1 pad_maximum_fusion.1
  26.4 0.0 copy-done.1
  26.4 1.1 reshape.136
  27.4 6.3 %all-to-all-done.2 = bf16[8,2,8192]{2,1,0:T(2,128)(2,1)S(1)} async-done(((bf16[8,2,8192]{2,1,0:T(2,128)(2,1)}), bf16[8,2,8192]{2,1,0:T(2,128)(2,1)S(1)}, u32[]{:S(2)}, u32[]{:S(2)}) %all-to-all-start.2) | async-done | bytes 262176 | tf_op jit(solution)/shard_map/all_to_all | solution.py:147
  33.8 18.8 %all-to-all-start.1 = ((bf16[64,52,128]{2,1,0:T(8,128)(2,1)}), bf16[64,52,128]{2,1,0:T(8,128)(2,1)S(1)}, u32[]{:S(2)}, u32[]{:S(2)}) async-start(bf16[64,52,128]{2,1,0:T(8,128)(2,1)} %reshape.136), calls=%async_computation.1 | async-start | bytes 1835008 | tf_op jit(solution)/shard_map/all_to_all | solution.py:114
  52.6 0.9 slice_bitcast_fusion
  53.5 0.3 reshape.158
  53.8 0.4 copy.35
  54.3 0.0 copy-start.2
  54.3 0.1 maximum_select_fusion
  54.3 46.1 %all-to-all-done.1 = bf16[64,52,128]{2,1,0:T(8,128)(2,1)S(1)} async-done(((bf16[64,52,128]{2,1,0:T(8,128)(2,1)}), bf16[64,52,128]{2,1,0:T(8,128)(2,1)S(1)}, u32[]{:S(2)}, u32[]{:S(2)}) %all-to-all-start.1) | async-done | bytes 852000 | tf_op jit(solution)/shard_map/all_to_all | solution.py:114
  100.4 0.2 reduce_sum.12
  100.6 1.0 broadcast_in_dim.45
  101.6 0.0 copy-done.2
  101.6 0.0 copy-start.8
  101.6 6.9 %all-to-all-start.3 = ((bf16[64,52,128]{2,1,0:T(8,128)(2,1)}), bf16[64,52,128]{2,1,0:T(8,128)(2,1)S(1)}, u32[]{:S(2)}, u32[]{:S(2)}) async-start(bf16[64,52,128]{2,1,0:T(8,128)(2,1)} %broadcast_in_dim.45), calls=%async_computation.3 | async-start | bytes 1835008 | tf_op jit(solution)/shard_map/all_to_all | solution.py:119
  108.6 3.4 %collective-permute-start = (bf16[2,512,128]{2,1,0:T(8,128)(2,1)S(1)}, bf16[2,512,128]{2,1,0:T(8,128)(2,1)S(1)}, u32[]{:S(2)}, u32[]{:S(2)}) collective-permute-start(bf16[2,512,128]{2,1,0:T(8,128)(2,1)S(1)} %maximum_select_fusion), channel_id=1, source_target_pairs={{504,0},{0,8},{8,16},{16,24},{24,32},{32,40},{40,48},{48,56},{56,6... | collective-permute-start | bytes 786440 | tf_op jit(solution)/shard_map/ppermute | solution.py:25
  112.0 0.0 copy-done.8
  112.0 0.1 copy.31
  112.0 0.6 reshape.135.diag_ref
  112.7 0.5 broadcast_select_fusion.slot_ref
  113.2 44.3 %all-to-all-done.3 = bf16[64,52,128]{2,1,0:T(8,128)(2,1)S(1)} async-done(((bf16[64,52,128]{2,1,0:T(8,128)(2,1)}), bf16[64,52,128]{2,1,0:T(8,128)(2,1)S(1)}, u32[]{:S(2)}, u32[]{:S(2)}) %all-to-all-start.3) | async-done | bytes 852000 | tf_op jit(solution)/shard_map/all_to_all | solution.py:119
  157.5 1.1 reshape.137.vk_ref.vv_ref.sk_ref.sv_ref
  158.6 0.0 collective-permute-done.prev_ref
  158.6 0.0 copy-start.5
  158.6 0.7 copy-done.5
  159.3 18.3 %shard_map.91 = bf16[512,1024]{1,0:T(8,128)(2,1)} custom-call(s32[8]{0:T(128)} %roles_ref.1, s32[8]{0:T(128)} %broadcast_select_fusion.slot_ref, s32[8]{0:T(128)} %count_ref.1, s32[32]{0:T(128)} %reshape.135.diag_ref, bf16[512,1024]{1,0:T(8,128)(2,1)} %bitcast.62, bf16[2,512,128]{2,1,0:T(8,128)(2,1)} %copy-done.5, bf16[2,512,128]{2,1,0:T(8,128)(2,1)} %bitcast.64, ...), custom_call_target="tpu_custom_call" | custom-call | tf_op jit(solution)/shard_map/pallas_call | solution.py:105
  (9 shorter events, 0.1 us)
Async XLA Ops:
  0.0 7.8 %copy-start = (s32[8,6]{1,0:T(8,128)S(1)}, s32[8,6]{1,0:T(8,128)}, u32[]{:S(2)}) copy-start(s32[8,6]{1,0:T(8,128)} %param.15) | copy-start | bytes 580
  2.3 4.6 %copy-start.9 = (s32[8]{0:T(128)S(1)}, s32[8]{0:T(128)}, u32[]{:S(2)}) copy-start(s32[8]{0:T(128)} %roles_ref.1) | copy-start | bytes 100
  2.3 6.3 %copy-start.3 = (bf16[2048,128]{1,0:T(8,128)(2,1)S(1)}, bf16[2048,128]{1,0:T(8,128)(2,1)}, u32[]{:S(2)}) copy-start(bf16[2048,128]{1,0:T(8,128)(2,1)} %param.13) | copy-start | bytes 1572868
  2.3 6.3 %copy-start.4 = (bf16[2048,128]{1,0:T(8,128)(2,1)S(1)}, bf16[2048,128]{1,0:T(8,128)(2,1)}, u32[]{:S(2)}) copy-start(bf16[2048,128]{1,0:T(8,128)(2,1)} %param.12) | copy-start | bytes 1572868
  2.3 20.6 %all-to-all-start = ((bf16[64,8,1024]{2,0,1:T(8,128)(2,1)}), bf16[64,8,1024]{2,0,1:T(8,128)(2,1)S(1)}, u32[]{:S(2)}, u32[]{:S(2)}) async-start(bf16[64,8,1024]{2,0,1:T(8,128)(2,1)} %bitcast.61), calls=%async_computation | async-start | bytes 2097152 | tf_op jit(solution)/shard_map/all_to_all | solution.py:150
  9.5 0.9 copy-start.6
  9.5 1.0 copy-start.7
  22.9 3.5 %copy-start.1 = (bf16[64,8,1024]{2,0,1:T(8,128)(2,1)}, bf16[64,8,1024]{2,0,1:T(8,128)(2,1)S(1)}, u32[]{:S(2)}) copy-start(bf16[64,8,1024]{2,0,1:T(8,128)(2,1)S(1)} %all-to-all-done) | copy-start | bytes 3145732
  22.9 10.9 %all-to-all-start.2 = ((bf16[8,2,8192]{2,1,0:T(2,128)(2,1)}), bf16[8,2,8192]{2,1,0:T(2,128)(2,1)S(1)}, u32[]{:S(2)}, u32[]{:S(2)}) async-start(bf16[8,2,8192]{2,1,0:T(2,128)(2,1)} %reshape.157), calls=%async_computation.2 | async-start | bytes 524288 | tf_op jit(solution)/shard_map/all_to_all | solution.py:147
  33.8 66.6 %all-to-all-start.1 = ((bf16[64,52,128]{2,1,0:T(8,128)(2,1)}), bf16[64,52,128]{2,1,0:T(8,128)(2,1)S(1)}, u32[]{:S(2)}, u32[]{:S(2)}) async-start(bf16[64,52,128]{2,1,0:T(8,128)(2,1)} %reshape.136), calls=%async_computation.1 | async-start | bytes 1835008 | tf_op jit(solution)/shard_map/all_to_all | solution.py:114
  54.3 47.4 %copy-start.2 = (bf16[2,64,8,128]{3,1,2,0:T(8,128)(2,1)}, bf16[2,64,8,128]{3,1,2,0:T(8,128)(2,1)S(1)}, u32[]{:S(2)}) copy-start(bf16[2,64,8,128]{3,1,2,0:T(8,128)(2,1)S(1)} %copy.35) | copy-start | bytes 786436
  101.6 10.3 %copy-start.8 = (s32[8,4]{0,1:T(4,128)S(1)}, s32[8,4]{0,1:T(4,128)}, u32[]{:S(2)}) copy-start(s32[8,4]{0,1:T(4,128)} %param.17) | copy-start | bytes 388
  101.6 55.9 %all-to-all-start.3 = ((bf16[64,52,128]{2,1,0:T(8,128)(2,1)}), bf16[64,52,128]{2,1,0:T(8,128)(2,1)S(1)}, u32[]{:S(2)}, u32[]{:S(2)}) async-start(bf16[64,52,128]{2,1,0:T(8,128)(2,1)} %broadcast_in_dim.45), calls=%async_computation.3 | async-start | bytes 1835008 | tf_op jit(solution)/shard_map/all_to_all | solution.py:119
  108.6 50.1 %collective-permute-start = (bf16[2,512,128]{2,1,0:T(8,128)(2,1)S(1)}, bf16[2,512,128]{2,1,0:T(8,128)(2,1)S(1)}, u32[]{:S(2)}, u32[]{:S(2)}) collective-permute-start(bf16[2,512,128]{2,1,0:T(8,128)(2,1)S(1)} %maximum_select_fusion), channel_id=1, source_target_pairs={{504,0},{0,8},{8,16},{16,24},{24,32},{32,40},{40,48},{48,56},{56,6... | collective-permute-start | bytes 786440 | tf_op jit(solution)/shard_map/ppermute | solution.py:25
  158.6 0.7 copy-start.5

commit v6 on v5

--- a/solution.py
+++ b/solution.py
@@ -26,66 +26,72 @@
 
 
 def attend_kernel(roles_ref, slot_ref, count_ref, diag_ref,
-                  q_ref, prev_ref, own_ref, vk_ref, vv_ref, sk_ref, sv_ref, o_ref):
+                  q_ref, ck_ref, cv_ref, vk_ref, vv_ref, sk_ref, sv_ref, o_ref):
     h = pl.program_id(0)
     rows = q_ref.shape[0]
+    back = ck_ref.shape[0] - rows
     scaling = 1.0 / math.sqrt(HEAD_SIZE)
-    q = q_ref[...]
     dims = (((1,), (1,)), ((), ()))
+    neg = -jnp.inf
 
-    def scores(keys):
+    def scores(q, keys):
         return lax.dot_general(q, keys, dims, preferred_element_type=jnp.float32) * scaling
 
-    s_prev = scores(prev_ref[0])
-    s_own = scores(own_ref[0])
-    row = lax.broadcasted_iota(jnp.int32, (rows, rows), 0)
-    col = lax.broadcasted_iota(jnp.int32, (rows, rows), 1)
-
-    def finish(s_side, ok_side, v_side, ok_prev, ok_own):
-        neg = -jnp.inf
-        m_side = jnp.max(jnp.where(ok_side, s_side, neg), axis=1, keepdims=True)
-        m_prev = jnp.max(jnp.where(ok_prev, s_prev, neg), axis=1, keepdims=True)
-        m_own = jnp.max(jnp.where(ok_own, s_own, neg), axis=1, keepdims=True)
-        m = jnp.maximum(jnp.maximum(m_side, m_prev), m_own)
-        e_side = jnp.where(ok_side, jnp.exp(s_side - m), 0.0)
-        e_prev = jnp.where(ok_prev, jnp.exp(s_prev - m), 0.0)
-        e_own = jnp.where(ok_own, jnp.exp(s_own - m), 0.0)
-        total = (jnp.sum(e_side, axis=1, keepdims=True)
-                 + jnp.sum(e_prev, axis=1, keepdims=True)
-                 + jnp.sum(e_own, axis=1, keepdims=True))
-        p_side = (e_side / total).astype(jnp.bfloat16)
-        p_prev = (e_prev / total).astype(jnp.bfloat16)
-        p_own = (e_own / total).astype(jnp.bfloat16)
-        out = jnp.dot(p_side, v_side, preferred_element_type=jnp.float32)
-        out = out + jnp.dot(p_prev, prev_ref[1], preferred_element_type=jnp.float32)
-        out = out + jnp.dot(p_own, own_ref[1], preferred_element_type=jnp.float32)
-        o_ref[...] = out.astype(o_ref.dtype)
+    def softmax_out(s_a, ok_a, v_a, s_b, ok_b, v_b):
+        m = jnp.maximum(jnp.max(jnp.where(ok_a, s_a, neg), axis=1, keepdims=True),
+                        jnp.max(jnp.where(ok_b, s_b, neg), axis=1, keepdims=True))
+        e_a = jnp.where(ok_a, jnp.exp(s_a - m), 0.0)
+        e_b = jnp.where(ok_b, jnp.exp(s_b - m), 0.0)
+        total = jnp.sum(e_a, axis=1, keepdims=True) + jnp.sum(e_b, axis=1, keepdims=True)
+        out = jnp.dot((e_a / total).astype(jnp.bfloat16), v_a, preferred_element_type=jnp.float32)
+        out = out + jnp.dot((e_b / total).astype(jnp.bfloat16), v_b, preferred_element_type=jnp.float32)
+        return out.astype(o_ref.dtype)
 
     @pl.when(roles_ref[h] != 1)
     def _():
-        s_side = scores(sk_ref[...])
-        ok_side = jnp.ones(s_side.shape, jnp.bool_)
-        finish(s_side, ok_side, sv_ref[...], col > row, col <= row)
+        sk = sk_ref[...]
+        sv = sv_ref[...]
+        span = WIN + BLK
+        r = lax.broadcasted_iota(jnp.int32, (BLK, span), 0)
+        c = lax.broadcasted_iota(jnp.int32, (BLK, span), 1)
+        ok_win = (c > r) & (c <= r + WIN)
+        ok_sink = jnp.ones((BLK, sk.shape[0]), jnp.bool_)
+        for qb in range(rows // BLK):
+            lo = qb * BLK + back - WIN
+            qv = q_ref[qb * BLK:(qb + 1) * BLK, :]
+            s_sink = scores(qv, sk)
+            s_win = scores(qv, ck_ref[lo:lo + span, :])
+            o_ref[qb * BLK:(qb + 1) * BLK, :] = softmax_out(
+                s_sink, ok_sink, sv, s_win, ok_win, cv_ref[lo:lo + span, :])
 
     @pl.when(roles_ref[h] == 1)
     def _():
-        s_side = scores(vk_ref[...])
-        side_col = lax.broadcasted_iota(jnp.int32, s_side.shape, 1)
-        ok_side = side_col // BLK < count_ref[h]
-        rel_prev = row // BLK + rows // BLK - col // BLK
-        rel_own = row // BLK - col // BLK
-        ok_prev = jnp.zeros((rows, rows), jnp.bool_)
-        ok_own = jnp.zeros((rows, rows), jnp.bool_)
+        vk = vk_ref[...]
+        vv = vv_ref[...]
+        cv_ = lax.broadcasted_iota(jnp.int32, (BLK, vk.shape[0]), 1)
+        ok_vert = cv_ // BLK < count_ref[h]
+        r = lax.broadcasted_iota(jnp.int32, (BLK, NSL * BLK), 0)
+        c = lax.broadcasted_iota(jnp.int32, (BLK, NSL * BLK), 1)
+        offs = [jnp.clip(diag_ref[h * NSL + d], 0, WIN // BLK - 1) for d in range(NSL)]
+        off_col = jnp.zeros((BLK, NSL * BLK), jnp.int32)
         for d in range(NSL):
-            off = diag_ref[h * NSL + d]
-            ok_prev = ok_prev | (rel_prev == off)
-            ok_own = ok_own | ((rel_own == off) & ((off > 0) | (col <= row)))
-        finish(s_side, ok_side, vv_ref[...], ok_prev, ok_own)
+            off_col = jnp.where(c // BLK == d, offs[d], off_col)
+        ok_slash = (off_col > 0) | (c % BLK <= r)
+        for qb in range(rows // BLK):
+            qv = q_ref[qb * BLK:(qb + 1) * BLK, :]
+            s_vert = scores(qv, vk)
+            starts = [pl.multiple_of((back // BLK + qb - offs[d]) * BLK, BLK) for d in range(NSL)]
+            keys = jnp.concatenate([ck_ref[pl.ds(st, BLK), :] for st in starts], 0)
+            vals = jnp.concatenate([cv_ref[pl.ds(st, BLK), :] for st in starts], 0)
+            s_slash = scores(qv, keys)
+            o_ref[qb * BLK:(qb + 1) * BLK, :] = softmax_out(
+                s_vert, ok_vert, vv, s_slash, ok_slash, vals)
 
 
-def attend(roles_l, slot_l, count_l, diag_l, q_local, prev_kv, own_kv, side):
+def attend(roles_l, slot_l, count_l, diag_l, q_local, comb, side):
     rows = q_local.shape[0]
     heads = q_local.shape[1] // HEAD_SIZE
+    crows = comb.shape[1]
     vrows = VB * BLK
     sink_block = MAX_RETRIEVERS * vrows // SINK
     grid_spec = pltpu.PrefetchScalarGridSpec(
@@ -93,8 +99,8 @@
         grid=(heads,),
         in_specs=[
             pl.BlockSpec((rows, HEAD_SIZE), lambda h, *_: (0, h)),
-            pl.BlockSpec((2, rows, HEAD_SIZE), lambda h, *_: (0, 0, 0)),
-            pl.BlockSpec((2, rows, HEAD_SIZE), lambda h, *_: (0, 0, 0)),
+            pl.BlockSpec((None, crows, HEAD_SIZE), lambda h, *_: (0, 0, 0)),
+            pl.BlockSpec((None, crows, HEAD_SIZE), lambda h, *_: (1, 0, 0)),
             pl.BlockSpec((None, vrows, HEAD_SIZE), lambda h, r, s, *_: (0, s[h], 0)),
             pl.BlockSpec((None, vrows, HEAD_SIZE), lambda h, r, s, *_: (1, s[h], 0)),
             pl.BlockSpec((None, SINK, HEAD_SIZE), lambda h, *_: (0, sink_block, 0)),
@@ -106,7 +112,7 @@
         attend_kernel,
         grid_spec=grid_spec,
         out_shape=jax.ShapeDtypeStruct(q_local.shape, jnp.bfloat16),
-    )(roles_l, slot_l, count_l, diag_l, q_local, prev_kv, own_kv, side, side, side, side)
+    )(roles_l, slot_l, count_l, diag_l, q_local, comb, comb, side, side, side, side)
 
 
 def scatter_sum(block, seq_devices):
@@ -161,8 +167,7 @@
         col_count.astype(jnp.int32),
         diagonals.reshape(heads * NSL).astype(jnp.int32),
         q_local,
-        prev_kv,
-        kv_local,
+        jnp.concatenate([prev_kv, kv_local], 1),
         side,
     )
 

time: 180 us -> 191 us (1.061)
  Pallas kernels: 18.3 us -> 30.2 us
    all_to_all x1, waiting for transfers between devices: 44.3 us -> 0.55 us  [gather_sums(): lax.all_to_all(jnp.broadcast_to(total, (seq_devices,) + total.shape[1:]),...]
    ppermute x1, waiting for transfers between devices: 0.01 us -> 42.8 us  [shifted(): return lax.ppermute(block, axis, route)]
    pallas_call x1, Pallas kernels: 18.3 us -> 30.2 us  [attend(): pl.pallas_call(attend_kernel, grid_spec=grid_spec, out_shape=jax.ShapeDty...]
  transfers between devices with their start and end apart: 5 -> 5, of which waited for: 4 -> 5; matrix products, arithmetic and copies ran while one was open for 6% -> 5% of each run, Pallas kernels for 0% -> 0%
where the time goes in v6:
time: 191 us; the launch traced here: 189 us
  waiting for transfers between devices  106 us (55%)
  starting transfers between devices  37.1 us (19%)
  Pallas kernels  30.2 us (16%)
  local copies, waits for them, and re-layouts  12.7 us (7%)
  other arithmetic  3.01 us (2%)
    all_to_all x1, waiting for transfers between devices, scatter_sum(): mine = lax.all_to_all(flat, 'seq', 0, 0, tiled=True)  46.1 us
    ppermute x1, waiting for transfers between devices, shifted(): return lax.ppermute(block, axis, route)  42.8 us
    pallas_call x1, Pallas kernels, attend(): pl.pallas_call(attend_kernel, grid_spec=grid_spec, out_shape=jax.ShapeDty...  30.2 us
    all_to_all x1, starting transfers between devices, scatter_sum(): mine = lax.all_to_all(flat, 'seq', 0, 0, tiled=True)  18.8 us
    all_to_all x1, waiting for transfers between devices, shards(): lax.all_to_all(queries, 'head', split_axis=1, concat_axis=0, tiled=True)  9.82 us
    all_to_all x1, starting transfers between devices, gather_sums(): lax.all_to_all(jnp.broadcast_to(total, (seq_devices,) + total.shape[1:]),...  6.94 us
    all_to_all x1, waiting for transfers between devices, shards(): lax.all_to_all(kv, 'head', split_axis=2, concat_axis=1, tiled=True)  6.31 us
    all_to_all x1, starting transfers between devices, shards(): lax.all_to_all(queries, 'head', split_axis=1, concat_axis=0, tiled=True)  4.6 us
  transfers between devices with their start and end apart: 5, of which 5 were waited for; matrix products, arithmetic and copies ran while one was open for 5% of the time, Pallas kernels for 0%

profile of v6, /device:TPU:6, one launch (start us, length us, event | category | flops | bytes accessed | tf_op | source)
XLA Modules:
  0.0 188.8 jit_solution(6368225956998083090)
XLA Ops:
  0.0 0.0 copy-start
  0.0 2.3 %copy.38 = bf16[8,8,8,1024]{3,2,0,1:T(8,128)(2,1)} copy(bf16[8,8,8,1024]{3,2,1,0:T(8,128)(2,1)} %bitcast.67) | data formatting | bytes 2097152 | tf_op jit(solution)/shard_map/all_to_all | solution.py:156
  2.3 0.0 copy-start.7
  2.3 0.0 copy-start.2
  2.3 0.0 copy-start.3
  2.3 4.6 %all-to-all-start = ((bf16[64,8,1024]{2,0,1:T(8,128)(2,1)}), bf16[64,8,1024]{2,0,1:T(8,128)(2,1)S(1)}, u32[]{:S(2)}, u32[]{:S(2)}) async-start(bf16[64,8,1024]{2,0,1:T(8,128)(2,1)} %bitcast.61), calls=%async_computation | async-start | bytes 2097152 | tf_op jit(solution)/shard_map/all_to_all | solution.py:156
  6.9 0.0 copy-done.7
  6.9 0.2 reduce-window.7
  7.1 0.7 iota_reduce_fusion
  7.8 0.0 copy-done
  7.8 0.6 gather_fusion
  8.4 0.1 broadcast_in_dim.39
  8.5 0.1 broadcast_in_dim.40
  8.6 0.1 reshape.149
  8.7 0.0 copy-done.2
  8.7 0.0 copy-done.3
  8.7 0.1 pad_maximum_fusion
  8.8 0.7 gather_fusion.1
  9.5 0.0 copy-start.4
  9.5 0.0 copy-start.5
  9.5 0.1 copy.32
  9.6 0.8 copy-done.4
  10.4 0.1 copy-done.5
  10.5 0.4 copy.34
  10.9 1.1 reshape.157
  12.0 0.8 slice_bitcast_fusion.2
  12.8 0.3 bitcast_select_fusion
  13.1 9.8 %all-to-all-done = bf16[64,8,1024]{2,0,1:T(8,128)(2,1)S(1)} async-done(((bf16[64,8,1024]{2,0,1:T(8,128)(2,1)}), bf16[64,8,1024]{2,0,1:T(8,128)(2,1)S(1)}, u32[]{:S(2)}, u32[]{:S(2)}) %all-to-all-start) | async-done | bytes 1048608 | tf_op jit(solution)/shard_map/all_to_all | solution.py:156
  22.9 0.0 copy-start.1
  22.9 3.4 %all-to-all-start.2 = ((bf16[8,2,8192]{2,1,0:T(2,128)(2,1)}), bf16[8,2,8192]{2,1,0:T(2,128)(2,1)S(1)}, u32[]{:S(2)}, u32[]{:S(2)}) async-start(bf16[8,2,8192]{2,1,0:T(2,128)(2,1)} %reshape.157), calls=%async_computation.2 | async-start | bytes 524288 | tf_op jit(solution)/shard_map/all_to_all | solution.py:153
  26.3 0.1 pad_maximum_fusion.1
  26.4 0.0 copy-done.1
  26.4 1.1 reshape.136
  27.4 6.3 %all-to-all-done.2 = bf16[8,2,8192]{2,1,0:T(2,128)(2,1)S(1)} async-done(((bf16[8,2,8192]{2,1,0:T(2,128)(2,1)}), bf16[8,2,8192]{2,1,0:T(2,128)(2,1)S(1)}, u32[]{:S(2)}, u32[]{:S(2)}) %all-to-all-start.2) | async-done | bytes 262176 | tf_op jit(solution)/shard_map/all_to_all | solution.py:153
  33.8 18.8 %all-to-all-start.1 = ((bf16[64,52,128]{2,1,0:T(8,128)(2,1)}), bf16[64,52,128]{2,1,0:T(8,128)(2,1)S(1)}, u32[]{:S(2)}, u32[]{:S(2)}) async-start(bf16[64,52,128]{2,1,0:T(8,128)(2,1)} %reshape.136), calls=%async_computation.1 | async-start | bytes 1835008 | tf_op jit(solution)/shard_map/all_to_all | solution.py:120
  52.6 0.9 slice_bitcast_fusion
  53.5 0.3 reshape.158
  53.8 0.4 copy.35
  54.3 0.1 maximum_select_fusion
  54.3 46.1 %all-to-all-done.1 = bf16[64,52,128]{2,1,0:T(8,128)(2,1)S(1)} async-done(((bf16[64,52,128]{2,1,0:T(8,128)(2,1)}), bf16[64,52,128]{2,1,0:T(8,128)(2,1)S(1)}, u32[]{:S(2)}, u32[]{:S(2)}) %all-to-all-start.1) | async-done | bytes 852000 | tf_op jit(solution)/shard_map/all_to_all | solution.py:120
  100.4 0.2 reduce_sum.12
  100.6 1.0 broadcast_in_dim.45
  101.6 0.0 copy-start.6
  101.6 6.9 %all-to-all-start.3 = ((bf16[64,52,128]{2,1,0:T(8,128)(2,1)}), bf16[64,52,128]{2,1,0:T(8,128)(2,1)S(1)}, u32[]{:S(2)}, u32[]{:S(2)}) async-start(bf16[64,52,128]{2,1,0:T(8,128)(2,1)} %broadcast_in_dim.45), calls=%async_computation.3 | async-start | bytes 1835008 | tf_op jit(solution)/shard_map/all_to_all | solution.py:125
  108.6 3.4 %collective-permute-start = (bf16[2,512,128]{2,1,0:T(8,128)(2,1)S(1)}, bf16[2,512,128]{2,1,0:T(8,128)(2,1)S(1)}, u32[]{:S(2)}, u32[]{:S(2)}) collective-permute-start(bf16[2,512,128]{2,1,0:T(8,128)(2,1)S(1)} %maximum_select_fusion), channel_id=1, source_target_pairs={{504,0},{0,8},{8,16},{16,24},{24,32},{32,40},{40,48},{48,56},{56,6... | collective-permute-start | bytes 786440 | tf_op jit(solution)/shard_map/ppermute | solution.py:25
  112.0 0.0 copy-done.6
  112.0 0.1 copy.31
  112.0 0.7 reshape.135.diag_ref
  112.7 0.6 broadcast_select_fusion.slot_ref
  113.3 42.8 %collective-permute-done = bf16[2,512,128]{2,1,0:T(8,128)(2,1)S(1)} collective-permute-done((bf16[2,512,128]{2,1,0:T(8,128)(2,1)S(1)}, bf16[2,512,128]{2,1,0:T(8,128)(2,1)S(1)}, u32[]{:S(2)}, u32[]{:S(2)}) %collective-permute-start) | collective-permute-done | bytes 262176 | tf_op jit(solution)/shard_map/ppermute | solution.py:25
  156.1 0.8 pad_maximum_fusion.2.ck_ref.cv_ref
  157.0 0.6 all-to-all-done.3
  157.5 1.1 reshape.137.vk_ref.vv_ref.sk_ref.sv_ref
  158.6 30.2 %shard_map.91 = bf16[512,1024]{1,0:T(8,128)(2,1)} custom-call(s32[8]{0:T(128)} %roles_ref.1, s32[8]{0:T(128)} %broadcast_select_fusion.slot_ref, s32[8]{0:T(128)} %count_ref.1, s32[32]{0:T(128)} %reshape.135.diag_ref, bf16[512,1024]{1,0:T(8,128)(2,1)} %bitcast.62, bf16[2,1024,128]{2,1,0:T(8,128)(2,1)} %pad_maximum_fusion.2.ck_ref.cv_ref, ...), custom_call_target="tpu_custom_call" | custom-call | tf_op jit(solution)/shard_map/pallas_call | solution.py:111
  (9 shorter events, 0.1 us)
Async XLA Ops:
  0.0 7.8 %copy-start = (s32[8,6]{1,0:T(8,128)S(1)}, s32[8,6]{1,0:T(8,128)}, u32[]{:S(2)}) copy-start(s32[8,6]{1,0:T(8,128)} %param.15) | copy-start | bytes 580
  2.3 4.6 %copy-start.7 = (s32[8]{0:T(128)S(1)}, s32[8]{0:T(128)}, u32[]{:S(2)}) copy-start(s32[8]{0:T(128)} %roles_ref.1) | copy-start | bytes 100
  2.3 6.4 %copy-start.2 = (bf16[2048,128]{1,0:T(8,128)(2,1)S(1)}, bf16[2048,128]{1,0:T(8,128)(2,1)}, u32[]{:S(2)}) copy-start(bf16[2048,128]{1,0:T(8,128)(2,1)} %param.13) | copy-start | bytes 1572868
  2.3 6.4 %copy-start.3 = (bf16[2048,128]{1,0:T(8,128)(2,1)S(1)}, bf16[2048,128]{1,0:T(8,128)(2,1)}, u32[]{:S(2)}) copy-start(bf16[2048,128]{1,0:T(8,128)(2,1)} %param.12) | copy-start | bytes 1572868
  2.3 20.6 %all-to-all-start = ((bf16[64,8,1024]{2,0,1:T(8,128)(2,1)}), bf16[64,8,1024]{2,0,1:T(8,128)(2,1)S(1)}, u32[]{:S(2)}, u32[]{:S(2)}) async-start(bf16[64,8,1024]{2,0,1:T(8,128)(2,1)} %bitcast.61), calls=%async_computation | async-start | bytes 2097152 | tf_op jit(solution)/shard_map/all_to_all | solution.py:156
  9.5 0.9 copy-start.4
  9.5 1.0 copy-start.5
  22.9 3.5 %copy-start.1 = (bf16[64,8,1024]{2,0,1:T(8,128)(2,1)}, bf16[64,8,1024]{2,0,1:T(8,128)(2,1)S(1)}, u32[]{:S(2)}) copy-start(bf16[64,8,1024]{2,0,1:T(8,128)(2,1)S(1)} %all-to-all-done) | copy-start | bytes 3145732
  22.9 10.9 %all-to-all-start.2 = ((bf16[8,2,8192]{2,1,0:T(2,128)(2,1)}), bf16[8,2,8192]{2,1,0:T(2,128)(2,1)S(1)}, u32[]{:S(2)}, u32[]{:S(2)}) async-start(bf16[8,2,8192]{2,1,0:T(2,128)(2,1)} %reshape.157), calls=%async_computation.2 | async-start | bytes 524288 | tf_op jit(solution)/shard_map/all_to_all | solution.py:153
  33.8 66.6 %all-to-all-start.1 = ((bf16[64,52,128]{2,1,0:T(8,128)(2,1)}), bf16[64,52,128]{2,1,0:T(8,128)(2,1)S(1)}, u32[]{:S(2)}, u32[]{:S(2)}) async-start(bf16[64,52,128]{2,1,0:T(8,128)(2,1)} %reshape.136), calls=%async_computation.1 | async-start | bytes 1835008 | tf_op jit(solution)/shard_map/all_to_all | solution.py:120
  101.6 10.3 %copy-start.6 = (s32[8,4]{0,1:T(4,128)S(1)}, s32[8,4]{0,1:T(4,128)}, u32[]{:S(2)}) copy-start(s32[8,4]{0,1:T(4,128)} %param.17) | copy-start | bytes 388
  101.6 55.9 %all-to-all-start.3 = ((bf16[64,52,128]{2,1,0:T(8,128)(2,1)}), bf16[64,52,128]{2,1,0:T(8,128)(2,1)S(1)}, u32[]{:S(2)}, u32[]{:S(2)}) async-start(bf16[64,52,128]{2,1,0:T(8,128)(2,1)} %broadcast_in_dim.45), calls=%async_computation.3 | async-start | bytes 1835008 | tf_op jit(solution)/shard_map/all_to_all | solution.py:125
  108.6 47.5 %collective-permute-start = (bf16[2,512,128]{2,1,0:T(8,128)(2,1)S(1)}, bf16[2,512,128]{2,1,0:T(8,128)(2,1)S(1)}, u32[]{:S(2)}, u32[]{:S(2)}) collective-permute-start(bf16[2,512,128]{2,1,0:T(8,128)(2,1)S(1)} %maximum_select_fusion), channel_id=1, source_target_pairs={{504,0},{0,8},{8,16},{16,24},{24,32},{32,40},{40,48},{48,56},{56,6... | collective-permute-start | bytes 786440 | tf_op jit(solution)/shard_map/ppermute | solution.py:25

commit v7 on v4

--- a/solution.py
+++ b/solution.py
@@ -143,14 +143,30 @@
     sink = jnp.where(my_seq == 0, sink, jnp.zeros_like(sink))
     both = jnp.concatenate([pieces, sink], 1)
 
-    kv = jnp.stack([keys, values], 0)
-    kv_local = lax.all_to_all(kv, "head", split_axis=2, concat_axis=1, tiled=True)
+    head_devices = lax.axis_size("head")
+    my_head = lax.axis_index("head")
+    q_width = queries.shape[1] // head_devices
+    kv_width = keys.shape[1] // head_devices
+
+    def columns_for(dest):
+        q_part = lax.dynamic_slice_in_dim(queries, dest * q_width, q_width, 1)
+        k_part = lax.dynamic_slice_in_dim(keys, dest * kv_width, kv_width, 1)
+        v_part = lax.dynamic_slice_in_dim(values, dest * kv_width, kv_width, 1)
+        return jnp.concatenate([q_part, k_part, v_part], 1)
+
+    received = [columns_for(my_head)]
+    for k in range(1, head_devices):
+        received.append(shifted(columns_for((my_head + k) % head_devices), "head", k))
+    total = scatter_sum(both, seq_devices)
+    total, received = lax.optimization_barrier((total, received))
+    by_shift = jnp.stack(received, 0)
+    order = (my_head - jnp.arange(head_devices, dtype=jnp.int32)) % head_devices
+    tokens = by_shift[order].reshape(-1, q_width + 2 * kv_width)
+    q_local = tokens[:, :q_width]
+    kv_local = jnp.stack([tokens[:, q_width:q_width + kv_width], tokens[:, q_width + kv_width:]], 0)
     tail_cache = jnp.stack([prefix_keys[cache_rows - WIN:], prefix_values[cache_rows - WIN:]], 0)
     outgoing = jnp.where(my_seq == seq_devices - 1, tail_cache, kv_local)
     prev_kv = shifted(outgoing, "seq", 1)
-    q_local = lax.all_to_all(queries, "head", split_axis=1, concat_axis=0, tiled=True)
-    total = scatter_sum(both, seq_devices)
-    total, prev_kv, q_local = lax.optimization_barrier((total, prev_kv, q_local))
     side = gather_sums(total, both.shape, seq_devices)
 
     slot_l = jnp.where(is_ret, slot, 0).astype(jnp.int32)

time: 176 us -> 156 us (0.89); the launches traced: 173 us -> 156 us
  waiting for transfers between devices: 108 us -> 65.7 us
  starting transfers between devices: 36.9 us -> 47.4 us
  Pallas kernels: 15.2 us -> 21.4 us
  local copies, waits for them, and re-layouts: 9.08 us -> 14.8 us
  other arithmetic: 3.16 us -> 5.73 us
    all_to_all x1, waiting for transfers between devices: 46.8 us -> 27 us  [scatter_sum(): mine = lax.all_to_all(flat, 'seq', 0, 0, tiled=True)]
    ppermute x1 -> x8, starting transfers between devices: 3.3 us -> 21.7 us  [shifted(): return lax.ppermute(block, axis, route)]
    ppermute x1 -> x8, waiting for transfers between devices: 9.13 us -> 0.02 us  [shifted(): return lax.ppermute(block, axis, route)]
    all_to_all x1, waiting for transfers between devices: 46.7 us -> 38.7 us  [gather_sums(): lax.all_to_all(jnp.broadcast_to(total, (seq_devices,) + total.shape[1:]),...]
    all_to_all x2 -> x0, starting transfers between devices: 8.03 us -> none  [the longest x1 4.47 us: shards(): lax.all_to_all(kv, 'head', split_axis=2, concat_axis=1, tiled=True)]
    pallas_call x1, Pallas kernels: 15.2 us -> 21.4 us  [attend(): pl.pallas_call(attend_kernel, grid_spec=grid_spec, out_shape=jax.ShapeDty...]
    all_to_all x2 -> x0, waiting for transfers between devices: 5.85 us -> none  [the longest x1 3.45 us: shards(): lax.all_to_all(kv, 'head', split_axis=2, concat_axis=1, tiled=True)]
    unnamed x21 -> x42, local copies, waits for them, and re-layouts: 1.69 us -> 4.84 us
  transfers between devices with their start and end apart: 5 -> 10, of which waited for: 5 -> 2; matrix products, arithmetic and copies ran while one was open for 4% -> 6% of each run, Pallas kernels for 0% -> 0%
where the time goes in v7:
time: 156 us
  waiting for transfers between devices  65.7 us (42%)
  starting transfers between devices  47.4 us (30%)
  Pallas kernels  21.4 us (14%)
  local copies, waits for them, and re-layouts  14.8 us (9%)
  other arithmetic  5.73 us (4%)
    all_to_all x1, waiting for transfers between devices, gather_sums(): lax.all_to_all(jnp.broadcast_to(total, (seq_devices,) + total.shape[1:]),...  38.7 us
    all_to_all x1, waiting for transfers between devices, scatter_sum(): mine = lax.all_to_all(flat, 'seq', 0, 0, tiled=True)  27 us
    ppermute x8, starting transfers between devices, shifted(): return lax.ppermute(block, axis, route)  21.7 us
    pallas_call x1, Pallas kernels, attend(): pl.pallas_call(attend_kernel, grid_spec=grid_spec, out_shape=jax.ShapeDty...  21.4 us
    all_to_all x1, starting transfers between devices, scatter_sum(): mine = lax.all_to_all(flat, 'seq', 0, 0, tiled=True)  18.9 us
    all_to_all x1, starting transfers between devices, gather_sums(): lax.all_to_all(jnp.broadcast_to(total, (seq_devices,) + total.shape[1:]),...  6.78 us
    unnamed x42, local copies, waits for them, and re-layouts  4.84 us
  transfers between devices with their start and end apart: 10, of which 2 were waited for; matrix products, arithmetic and copies ran while one was open for 6% of the time, Pallas kernels for 0%

profile of v7, /device:TPU:6, one launch (start us, length us, event | category | flops | bytes accessed | tf_op | source)
XLA Modules:
  0.0 155.7 jit_solution(7624357395218415729)
XLA Ops:
  0.0 0.0 copy-start
  0.0 0.7 broadcast_compare_fusion
  0.7 0.2 reduce-window.7
  0.9 0.6 iota_reduce_fusion
  1.5 0.0 copy-done
  1.5 0.6 gather_fusion
  2.1 0.1 reshape.199
  2.2 0.8 slice_bitcast_fusion.4
  3.0 1.3 pad_maximum_fusion
  4.3 0.7 gather_fusion.1
  5.0 0.1 copy.15
  5.1 0.1 broadcast_in_dim.40
  5.2 0.1 broadcast_in_dim.41
  5.3 0.3 bitcast_select_fusion
  5.6 0.1 pad_maximum_fusion.1
  5.6 1.1 reshape.185
  6.7 18.9 %all-to-all-start = ((bf16[64,52,128]{2,1,0:T(8,128)(2,1)}), bf16[64,52,128]{2,1,0:T(8,128)(2,1)S(1)}, u32[]{:S(2)}, u32[]{:S(2)}) async-start(bf16[64,52,128]{2,1,0:T(8,128)(2,1)} %reshape.185), calls=%async_computation | async-start | bytes 1835008 | tf_op jit(solution)/shard_map/all_to_all | solution.py:114
  25.8 0.0 copy-done.13
  25.8 0.0 copy-done.14
  25.8 0.1 constant_dynamic-slice_fusion
  25.9 0.0 copy-done.1
  25.9 0.1 constant_dynamic-slice_fusion.2
  26.0 0.0 collective-permute-start
  26.1 3.5 %collective-permute-start.1 = (bf16[64,1280]{1,0:T(8,128)(2,1)S(1)}, bf16[64,1280]{1,0:T(8,128)(2,1)S(1)}, u32[]{:S(2)}, u32[]{:S(2)}) collective-permute-start(bf16[64,1280]{1,0:T(8,128)(2,1)S(1)} %pad_maximum_fusion.5), channel_id=1, source_target_pairs={{6,0},{7,1},{0,2},{1,3},{2,4},{3,5},{4,6},{5,7},{14,8},{15,9},{8,1... | collective-permute-start | bytes 491528 | tf_op jit(solution)/shard_map/ppermute | solution.py:25
  29.6 4.2 %collective-permute-start.2 = (bf16[64,1280]{1,0:T(8,128)(2,1)S(1)}, bf16[64,1280]{1,0:T(8,128)(2,1)S(1)}, u32[]{:S(2)}, u32[]{:S(2)}) collective-permute-start(bf16[64,1280]{1,0:T(8,128)(2,1)S(1)} %pad_maximum_fusion.6), channel_id=1, source_target_pairs={{5,0},{6,1},{7,2},{0,3},{1,4},{2,5},{3,6},{4,7},{13,8},{14,9},{15,... | collective-permute-start | bytes 491528 | tf_op jit(solution)/shard_map/ppermute | solution.py:25
  33.8 3.7 %collective-permute-start.3 = (bf16[64,1280]{1,0:T(8,128)(2,1)S(1)}, bf16[64,1280]{1,0:T(8,128)(2,1)S(1)}, u32[]{:S(2)}, u32[]{:S(2)}) collective-permute-start(bf16[64,1280]{1,0:T(8,128)(2,1)S(1)} %pad_maximum_fusion.7), channel_id=1, source_target_pairs={{4,0},{5,1},{6,2},{7,3},{0,4},{1,5},{2,6},{3,7},{12,8},{13,9},{14,... | collective-permute-start | bytes 491528 | tf_op jit(solution)/shard_map/ppermute | solution.py:25
  37.6 3.7 %collective-permute-start.4 = (bf16[64,1280]{1,0:T(8,128)(2,1)S(1)}, bf16[64,1280]{1,0:T(8,128)(2,1)S(1)}, u32[]{:S(2)}, u32[]{:S(2)}) collective-permute-start(bf16[64,1280]{1,0:T(8,128)(2,1)S(1)} %pad_maximum_fusion.8), channel_id=1, source_target_pairs={{3,0},{4,1},{5,2},{6,3},{7,4},{0,5},{1,6},{2,7},{11,8},{12,9},{13,... | collective-permute-start | bytes 491528 | tf_op jit(solution)/shard_map/ppermute | solution.py:25
  41.3 1.7 %slice_bitcast_fusion.2 = (bf16[1,512,128]{2,1,0:T(8,128)(2,1)}, bf16[1,512,128]{2,1,0:T(8,128)(2,1)}) fusion(bf16[2048,128]{1,0:T(8,128)(2,1)} %param.13, bf16[2048,128]{1,0:T(8,128)(2,1)} %param.12), kind=kLoop, calls=%fused_computation.26 | loop fusion | bytes 524288 | tf_op jit(solution)/shard_map/stack | solution.py:167
  43.0 0.0 collective-permute-done
  43.0 3.3 %collective-permute-start.5 = (bf16[64,1280]{1,0:T(8,128)(2,1)S(1)}, bf16[64,1280]{1,0:T(8,128)(2,1)S(1)}, u32[]{:S(2)}, u32[]{:S(2)}) collective-permute-start(bf16[64,1280]{1,0:T(8,128)(2,1)S(1)} %pad_maximum_fusion.9), channel_id=1, source_target_pairs={{2,0},{3,1},{4,2},{5,3},{6,4},{7,5},{0,6},{1,7},{10,8},{11,9},{12,... | collective-permute-start | bytes 491528 | tf_op jit(solution)/shard_map/ppermute | solution.py:25
  46.3 0.0 collective-permute-done.1
  46.3 0.0 copy-start.3
  46.3 0.0 collective-permute-start.6
  46.4 0.6 copy-done.3
  47.0 27.0 %all-to-all-done = bf16[64,52,128]{2,1,0:T(8,128)(2,1)S(1)} async-done(((bf16[64,52,128]{2,1,0:T(8,128)(2,1)}), bf16[64,52,128]{2,1,0:T(8,128)(2,1)S(1)}, u32[]{:S(2)}, u32[]{:S(2)}) %all-to-all-start) | async-done | bytes 852000 | tf_op jit(solution)/shard_map/all_to_all | solution.py:114
  74.0 0.2 reduce_sum.12
  74.2 0.0 collective-permute-done.2
  74.2 0.0 copy-start.5
  74.2 0.0 collective-permute-done.3
  74.2 0.0 copy-start.6
  74.2 0.0 collective-permute-done.4
  74.2 0.0 collective-permute-done.5
  74.3 0.0 collective-permute-done.6
  74.3 0.7 copy-done.9
  75.0 0.7 copy-done.11
  75.7 1.0 broadcast_in_dim.46
  76.8 6.8 %all-to-all-start.1 = ((bf16[64,52,128]{2,1,0:T(8,128)(2,1)}), bf16[64,52,128]{2,1,0:T(8,128)(2,1)S(1)}, u32[]{:S(2)}, u32[]{:S(2)}) async-start(bf16[64,52,128]{2,1,0:T(8,128)(2,1)} %broadcast_in_dim.46), calls=%async_computation.1 | async-start | bytes 1835008 | tf_op jit(solution)/shard_map/all_to_all | solution.py:119
  83.6 1.0 bitcast_dynamic-update-slice_fusion.4
  84.6 0.9 bitcast_dynamic-update-slice_fusion.3
  85.6 0.6 gather_fusion.2
  86.3 0.0 copy-start.15
  86.3 0.0 copy-start.16
  86.3 1.7 %pad_maximum_fusion.2 = (bf16[2,512,128]{2,1,0:T(8,128)(2,1)}, bf16[2,512,128]{2,1,0:T(8,128)(2,1)S(1)}) fusion(bf16[1,512,128]{2,1,0:T(8,128)(2,1)S(1)} %get-tuple-element.26, bf16[1,512,128]{2,1,0:T(8,128)(2,1)S(1)} %get-tuple-element.25, bf16[1,512,128]{2,1,0:T(8,128)(2,1)} %get-tuple-element.67, bf16[1,512,128]{2,1,0:T(8,128)(2,1)} %get-tuple-element.68, ...), kind=kLoop, calls=%fused_computation.7 | loop fusion | flops 393216 | bytes 1048577 | tf_op jit(solution)/shard_map/stack | solution.py:166
  88.0 3.4 %collective-permute-start.7 = (bf16[2,512,128]{2,1,0:T(8,128)(2,1)S(1)}, bf16[2,512,128]{2,1,0:T(8,128)(2,1)S(1)}, u32[]{:S(2)}, u32[]{:S(2)}) collective-permute-start(bf16[2,512,128]{2,1,0:T(8,128)(2,1)S(1)} %get-tuple-element.36), channel_id=1, source_target_pairs={{504,0},{0,8},{8,16},{16,24},{24,32},{32,40},{40,48},{48,56},{56,6... | collective-permute-start | bytes 786440 | tf_op jit(solution)/shard_map/ppermute | solution.py:25
  91.4 0.1 copy.14
  91.5 0.7 reshape.184.diag_ref
  92.2 0.0 copy-done.16
  92.2 0.5 broadcast_select_fusion.slot_ref
  92.7 1.1 slice.34.q_ref
  93.8 38.7 %all-to-all-done.1 = bf16[64,52,128]{2,1,0:T(8,128)(2,1)S(1)} async-done(((bf16[64,52,128]{2,1,0:T(8,128)(2,1)}), bf16[64,52,128]{2,1,0:T(8,128)(2,1)S(1)}, u32[]{:S(2)}, u32[]{:S(2)}) %all-to-all-start.1) | async-done | bytes 852000 | tf_op jit(solution)/shard_map/all_to_all | solution.py:119
  132.5 1.1 reshape.187.vk_ref.vv_ref.sk_ref.sv_ref
  133.6 0.0 collective-permute-done.7.prev_ref
  133.6 0.7 copy-done.2
  134.3 21.4 %shard_map.91 = bf16[512,1024]{1,0:T(8,128)(2,1)} custom-call(s32[8]{0:T(128)} %roles_ref.1, s32[8]{0:T(128)} %broadcast_select_fusion.slot_ref, s32[8]{0:T(128)} %count_ref.1, s32[32]{0:T(128)} %reshape.184.diag_ref, bf16[512,1024]{1,0:T(8,128)(2,1)} %slice.34.q_ref, bf16[2,512,128]{2,1,0:T(8,128)(2,1)} %copy-done.2, ...), custom_call_target="tpu_custom_call" | custom-call | tf_op jit(solution)/shard_map/pallas_call | solution.py:105
  (42 shorter events, 0.3 us)
Async XLA Ops:
  0.0 1.5 copy-start
  6.7 19.1 %copy-start.13 = (bf16[64,1024]{1,0:T(8,128)(2,1)S(1)}, bf16[64,1024]{1,0:T(8,128)(2,1)}, u32[]{:S(2)}) copy-start(bf16[64,1024]{1,0:T(8,128)(2,1)} %param.11) | copy-start | bytes 393220
  6.7 19.1 %copy-start.14 = (bf16[64,1024]{1,0:T(8,128)(2,1)S(1)}, bf16[64,1024]{1,0:T(8,128)(2,1)}, u32[]{:S(2)}) copy-start(bf16[64,1024]{1,0:T(8,128)(2,1)} %param.10) | copy-start | bytes 393220
  6.7 19.2 %copy-start.1 = (bf16[64,8192]{1,0:T(8,128)(2,1)S(1)}, bf16[64,8192]{1,0:T(8,128)(2,1)}, u32[]{:S(2)}) copy-start(bf16[64,8192]{1,0:T(8,128)(2,1)} %param.9) | copy-start | bytes 3145732
  6.7 67.3 %all-to-all-start = ((bf16[64,52,128]{2,1,0:T(8,128)(2,1)}), bf16[64,52,128]{2,1,0:T(8,128)(2,1)S(1)}, u32[]{:S(2)}, u32[]{:S(2)}) async-start(bf16[64,52,128]{2,1,0:T(8,128)(2,1)} %reshape.185), calls=%async_computation | async-start | bytes 1835008 | tf_op jit(solution)/shard_map/all_to_all | solution.py:114
  26.0 17.0 %collective-permute-start = (bf16[64,1280]{1,0:T(8,128)(2,1)S(1)}, bf16[64,1280]{1,0:T(8,128)(2,1)S(1)}, u32[]{:S(2)}, u32[]{:S(2)}) collective-permute-start(bf16[64,1280]{1,0:T(8,128)(2,1)S(1)} %pad_maximum_fusion.4), channel_id=1, source_target_pairs={{7,0},{0,1},{1,2},{2,3},{3,4},{4,5},{5,6},{6,7},{15,8},{8,9},{9,10... | collective-permute-start | bytes 491528 | tf_op jit(solution)/shard_map/ppermute | solution.py:25
  26.1 20.2 %collective-permute-start.1 = (bf16[64,1280]{1,0:T(8,128)(2,1)S(1)}, bf16[64,1280]{1,0:T(8,128)(2,1)S(1)}, u32[]{:S(2)}, u32[]{:S(2)}) collective-permute-start(bf16[64,1280]{1,0:T(8,128)(2,1)S(1)} %pad_maximum_fusion.5), channel_id=1, source_target_pairs={{6,0},{7,1},{0,2},{1,3},{2,4},{3,5},{4,6},{5,7},{14,8},{15,9},{8,1... | collective-permute-start | bytes 491528 | tf_op jit(solution)/shard_map/ppermute | solution.py:25
  29.6 44.6 %collective-permute-start.2 = (bf16[64,1280]{1,0:T(8,128)(2,1)S(1)}, bf16[64,1280]{1,0:T(8,128)(2,1)S(1)}, u32[]{:S(2)}, u32[]{:S(2)}) collective-permute-start(bf16[64,1280]{1,0:T(8,128)(2,1)S(1)} %pad_maximum_fusion.6), channel_id=1, source_target_pairs={{5,0},{6,1},{7,2},{0,3},{1,4},{2,5},{3,6},{4,7},{13,8},{14,9},{15,... | collective-permute-start | bytes 491528 | tf_op jit(solution)/shard_map/ppermute | solution.py:25
  33.8 40.4 %collective-permute-start.3 = (bf16[64,1280]{1,0:T(8,128)(2,1)S(1)}, bf16[64,1280]{1,0:T(8,128)(2,1)S(1)}, u32[]{:S(2)}, u32[]{:S(2)}) collective-permute-start(bf16[64,1280]{1,0:T(8,128)(2,1)S(1)} %pad_maximum_fusion.7), channel_id=1, source_target_pairs={{4,0},{5,1},{6,2},{7,3},{0,4},{1,5},{2,6},{3,7},{12,8},{13,9},{14,... | collective-permute-start | bytes 491528 | tf_op jit(solution)/shard_map/ppermute | solution.py:25
  37.6 36.6 %collective-permute-start.4 = (bf16[64,1280]{1,0:T(8,128)(2,1)S(1)}, bf16[64,1280]{1,0:T(8,128)(2,1)S(1)}, u32[]{:S(2)}, u32[]{:S(2)}) collective-permute-start(bf16[64,1280]{1,0:T(8,128)(2,1)S(1)} %pad_maximum_fusion.8), channel_id=1, source_target_pairs={{3,0},{4,1},{5,2},{6,3},{7,4},{0,5},{1,6},{2,7},{11,8},{12,9},{13,... | collective-permute-start | bytes 491528 | tf_op jit(solution)/shard_map/ppermute | solution.py:25
  43.0 31.2 %collective-permute-start.5 = (bf16[64,1280]{1,0:T(8,128)(2,1)S(1)}, bf16[64,1280]{1,0:T(8,128)(2,1)S(1)}, u32[]{:S(2)}, u32[]{:S(2)}) collective-permute-start(bf16[64,1280]{1,0:T(8,128)(2,1)S(1)} %pad_maximum_fusion.9), channel_id=1, source_target_pairs={{2,0},{3,1},{4,2},{5,3},{6,4},{7,5},{0,6},{1,7},{10,8},{11,9},{12,... | collective-permute-start | bytes 491528 | tf_op jit(solution)/shard_map/ppermute | solution.py:25
  46.3 0.7 copy-start.3
  46.3 27.9 %collective-permute-start.6 = (bf16[64,1280]{1,0:T(8,128)(2,1)S(1)}, bf16[64,1280]{1,0:T(8,128)(2,1)S(1)}, u32[]{:S(2)}, u32[]{:S(2)}) collective-permute-start(bf16[64,1280]{1,0:T(8,128)(2,1)S(1)} %pad_maximum_fusion.10), channel_id=1, source_target_pairs={{1,0},{2,1},{3,2},{4,3},{5,4},{6,5},{7,6},{0,7},{9,8},{10,9},{11,1... | collective-permute-start | bytes 491528 | tf_op jit(solution)/shard_map/ppermute | solution.py:25
  74.2 2.6 %copy-start.5 = (bf16[64,1280]{1,0:T(8,128)(2,1)}, bf16[64,1280]{1,0:T(8,128)(2,1)S(1)}, u32[]{:S(2)}) copy-start(bf16[64,1280]{1,0:T(8,128)(2,1)S(1)} %collective-permute-done.2) | copy-start | bytes 491524
  74.2 2.5 %copy-start.6 = (bf16[64,1280]{1,0:T(8,128)(2,1)}, bf16[64,1280]{1,0:T(8,128)(2,1)S(1)}, u32[]{:S(2)}) copy-start(bf16[64,1280]{1,0:T(8,128)(2,1)S(1)} %collective-permute-done.3) | copy-start | bytes 491524
  74.2 2.5 %copy-start.7 = (bf16[64,1280]{1,0:T(8,128)(2,1)}, bf16[64,1280]{1,0:T(8,128)(2,1)S(1)}, u32[]{:S(2)}) copy-start(bf16[64,1280]{1,0:T(8,128)(2,1)S(1)} %collective-permute-done.4) | copy-start | bytes 491524
  74.3 0.8 copy-start.9
  75.0 0.7 copy-start.11
  76.7 6.8 %copy-start.4 = (bf16[64,1280]{1,0:T(8,128)(2,1)S(1)}, bf16[64,1280]{1,0:T(8,128)(2,1)}, u32[]{:S(2)}) copy-start(bf16[64,1280]{1,0:T(8,128)(2,1)} %copy-done.3) | copy-start | bytes 491524
  76.7 8.8 %copy-start.10 = (bf16[64,1280]{1,0:T(8,128)(2,1)S(1)}, bf16[64,1280]{1,0:T(8,128)(2,1)}, u32[]{:S(2)}) copy-start(bf16[64,1280]{1,0:T(8,128)(2,1)} %copy-done.9) | copy-start | bytes 491524
  76.8 55.7 %all-to-all-start.1 = ((bf16[64,52,128]{2,1,0:T(8,128)(2,1)}), bf16[64,52,128]{2,1,0:T(8,128)(2,1)S(1)}, u32[]{:S(2)}, u32[]{:S(2)}) async-start(bf16[64,52,128]{2,1,0:T(8,128)(2,1)} %broadcast_in_dim.46), calls=%async_computation.1 | async-start | bytes 1835008 | tf_op jit(solution)/shard_map/all_to_all | solution.py:119
  83.6 2.0 %copy-start.8 = (bf16[64,1280]{1,0:T(8,128)(2,1)S(1)}, bf16[64,1280]{1,0:T(8,128)(2,1)}, u32[]{:S(2)}) copy-start(bf16[64,1280]{1,0:T(8,128)(2,1)} %copy-done.7) | copy-start | bytes 491524
  83.6 2.0 %copy-start.12 = (bf16[64,1280]{1,0:T(8,128)(2,1)S(1)}, bf16[64,1280]{1,0:T(8,128)(2,1)}, u32[]{:S(2)}) copy-start(bf16[64,1280]{1,0:T(8,128)(2,1)} %copy-done.11) | copy-start | bytes 491524
  86.3 5.1 %copy-start.15 = (s32[8,4]{0,1:T(4,128)S(1)}, s32[8,4]{0,1:T(4,128)}, u32[]{:S(2)}) copy-start(s32[8,4]{0,1:T(4,128)} %param.17) | copy-start | bytes 388
  86.3 5.9 %copy-start.16 = (s32[8]{0:T(128)S(1)}, s32[8]{0:T(128)}, u32[]{:S(2)}) copy-start(s32[8]{0:T(128)} %roles_ref.1) | copy-start | bytes 100
  88.0 45.6 %collective-permute-start.7 = (bf16[2,512,128]{2,1,0:T(8,128)(2,1)S(1)}, bf16[2,512,128]{2,1,0:T(8,128)(2,1)S(1)}, u32[]{:S(2)}, u32[]{:S(2)}) collective-permute-start(bf16[2,512,128]{2,1,0:T(8,128)(2,1)S(1)} %get-tuple-element.36), channel_id=1, source_target_pairs={{504,0},{0,8},{8,16},{16,24},{24,32},{32,40},{40,48},{48,56},{56,6... | collective-permute-start | bytes 786440 | tf_op jit(solution)/shard_map/ppermute | solution.py:25
  133.6 0.7 copy-start.2

commit v8 on v7

--- a/solution.py
+++ b/solution.py
@@ -25,8 +25,14 @@
     return lax.ppermute(block, axis, route)
 
 
-def attend_kernel(roles_ref, slot_ref, count_ref, diag_ref,
-                  q_ref, prev_ref, own_ref, vk_ref, vv_ref, sk_ref, sv_ref, o_ref):
+def exact_dot(weights, vals):
+    hi = weights.astype(jnp.bfloat16)
+    lo = (weights - hi.astype(jnp.float32)).astype(jnp.bfloat16)
+    out = jnp.dot(hi, vals, preferred_element_type=jnp.float32)
+    return out + jnp.dot(lo, vals, preferred_element_type=jnp.float32)
+
+
+def local_kernel(roles_ref, diag_ref, q_ref, prev_ref, own_ref, o_ref, m_ref, l_ref):
     h = pl.program_id(0)
     rows = q_ref.shape[0]
     scaling = 1.0 / math.sqrt(HEAD_SIZE)
@@ -41,37 +47,23 @@
     row = lax.broadcasted_iota(jnp.int32, (rows, rows), 0)
     col = lax.broadcasted_iota(jnp.int32, (rows, rows), 1)
 
-    def finish(s_side, ok_side, v_side, ok_prev, ok_own):
+    def finish(ok_prev, ok_own):
         neg = -jnp.inf
-        m_side = jnp.max(jnp.where(ok_side, s_side, neg), axis=1, keepdims=True)
-        m_prev = jnp.max(jnp.where(ok_prev, s_prev, neg), axis=1, keepdims=True)
-        m_own = jnp.max(jnp.where(ok_own, s_own, neg), axis=1, keepdims=True)
-        m = jnp.maximum(jnp.maximum(m_side, m_prev), m_own)
-        e_side = jnp.where(ok_side, jnp.exp(s_side - m), 0.0)
+        m = jnp.maximum(jnp.max(jnp.where(ok_prev, s_prev, neg), axis=1, keepdims=True),
+                        jnp.max(jnp.where(ok_own, s_own, neg), axis=1, keepdims=True))
         e_prev = jnp.where(ok_prev, jnp.exp(s_prev - m), 0.0)
         e_own = jnp.where(ok_own, jnp.exp(s_own - m), 0.0)
-        total = (jnp.sum(e_side, axis=1, keepdims=True)
-                 + jnp.sum(e_prev, axis=1, keepdims=True)
-                 + jnp.sum(e_own, axis=1, keepdims=True))
-        p_side = (e_side / total).astype(jnp.bfloat16)
-        p_prev = (e_prev / total).astype(jnp.bfloat16)
-        p_own = (e_own / total).astype(jnp.bfloat16)
-        out = jnp.dot(p_side, v_side, preferred_element_type=jnp.float32)
-        out = out + jnp.dot(p_prev, prev_ref[1], preferred_element_type=jnp.float32)
-        out = out + jnp.dot(p_own, own_ref[1], preferred_element_type=jnp.float32)
-        o_ref[...] = out.astype(o_ref.dtype)
+        total = jnp.sum(e_prev, axis=1, keepdims=True) + jnp.sum(e_own, axis=1, keepdims=True)
+        o_ref[...] = exact_dot(e_prev, prev_ref[1]) + exact_dot(e_own, own_ref[1])
+        m_ref[...] = jnp.broadcast_to(m, m_ref.shape)
+        l_ref[...] = jnp.broadcast_to(total, l_ref.shape)
 
     @pl.when(roles_ref[h] != 1)
     def _():
-        s_side = scores(sk_ref[...])
-        ok_side = jnp.ones(s_side.shape, jnp.bool_)
-        finish(s_side, ok_side, sv_ref[...], col > row, col <= row)
+        finish(col > row, col <= row)
 
     @pl.when(roles_ref[h] == 1)
     def _():
-        s_side = scores(vk_ref[...])
-        side_col = lax.broadcasted_iota(jnp.int32, s_side.shape, 1)
-        ok_side = side_col // BLK < count_ref[h]
         rel_prev = row // BLK + rows // BLK - col // BLK
         rel_own = row // BLK - col // BLK
         ok_prev = jnp.zeros((rows, rows), jnp.bool_)
@@ -80,21 +72,77 @@
             off = diag_ref[h * NSL + d]
             ok_prev = ok_prev | (rel_prev == off)
             ok_own = ok_own | ((rel_own == off) & ((off > 0) | (col <= row)))
-        finish(s_side, ok_side, vv_ref[...], ok_prev, ok_own)
-
-
-def attend(roles_l, slot_l, count_l, diag_l, q_local, prev_kv, own_kv, side):
+        finish(ok_prev, ok_own)
+
+
+def side_kernel(roles_ref, slot_ref, count_ref, q_ref, o_loc_ref, m_ref, l_ref,
+                vk_ref, vv_ref, sk_ref, sv_ref, o_ref):
+    h = pl.program_id(0)
+    scaling = 1.0 / math.sqrt(HEAD_SIZE)
+    q = q_ref[...]
+    dims = (((1,), (1,)), ((), ()))
+
+    def merge(keys, vals, ok):
+        s = lax.dot_general(q, keys, dims, preferred_element_type=jnp.float32) * scaling
+        m_loc = m_ref[:, 0:1]
+        m = jnp.maximum(m_loc, jnp.max(jnp.where(ok, s, -jnp.inf), axis=1, keepdims=True))
+        e = jnp.where(ok, jnp.exp(s - m), 0.0)
+        scale_loc = jnp.exp(m_loc - m)
+        total = l_ref[:, 0:1] * scale_loc + jnp.sum(e, axis=1, keepdims=True)
+        out = o_loc_ref[...] * scale_loc + exact_dot(e, vals)
+        o_ref[...] = (out / total).astype(o_ref.dtype)
+
+    @pl.when(roles_ref[h] != 1)
+    def _():
+        merge(sk_ref[...], sv_ref[...], jnp.ones((q.shape[0], sk_ref.shape[0]), jnp.bool_))
+
+    @pl.when(roles_ref[h] == 1)
+    def _():
+        side_col = lax.broadcasted_iota(jnp.int32, (q.shape[0], vk_ref.shape[0]), 1)
+        merge(vk_ref[...], vv_ref[...], side_col // BLK < count_ref[h])
+
+
+def attend_local(roles_l, diag_l, q_local, prev_kv, own_kv):
+    rows = q_local.shape[0]
+    heads = q_local.shape[1] // HEAD_SIZE
+    grid_spec = pltpu.PrefetchScalarGridSpec(
+        num_scalar_prefetch=2,
+        grid=(heads,),
+        in_specs=[
+            pl.BlockSpec((rows, HEAD_SIZE), lambda h, *_: (0, h)),
+            pl.BlockSpec((2, rows, HEAD_SIZE), lambda h, *_: (0, 0, 0)),
+            pl.BlockSpec((2, rows, HEAD_SIZE), lambda h, *_: (0, 0, 0)),
+        ],
+        out_specs=[
+            pl.BlockSpec((rows, HEAD_SIZE), lambda h, *_: (0, h)),
+            pl.BlockSpec((None, rows, HEAD_SIZE), lambda h, *_: (h, 0, 0)),
+            pl.BlockSpec((None, rows, HEAD_SIZE), lambda h, *_: (h, 0, 0)),
+        ],
+    )
+    return pl.pallas_call(
+        local_kernel,
+        grid_spec=grid_spec,
+        out_shape=[
+            jax.ShapeDtypeStruct(q_local.shape, jnp.float32),
+            jax.ShapeDtypeStruct((heads, rows, HEAD_SIZE), jnp.float32),
+            jax.ShapeDtypeStruct((heads, rows, HEAD_SIZE), jnp.float32),
+        ],
+    )(roles_l, diag_l, q_local, prev_kv, own_kv)
+
+
+def attend_side(roles_l, slot_l, count_l, q_local, o_loc, m_loc, l_loc, side):
     rows = q_local.shape[0]
     heads = q_local.shape[1] // HEAD_SIZE
     vrows = VB * BLK
     sink_block = MAX_RETRIEVERS * vrows // SINK
     grid_spec = pltpu.PrefetchScalarGridSpec(
-        num_scalar_prefetch=4,
+        num_scalar_prefetch=3,
         grid=(heads,),
         in_specs=[
             pl.BlockSpec((rows, HEAD_SIZE), lambda h, *_: (0, h)),
-            pl.BlockSpec((2, rows, HEAD_SIZE), lambda h, *_: (0, 0, 0)),
-            pl.BlockSpec((2, rows, HEAD_SIZE), lambda h, *_: (0, 0, 0)),
+            pl.BlockSpec((rows, HEAD_SIZE), lambda h, *_: (0, h)),
+            pl.BlockSpec((None, rows, HEAD_SIZE), lambda h, *_: (h, 0, 0)),
+            pl.BlockSpec((None, rows, HEAD_SIZE), lambda h, *_: (h, 0, 0)),
             pl.BlockSpec((None, vrows, HEAD_SIZE), lambda h, r, s, *_: (0, s[h], 0)),
             pl.BlockSpec((None, vrows, HEAD_SIZE), lambda h, r, s, *_: (1, s[h], 0)),
             pl.BlockSpec((None, SINK, HEAD_SIZE), lambda h, *_: (0, sink_block, 0)),
@@ -103,10 +151,10 @@
         out_specs=pl.BlockSpec((rows, HEAD_SIZE), lambda h, *_: (0, h)),
     )
     return pl.pallas_call(
-        attend_kernel,
+        side_kernel,
         grid_spec=grid_spec,
         out_shape=jax.ShapeDtypeStruct(q_local.shape, jnp.bfloat16),
-    )(roles_l, slot_l, count_l, diag_l, q_local, prev_kv, own_kv, side, side, side, side)
+    )(roles_l, slot_l, count_l, q_local, o_loc, m_loc, l_loc, side, side, side, side)
 
 
 def scatter_sum(block, seq_devices):
@@ -170,16 +218,10 @@
     side = gather_sums(total, both.shape, seq_devices)
 
     slot_l = jnp.where(is_ret, slot, 0).astype(jnp.int32)
-    return attend(
-        roles.astype(jnp.int32),
-        slot_l,
-        col_count.astype(jnp.int32),
-        diagonals.reshape(heads * NSL).astype(jnp.int32),
-        q_local,
-        prev_kv,
-        kv_local,
-        side,
-    )
+    roles_l = roles.astype(jnp.int32)
+    o_loc, m_loc, l_loc = attend_local(
+        roles_l, diagonals.reshape(heads * NSL).astype(jnp.int32), q_local, prev_kv, kv_local)
+    return attend_side(roles_l, slot_l, col_count.astype(jnp.int32), q_local, o_loc, m_loc, l_loc, side)
 
 
 def solution(mesh):

time: 156 us -> 164 us (1.051); the launches traced: 156 us -> 162 us
  Pallas kernels: 21.4 us -> 30.3 us
  local copies, waits for them, and re-layouts: 14.8 us -> 11.6 us
    all_to_all x1, waiting for transfers between devices: 38.7 us -> 0.01 us  [gather_sums(): lax.all_to_all(jnp.broadcast_to(total, (seq_devices,) + total.shape[1:]),...]
    ppermute x8, waiting for transfers between devices: 0.02 us -> 38.4 us  [shifted(): return lax.ppermute(block, axis, route)]
    pallas_call x1 -> x2, Pallas kernels: 21.4 us -> 30.3 us  [the longest x1 19.8 us: attend_local(): pl.pallas_call(local_kernel, grid_spec=grid_spec, out_shape=[jax.ShapeDty...]
    unnamed x42 -> x30, local copies, waits for them, and re-layouts: 4.84 us -> 1.74 us
  transfers between devices with their start and end apart: 10 -> 10, of which waited for: 2 -> 2; matrix products, arithmetic and copies ran while one was open for 6% -> 4% of each run, Pallas kernels for 0% -> 12%
where the time goes in v8:
time: 164 us; the launch traced here: 162 us
  waiting for transfers between devices  65.7 us (40%)
  starting transfers between devices  47.7 us (29%)
  Pallas kernels  30.3 us (18%)
  local copies, waits for them, and re-layouts  11.6 us (7%)
  other arithmetic  5.68 us (3%)
    ppermute x8, waiting for transfers between devices, shifted(): return lax.ppermute(block, axis, route)  38.4 us
    all_to_all x1, waiting for transfers between devices, scatter_sum(): mine = lax.all_to_all(flat, 'seq', 0, 0, tiled=True)  27.3 us
    ppermute x8, starting transfers between devices, shifted(): return lax.ppermute(block, axis, route)  22.2 us
    pallas_call x1, Pallas kernels, attend_local(): pl.pallas_call(local_kernel, grid_spec=grid_spec, out_shape=[jax.ShapeDty...  19.8 us
    all_to_all x1, starting transfers between devices, scatter_sum(): mine = lax.all_to_all(flat, 'seq', 0, 0, tiled=True)  18.9 us
    pallas_call x1, Pallas kernels, attend_side(): pl.pallas_call(side_kernel, grid_spec=grid_spec, out_shape=jax.ShapeDtype...  10.5 us
    all_to_all x1, starting transfers between devices, gather_sums(): lax.all_to_all(jnp.broadcast_to(total, (seq_devices,) + total.shape[1:]),...  6.63 us
  transfers between devices with their start and end apart: 10, of which 2 were waited for; matrix products, arithmetic and copies ran while one was open for 4% of the time, Pallas kernels for 12%

profile of v8, /device:TPU:6, one launch (start us, length us, event | category | flops | bytes accessed | tf_op | source)
XLA Modules:
  0.0 161.5 jit_solution(18052400085344134737)
XLA Ops:
  0.0 0.0 copy-start
  0.0 0.7 broadcast_compare_fusion
  0.7 0.2 reduce-window.7
  0.9 0.6 iota_reduce_fusion
  1.5 0.0 copy-done
  1.5 0.6 gather_fusion
  2.1 0.1 reshape.199
  2.2 0.1 broadcast_in_dim.40
  2.3 0.1 broadcast_in_dim.41
  2.4 0.8 slice_bitcast_fusion.4
  3.2 1.3 pad_maximum_fusion
  4.5 0.7 gather_fusion.1
  5.2 0.1 copy.14
  5.2 0.3 bitcast_select_fusion
  5.6 0.1 pad_maximum_fusion.1
  5.6 1.1 reshape.184
  6.7 18.9 %all-to-all-start = ((bf16[64,52,128]{2,1,0:T(8,128)(2,1)}), bf16[64,52,128]{2,1,0:T(8,128)(2,1)S(1)}, u32[]{:S(2)}, u32[]{:S(2)}) async-start(bf16[64,52,128]{2,1,0:T(8,128)(2,1)} %reshape.184), calls=%async_computation | async-start | bytes 1835008 | tf_op jit(solution)/shard_map/all_to_all | solution.py:162
  25.8 0.0 copy-done.7
  25.8 0.0 copy-done.8
  25.8 0.1 constant_dynamic-slice_fusion
  25.9 0.0 copy-done.1
  25.9 0.1 constant_dynamic-slice_fusion.2
  26.0 4.9 %collective-permute-start.5 = (bf16[64,1280]{1,0:T(8,128)(2,1)S(1)}, bf16[64,1280]{1,0:T(8,128)(2,1)S(1)}, u32[]{:S(2)}, u32[]{:S(2)}) collective-permute-start(bf16[64,1280]{1,0:T(8,128)(2,1)S(1)} %pad_maximum_fusion.9), channel_id=1, source_target_pairs={{2,0},{3,1},{4,2},{5,3},{6,4},{7,5},{0,6},{1,7},{10,8},{11,9},{12,... | collective-permute-start | bytes 491528 | tf_op jit(solution)/shard_map/ppermute | solution.py:25
  31.0 0.0 collective-permute-start
  31.0 1.9 %collective-permute-start.1 = (bf16[64,1280]{1,0:T(8,128)(2,1)S(1)}, bf16[64,1280]{1,0:T(8,128)(2,1)S(1)}, u32[]{:S(2)}, u32[]{:S(2)}) collective-permute-start(bf16[64,1280]{1,0:T(8,128)(2,1)S(1)} %pad_maximum_fusion.5), channel_id=1, source_target_pairs={{6,0},{7,1},{0,2},{1,3},{2,4},{3,5},{4,6},{5,7},{14,8},{15,9},{8,1... | collective-permute-start | bytes 491528 | tf_op jit(solution)/shard_map/ppermute | solution.py:25
  33.0 3.5 %collective-permute-start.2 = (bf16[64,1280]{1,0:T(8,128)(2,1)S(1)}, bf16[64,1280]{1,0:T(8,128)(2,1)S(1)}, u32[]{:S(2)}, u32[]{:S(2)}) collective-permute-start(bf16[64,1280]{1,0:T(8,128)(2,1)S(1)} %pad_maximum_fusion.6), channel_id=1, source_target_pairs={{5,0},{6,1},{7,2},{0,3},{1,4},{2,5},{3,6},{4,7},{13,8},{14,9},{15,... | collective-permute-start | bytes 491528 | tf_op jit(solution)/shard_map/ppermute | solution.py:25
  36.5 4.7 %collective-permute-start.3 = (bf16[64,1280]{1,0:T(8,128)(2,1)S(1)}, bf16[64,1280]{1,0:T(8,128)(2,1)S(1)}, u32[]{:S(2)}, u32[]{:S(2)}) collective-permute-start(bf16[64,1280]{1,0:T(8,128)(2,1)S(1)} %pad_maximum_fusion.7), channel_id=1, source_target_pairs={{4,0},{5,1},{6,2},{7,3},{0,4},{1,5},{2,6},{3,7},{12,8},{13,9},{14,... | collective-permute-start | bytes 491528 | tf_op jit(solution)/shard_map/ppermute | solution.py:25
  41.3 1.7 %slice_bitcast_fusion.2 = (bf16[1,512,128]{2,1,0:T(8,128)(2,1)}, bf16[1,512,128]{2,1,0:T(8,128)(2,1)}) fusion(bf16[2048,128]{1,0:T(8,128)(2,1)} %param.13, bf16[2048,128]{1,0:T(8,128)(2,1)} %param.12), kind=kLoop, calls=%fused_computation.26 | loop fusion | bytes 524288 | tf_op jit(solution)/shard_map/stack | solution.py:215
  43.0 0.0 collective-permute-done.5
  43.0 2.7 %collective-permute-start.4 = (bf16[64,1280]{1,0:T(8,128)(2,1)S(1)}, bf16[64,1280]{1,0:T(8,128)(2,1)S(1)}, u32[]{:S(2)}, u32[]{:S(2)}) collective-permute-start(bf16[64,1280]{1,0:T(8,128)(2,1)S(1)} %pad_maximum_fusion.8), channel_id=1, source_target_pairs={{3,0},{4,1},{5,2},{6,3},{7,4},{0,5},{1,6},{2,7},{11,8},{12,9},{13,... | collective-permute-start | bytes 491528 | tf_op jit(solution)/shard_map/ppermute | solution.py:25
  45.7 0.0 collective-permute-done
  45.7 1.1 collective-permute-start.6
  46.7 27.3 %all-to-all-done = bf16[64,52,128]{2,1,0:T(8,128)(2,1)S(1)} async-done(((bf16[64,52,128]{2,1,0:T(8,128)(2,1)}), bf16[64,52,128]{2,1,0:T(8,128)(2,1)S(1)}, u32[]{:S(2)}, u32[]{:S(2)}) %all-to-all-start) | async-done | bytes 852000 | tf_op jit(solution)/shard_map/all_to_all | solution.py:162
  74.0 0.2 reduce_sum.12
  74.2 0.0 collective-permute-done.1
  74.2 0.0 collective-permute-done.2
  74.2 0.0 collective-permute-done.3
  74.2 0.0 collective-permute-done.4
  74.2 0.0 copy-start.3
  74.2 0.0 collective-permute-done.6
  74.2 0.0 copy-start.5
  74.3 1.0 broadcast_in_dim.46
  75.3 0.0 copy-done.3
  75.3 6.6 %all-to-all-start.1 = ((bf16[64,52,128]{2,1,0:T(8,128)(2,1)}), bf16[64,52,128]{2,1,0:T(8,128)(2,1)S(1)}, u32[]{:S(2)}, u32[]{:S(2)}) async-start(bf16[64,52,128]{2,1,0:T(8,128)(2,1)} %broadcast_in_dim.46), calls=%async_computation.1 | async-start | bytes 1835008 | tf_op jit(solution)/shard_map/all_to_all | solution.py:167
  81.9 0.0 copy-start.4
  81.9 0.0 copy-start.6
  82.1 0.8 copy-done.4
  82.9 0.0 copy-done.6
  83.0 0.6 gather_fusion.2
  83.6 0.0 copy-start.10
  83.6 0.0 copy-start.9
  83.6 1.7 %pad_maximum_fusion.2 = (bf16[2,512,128]{2,1,0:T(8,128)(2,1)}, bf16[2,512,128]{2,1,0:T(8,128)(2,1)S(1)}) fusion(bf16[1,512,128]{2,1,0:T(8,128)(2,1)S(1)} %get-tuple-element.32, bf16[1,512,128]{2,1,0:T(8,128)(2,1)S(1)} %get-tuple-element.31, bf16[1,512,128]{2,1,0:T(8,128)(2,1)} %get-tuple-element.73, bf16[1,512,128]{2,1,0:T(8,128)(2,1)} %get-tuple-element.74, ...), kind=kLoop, calls=%fused_computation.7 | loop fusion | flops 393216 | bytes 1048577 | tf_op jit(solution)/shard_map/stack | solution.py:214
  85.4 3.4 %collective-permute-start.7 = (bf16[2,512,128]{2,1,0:T(8,128)(2,1)S(1)}, bf16[2,512,128]{2,1,0:T(8,128)(2,1)S(1)}, u32[]{:S(2)}, u32[]{:S(2)}) collective-permute-start(bf16[2,512,128]{2,1,0:T(8,128)(2,1)S(1)} %get-tuple-element.42), channel_id=1, source_target_pairs={{504,0},{0,8},{8,16},{16,24},{24,32},{32,40},{40,48},{48,56},{56,6... | collective-permute-start | bytes 786440 | tf_op jit(solution)/shard_map/ppermute | solution.py:25
  88.7 0.0 copy-done.10
  88.7 0.1 copy.15
  88.8 0.7 reshape.186.diag_ref
  89.5 0.5 broadcast_select_fusion.slot_ref
  90.0 1.1 slice.34.q_ref
  91.1 38.4 %collective-permute-done.7.prev_ref = bf16[2,512,128]{2,1,0:T(8,128)(2,1)S(1)} collective-permute-done((bf16[2,512,128]{2,1,0:T(8,128)(2,1)S(1)}, bf16[2,512,128]{2,1,0:T(8,128)(2,1)S(1)}, u32[]{:S(2)}, u32[]{:S(2)}) %collective-permute-start.7) | collective-permute-done | bytes 262176 | tf_op jit(solution)/shard_map/ppermute | solution.py:25
  129.5 0.7 copy-done.2
  130.2 19.8 %shard_map.91 = (f32[512,1024]{1,0:T(8,128)}, f32[8,512,128]{2,1,0:T(8,128)}, f32[8,512,128]{2,1,0:T(8,128)}) custom-call(s32[8]{0:T(128)} %roles_ref.3, s32[32]{0:T(128)} %reshape.186.diag_ref, bf16[512,1024]{1,0:T(8,128)(2,1)} %slice.34.q_ref, bf16[2,512,128]{2,1,0:T(8,128)(2,1)} %copy-done.2, bf16[2,512,128]{2,1,0:T(8,128)(2,1)} %get-tuple-element.41.own_ref), custom_call_target="tpu_custom_call" | custom-call | tf_op jit(solution)/shard_map/pallas_call | solution.py:122
  150.0 0.0 all-to-all-done.1
  150.0 1.1 reshape.187.vk_ref.vv_ref.sk_ref.sv_ref
  151.1 10.5 %shard_map.92 = bf16[512,1024]{1,0:T(8,128)(2,1)} custom-call(s32[8]{0:T(128)} %roles_ref.3, s32[8]{0:T(128)} %broadcast_select_fusion.slot_ref, s32[8]{0:T(128)} %count_ref.1, bf16[512,1024]{1,0:T(8,128)(2,1)} %slice.34.q_ref, f32[512,1024]{1,0:T(8,128)} %get-tuple-element.27.o_loc_ref, f32[8,512,128]{2,1,0:T(8,128)} %get-tuple-element.28.m_ref, ...), custom_call_target="tpu_custom_call" | custom-call | tf_op jit(solution)/shard_map/pallas_call | solution.py:153
  (31 shorter events, 0.3 us)
Async XLA Ops:
  0.0 1.5 copy-start
  6.7 19.1 %copy-start.7 = (bf16[64,1024]{1,0:T(8,128)(2,1)S(1)}, bf16[64,1024]{1,0:T(8,128)(2,1)}, u32[]{:S(2)}) copy-start(bf16[64,1024]{1,0:T(8,128)(2,1)} %param.11) | copy-start | bytes 393220
  6.7 19.1 %copy-start.8 = (bf16[64,1024]{1,0:T(8,128)(2,1)S(1)}, bf16[64,1024]{1,0:T(8,128)(2,1)}, u32[]{:S(2)}) copy-start(bf16[64,1024]{1,0:T(8,128)(2,1)} %param.10) | copy-start | bytes 393220
  6.7 19.2 %copy-start.1 = (bf16[64,8192]{1,0:T(8,128)(2,1)S(1)}, bf16[64,8192]{1,0:T(8,128)(2,1)}, u32[]{:S(2)}) copy-start(bf16[64,8192]{1,0:T(8,128)(2,1)} %param.9) | copy-start | bytes 3145732
  6.7 67.3 %all-to-all-start = ((bf16[64,52,128]{2,1,0:T(8,128)(2,1)}), bf16[64,52,128]{2,1,0:T(8,128)(2,1)S(1)}, u32[]{:S(2)}, u32[]{:S(2)}) async-start(bf16[64,52,128]{2,1,0:T(8,128)(2,1)} %reshape.184), calls=%async_computation | async-start | bytes 1835008 | tf_op jit(solution)/shard_map/all_to_all | solution.py:162
  26.0 16.9 %collective-permute-start.5 = (bf16[64,1280]{1,0:T(8,128)(2,1)S(1)}, bf16[64,1280]{1,0:T(8,128)(2,1)S(1)}, u32[]{:S(2)}, u32[]{:S(2)}) collective-permute-start(bf16[64,1280]{1,0:T(8,128)(2,1)S(1)} %pad_maximum_fusion.9), channel_id=1, source_target_pairs={{2,0},{3,1},{4,2},{5,3},{6,4},{7,5},{0,6},{1,7},{10,8},{11,9},{12,... | collective-permute-start | bytes 491528 | tf_op jit(solution)/shard_map/ppermute | solution.py:25
  31.0 14.7 %collective-permute-start = (bf16[64,1280]{1,0:T(8,128)(2,1)S(1)}, bf16[64,1280]{1,0:T(8,128)(2,1)S(1)}, u32[]{:S(2)}, u32[]{:S(2)}) collective-permute-start(bf16[64,1280]{1,0:T(8,128)(2,1)S(1)} %pad_maximum_fusion.4), channel_id=1, source_target_pairs={{7,0},{0,1},{1,2},{2,3},{3,4},{4,5},{5,6},{6,7},{15,8},{8,9},{9,10... | collective-permute-start | bytes 491528 | tf_op jit(solution)/shard_map/ppermute | solution.py:25
  31.0 43.1 %collective-permute-start.1 = (bf16[64,1280]{1,0:T(8,128)(2,1)S(1)}, bf16[64,1280]{1,0:T(8,128)(2,1)S(1)}, u32[]{:S(2)}, u32[]{:S(2)}) collective-permute-start(bf16[64,1280]{1,0:T(8,128)(2,1)S(1)} %pad_maximum_fusion.5), channel_id=1, source_target_pairs={{6,0},{7,1},{0,2},{1,3},{2,4},{3,5},{4,6},{5,7},{14,8},{15,9},{8,1... | collective-permute-start | bytes 491528 | tf_op jit(solution)/shard_map/ppermute | solution.py:25
  33.0 41.2 %collective-permute-start.2 = (bf16[64,1280]{1,0:T(8,128)(2,1)S(1)}, bf16[64,1280]{1,0:T(8,128)(2,1)S(1)}, u32[]{:S(2)}, u32[]{:S(2)}) collective-permute-start(bf16[64,1280]{1,0:T(8,128)(2,1)S(1)} %pad_maximum_fusion.6), channel_id=1, source_target_pairs={{5,0},{6,1},{7,2},{0,3},{1,4},{2,5},{3,6},{4,7},{13,8},{14,9},{15,... | collective-permute-start | bytes 491528 | tf_op jit(solution)/shard_map/ppermute | solution.py:25
  36.5 37.7 %collective-permute-start.3 = (bf16[64,1280]{1,0:T(8,128)(2,1)S(1)}, bf16[64,1280]{1,0:T(8,128)(2,1)S(1)}, u32[]{:S(2)}, u32[]{:S(2)}) collective-permute-start(bf16[64,1280]{1,0:T(8,128)(2,1)S(1)} %pad_maximum_fusion.7), channel_id=1, source_target_pairs={{4,0},{5,1},{6,2},{7,3},{0,4},{1,5},{2,6},{3,7},{12,8},{13,9},{14,... | collective-permute-start | bytes 491528 | tf_op jit(solution)/shard_map/ppermute | solution.py:25
  43.0 31.2 %collective-permute-start.4 = (bf16[64,1280]{1,0:T(8,128)(2,1)S(1)}, bf16[64,1280]{1,0:T(8,128)(2,1)S(1)}, u32[]{:S(2)}, u32[]{:S(2)}) collective-permute-start(bf16[64,1280]{1,0:T(8,128)(2,1)S(1)} %pad_maximum_fusion.8), channel_id=1, source_target_pairs={{3,0},{4,1},{5,2},{6,3},{7,4},{0,5},{1,6},{2,7},{11,8},{12,9},{13,... | collective-permute-start | bytes 491528 | tf_op jit(solution)/shard_map/ppermute | solution.py:25
  45.7 28.6 %collective-permute-start.6 = (bf16[64,1280]{1,0:T(8,128)(2,1)S(1)}, bf16[64,1280]{1,0:T(8,128)(2,1)S(1)}, u32[]{:S(2)}, u32[]{:S(2)}) collective-permute-start(bf16[64,1280]{1,0:T(8,128)(2,1)S(1)} %pad_maximum_fusion.10), channel_id=1, source_target_pairs={{1,0},{2,1},{3,2},{4,3},{5,4},{6,5},{7,6},{0,7},{9,8},{10,9},{11,1... | collective-permute-start | bytes 491528 | tf_op jit(solution)/shard_map/ppermute | solution.py:25
  74.2 1.1 copy-start.3
  74.2 1.1 copy-start.5
  75.3 74.7 %all-to-all-start.1 = ((bf16[64,52,128]{2,1,0:T(8,128)(2,1)}), bf16[64,52,128]{2,1,0:T(8,128)(2,1)S(1)}, u32[]{:S(2)}, u32[]{:S(2)}) async-start(bf16[64,52,128]{2,1,0:T(8,128)(2,1)} %broadcast_in_dim.46), calls=%async_computation.1 | async-start | bytes 1835008 | tf_op jit(solution)/shard_map/all_to_all | solution.py:167
  81.9 0.9 copy-start.4
  81.9 1.0 copy-start.6
  83.6 5.1 %copy-start.10 = (s32[8,4]{0,1:T(4,128)S(1)}, s32[8,4]{0,1:T(4,128)}, u32[]{:S(2)}) copy-start(s32[8,4]{0,1:T(4,128)} %param.17) | copy-start | bytes 388
  83.6 5.9 %copy-start.9 = (s32[8]{0:T(128)S(1)}, s32[8]{0:T(128)}, u32[]{:S(2)}) copy-start(s32[8]{0:T(128)} %roles_ref.3) | copy-start | bytes 100
  85.4 44.1 %collective-permute-start.7 = (bf16[2,512,128]{2,1,0:T(8,128)(2,1)S(1)}, bf16[2,512,128]{2,1,0:T(8,128)(2,1)S(1)}, u32[]{:S(2)}, u32[]{:S(2)}) collective-permute-start(bf16[2,512,128]{2,1,0:T(8,128)(2,1)S(1)} %get-tuple-element.42), channel_id=1, source_target_pairs={{504,0},{0,8},{8,16},{16,24},{24,32},{32,40},{40,48},{48,56},{56,6... | collective-permute-start | bytes 786440 | tf_op jit(solution)/shard_map/ppermute | solution.py:25
  129.5 0.7 copy-start.2

commit v9 on v8

--- a/solution.py
+++ b/solution.py
@@ -205,16 +205,23 @@
     received = [columns_for(my_head)]
     for k in range(1, head_devices):
         received.append(shifted(columns_for((my_head + k) % head_devices), "head", k))
+    earlier = []
+    for k in range(head_devices):
+        route = [(sp * head_devices + j, (sp + 1) * head_devices + (j + k) % head_devices)
+                 for sp in range(seq_devices - 1) for j in range(head_devices)]
+        part = columns_for((my_head + k) % head_devices)[:, q_width:]
+        earlier.append(lax.ppermute(part, ("seq", "head"), route))
+    tail_cache = jnp.concatenate([prefix_keys[cache_rows - WIN:], prefix_values[cache_rows - WIN:]], 1)
+    cache_tail = lax.ppermute(tail_cache, "seq", [(seq_devices - 1, 0)])
     total = scatter_sum(both, seq_devices)
-    total, received = lax.optimization_barrier((total, received))
-    by_shift = jnp.stack(received, 0)
+    total, received, earlier, cache_tail = lax.optimization_barrier((total, received, earlier, cache_tail))
     order = (my_head - jnp.arange(head_devices, dtype=jnp.int32)) % head_devices
-    tokens = by_shift[order].reshape(-1, q_width + 2 * kv_width)
+    tokens = jnp.stack(received, 0)[order].reshape(-1, q_width + 2 * kv_width)
     q_local = tokens[:, :q_width]
     kv_local = jnp.stack([tokens[:, q_width:q_width + kv_width], tokens[:, q_width + kv_width:]], 0)
-    tail_cache = jnp.stack([prefix_keys[cache_rows - WIN:], prefix_values[cache_rows - WIN:]], 0)
-    outgoing = jnp.where(my_seq == seq_devices - 1, tail_cache, kv_local)
-    prev_kv = shifted(outgoing, "seq", 1)
+    before = jnp.stack(earlier, 0)[order].reshape(-1, 2 * kv_width)
+    before = jnp.where(my_seq == 0, cache_tail, before)
+    prev_kv = jnp.stack([before[:, :kv_width], before[:, kv_width:]], 0)
     side = gather_sums(total, both.shape, seq_devices)
 
     slot_l = jnp.where(is_ret, slot, 0).astype(jnp.int32)

time: 164 us -> 182 us (1.11)
  starting transfers between devices: 47.7 us -> 86 us
  waiting for transfers between devices: 65.7 us -> 43.8 us
  local copies, waits for them, and re-layouts: 11.6 us -> 14.4 us
    ppermute x0 -> x9, starting transfers between devices: none -> 36.2 us  [the longest x8 35.6 us: shards(): earlier.append(lax.ppermute(part, ('seq', 'head'), route))]
    ppermute x8 -> x7, waiting for transfers between devices: 38.4 us -> 4.86 us  [shifted(): return lax.ppermute(block, axis, route)]
    all_to_all x1, waiting for transfers between devices: 27.3 us -> 0.01 us  [scatter_sum(): mine = lax.all_to_all(flat, 'seq', 0, 0, tiled=True)]
    all_to_all x1, waiting for transfers between devices: 0.01 us -> 23.2 us  [gather_sums(): lax.all_to_all(jnp.broadcast_to(total, (seq_devices,) + total.shape[1:]),...]
    ppermute x0 -> x9, waiting for transfers between devices: none -> 15.8 us  [the longest x8 15.8 us: shards(): earlier.append(lax.ppermute(part, ('seq', 'head'), route))]
    all_to_all x1, starting transfers between devices: 6.63 us -> 14.9 us  [gather_sums(): lax.all_to_all(jnp.broadcast_to(total, (seq_devices,) + total.shape[1:]),...]
    ppermute x8 -> x7, starting transfers between devices: 22.2 us -> 16 us  [shifted(): return lax.ppermute(block, axis, route)]
    slice x0 -> x2, local copies, waits for them, and re-layouts: none -> 1.83 us  [the longest x1 0.92 us: shards(): prefix_keys[cache_rows - WIN:]]
  transfers between devices with their start and end apart: 10 -> 18, of which waited for: 2 -> 5; matrix products, arithmetic and copies ran while one was open for 4% -> 7% of each run, Pallas kernels for 12% -> 10%
where the time goes in v9:
time: 182 us; the launch traced here: 180 us
  starting transfers between devices  86 us (47%)
  waiting for transfers between devices  43.8 us (24%)
  Pallas kernels  28.8 us (16%)
  local copies, waits for them, and re-layouts  14.4 us (8%)
  other arithmetic  6.31 us (3%)
    ppermute x8, starting transfers between devices, shards(): earlier.append(lax.ppermute(part, ('seq', 'head'), route))  35.6 us
    all_to_all x1, waiting for transfers between devices, gather_sums(): lax.all_to_all(jnp.broadcast_to(total, (seq_devices,) + total.shape[1:]),...  23.2 us
    all_to_all x1, starting transfers between devices, scatter_sum(): mine = lax.all_to_all(flat, 'seq', 0, 0, tiled=True)  18.9 us
    pallas_call x1, Pallas kernels, attend_local(): pl.pallas_call(local_kernel, grid_spec=grid_spec, out_shape=[jax.ShapeDty...  18.4 us
    ppermute x7, starting transfers between devices, shifted(): return lax.ppermute(block, axis, route)  16 us
    ppermute x8, waiting for transfers between devices, shards(): earlier.append(lax.ppermute(part, ('seq', 'head'), route))  15.8 us
    all_to_all x1, starting transfers between devices, gather_sums(): lax.all_to_all(jnp.broadcast_to(total, (seq_devices,) + total.shape[1:]),...  14.9 us
    pallas_call x1, Pallas kernels, attend_side(): pl.pallas_call(side_kernel, grid_spec=grid_spec, out_shape=jax.ShapeDtype...  10.4 us
  transfers between devices with their start and end apart: 18, of which 5 were waited for; matrix products, arithmetic and copies ran while one was open for 7% of the time, Pallas kernels for 10%

profile of v9, /device:TPU:6, one launch (start us, length us, event | category | flops | bytes accessed | tf_op | source)
XLA Modules:
  0.0 180.5 jit_solution(2532580184907707599)
XLA Ops:
  0.0 0.7 broadcast_compare_fusion
  0.7 0.2 reduce-window.7
  0.9 0.6 iota_reduce_fusion
  1.5 0.6 gather_fusion
  2.1 0.1 reshape.203
  2.2 0.1 broadcast_in_dim.41
  2.3 0.1 broadcast_in_dim.42
  2.4 0.8 slice_bitcast_fusion.4
  3.2 1.3 pad_maximum_fusion
  4.5 0.7 gather_fusion.1
  5.2 0.1 copy.14
  5.2 0.3 bitcast_select_fusion
  5.5 0.1 pad_maximum_fusion.1
  5.6 1.1 reshape.187
  6.7 18.9 %all-to-all-start = ((bf16[64,52,128]{2,1,0:T(8,128)(2,1)}), bf16[64,52,128]{2,1,0:T(8,128)(2,1)S(1)}, u32[]{:S(2)}, u32[]{:S(2)}) async-start(bf16[64,52,128]{2,1,0:T(8,128)(2,1)} %reshape.187), calls=%async_computation | async-start | bytes 1835008 | tf_op jit(solution)/shard_map/all_to_all | solution.py:162
  25.6 0.0 copy-start.1
  25.8 0.1 constant_dynamic-slice_fusion
  25.9 4.8 %collective-permute-start.14 = (bf16[64,256]{1,0:T(8,128)(2,1)S(1)}, bf16[64,256]{1,0:T(8,128)(2,1)S(1)}, u32[]{:S(2)}, u32[]{:S(2)}) collective-permute-start(bf16[64,256]{1,0:T(8,128)(2,1)S(1)} %pad_maximum_fusion.20), channel_id=1, source_target_pairs={{0,15},{1,8},{2,9},{3,10},{4,11},{5,12},{6,13},{7,14},{8,23},{9,16... | collective-permute-start | bytes 98312 | tf_op jit(solution)/shard_map/ppermute | solution.py:213
  30.8 1.9 %collective-permute-start.8 = (bf16[64,256]{1,0:T(8,128)(2,1)S(1)}, bf16[64,256]{1,0:T(8,128)(2,1)S(1)}, u32[]{:S(2)}, u32[]{:S(2)}) collective-permute-start(bf16[64,256]{1,0:T(8,128)(2,1)S(1)} %pad_maximum_fusion.14), channel_id=1, source_target_pairs={{0,9},{1,10},{2,11},{3,12},{4,13},{5,14},{6,15},{7,8},{8,17},{9,18... | collective-permute-start | bytes 98312 | tf_op jit(solution)/shard_map/ppermute | solution.py:213
  32.7 4.2 %collective-permute-start.9 = (bf16[64,256]{1,0:T(8,128)(2,1)S(1)}, bf16[64,256]{1,0:T(8,128)(2,1)S(1)}, u32[]{:S(2)}, u32[]{:S(2)}) collective-permute-start(bf16[64,256]{1,0:T(8,128)(2,1)S(1)} %pad_maximum_fusion.15), channel_id=1, source_target_pairs={{0,10},{1,11},{2,12},{3,13},{4,14},{5,15},{6,8},{7,9},{8,18},{9,19... | collective-permute-start | bytes 98312 | tf_op jit(solution)/shard_map/ppermute | solution.py:213
  37.0 5.1 %collective-permute-start.10 = (bf16[64,256]{1,0:T(8,128)(2,1)S(1)}, bf16[64,256]{1,0:T(8,128)(2,1)S(1)}, u32[]{:S(2)}, u32[]{:S(2)}) collective-permute-start(bf16[64,256]{1,0:T(8,128)(2,1)S(1)} %pad_maximum_fusion.16), channel_id=1, source_target_pairs={{0,11},{1,12},{2,13},{3,14},{4,15},{5,8},{6,9},{7,10},{8,19},{9,20... | collective-permute-start | bytes 98312 | tf_op jit(solution)/shard_map/ppermute | solution.py:213
  42.1 4.7 %collective-permute-start.11 = (bf16[64,256]{1,0:T(8,128)(2,1)S(1)}, bf16[64,256]{1,0:T(8,128)(2,1)S(1)}, u32[]{:S(2)}, u32[]{:S(2)}) collective-permute-start(bf16[64,256]{1,0:T(8,128)(2,1)S(1)} %pad_maximum_fusion.17), channel_id=1, source_target_pairs={{0,12},{1,13},{2,14},{3,15},{4,8},{5,9},{6,10},{7,11},{8,20},{9,21... | collective-permute-start | bytes 98312 | tf_op jit(solution)/shard_map/ppermute | solution.py:213
  46.9 0.9 slice.29
  47.8 0.9 slice.30
  48.8 0.1 constant_dynamic-slice_fusion.4
  48.9 0.0 copy-start.33
  49.0 0.0 copy-start.32
  49.1 15.8 %collective-permute-done.14 = bf16[64,256]{1,0:T(8,128)(2,1)S(1)} collective-permute-done((bf16[64,256]{1,0:T(8,128)(2,1)S(1)}, bf16[64,256]{1,0:T(8,128)(2,1)S(1)}, u32[]{:S(2)}, u32[]{:S(2)}) %collective-permute-start.14) | collective-permute-done | bytes 32800 | tf_op jit(solution)/shard_map/ppermute | solution.py:213
  64.9 7.5 %collective-permute-start.12 = (bf16[64,256]{1,0:T(8,128)(2,1)S(1)}, bf16[64,256]{1,0:T(8,128)(2,1)S(1)}, u32[]{:S(2)}, u32[]{:S(2)}) collective-permute-start(bf16[64,256]{1,0:T(8,128)(2,1)S(1)} %pad_maximum_fusion.18), channel_id=1, source_target_pairs={{0,13},{1,14},{2,15},{3,8},{4,9},{5,10},{6,11},{7,12},{8,21},{9,22... | collective-permute-start | bytes 98312 | tf_op jit(solution)/shard_map/ppermute | solution.py:213
  72.5 0.0 collective-permute-done.8
  72.5 3.1 %collective-permute-start.13 = (bf16[64,256]{1,0:T(8,128)(2,1)S(1)}, bf16[64,256]{1,0:T(8,128)(2,1)S(1)}, u32[]{:S(2)}, u32[]{:S(2)}) collective-permute-start(bf16[64,256]{1,0:T(8,128)(2,1)S(1)} %pad_maximum_fusion.19), channel_id=1, source_target_pairs={{0,14},{1,15},{2,8},{3,9},{4,10},{5,11},{6,12},{7,13},{8,22},{9,23... | collective-permute-start | bytes 98312 | tf_op jit(solution)/shard_map/ppermute | solution.py:213
  75.7 0.7 collective-permute-start.15
  76.4 0.0 collective-permute-done.10
  76.4 4.1 %collective-permute-start.7 = (bf16[64,256]{1,0:T(8,128)(2,1)S(1)}, bf16[64,256]{1,0:T(8,128)(2,1)S(1)}, u32[]{:S(2)}, u32[]{:S(2)}) collective-permute-start(bf16[64,256]{1,0:T(8,128)(2,1)S(1)} %pad_maximum_fusion.13), channel_id=1, source_target_pairs={{0,8},{1,9},{2,10},{3,11},{4,12},{5,13},{6,14},{7,15},{8,16},{9,17... | collective-permute-start | bytes 98312 | tf_op jit(solution)/shard_map/ppermute | solution.py:213
  80.4 0.0 collective-permute-done.11
  80.5 1.9 %collective-permute-start.5 = (bf16[64,1280]{1,0:T(8,128)(2,1)S(1)}, bf16[64,1280]{1,0:T(8,128)(2,1)S(1)}, u32[]{:S(2)}, u32[]{:S(2)}) collective-permute-start(bf16[64,1280]{1,0:T(8,128)(2,1)S(1)} %pad_maximum_fusion.11), channel_id=1, source_target_pairs={{2,0},{3,1},{4,2},{5,3},{6,4},{7,5},{0,6},{1,7},{10,8},{11,9},{12,... | collective-permute-start | bytes 491528 | tf_op jit(solution)/shard_map/ppermute | solution.py:25
  82.4 0.0 collective-permute-start
  82.5 0.0 collective-permute-done.13
  82.5 3.9 %collective-permute-start.1 = (bf16[64,1280]{1,0:T(8,128)(2,1)S(1)}, bf16[64,1280]{1,0:T(8,128)(2,1)S(1)}, u32[]{:S(2)}, u32[]{:S(2)}) collective-permute-start(bf16[64,1280]{1,0:T(8,128)(2,1)S(1)} %pad_maximum_fusion.7), channel_id=1, source_target_pairs={{6,0},{7,1},{0,2},{1,3},{2,4},{3,5},{4,6},{5,7},{14,8},{15,9},{8,1... | collective-permute-start | bytes 491528 | tf_op jit(solution)/shard_map/ppermute | solution.py:25
  86.4 0.1 copy.15
  86.5 0.6 reshape.189.diag_ref
  87.1 2.3 %collective-permute-start.2 = (bf16[64,1280]{1,0:T(8,128)(2,1)S(1)}, bf16[64,1280]{1,0:T(8,128)(2,1)S(1)}, u32[]{:S(2)}, u32[]{:S(2)}) collective-permute-start(bf16[64,1280]{1,0:T(8,128)(2,1)S(1)} %pad_maximum_fusion.8), channel_id=1, source_target_pairs={{5,0},{6,1},{7,2},{0,3},{1,4},{2,5},{3,6},{4,7},{13,8},{14,9},{15,... | collective-permute-start | bytes 491528 | tf_op jit(solution)/shard_map/ppermute | solution.py:25
  89.4 5.6 %collective-permute-start.3 = (bf16[64,1280]{1,0:T(8,128)(2,1)S(1)}, bf16[64,1280]{1,0:T(8,128)(2,1)S(1)}, u32[]{:S(2)}, u32[]{:S(2)}) collective-permute-start(bf16[64,1280]{1,0:T(8,128)(2,1)S(1)} %pad_maximum_fusion.9), channel_id=1, source_target_pairs={{4,0},{5,1},{6,2},{7,3},{0,4},{1,5},{2,6},{3,7},{12,8},{13,9},{14,... | collective-permute-start | bytes 491528 | tf_op jit(solution)/shard_map/ppermute | solution.py:25
  95.1 2.0 %collective-permute-start.4 = (bf16[64,1280]{1,0:T(8,128)(2,1)S(1)}, bf16[64,1280]{1,0:T(8,128)(2,1)S(1)}, u32[]{:S(2)}, u32[]{:S(2)}) collective-permute-start(bf16[64,1280]{1,0:T(8,128)(2,1)S(1)} %pad_maximum_fusion.10), channel_id=1, source_target_pairs={{3,0},{4,1},{5,2},{6,3},{7,4},{0,5},{1,6},{2,7},{11,8},{12,9},{13,... | collective-permute-start | bytes 491528 | tf_op jit(solution)/shard_map/ppermute | solution.py:25
  97.2 0.2 collective-permute-start.6
  97.4 1.2 broadcast_select_fusion.slot_ref
  98.6 0.2 reduce_sum.12
  98.8 1.8 collective-permute-done.3
  100.5 2.9 %collective-permute-done.4 = bf16[64,1280]{1,0:T(8,128)(2,1)S(1)} collective-permute-done((bf16[64,1280]{1,0:T(8,128)(2,1)S(1)}, bf16[64,1280]{1,0:T(8,128)(2,1)S(1)}, u32[]{:S(2)}, u32[]{:S(2)}) %collective-permute-start.4) | collective-permute-done | bytes 163872 | tf_op jit(solution)/shard_map/ppermute | solution.py:25
  103.4 0.2 collective-permute-done.6
  103.6 1.0 broadcast_in_dim.47
  104.8 14.9 %all-to-all-start.1 = ((bf16[64,52,128]{2,1,0:T(8,128)(2,1)}), bf16[64,52,128]{2,1,0:T(8,128)(2,1)S(1)}, u32[]{:S(2)}, u32[]{:S(2)}) async-start(bf16[64,52,128]{2,1,0:T(8,128)(2,1)} %broadcast_in_dim.47), calls=%async_computation.1 | async-start | bytes 1835008 | tf_op jit(solution)/shard_map/all_to_all | solution.py:167
  119.8 0.9 constant_dynamic-update-slice_fusion.1
  120.7 0.9 bitcast_dynamic-update-slice_fusion.6
  121.6 0.9 bitcast_dynamic-update-slice_fusion.5
  122.6 1.3 gather_fusion.3
  124.0 0.6 gather_fusion.2
  124.7 1.1 slice.44.q_ref
  125.9 0.7 pad_maximum_fusion.3.prev_ref
  126.6 0.7 pad_maximum_fusion.4.own_ref
  127.4 18.4 %shard_map.91 = (f32[512,1024]{1,0:T(8,128)}, f32[8,512,128]{2,1,0:T(8,128)}, f32[8,512,128]{2,1,0:T(8,128)}) custom-call(s32[8]{0:T(128)} %roles_ref.3, s32[32]{0:T(128)} %reshape.189.diag_ref, bf16[512,1024]{1,0:T(8,128)(2,1)} %slice.44.q_ref, bf16[2,512,128]{2,1,0:T(8,128)(2,1)} %pad_maximum_fusion.3.prev_ref, bf16[2,512,128]{2,1,0:T(8,128)(2,1)} %pad_maximum_fusion.4.own_ref), custom_call_target="tpu_custom_call" | custom-call | tf_op jit(solution)/shard_map/pallas_call | solution.py:122
  145.8 23.2 %all-to-all-done.1 = bf16[64,52,128]{2,1,0:T(8,128)(2,1)S(1)} async-done(((bf16[64,52,128]{2,1,0:T(8,128)(2,1)}), bf16[64,52,128]{2,1,0:T(8,128)(2,1)S(1)}, u32[]{:S(2)}, u32[]{:S(2)}) %all-to-all-start.1) | async-done | bytes 852000 | tf_op jit(solution)/shard_map/all_to_all | solution.py:167
  169.0 1.1 reshape.191.vk_ref.vv_ref.sk_ref.sv_ref
  170.1 10.4 %shard_map.92 = bf16[512,1024]{1,0:T(8,128)(2,1)} custom-call(s32[8]{0:T(128)} %roles_ref.3, s32[8]{0:T(128)} %broadcast_select_fusion.slot_ref, s32[8]{0:T(128)} %count_ref.1, bf16[512,1024]{1,0:T(8,128)(2,1)} %slice.44.q_ref, f32[512,1024]{1,0:T(8,128)} %get-tuple-element.45.o_loc_ref, f32[8,512,128]{2,1,0:T(8,128)} %get-tuple-element.46.m_ref, ...), custom_call_target="tpu_custom_call" | custom-call | tf_op jit(solution)/shard_map/pallas_call | solution.py:153
  (117 shorter events, 0.6 us)
Async XLA Ops:
  0.0 1.5 copy-start
  0.9 0.6 copy-start.34
  6.7 19.1 %copy-start.5 = (bf16[64,1024]{1,0:T(8,128)(2,1)S(1)}, bf16[64,1024]{1,0:T(8,128)(2,1)}, u32[]{:S(2)}) copy-start(bf16[64,1024]{1,0:T(8,128)(2,1)} %param.11) | copy-start | bytes 393220
  6.7 19.1 %copy-start.6 = (bf16[64,1024]{1,0:T(8,128)(2,1)S(1)}, bf16[64,1024]{1,0:T(8,128)(2,1)}, u32[]{:S(2)}) copy-start(bf16[64,1024]{1,0:T(8,128)(2,1)} %param.10) | copy-start | bytes 393220
  6.7 91.9 %all-to-all-start = ((bf16[64,52,128]{2,1,0:T(8,128)(2,1)}), bf16[64,52,128]{2,1,0:T(8,128)(2,1)S(1)}, u32[]{:S(2)}, u32[]{:S(2)}) async-start(bf16[64,52,128]{2,1,0:T(8,128)(2,1)} %reshape.187), calls=%async_computation | async-start | bytes 1835008 | tf_op jit(solution)/shard_map/all_to_all | solution.py:162
  25.6 23.2 %copy-start.1 = (bf16[64,8192]{1,0:T(8,128)(2,1)S(1)}, bf16[64,8192]{1,0:T(8,128)(2,1)}, u32[]{:S(2)}) copy-start(bf16[64,8192]{1,0:T(8,128)(2,1)} %param.9) | copy-start | bytes 3145732
  25.9 39.0 %collective-permute-start.14 = (bf16[64,256]{1,0:T(8,128)(2,1)S(1)}, bf16[64,256]{1,0:T(8,128)(2,1)S(1)}, u32[]{:S(2)}, u32[]{:S(2)}) collective-permute-start(bf16[64,256]{1,0:T(8,128)(2,1)S(1)} %pad_maximum_fusion.20), channel_id=1, source_target_pairs={{0,15},{1,8},{2,9},{3,10},{4,11},{5,12},{6,13},{7,14},{8,23},{9,16... | collective-permute-start | bytes 98312 | tf_op jit(solution)/shard_map/ppermute | solution.py:213
  30.8 41.7 %collective-permute-start.8 = (bf16[64,256]{1,0:T(8,128)(2,1)S(1)}, bf16[64,256]{1,0:T(8,128)(2,1)S(1)}, u32[]{:S(2)}, u32[]{:S(2)}) collective-permute-start(bf16[64,256]{1,0:T(8,128)(2,1)S(1)} %pad_maximum_fusion.14), channel_id=1, source_target_pairs={{0,9},{1,10},{2,11},{3,12},{4,13},{5,14},{6,15},{7,8},{8,17},{9,18... | collective-permute-start | bytes 98312 | tf_op jit(solution)/shard_map/ppermute | solution.py:213
  32.7 43.0 %collective-permute-start.9 = (bf16[64,256]{1,0:T(8,128)(2,1)S(1)}, bf16[64,256]{1,0:T(8,128)(2,1)S(1)}, u32[]{:S(2)}, u32[]{:S(2)}) collective-permute-start(bf16[64,256]{1,0:T(8,128)(2,1)S(1)} %pad_maximum_fusion.15), channel_id=1, source_target_pairs={{0,10},{1,11},{2,12},{3,13},{4,14},{5,15},{6,8},{7,9},{8,18},{9,19... | collective-permute-start | bytes 98312 | tf_op jit(solution)/shard_map/ppermute | solution.py:213
  37.0 39.4 %collective-permute-start.10 = (bf16[64,256]{1,0:T(8,128)(2,1)S(1)}, bf16[64,256]{1,0:T(8,128)(2,1)S(1)}, u32[]{:S(2)}, u32[]{:S(2)}) collective-permute-start(bf16[64,256]{1,0:T(8,128)(2,1)S(1)} %pad_maximum_fusion.16), channel_id=1, source_target_pairs={{0,11},{1,12},{2,13},{3,14},{4,15},{5,8},{6,9},{7,10},{8,19},{9,20... | collective-permute-start | bytes 98312 | tf_op jit(solution)/shard_map/ppermute | solution.py:213
  42.1 38.4 %collective-permute-start.11 = (bf16[64,256]{1,0:T(8,128)(2,1)S(1)}, bf16[64,256]{1,0:T(8,128)(2,1)S(1)}, u32[]{:S(2)}, u32[]{:S(2)}) collective-permute-start(bf16[64,256]{1,0:T(8,128)(2,1)S(1)} %pad_maximum_fusion.17), channel_id=1, source_target_pairs={{0,12},{1,13},{2,14},{3,15},{4,8},{5,9},{6,10},{7,11},{8,20},{9,21... | collective-permute-start | bytes 98312 | tf_op jit(solution)/shard_map/ppermute | solution.py:213
  48.9 37.5 %copy-start.33 = (s32[8,4]{0,1:T(4,128)S(1)}, s32[8,4]{0,1:T(4,128)}, u32[]{:S(2)}) copy-start(s32[8,4]{0,1:T(4,128)} %param.17) | copy-start | bytes 388
  49.0 48.4 %copy-start.32 = (s32[8]{0:T(128)S(1)}, s32[8]{0:T(128)}, u32[]{:S(2)}) copy-start(s32[8]{0:T(128)} %roles_ref.3) | copy-start | bytes 100
  64.9 22.2 %copy-start.19 = (bf16[64,256]{1,0:T(8,128)(2,1)}, bf16[64,256]{1,0:T(8,128)(2,1)S(1)}, u32[]{:S(2)}) copy-start(bf16[64,256]{1,0:T(8,128)(2,1)S(1)} %collective-permute-done.14) | copy-start | bytes 98308
  64.9 17.5 %collective-permute-start.12 = (bf16[64,256]{1,0:T(8,128)(2,1)S(1)}, bf16[64,256]{1,0:T(8,128)(2,1)S(1)}, u32[]{:S(2)}, u32[]{:S(2)}) collective-permute-start(bf16[64,256]{1,0:T(8,128)(2,1)S(1)} %pad_maximum_fusion.18), channel_id=1, source_target_pairs={{0,13},{1,14},{2,15},{3,8},{4,9},{5,10},{6,11},{7,12},{8,21},{9,22... | collective-permute-start | bytes 98312 | tf_op jit(solution)/shard_map/ppermute | solution.py:213
  72.5 14.6 %copy-start.21 = (bf16[64,256]{1,0:T(8,128)(2,1)}, bf16[64,256]{1,0:T(8,128)(2,1)S(1)}, u32[]{:S(2)}) copy-start(bf16[64,256]{1,0:T(8,128)(2,1)S(1)} %collective-permute-done.8) | copy-start | bytes 98308
  72.5 10.0 %collective-permute-start.13 = (bf16[64,256]{1,0:T(8,128)(2,1)S(1)}, bf16[64,256]{1,0:T(8,128)(2,1)S(1)}, u32[]{:S(2)}, u32[]{:S(2)}) collective-permute-start(bf16[64,256]{1,0:T(8,128)(2,1)S(1)} %pad_maximum_fusion.19), channel_id=1, source_target_pairs={{0,14},{1,15},{2,8},{3,9},{4,10},{5,11},{6,12},{7,13},{8,22},{9,23... | collective-permute-start | bytes 98312 | tf_op jit(solution)/shard_map/ppermute | solution.py:213
  75.7 11.5 %copy-start.23 = (bf16[64,256]{1,0:T(8,128)(2,1)}, bf16[64,256]{1,0:T(8,128)(2,1)S(1)}, u32[]{:S(2)}) copy-start(bf16[64,256]{1,0:T(8,128)(2,1)S(1)} %collective-permute-done.9) | copy-start | bytes 98308
  75.7 27.9 %collective-permute-start.15 = (bf16[512,256]{1,0:T(8,128)(2,1)S(1)}, bf16[512,256]{1,0:T(8,128)(2,1)S(1)}, u32[]{:S(2)}, u32[]{:S(2)}) collective-permute-start(bf16[512,256]{1,0:T(8,128)(2,1)S(1)} %pad_maximum_fusion.2), channel_id=1, source_target_pairs={{504,0},{505,1},{506,2},{507,3},{508,4},{509,5},{510,6},{511,7}} | collective-permute-start | bytes 786440 | tf_op jit(solution)/shard_map/ppermute | solution.py:215
  76.4 6.1 %copy-start.25 = (bf16[64,256]{1,0:T(8,128)(2,1)}, bf16[64,256]{1,0:T(8,128)(2,1)S(1)}, u32[]{:S(2)}) copy-start(bf16[64,256]{1,0:T(8,128)(2,1)S(1)} %collective-permute-done.10) | copy-start | bytes 98308
  76.4 10.7 %collective-permute-start.7 = (bf16[64,256]{1,0:T(8,128)(2,1)S(1)}, bf16[64,256]{1,0:T(8,128)(2,1)S(1)}, u32[]{:S(2)}, u32[]{:S(2)}) collective-permute-start(bf16[64,256]{1,0:T(8,128)(2,1)S(1)} %pad_maximum_fusion.13), channel_id=1, source_target_pairs={{0,8},{1,9},{2,10},{3,11},{4,12},{5,13},{6,14},{7,15},{8,16},{9,17... | collective-permute-start | bytes 98312 | tf_op jit(solution)/shard_map/ppermute | solution.py:213
  80.5 2.0 %copy-start.27 = (bf16[64,256]{1,0:T(8,128)(2,1)}, bf16[64,256]{1,0:T(8,128)(2,1)S(1)}, u32[]{:S(2)}) copy-start(bf16[64,256]{1,0:T(8,128)(2,1)S(1)} %collective-permute-done.11) | copy-start | bytes 98308
  80.5 9.0 %collective-permute-start.5 = (bf16[64,1280]{1,0:T(8,128)(2,1)S(1)}, bf16[64,1280]{1,0:T(8,128)(2,1)S(1)}, u32[]{:S(2)}, u32[]{:S(2)}) collective-permute-start(bf16[64,1280]{1,0:T(8,128)(2,1)S(1)} %pad_maximum_fusion.11), channel_id=1, source_target_pairs={{2,0},{3,1},{4,2},{5,3},{6,4},{7,5},{0,6},{1,7},{10,8},{11,9},{12,... | collective-permute-start | bytes 491528 | tf_op jit(solution)/shard_map/ppermute | solution.py:25
  82.4 16.2 %copy-start.29 = (bf16[64,256]{1,0:T(8,128)(2,1)}, bf16[64,256]{1,0:T(8,128)(2,1)S(1)}, u32[]{:S(2)}) copy-start(bf16[64,256]{1,0:T(8,128)(2,1)S(1)} %collective-permute-done.12) | copy-start | bytes 98308
  82.4 12.7 %collective-permute-start = (bf16[64,1280]{1,0:T(8,128)(2,1)S(1)}, bf16[64,1280]{1,0:T(8,128)(2,1)S(1)}, u32[]{:S(2)}, u32[]{:S(2)}) collective-permute-start(bf16[64,1280]{1,0:T(8,128)(2,1)S(1)} %pad_maximum_fusion.6), channel_id=1, source_target_pairs={{7,0},{0,1},{1,2},{2,3},{3,4},{4,5},{5,6},{6,7},{15,8},{8,9},{9,10... | collective-permute-start | bytes 491528 | tf_op jit(solution)/shard_map/ppermute | solution.py:25
  82.5 22.2 %copy-start.31 = (bf16[64,256]{1,0:T(8,128)(2,1)}, bf16[64,256]{1,0:T(8,128)(2,1)S(1)}, u32[]{:S(2)}) copy-start(bf16[64,256]{1,0:T(8,128)(2,1)S(1)} %collective-permute-done.13) | copy-start | bytes 98308
  82.5 14.7 %collective-permute-start.1 = (bf16[64,1280]{1,0:T(8,128)(2,1)S(1)}, bf16[64,1280]{1,0:T(8,128)(2,1)S(1)}, u32[]{:S(2)}, u32[]{:S(2)}) collective-permute-start(bf16[64,1280]{1,0:T(8,128)(2,1)S(1)} %pad_maximum_fusion.7), channel_id=1, source_target_pairs={{6,0},{7,1},{0,2},{1,3},{2,4},{3,5},{4,6},{5,7},{14,8},{15,9},{8,1... | collective-permute-start | bytes 491528 | tf_op jit(solution)/shard_map/ppermute | solution.py:25
  87.1 11.6 %collective-permute-start.2 = (bf16[64,1280]{1,0:T(8,128)(2,1)S(1)}, bf16[64,1280]{1,0:T(8,128)(2,1)S(1)}, u32[]{:S(2)}, u32[]{:S(2)}) collective-permute-start(bf16[64,1280]{1,0:T(8,128)(2,1)S(1)} %pad_maximum_fusion.8), channel_id=1, source_target_pairs={{5,0},{6,1},{7,2},{0,3},{1,4},{2,5},{3,6},{4,7},{13,8},{14,9},{15,... | collective-permute-start | bytes 491528 | tf_op jit(solution)/shard_map/ppermute | solution.py:25
  89.4 15.3 %copy-start.7 = (bf16[64,1280]{1,0:T(8,128)(2,1)}, bf16[64,1280]{1,0:T(8,128)(2,1)S(1)}, u32[]{:S(2)}) copy-start(bf16[64,1280]{1,0:T(8,128)(2,1)S(1)} %collective-permute-done.5) | copy-start | bytes 491524
  89.4 11.1 %collective-permute-start.3 = (bf16[64,1280]{1,0:T(8,128)(2,1)S(1)}, bf16[64,1280]{1,0:T(8,128)(2,1)S(1)}, u32[]{:S(2)}, u32[]{:S(2)}) collective-permute-start(bf16[64,1280]{1,0:T(8,128)(2,1)S(1)} %pad_maximum_fusion.9), channel_id=1, source_target_pairs={{4,0},{5,1},{6,2},{7,3},{0,4},{1,5},{2,6},{3,7},{12,8},{13,9},{14,... | collective-permute-start | bytes 491528 | tf_op jit(solution)/shard_map/ppermute | solution.py:25
  95.1 9.6 %copy-start.9 = (bf16[64,1280]{1,0:T(8,128)(2,1)}, bf16[64,1280]{1,0:T(8,128)(2,1)S(1)}, u32[]{:S(2)}) copy-start(bf16[64,1280]{1,0:T(8,128)(2,1)S(1)} %collective-permute-done) | copy-start | bytes 491524
  95.1 8.3 %collective-permute-start.4 = (bf16[64,1280]{1,0:T(8,128)(2,1)S(1)}, bf16[64,1280]{1,0:T(8,128)(2,1)S(1)}, u32[]{:S(2)}, u32[]{:S(2)}) collective-permute-start(bf16[64,1280]{1,0:T(8,128)(2,1)S(1)} %pad_maximum_fusion.10), channel_id=1, source_target_pairs={{3,0},{4,1},{5,2},{6,3},{7,4},{0,5},{1,6},{2,7},{11,8},{12,9},{13,... | collective-permute-start | bytes 491528 | tf_op jit(solution)/shard_map/ppermute | solution.py:25
  97.2 7.6 %copy-start.10 = (bf16[64,1280]{1,0:T(8,128)(2,1)}, bf16[64,1280]{1,0:T(8,128)(2,1)S(1)}, u32[]{:S(2)}) copy-start(bf16[64,1280]{1,0:T(8,128)(2,1)S(1)} %collective-permute-done.1) | copy-start | bytes 491524
  97.2 6.4 %collective-permute-start.6 = (bf16[64,1280]{1,0:T(8,128)(2,1)S(1)}, bf16[64,1280]{1,0:T(8,128)(2,1)S(1)}, u32[]{:S(2)}, u32[]{:S(2)}) collective-permute-start(bf16[64,1280]{1,0:T(8,128)(2,1)S(1)} %pad_maximum_fusion.12), channel_id=1, source_target_pairs={{1,0},{2,1},{3,2},{4,3},{5,4},{6,5},{7,6},{0,7},{9,8},{10,9},{11,1... | collective-permute-start | bytes 491528 | tf_op jit(solution)/shard_map/ppermute | solution.py:25
  98.7 6.0 %copy-start.11 = (bf16[64,1280]{1,0:T(8,128)(2,1)}, bf16[64,1280]{1,0:T(8,128)(2,1)S(1)}, u32[]{:S(2)}) copy-start(bf16[64,1280]{1,0:T(8,128)(2,1)S(1)} %collective-permute-done.2) | copy-start | bytes 491524
  100.5 4.2 %copy-start.13 = (bf16[64,1280]{1,0:T(8,128)(2,1)}, bf16[64,1280]{1,0:T(8,128)(2,1)S(1)}, u32[]{:S(2)}) copy-start(bf16[64,1280]{1,0:T(8,128)(2,1)S(1)} %collective-permute-done.3) | copy-start | bytes 491524
  103.4 1.3 copy-start.15
  103.6 1.2 copy-start.17
  103.6 1.1 copy-start.3
  104.7 15.0 %copy-start.22 = (bf16[64,256]{1,0:T(8,128)(2,1)S(1)}, bf16[64,256]{1,0:T(8,128)(2,1)}, u32[]{:S(2)}) copy-start(bf16[64,256]{1,0:T(8,128)(2,1)} %copy-done.21) | copy-start | bytes 98308
  104.7 15.1 %copy-start.24 = (bf16[64,256]{1,0:T(8,128)(2,1)S(1)}, bf16[64,256]{1,0:T(8,128)(2,1)}, u32[]{:S(2)}) copy-start(bf16[64,256]{1,0:T(8,128)(2,1)} %copy-done.23) | copy-start | bytes 98308
  104.7 15.1 %copy-start.26 = (bf16[64,256]{1,0:T(8,128)(2,1)S(1)}, bf16[64,256]{1,0:T(8,128)(2,1)}, u32[]{:S(2)}) copy-start(bf16[64,256]{1,0:T(8,128)(2,1)} %copy-done.25) | copy-start | bytes 98308
  104.7 15.1 %copy-start.28 = (bf16[64,256]{1,0:T(8,128)(2,1)S(1)}, bf16[64,256]{1,0:T(8,128)(2,1)}, u32[]{:S(2)}) copy-start(bf16[64,256]{1,0:T(8,128)(2,1)} %copy-done.27) | copy-start | bytes 98308
  104.7 15.1 %copy-start.30 = (bf16[64,256]{1,0:T(8,128)(2,1)S(1)}, bf16[64,256]{1,0:T(8,128)(2,1)}, u32[]{:S(2)}) copy-start(bf16[64,256]{1,0:T(8,128)(2,1)} %copy-done.29) | copy-start | bytes 98308
  104.8 64.2 %all-to-all-start.1 = ((bf16[64,52,128]{2,1,0:T(8,128)(2,1)}), bf16[64,52,128]{2,1,0:T(8,128)(2,1)S(1)}, u32[]{:S(2)}, u32[]{:S(2)}) async-start(bf16[64,52,128]{2,1,0:T(8,128)(2,1)} %broadcast_in_dim.47), calls=%async_computation.1 | async-start | bytes 1835008 | tf_op jit(solution)/shard_map/all_to_all | solution.py:167
  119.6 2.9 %copy-start.20 = (bf16[64,256]{1,0:T(8,128)(2,1)S(1)}, bf16[64,256]{1,0:T(8,128)(2,1)}, u32[]{:S(2)}) copy-start(bf16[64,256]{1,0:T(8,128)(2,1)} %copy-done.19) | copy-start | bytes 98308
  119.7 4.2 %copy-start.12 = (bf16[64,1280]{1,0:T(8,128)(2,1)S(1)}, bf16[64,1280]{1,0:T(8,128)(2,1)}, u32[]{:S(2)}) copy-start(bf16[64,1280]{1,0:T(8,128)(2,1)} %copy-done.11) | copy-start | bytes 491524
  119.7 4.2 %copy-start.14 = (bf16[64,1280]{1,0:T(8,128)(2,1)S(1)}, bf16[64,1280]{1,0:T(8,128)(2,1)}, u32[]{:S(2)}) copy-start(bf16[64,1280]{1,0:T(8,128)(2,1)} %copy-done.13) | copy-start | bytes 491524
  119.7 4.3 %copy-start.16 = (bf16[64,1280]{1,0:T(8,128)(2,1)S(1)}, bf16[64,1280]{1,0:T(8,128)(2,1)}, u32[]{:S(2)}) copy-start(bf16[64,1280]{1,0:T(8,128)(2,1)} %copy-done.15) | copy-start | bytes 491524
  119.7 4.3 %copy-start.8 = (bf16[64,1280]{1,0:T(8,128)(2,1)S(1)}, bf16[64,1280]{1,0:T(8,128)(2,1)}, u32[]{:S(2)}) copy-start(bf16[64,1280]{1,0:T(8,128)(2,1)} %copy-done.7) | copy-start | bytes 491524
  119.8 4.2 %copy-start.18 = (bf16[64,1280]{1,0:T(8,128)(2,1)S(1)}, bf16[64,1280]{1,0:T(8,128)(2,1)}, u32[]{:S(2)}) copy-start(bf16[64,1280]{1,0:T(8,128)(2,1)} %copy-done.17) | copy-start | bytes 491524
  124.7 1.1 copy-start.2
  124.7 1.1 copy-start.4

commit v10 on v7

--- a/solution.py
+++ b/solution.py
@@ -29,20 +29,45 @@
                   q_ref, prev_ref, own_ref, vk_ref, vv_ref, sk_ref, sv_ref, o_ref):
     h = pl.program_id(0)
     rows = q_ref.shape[0]
+    half = rows // 2
     scaling = 1.0 / math.sqrt(HEAD_SIZE)
-    q = q_ref[...]
     dims = (((1,), (1,)), ((), ()))
-
-    def scores(keys):
+    neg = -jnp.inf
+
+    def scores(q, keys):
         return lax.dot_general(q, keys, dims, preferred_element_type=jnp.float32) * scaling
 
-    s_prev = scores(prev_ref[0])
-    s_own = scores(own_ref[0])
-    row = lax.broadcasted_iota(jnp.int32, (rows, rows), 0)
-    col = lax.broadcasted_iota(jnp.int32, (rows, rows), 1)
-
-    def finish(s_side, ok_side, v_side, ok_prev, ok_own):
-        neg = -jnp.inf
+    def one_half(part, role_ret):
+        r0 = part * half
+        p0 = part * half
+        p1 = rows
+        w_own = half + part * half
+        q = q_ref[r0:r0 + half, :]
+        s_prev = scores(q, prev_ref[0, p0:p1, :])
+        s_own = scores(q, own_ref[0, 0:w_own, :])
+        row_p = lax.broadcasted_iota(jnp.int32, s_prev.shape, 0) + r0
+        col_p = lax.broadcasted_iota(jnp.int32, s_prev.shape, 1) + p0
+        row_o = lax.broadcasted_iota(jnp.int32, s_own.shape, 0) + r0
+        col_o = lax.broadcasted_iota(jnp.int32, s_own.shape, 1)
+        if role_ret:
+            s_side = scores(q, vk_ref[...])
+            v_side = vv_ref[...]
+            side_col = lax.broadcasted_iota(jnp.int32, s_side.shape, 1)
+            ok_side = side_col // BLK < count_ref[h]
+            rel_prev = row_p // BLK + rows // BLK - col_p // BLK
+            rel_own = row_o // BLK - col_o // BLK
+            ok_prev = jnp.zeros(s_prev.shape, jnp.bool_)
+            ok_own = jnp.zeros(s_own.shape, jnp.bool_)
+            for d in range(NSL):
+                off = diag_ref[h * NSL + d]
+                ok_prev = ok_prev | (rel_prev == off)
+                ok_own = ok_own | ((rel_own == off) & ((off > 0) | (col_o <= row_o)))
+        else:
+            s_side = scores(q, sk_ref[...])
+            v_side = sv_ref[...]
+            ok_side = jnp.ones(s_side.shape, jnp.bool_)
+            ok_prev = col_p > row_p
+            ok_own = col_o <= row_o
         m_side = jnp.max(jnp.where(ok_side, s_side, neg), axis=1, keepdims=True)
         m_prev = jnp.max(jnp.where(ok_prev, s_prev, neg), axis=1, keepdims=True)
         m_own = jnp.max(jnp.where(ok_own, s_own, neg), axis=1, keepdims=True)
@@ -57,30 +82,19 @@
         p_prev = (e_prev / total).astype(jnp.bfloat16)
         p_own = (e_own / total).astype(jnp.bfloat16)
         out = jnp.dot(p_side, v_side, preferred_element_type=jnp.float32)
-        out = out + jnp.dot(p_prev, prev_ref[1], preferred_element_type=jnp.float32)
-        out = out + jnp.dot(p_own, own_ref[1], preferred_element_type=jnp.float32)
-        o_ref[...] = out.astype(o_ref.dtype)
+        out = out + jnp.dot(p_prev, prev_ref[1, p0:p1, :], preferred_element_type=jnp.float32)
+        out = out + jnp.dot(p_own, own_ref[1, 0:w_own, :], preferred_element_type=jnp.float32)
+        o_ref[r0:r0 + half, :] = out.astype(o_ref.dtype)
 
     @pl.when(roles_ref[h] != 1)
     def _():
-        s_side = scores(sk_ref[...])
-        ok_side = jnp.ones(s_side.shape, jnp.bool_)
-        finish(s_side, ok_side, sv_ref[...], col > row, col <= row)
+        one_half(0, False)
+        one_half(1, False)
 
     @pl.when(roles_ref[h] == 1)
     def _():
-        s_side = scores(vk_ref[...])
-        side_col = lax.broadcasted_iota(jnp.int32, s_side.shape, 1)
-        ok_side = side_col // BLK < count_ref[h]
-        rel_prev = row // BLK + rows // BLK - col // BLK
-        rel_own = row // BLK - col // BLK
-        ok_prev = jnp.zeros((rows, rows), jnp.bool_)
-        ok_own = jnp.zeros((rows, rows), jnp.bool_)
-        for d in range(NSL):
-            off = diag_ref[h * NSL + d]
-            ok_prev = ok_prev | (rel_prev == off)
-            ok_own = ok_own | ((rel_own == off) & ((off > 0) | (col <= row)))
-        finish(s_side, ok_side, vv_ref[...], ok_prev, ok_own)
+        one_half(0, True)
+        one_half(1, True)
 
 
 def attend(roles_l, slot_l, count_l, diag_l, q_local, prev_kv, own_kv, side):

time: 156 us -> 154 us (0.987)
  Pallas kernels: 21.4 us -> 18.6 us
    pallas_call x1, Pallas kernels: 21.4 us -> 18.6 us  [attend(): pl.pallas_call(attend_kernel, grid_spec=grid_spec, out_shape=jax.ShapeDty...]
  transfers between devices with their start and end apart: 10 -> 10, of which waited for: 2 -> 2; matrix products, arithmetic and copies ran while one was open for 6% -> 7% of each run, Pallas kernels for 0% -> 0%
where the time goes in v10:
time: 154 us; the launch traced here: 153 us
  waiting for transfers between devices  65.7 us (43%)
  starting transfers between devices  47.4 us (31%)
  Pallas kernels  18.6 us (12%)
  local copies, waits for them, and re-layouts  14.8 us (10%)
  other arithmetic  5.73 us (4%)
    all_to_all x1, waiting for transfers between devices, gather_sums(): lax.all_to_all(jnp.broadcast_to(total, (seq_devices,) + total.shape[1:]),...  38.7 us
    all_to_all x1, waiting for transfers between devices, scatter_sum(): mine = lax.all_to_all(flat, 'seq', 0, 0, tiled=True)  27 us
    ppermute x8, starting transfers between devices, shifted(): return lax.ppermute(block, axis, route)  21.7 us
    all_to_all x1, starting transfers between devices, scatter_sum(): mine = lax.all_to_all(flat, 'seq', 0, 0, tiled=True)  18.9 us
    pallas_call x1, Pallas kernels, attend(): pl.pallas_call(attend_kernel, grid_spec=grid_spec, out_shape=jax.ShapeDty...  18.6 us
    all_to_all x1, starting transfers between devices, gather_sums(): lax.all_to_all(jnp.broadcast_to(total, (seq_devices,) + total.shape[1:]),...  6.78 us
    unnamed x42, local copies, waits for them, and re-layouts  4.84 us
  transfers between devices with their start and end apart: 10, of which 2 were waited for; matrix products, arithmetic and copies ran while one was open for 7% of the time, Pallas kernels for 0%

profile of v10, /device:TPU:6, one launch (start us, length us, event | category | flops | bytes accessed | tf_op | source)
XLA Modules:
  0.0 152.8 jit_solution(17802236822183288636)
XLA Ops:
  0.0 0.0 copy-start
  0.0 0.7 broadcast_compare_fusion
  0.7 0.2 reduce-window.7
  0.9 0.6 iota_reduce_fusion
  1.5 0.0 copy-done
  1.5 0.6 gather_fusion
  2.1 0.1 reshape.199
  2.2 0.8 slice_bitcast_fusion.4
  3.0 1.3 pad_maximum_fusion
  4.3 0.7 gather_fusion.1
  5.0 0.1 copy.15
  5.1 0.1 broadcast_in_dim.40
  5.2 0.1 broadcast_in_dim.41
  5.3 0.3 bitcast_select_fusion
  5.6 0.1 pad_maximum_fusion.1
  5.6 1.1 reshape.185
  6.7 18.9 %all-to-all-start = ((bf16[64,52,128]{2,1,0:T(8,128)(2,1)}), bf16[64,52,128]{2,1,0:T(8,128)(2,1)S(1)}, u32[]{:S(2)}, u32[]{:S(2)}) async-start(bf16[64,52,128]{2,1,0:T(8,128)(2,1)} %reshape.185), calls=%async_computation | async-start | bytes 1835008 | tf_op jit(solution)/shard_map/all_to_all | solution.py:128
  25.8 0.0 copy-done.13
  25.8 0.0 copy-done.14
  25.8 0.1 constant_dynamic-slice_fusion
  25.9 0.0 copy-done.1
  25.9 0.1 constant_dynamic-slice_fusion.2
  26.0 0.0 collective-permute-start
  26.1 3.5 %collective-permute-start.1 = (bf16[64,1280]{1,0:T(8,128)(2,1)S(1)}, bf16[64,1280]{1,0:T(8,128)(2,1)S(1)}, u32[]{:S(2)}, u32[]{:S(2)}) collective-permute-start(bf16[64,1280]{1,0:T(8,128)(2,1)S(1)} %pad_maximum_fusion.5), channel_id=1, source_target_pairs={{6,0},{7,1},{0,2},{1,3},{2,4},{3,5},{4,6},{5,7},{14,8},{15,9},{8,1... | collective-permute-start | bytes 491528 | tf_op jit(solution)/shard_map/ppermute | solution.py:25
  29.6 4.2 %collective-permute-start.2 = (bf16[64,1280]{1,0:T(8,128)(2,1)S(1)}, bf16[64,1280]{1,0:T(8,128)(2,1)S(1)}, u32[]{:S(2)}, u32[]{:S(2)}) collective-permute-start(bf16[64,1280]{1,0:T(8,128)(2,1)S(1)} %pad_maximum_fusion.6), channel_id=1, source_target_pairs={{5,0},{6,1},{7,2},{0,3},{1,4},{2,5},{3,6},{4,7},{13,8},{14,9},{15,... | collective-permute-start | bytes 491528 | tf_op jit(solution)/shard_map/ppermute | solution.py:25
  33.8 3.7 %collective-permute-start.3 = (bf16[64,1280]{1,0:T(8,128)(2,1)S(1)}, bf16[64,1280]{1,0:T(8,128)(2,1)S(1)}, u32[]{:S(2)}, u32[]{:S(2)}) collective-permute-start(bf16[64,1280]{1,0:T(8,128)(2,1)S(1)} %pad_maximum_fusion.7), channel_id=1, source_target_pairs={{4,0},{5,1},{6,2},{7,3},{0,4},{1,5},{2,6},{3,7},{12,8},{13,9},{14,... | collective-permute-start | bytes 491528 | tf_op jit(solution)/shard_map/ppermute | solution.py:25
  37.6 3.7 %collective-permute-start.4 = (bf16[64,1280]{1,0:T(8,128)(2,1)S(1)}, bf16[64,1280]{1,0:T(8,128)(2,1)S(1)}, u32[]{:S(2)}, u32[]{:S(2)}) collective-permute-start(bf16[64,1280]{1,0:T(8,128)(2,1)S(1)} %pad_maximum_fusion.8), channel_id=1, source_target_pairs={{3,0},{4,1},{5,2},{6,3},{7,4},{0,5},{1,6},{2,7},{11,8},{12,9},{13,... | collective-permute-start | bytes 491528 | tf_op jit(solution)/shard_map/ppermute | solution.py:25
  41.3 1.7 %slice_bitcast_fusion.2 = (bf16[1,512,128]{2,1,0:T(8,128)(2,1)}, bf16[1,512,128]{2,1,0:T(8,128)(2,1)}) fusion(bf16[2048,128]{1,0:T(8,128)(2,1)} %param.13, bf16[2048,128]{1,0:T(8,128)(2,1)} %param.12), kind=kLoop, calls=%fused_computation.26 | loop fusion | bytes 524288 | tf_op jit(solution)/shard_map/stack | solution.py:181
  43.0 0.0 collective-permute-done
  43.0 3.3 %collective-permute-start.5 = (bf16[64,1280]{1,0:T(8,128)(2,1)S(1)}, bf16[64,1280]{1,0:T(8,128)(2,1)S(1)}, u32[]{:S(2)}, u32[]{:S(2)}) collective-permute-start(bf16[64,1280]{1,0:T(8,128)(2,1)S(1)} %pad_maximum_fusion.9), channel_id=1, source_target_pairs={{2,0},{3,1},{4,2},{5,3},{6,4},{7,5},{0,6},{1,7},{10,8},{11,9},{12,... | collective-permute-start | bytes 491528 | tf_op jit(solution)/shard_map/ppermute | solution.py:25
  46.3 0.0 collective-permute-done.1
  46.3 0.0 copy-start.3
  46.3 0.0 collective-permute-start.6
  46.4 0.6 copy-done.3
  47.0 27.0 %all-to-all-done = bf16[64,52,128]{2,1,0:T(8,128)(2,1)S(1)} async-done(((bf16[64,52,128]{2,1,0:T(8,128)(2,1)}), bf16[64,52,128]{2,1,0:T(8,128)(2,1)S(1)}, u32[]{:S(2)}, u32[]{:S(2)}) %all-to-all-start) | async-done | bytes 852000 | tf_op jit(solution)/shard_map/all_to_all | solution.py:128
  74.0 0.2 reduce_sum.12
  74.2 0.0 collective-permute-done.2
  74.2 0.0 copy-start.5
  74.2 0.0 collective-permute-done.3
  74.2 0.0 copy-start.6
  74.2 0.0 collective-permute-done.4
  74.2 0.0 collective-permute-done.5
  74.3 0.0 collective-permute-done.6
  74.3 0.7 copy-done.9
  75.0 0.7 copy-done.11
  75.7 1.0 broadcast_in_dim.46
  76.8 6.8 %all-to-all-start.1 = ((bf16[64,52,128]{2,1,0:T(8,128)(2,1)}), bf16[64,52,128]{2,1,0:T(8,128)(2,1)S(1)}, u32[]{:S(2)}, u32[]{:S(2)}) async-start(bf16[64,52,128]{2,1,0:T(8,128)(2,1)} %broadcast_in_dim.46), calls=%async_computation.1 | async-start | bytes 1835008 | tf_op jit(solution)/shard_map/all_to_all | solution.py:133
  83.6 1.0 bitcast_dynamic-update-slice_fusion.4
  84.6 0.9 bitcast_dynamic-update-slice_fusion.3
  85.6 0.6 gather_fusion.2
  86.3 0.0 copy-start.15
  86.3 0.0 copy-start.16
  86.3 1.7 %pad_maximum_fusion.2 = (bf16[2,512,128]{2,1,0:T(8,128)(2,1)}, bf16[2,512,128]{2,1,0:T(8,128)(2,1)S(1)}) fusion(bf16[1,512,128]{2,1,0:T(8,128)(2,1)S(1)} %get-tuple-element.26, bf16[1,512,128]{2,1,0:T(8,128)(2,1)S(1)} %get-tuple-element.25, bf16[1,512,128]{2,1,0:T(8,128)(2,1)} %get-tuple-element.67, bf16[1,512,128]{2,1,0:T(8,128)(2,1)} %get-tuple-element.68, ...), kind=kLoop, calls=%fused_computation.7 | loop fusion | flops 393216 | bytes 1048577 | tf_op jit(solution)/shard_map/stack | solution.py:180
  88.0 3.4 %collective-permute-start.7 = (bf16[2,512,128]{2,1,0:T(8,128)(2,1)S(1)}, bf16[2,512,128]{2,1,0:T(8,128)(2,1)S(1)}, u32[]{:S(2)}, u32[]{:S(2)}) collective-permute-start(bf16[2,512,128]{2,1,0:T(8,128)(2,1)S(1)} %get-tuple-element.36), channel_id=1, source_target_pairs={{504,0},{0,8},{8,16},{16,24},{24,32},{32,40},{40,48},{48,56},{56,6... | collective-permute-start | bytes 786440 | tf_op jit(solution)/shard_map/ppermute | solution.py:25
  91.4 0.1 copy.14
  91.5 0.7 reshape.184.diag_ref
  92.2 0.0 copy-done.16
  92.2 0.5 broadcast_select_fusion.slot_ref
  92.7 1.1 slice.34.q_ref
  93.8 38.7 %all-to-all-done.1 = bf16[64,52,128]{2,1,0:T(8,128)(2,1)S(1)} async-done(((bf16[64,52,128]{2,1,0:T(8,128)(2,1)}), bf16[64,52,128]{2,1,0:T(8,128)(2,1)S(1)}, u32[]{:S(2)}, u32[]{:S(2)}) %all-to-all-start.1) | async-done | bytes 852000 | tf_op jit(solution)/shard_map/all_to_all | solution.py:133
  132.5 1.1 reshape.187.vk_ref.vv_ref.sk_ref.sv_ref
  133.6 0.0 collective-permute-done.7.prev_ref
  133.6 0.7 copy-done.2
  134.3 18.6 %shard_map.91 = bf16[512,1024]{1,0:T(8,128)(2,1)} custom-call(s32[8]{0:T(128)} %roles_ref.1, s32[8]{0:T(128)} %broadcast_select_fusion.slot_ref, s32[8]{0:T(128)} %count_ref.1, s32[32]{0:T(128)} %reshape.184.diag_ref, bf16[512,1024]{1,0:T(8,128)(2,1)} %slice.34.q_ref, bf16[2,512,128]{2,1,0:T(8,128)(2,1)} %copy-done.2, ...), custom_call_target="tpu_custom_call" | custom-call | tf_op jit(solution)/shard_map/pallas_call | solution.py:119
  (42 shorter events, 0.3 us)
Async XLA Ops:
  0.0 1.5 copy-start
  6.7 19.1 %copy-start.13 = (bf16[64,1024]{1,0:T(8,128)(2,1)S(1)}, bf16[64,1024]{1,0:T(8,128)(2,1)}, u32[]{:S(2)}) copy-start(bf16[64,1024]{1,0:T(8,128)(2,1)} %param.11) | copy-start | bytes 393220
  6.7 19.1 %copy-start.14 = (bf16[64,1024]{1,0:T(8,128)(2,1)S(1)}, bf16[64,1024]{1,0:T(8,128)(2,1)}, u32[]{:S(2)}) copy-start(bf16[64,1024]{1,0:T(8,128)(2,1)} %param.10) | copy-start | bytes 393220
  6.7 19.2 %copy-start.1 = (bf16[64,8192]{1,0:T(8,128)(2,1)S(1)}, bf16[64,8192]{1,0:T(8,128)(2,1)}, u32[]{:S(2)}) copy-start(bf16[64,8192]{1,0:T(8,128)(2,1)} %param.9) | copy-start | bytes 3145732
  6.7 67.3 %all-to-all-start = ((bf16[64,52,128]{2,1,0:T(8,128)(2,1)}), bf16[64,52,128]{2,1,0:T(8,128)(2,1)S(1)}, u32[]{:S(2)}, u32[]{:S(2)}) async-start(bf16[64,52,128]{2,1,0:T(8,128)(2,1)} %reshape.185), calls=%async_computation | async-start | bytes 1835008 | tf_op jit(solution)/shard_map/all_to_all | solution.py:128
  26.0 17.0 %collective-permute-start = (bf16[64,1280]{1,0:T(8,128)(2,1)S(1)}, bf16[64,1280]{1,0:T(8,128)(2,1)S(1)}, u32[]{:S(2)}, u32[]{:S(2)}) collective-permute-start(bf16[64,1280]{1,0:T(8,128)(2,1)S(1)} %pad_maximum_fusion.4), channel_id=1, source_target_pairs={{7,0},{0,1},{1,2},{2,3},{3,4},{4,5},{5,6},{6,7},{15,8},{8,9},{9,10... | collective-permute-start | bytes 491528 | tf_op jit(solution)/shard_map/ppermute | solution.py:25
  26.1 20.2 %collective-permute-start.1 = (bf16[64,1280]{1,0:T(8,128)(2,1)S(1)}, bf16[64,1280]{1,0:T(8,128)(2,1)S(1)}, u32[]{:S(2)}, u32[]{:S(2)}) collective-permute-start(bf16[64,1280]{1,0:T(8,128)(2,1)S(1)} %pad_maximum_fusion.5), channel_id=1, source_target_pairs={{6,0},{7,1},{0,2},{1,3},{2,4},{3,5},{4,6},{5,7},{14,8},{15,9},{8,1... | collective-permute-start | bytes 491528 | tf_op jit(solution)/shard_map/ppermute | solution.py:25
  29.6 44.6 %collective-permute-start.2 = (bf16[64,1280]{1,0:T(8,128)(2,1)S(1)}, bf16[64,1280]{1,0:T(8,128)(2,1)S(1)}, u32[]{:S(2)}, u32[]{:S(2)}) collective-permute-start(bf16[64,1280]{1,0:T(8,128)(2,1)S(1)} %pad_maximum_fusion.6), channel_id=1, source_target_pairs={{5,0},{6,1},{7,2},{0,3},{1,4},{2,5},{3,6},{4,7},{13,8},{14,9},{15,... | collective-permute-start | bytes 491528 | tf_op jit(solution)/shard_map/ppermute | solution.py:25
  33.8 40.4 %collective-permute-start.3 = (bf16[64,1280]{1,0:T(8,128)(2,1)S(1)}, bf16[64,1280]{1,0:T(8,128)(2,1)S(1)}, u32[]{:S(2)}, u32[]{:S(2)}) collective-permute-start(bf16[64,1280]{1,0:T(8,128)(2,1)S(1)} %pad_maximum_fusion.7), channel_id=1, source_target_pairs={{4,0},{5,1},{6,2},{7,3},{0,4},{1,5},{2,6},{3,7},{12,8},{13,9},{14,... | collective-permute-start | bytes 491528 | tf_op jit(solution)/shard_map/ppermute | solution.py:25
  37.6 36.6 %collective-permute-start.4 = (bf16[64,1280]{1,0:T(8,128)(2,1)S(1)}, bf16[64,1280]{1,0:T(8,128)(2,1)S(1)}, u32[]{:S(2)}, u32[]{:S(2)}) collective-permute-start(bf16[64,1280]{1,0:T(8,128)(2,1)S(1)} %pad_maximum_fusion.8), channel_id=1, source_target_pairs={{3,0},{4,1},{5,2},{6,3},{7,4},{0,5},{1,6},{2,7},{11,8},{12,9},{13,... | collective-permute-start | bytes 491528 | tf_op jit(solution)/shard_map/ppermute | solution.py:25
  43.0 31.2 %collective-permute-start.5 = (bf16[64,1280]{1,0:T(8,128)(2,1)S(1)}, bf16[64,1280]{1,0:T(8,128)(2,1)S(1)}, u32[]{:S(2)}, u32[]{:S(2)}) collective-permute-start(bf16[64,1280]{1,0:T(8,128)(2,1)S(1)} %pad_maximum_fusion.9), channel_id=1, source_target_pairs={{2,0},{3,1},{4,2},{5,3},{6,4},{7,5},{0,6},{1,7},{10,8},{11,9},{12,... | collective-permute-start | bytes 491528 | tf_op jit(solution)/shard_map/ppermute | solution.py:25
  46.3 0.7 copy-start.3
  46.3 27.9 %collective-permute-start.6 = (bf16[64,1280]{1,0:T(8,128)(2,1)S(1)}, bf16[64,1280]{1,0:T(8,128)(2,1)S(1)}, u32[]{:S(2)}, u32[]{:S(2)}) collective-permute-start(bf16[64,1280]{1,0:T(8,128)(2,1)S(1)} %pad_maximum_fusion.10), channel_id=1, source_target_pairs={{1,0},{2,1},{3,2},{4,3},{5,4},{6,5},{7,6},{0,7},{9,8},{10,9},{11,1... | collective-permute-start | bytes 491528 | tf_op jit(solution)/shard_map/ppermute | solution.py:25
  74.2 2.6 %copy-start.5 = (bf16[64,1280]{1,0:T(8,128)(2,1)}, bf16[64,1280]{1,0:T(8,128)(2,1)S(1)}, u32[]{:S(2)}) copy-start(bf16[64,1280]{1,0:T(8,128)(2,1)S(1)} %collective-permute-done.2) | copy-start | bytes 491524
  74.2 2.5 %copy-start.6 = (bf16[64,1280]{1,0:T(8,128)(2,1)}, bf16[64,1280]{1,0:T(8,128)(2,1)S(1)}, u32[]{:S(2)}) copy-start(bf16[64,1280]{1,0:T(8,128)(2,1)S(1)} %collective-permute-done.3) | copy-start | bytes 491524
  74.2 2.5 %copy-start.7 = (bf16[64,1280]{1,0:T(8,128)(2,1)}, bf16[64,1280]{1,0:T(8,128)(2,1)S(1)}, u32[]{:S(2)}) copy-start(bf16[64,1280]{1,0:T(8,128)(2,1)S(1)} %collective-permute-done.4) | copy-start | bytes 491524
  74.3 0.8 copy-start.9
  75.0 0.7 copy-start.11
  76.7 6.8 %copy-start.4 = (bf16[64,1280]{1,0:T(8,128)(2,1)S(1)}, bf16[64,1280]{1,0:T(8,128)(2,1)}, u32[]{:S(2)}) copy-start(bf16[64,1280]{1,0:T(8,128)(2,1)} %copy-done.3) | copy-start | bytes 491524
  76.7 8.8 %copy-start.10 = (bf16[64,1280]{1,0:T(8,128)(2,1)S(1)}, bf16[64,1280]{1,0:T(8,128)(2,1)}, u32[]{:S(2)}) copy-start(bf16[64,1280]{1,0:T(8,128)(2,1)} %copy-done.9) | copy-start | bytes 491524
  76.8 55.7 %all-to-all-start.1 = ((bf16[64,52,128]{2,1,0:T(8,128)(2,1)}), bf16[64,52,128]{2,1,0:T(8,128)(2,1)S(1)}, u32[]{:S(2)}, u32[]{:S(2)}) async-start(bf16[64,52,128]{2,1,0:T(8,128)(2,1)} %broadcast_in_dim.46), calls=%async_computation.1 | async-start | bytes 1835008 | tf_op jit(solution)/shard_map/all_to_all | solution.py:133
  83.6 2.0 %copy-start.8 = (bf16[64,1280]{1,0:T(8,128)(2,1)S(1)}, bf16[64,1280]{1,0:T(8,128)(2,1)}, u32[]{:S(2)}) copy-start(bf16[64,1280]{1,0:T(8,128)(2,1)} %copy-done.7) | copy-start | bytes 491524
  83.6 2.0 %copy-start.12 = (bf16[64,1280]{1,0:T(8,128)(2,1)S(1)}, bf16[64,1280]{1,0:T(8,128)(2,1)}, u32[]{:S(2)}) copy-start(bf16[64,1280]{1,0:T(8,128)(2,1)} %copy-done.11) | copy-start | bytes 491524
  86.3 5.1 %copy-start.15 = (s32[8,4]{0,1:T(4,128)S(1)}, s32[8,4]{0,1:T(4,128)}, u32[]{:S(2)}) copy-start(s32[8,4]{0,1:T(4,128)} %param.17) | copy-start | bytes 388
  86.3 5.9 %copy-start.16 = (s32[8]{0:T(128)S(1)}, s32[8]{0:T(128)}, u32[]{:S(2)}) copy-start(s32[8]{0:T(128)} %roles_ref.1) | copy-start | bytes 100
  88.0 45.6 %collective-permute-start.7 = (bf16[2,512,128]{2,1,0:T(8,128)(2,1)S(1)}, bf16[2,512,128]{2,1,0:T(8,128)(2,1)S(1)}, u32[]{:S(2)}, u32[]{:S(2)}) collective-permute-start(bf16[2,512,128]{2,1,0:T(8,128)(2,1)S(1)} %get-tuple-element.36), channel_id=1, source_target_pairs={{504,0},{0,8},{8,16},{16,24},{24,32},{32,40},{40,48},{48,56},{56,6... | collective-permute-start | bytes 786440 | tf_op jit(solution)/shard_map/ppermute | solution.py:25
  133.6 0.7 copy-start.2

commit v11 on v10

--- a/solution.py
+++ b/solution.py
@@ -29,7 +29,8 @@
                   q_ref, prev_ref, own_ref, vk_ref, vv_ref, sk_ref, sv_ref, o_ref):
     h = pl.program_id(0)
     rows = q_ref.shape[0]
-    half = rows // 2
+    parts = 4
+    half = rows // parts
     scaling = 1.0 / math.sqrt(HEAD_SIZE)
     dims = (((1,), (1,)), ((), ()))
     neg = -jnp.inf
@@ -41,7 +42,7 @@
         r0 = part * half
         p0 = part * half
         p1 = rows
-        w_own = half + part * half
+        w_own = (part + 1) * half
         q = q_ref[r0:r0 + half, :]
         s_prev = scores(q, prev_ref[0, p0:p1, :])
         s_own = scores(q, own_ref[0, 0:w_own, :])
@@ -88,13 +89,13 @@
 
     @pl.when(roles_ref[h] != 1)
     def _():
-        one_half(0, False)
-        one_half(1, False)
+        for part in range(parts):
+            one_half(part, False)
 
     @pl.when(roles_ref[h] == 1)
     def _():
-        one_half(0, True)
-        one_half(1, True)
+        for part in range(parts):
+            one_half(part, True)
 
 
 def attend(roles_l, slot_l, count_l, diag_l, q_local, prev_kv, own_kv, side):

time: 154 us -> 156 us (1.013)
  no operation moved by 1% of the time
where the time goes in v11:
time: 156 us; the launch traced here: 154 us
  waiting for transfers between devices  65.7 us (42%)
  starting transfers between devices  47.4 us (30%)
  Pallas kernels  20 us (13%)
  local copies, waits for them, and re-layouts  14.8 us (9%)
  other arithmetic  5.73 us (4%)
    all_to_all x1, waiting for transfers between devices, gather_sums(): lax.all_to_all(jnp.broadcast_to(total, (seq_devices,) + total.shape[1:]),...  38.7 us
    all_to_all x1, waiting for transfers between devices, scatter_sum(): mine = lax.all_to_all(flat, 'seq', 0, 0, tiled=True)  27 us
    ppermute x8, starting transfers between devices, shifted(): return lax.ppermute(block, axis, route)  21.7 us
    pallas_call x1, Pallas kernels, attend(): pl.pallas_call(attend_kernel, grid_spec=grid_spec, out_shape=jax.ShapeDty...  20 us
    all_to_all x1, starting transfers between devices, scatter_sum(): mine = lax.all_to_all(flat, 'seq', 0, 0, tiled=True)  18.9 us
    all_to_all x1, starting transfers between devices, gather_sums(): lax.all_to_all(jnp.broadcast_to(total, (seq_devices,) + total.shape[1:]),...  6.78 us
    unnamed x42, local copies, waits for them, and re-layouts  4.84 us
  transfers between devices with their start and end apart: 10, of which 2 were waited for; matrix products, arithmetic and copies ran while one was open for 7% of the time, Pallas kernels for 0%

profile of v11, /device:TPU:6, one launch (start us, length us, event | category | flops | bytes accessed | tf_op | source)
XLA Modules:
  0.0 154.3 jit_solution(11644851132787102159)
XLA Ops:
  0.0 0.0 copy-start
  0.0 0.7 broadcast_compare_fusion
  0.7 0.2 reduce-window.7
  0.9 0.6 iota_reduce_fusion
  1.5 0.0 copy-done
  1.5 0.6 gather_fusion
  2.1 0.1 reshape.199
  2.2 0.8 slice_bitcast_fusion.4
  3.0 1.3 pad_maximum_fusion
  4.3 0.7 gather_fusion.1
  5.0 0.1 copy.15
  5.1 0.1 broadcast_in_dim.40
  5.2 0.1 broadcast_in_dim.41
  5.3 0.3 bitcast_select_fusion
  5.6 0.1 pad_maximum_fusion.1
  5.6 1.1 reshape.185
  6.7 18.9 %all-to-all-start = ((bf16[64,52,128]{2,1,0:T(8,128)(2,1)}), bf16[64,52,128]{2,1,0:T(8,128)(2,1)S(1)}, u32[]{:S(2)}, u32[]{:S(2)}) async-start(bf16[64,52,128]{2,1,0:T(8,128)(2,1)} %reshape.185), calls=%async_computation | async-start | bytes 1835008 | tf_op jit(solution)/shard_map/all_to_all | solution.py:129
  25.8 0.0 copy-done.13
  25.8 0.0 copy-done.14
  25.8 0.1 constant_dynamic-slice_fusion
  25.9 0.0 copy-done.1
  25.9 0.1 constant_dynamic-slice_fusion.2
  26.0 0.0 collective-permute-start
  26.1 3.5 %collective-permute-start.1 = (bf16[64,1280]{1,0:T(8,128)(2,1)S(1)}, bf16[64,1280]{1,0:T(8,128)(2,1)S(1)}, u32[]{:S(2)}, u32[]{:S(2)}) collective-permute-start(bf16[64,1280]{1,0:T(8,128)(2,1)S(1)} %pad_maximum_fusion.5), channel_id=1, source_target_pairs={{6,0},{7,1},{0,2},{1,3},{2,4},{3,5},{4,6},{5,7},{14,8},{15,9},{8,1... | collective-permute-start | bytes 491528 | tf_op jit(solution)/shard_map/ppermute | solution.py:25
  29.6 4.2 %collective-permute-start.2 = (bf16[64,1280]{1,0:T(8,128)(2,1)S(1)}, bf16[64,1280]{1,0:T(8,128)(2,1)S(1)}, u32[]{:S(2)}, u32[]{:S(2)}) collective-permute-start(bf16[64,1280]{1,0:T(8,128)(2,1)S(1)} %pad_maximum_fusion.6), channel_id=1, source_target_pairs={{5,0},{6,1},{7,2},{0,3},{1,4},{2,5},{3,6},{4,7},{13,8},{14,9},{15,... | collective-permute-start | bytes 491528 | tf_op jit(solution)/shard_map/ppermute | solution.py:25
  33.8 3.7 %collective-permute-start.3 = (bf16[64,1280]{1,0:T(8,128)(2,1)S(1)}, bf16[64,1280]{1,0:T(8,128)(2,1)S(1)}, u32[]{:S(2)}, u32[]{:S(2)}) collective-permute-start(bf16[64,1280]{1,0:T(8,128)(2,1)S(1)} %pad_maximum_fusion.7), channel_id=1, source_target_pairs={{4,0},{5,1},{6,2},{7,3},{0,4},{1,5},{2,6},{3,7},{12,8},{13,9},{14,... | collective-permute-start | bytes 491528 | tf_op jit(solution)/shard_map/ppermute | solution.py:25
  37.6 3.7 %collective-permute-start.4 = (bf16[64,1280]{1,0:T(8,128)(2,1)S(1)}, bf16[64,1280]{1,0:T(8,128)(2,1)S(1)}, u32[]{:S(2)}, u32[]{:S(2)}) collective-permute-start(bf16[64,1280]{1,0:T(8,128)(2,1)S(1)} %pad_maximum_fusion.8), channel_id=1, source_target_pairs={{3,0},{4,1},{5,2},{6,3},{7,4},{0,5},{1,6},{2,7},{11,8},{12,9},{13,... | collective-permute-start | bytes 491528 | tf_op jit(solution)/shard_map/ppermute | solution.py:25
  41.3 1.7 %slice_bitcast_fusion.2 = (bf16[1,512,128]{2,1,0:T(8,128)(2,1)}, bf16[1,512,128]{2,1,0:T(8,128)(2,1)}) fusion(bf16[2048,128]{1,0:T(8,128)(2,1)} %param.13, bf16[2048,128]{1,0:T(8,128)(2,1)} %param.12), kind=kLoop, calls=%fused_computation.26 | loop fusion | bytes 524288 | tf_op jit(solution)/shard_map/stack | solution.py:182
  43.0 0.0 collective-permute-done
  43.0 3.3 %collective-permute-start.5 = (bf16[64,1280]{1,0:T(8,128)(2,1)S(1)}, bf16[64,1280]{1,0:T(8,128)(2,1)S(1)}, u32[]{:S(2)}, u32[]{:S(2)}) collective-permute-start(bf16[64,1280]{1,0:T(8,128)(2,1)S(1)} %pad_maximum_fusion.9), channel_id=1, source_target_pairs={{2,0},{3,1},{4,2},{5,3},{6,4},{7,5},{0,6},{1,7},{10,8},{11,9},{12,... | collective-permute-start | bytes 491528 | tf_op jit(solution)/shard_map/ppermute | solution.py:25
  46.3 0.0 collective-permute-done.1
  46.3 0.0 copy-start.3
  46.3 0.0 collective-permute-start.6
  46.4 0.6 copy-done.3
  47.0 27.0 %all-to-all-done = bf16[64,52,128]{2,1,0:T(8,128)(2,1)S(1)} async-done(((bf16[64,52,128]{2,1,0:T(8,128)(2,1)}), bf16[64,52,128]{2,1,0:T(8,128)(2,1)S(1)}, u32[]{:S(2)}, u32[]{:S(2)}) %all-to-all-start) | async-done | bytes 852000 | tf_op jit(solution)/shard_map/all_to_all | solution.py:129
  74.0 0.2 reduce_sum.12
  74.2 0.0 collective-permute-done.2
  74.2 0.0 copy-start.5
  74.2 0.0 collective-permute-done.3
  74.2 0.0 copy-start.6
  74.2 0.0 collective-permute-done.4
  74.2 0.0 collective-permute-done.5
  74.3 0.0 collective-permute-done.6
  74.3 0.7 copy-done.9
  75.0 0.7 copy-done.11
  75.7 1.0 broadcast_in_dim.46
  76.8 6.8 %all-to-all-start.1 = ((bf16[64,52,128]{2,1,0:T(8,128)(2,1)}), bf16[64,52,128]{2,1,0:T(8,128)(2,1)S(1)}, u32[]{:S(2)}, u32[]{:S(2)}) async-start(bf16[64,52,128]{2,1,0:T(8,128)(2,1)} %broadcast_in_dim.46), calls=%async_computation.1 | async-start | bytes 1835008 | tf_op jit(solution)/shard_map/all_to_all | solution.py:134
  83.6 1.0 bitcast_dynamic-update-slice_fusion.4
  84.6 0.9 bitcast_dynamic-update-slice_fusion.3
  85.6 0.6 gather_fusion.2
  86.3 0.0 copy-start.15
  86.3 0.0 copy-start.16
  86.3 1.7 %pad_maximum_fusion.2 = (bf16[2,512,128]{2,1,0:T(8,128)(2,1)}, bf16[2,512,128]{2,1,0:T(8,128)(2,1)S(1)}) fusion(bf16[1,512,128]{2,1,0:T(8,128)(2,1)S(1)} %get-tuple-element.26, bf16[1,512,128]{2,1,0:T(8,128)(2,1)S(1)} %get-tuple-element.25, bf16[1,512,128]{2,1,0:T(8,128)(2,1)} %get-tuple-element.67, bf16[1,512,128]{2,1,0:T(8,128)(2,1)} %get-tuple-element.68, ...), kind=kLoop, calls=%fused_computation.7 | loop fusion | flops 393216 | bytes 1048577 | tf_op jit(solution)/shard_map/stack | solution.py:181
  88.0 3.4 %collective-permute-start.7 = (bf16[2,512,128]{2,1,0:T(8,128)(2,1)S(1)}, bf16[2,512,128]{2,1,0:T(8,128)(2,1)S(1)}, u32[]{:S(2)}, u32[]{:S(2)}) collective-permute-start(bf16[2,512,128]{2,1,0:T(8,128)(2,1)S(1)} %get-tuple-element.36), channel_id=1, source_target_pairs={{504,0},{0,8},{8,16},{16,24},{24,32},{32,40},{40,48},{48,56},{56,6... | collective-permute-start | bytes 786440 | tf_op jit(solution)/shard_map/ppermute | solution.py:25
  91.4 0.1 copy.14
  91.5 0.7 reshape.184.diag_ref
  92.2 0.0 copy-done.16
  92.2 0.5 broadcast_select_fusion.slot_ref
  92.7 1.1 slice.34.q_ref
  93.8 38.7 %all-to-all-done.1 = bf16[64,52,128]{2,1,0:T(8,128)(2,1)S(1)} async-done(((bf16[64,52,128]{2,1,0:T(8,128)(2,1)}), bf16[64,52,128]{2,1,0:T(8,128)(2,1)S(1)}, u32[]{:S(2)}, u32[]{:S(2)}) %all-to-all-start.1) | async-done | bytes 852000 | tf_op jit(solution)/shard_map/all_to_all | solution.py:134
  132.5 1.1 reshape.187.vk_ref.vv_ref.sk_ref.sv_ref
  133.6 0.0 collective-permute-done.7.prev_ref
  133.6 0.7 copy-done.2
  134.3 20.0 %shard_map.91 = bf16[512,1024]{1,0:T(8,128)(2,1)} custom-call(s32[8]{0:T(128)} %roles_ref.1, s32[8]{0:T(128)} %broadcast_select_fusion.slot_ref, s32[8]{0:T(128)} %count_ref.1, s32[32]{0:T(128)} %reshape.184.diag_ref, bf16[512,1024]{1,0:T(8,128)(2,1)} %slice.34.q_ref, bf16[2,512,128]{2,1,0:T(8,128)(2,1)} %copy-done.2, ...), custom_call_target="tpu_custom_call" | custom-call | tf_op jit(solution)/shard_map/pallas_call | solution.py:120
  (42 shorter events, 0.3 us)
Async XLA Ops:
  0.0 1.5 copy-start
  6.7 19.1 %copy-start.13 = (bf16[64,1024]{1,0:T(8,128)(2,1)S(1)}, bf16[64,1024]{1,0:T(8,128)(2,1)}, u32[]{:S(2)}) copy-start(bf16[64,1024]{1,0:T(8,128)(2,1)} %param.11) | copy-start | bytes 393220
  6.7 19.1 %copy-start.14 = (bf16[64,1024]{1,0:T(8,128)(2,1)S(1)}, bf16[64,1024]{1,0:T(8,128)(2,1)}, u32[]{:S(2)}) copy-start(bf16[64,1024]{1,0:T(8,128)(2,1)} %param.10) | copy-start | bytes 393220
  6.7 19.2 %copy-start.1 = (bf16[64,8192]{1,0:T(8,128)(2,1)S(1)}, bf16[64,8192]{1,0:T(8,128)(2,1)}, u32[]{:S(2)}) copy-start(bf16[64,8192]{1,0:T(8,128)(2,1)} %param.9) | copy-start | bytes 3145732
  6.7 67.3 %all-to-all-start = ((bf16[64,52,128]{2,1,0:T(8,128)(2,1)}), bf16[64,52,128]{2,1,0:T(8,128)(2,1)S(1)}, u32[]{:S(2)}, u32[]{:S(2)}) async-start(bf16[64,52,128]{2,1,0:T(8,128)(2,1)} %reshape.185), calls=%async_computation | async-start | bytes 1835008 | tf_op jit(solution)/shard_map/all_to_all | solution.py:129
  26.0 17.0 %collective-permute-start = (bf16[64,1280]{1,0:T(8,128)(2,1)S(1)}, bf16[64,1280]{1,0:T(8,128)(2,1)S(1)}, u32[]{:S(2)}, u32[]{:S(2)}) collective-permute-start(bf16[64,1280]{1,0:T(8,128)(2,1)S(1)} %pad_maximum_fusion.4), channel_id=1, source_target_pairs={{7,0},{0,1},{1,2},{2,3},{3,4},{4,5},{5,6},{6,7},{15,8},{8,9},{9,10... | collective-permute-start | bytes 491528 | tf_op jit(solution)/shard_map/ppermute | solution.py:25
  26.1 20.2 %collective-permute-start.1 = (bf16[64,1280]{1,0:T(8,128)(2,1)S(1)}, bf16[64,1280]{1,0:T(8,128)(2,1)S(1)}, u32[]{:S(2)}, u32[]{:S(2)}) collective-permute-start(bf16[64,1280]{1,0:T(8,128)(2,1)S(1)} %pad_maximum_fusion.5), channel_id=1, source_target_pairs={{6,0},{7,1},{0,2},{1,3},{2,4},{3,5},{4,6},{5,7},{14,8},{15,9},{8,1... | collective-permute-start | bytes 491528 | tf_op jit(solution)/shard_map/ppermute | solution.py:25
  29.6 44.6 %collective-permute-start.2 = (bf16[64,1280]{1,0:T(8,128)(2,1)S(1)}, bf16[64,1280]{1,0:T(8,128)(2,1)S(1)}, u32[]{:S(2)}, u32[]{:S(2)}) collective-permute-start(bf16[64,1280]{1,0:T(8,128)(2,1)S(1)} %pad_maximum_fusion.6), channel_id=1, source_target_pairs={{5,0},{6,1},{7,2},{0,3},{1,4},{2,5},{3,6},{4,7},{13,8},{14,9},{15,... | collective-permute-start | bytes 491528 | tf_op jit(solution)/shard_map/ppermute | solution.py:25
  33.8 40.4 %collective-permute-start.3 = (bf16[64,1280]{1,0:T(8,128)(2,1)S(1)}, bf16[64,1280]{1,0:T(8,128)(2,1)S(1)}, u32[]{:S(2)}, u32[]{:S(2)}) collective-permute-start(bf16[64,1280]{1,0:T(8,128)(2,1)S(1)} %pad_maximum_fusion.7), channel_id=1, source_target_pairs={{4,0},{5,1},{6,2},{7,3},{0,4},{1,5},{2,6},{3,7},{12,8},{13,9},{14,... | collective-permute-start | bytes 491528 | tf_op jit(solution)/shard_map/ppermute | solution.py:25
  37.6 36.6 %collective-permute-start.4 = (bf16[64,1280]{1,0:T(8,128)(2,1)S(1)}, bf16[64,1280]{1,0:T(8,128)(2,1)S(1)}, u32[]{:S(2)}, u32[]{:S(2)}) collective-permute-start(bf16[64,1280]{1,0:T(8,128)(2,1)S(1)} %pad_maximum_fusion.8), channel_id=1, source_target_pairs={{3,0},{4,1},{5,2},{6,3},{7,4},{0,5},{1,6},{2,7},{11,8},{12,9},{13,... | collective-permute-start | bytes 491528 | tf_op jit(solution)/shard_map/ppermute | solution.py:25
  43.0 31.2 %collective-permute-start.5 = (bf16[64,1280]{1,0:T(8,128)(2,1)S(1)}, bf16[64,1280]{1,0:T(8,128)(2,1)S(1)}, u32[]{:S(2)}, u32[]{:S(2)}) collective-permute-start(bf16[64,1280]{1,0:T(8,128)(2,1)S(1)} %pad_maximum_fusion.9), channel_id=1, source_target_pairs={{2,0},{3,1},{4,2},{5,3},{6,4},{7,5},{0,6},{1,7},{10,8},{11,9},{12,... | collective-permute-start | bytes 491528 | tf_op jit(solution)/shard_map/ppermute | solution.py:25
  46.3 0.7 copy-start.3
  46.3 27.9 %collective-permute-start.6 = (bf16[64,1280]{1,0:T(8,128)(2,1)S(1)}, bf16[64,1280]{1,0:T(8,128)(2,1)S(1)}, u32[]{:S(2)}, u32[]{:S(2)}) collective-permute-start(bf16[64,1280]{1,0:T(8,128)(2,1)S(1)} %pad_maximum_fusion.10), channel_id=1, source_target_pairs={{1,0},{2,1},{3,2},{4,3},{5,4},{6,5},{7,6},{0,7},{9,8},{10,9},{11,1... | collective-permute-start | bytes 491528 | tf_op jit(solution)/shard_map/ppermute | solution.py:25
  74.2 2.6 %copy-start.5 = (bf16[64,1280]{1,0:T(8,128)(2,1)}, bf16[64,1280]{1,0:T(8,128)(2,1)S(1)}, u32[]{:S(2)}) copy-start(bf16[64,1280]{1,0:T(8,128)(2,1)S(1)} %collective-permute-done.2) | copy-start | bytes 491524
  74.2 2.5 %copy-start.6 = (bf16[64,1280]{1,0:T(8,128)(2,1)}, bf16[64,1280]{1,0:T(8,128)(2,1)S(1)}, u32[]{:S(2)}) copy-start(bf16[64,1280]{1,0:T(8,128)(2,1)S(1)} %collective-permute-done.3) | copy-start | bytes 491524
  74.2 2.5 %copy-start.7 = (bf16[64,1280]{1,0:T(8,128)(2,1)}, bf16[64,1280]{1,0:T(8,128)(2,1)S(1)}, u32[]{:S(2)}) copy-start(bf16[64,1280]{1,0:T(8,128)(2,1)S(1)} %collective-permute-done.4) | copy-start | bytes 491524
  74.3 0.8 copy-start.9
  75.0 0.7 copy-start.11
  76.7 6.8 %copy-start.4 = (bf16[64,1280]{1,0:T(8,128)(2,1)S(1)}, bf16[64,1280]{1,0:T(8,128)(2,1)}, u32[]{:S(2)}) copy-start(bf16[64,1280]{1,0:T(8,128)(2,1)} %copy-done.3) | copy-start | bytes 491524
  76.7 8.8 %copy-start.10 = (bf16[64,1280]{1,0:T(8,128)(2,1)S(1)}, bf16[64,1280]{1,0:T(8,128)(2,1)}, u32[]{:S(2)}) copy-start(bf16[64,1280]{1,0:T(8,128)(2,1)} %copy-done.9) | copy-start | bytes 491524
  76.8 55.7 %all-to-all-start.1 = ((bf16[64,52,128]{2,1,0:T(8,128)(2,1)}), bf16[64,52,128]{2,1,0:T(8,128)(2,1)S(1)}, u32[]{:S(2)}, u32[]{:S(2)}) async-start(bf16[64,52,128]{2,1,0:T(8,128)(2,1)} %broadcast_in_dim.46), calls=%async_computation.1 | async-start | bytes 1835008 | tf_op jit(solution)/shard_map/all_to_all | solution.py:134
  83.6 2.0 %copy-start.8 = (bf16[64,1280]{1,0:T(8,128)(2,1)S(1)}, bf16[64,1280]{1,0:T(8,128)(2,1)}, u32[]{:S(2)}) copy-start(bf16[64,1280]{1,0:T(8,128)(2,1)} %copy-done.7) | copy-start | bytes 491524
  83.6 2.0 %copy-start.12 = (bf16[64,1280]{1,0:T(8,128)(2,1)S(1)}, bf16[64,1280]{1,0:T(8,128)(2,1)}, u32[]{:S(2)}) copy-start(bf16[64,1280]{1,0:T(8,128)(2,1)} %copy-done.11) | copy-start | bytes 491524
  86.3 5.1 %copy-start.15 = (s32[8,4]{0,1:T(4,128)S(1)}, s32[8,4]{0,1:T(4,128)}, u32[]{:S(2)}) copy-start(s32[8,4]{0,1:T(4,128)} %param.17) | copy-start | bytes 388
  86.3 5.9 %copy-start.16 = (s32[8]{0:T(128)S(1)}, s32[8]{0:T(128)}, u32[]{:S(2)}) copy-start(s32[8]{0:T(128)} %roles_ref.1) | copy-start | bytes 100
  88.0 45.6 %collective-permute-start.7 = (bf16[2,512,128]{2,1,0:T(8,128)(2,1)S(1)}, bf16[2,512,128]{2,1,0:T(8,128)(2,1)S(1)}, u32[]{:S(2)}, u32[]{:S(2)}) collective-permute-start(bf16[2,512,128]{2,1,0:T(8,128)(2,1)S(1)} %get-tuple-element.36), channel_id=1, source_target_pairs={{504,0},{0,8},{8,16},{16,24},{24,32},{32,40},{40,48},{48,56},{56,6... | collective-permute-start | bytes 786440 | tf_op jit(solution)/shard_map/ppermute | solution.py:25
  133.6 0.7 copy-start.2

commit v12 on v10

--- a/solution.py
+++ b/solution.py
@@ -149,13 +149,14 @@
     owner = cols_s // blocks_dev
     local_block = cols_s - owner * blocks_dev
     mine = (owner == my_seq)[:, :, None, None]
-    kv_blocks = jnp.stack([prefix_keys, prefix_values], 0).reshape(2, blocks_dev, BLK, HEAD_SIZE)
-    pieces = kv_blocks[:, local_block]
-    pieces = jnp.where(mine[None], pieces, jnp.zeros_like(pieces))
-    pieces = pieces.reshape(2, MAX_RETRIEVERS * VB * BLK, HEAD_SIZE)
-    sink = jnp.stack([prefix_keys[:SINK], prefix_values[:SINK]], 0)
-    sink = jnp.where(my_seq == 0, sink, jnp.zeros_like(sink))
-    both = jnp.concatenate([pieces, sink], 1)
+
+    def held(cache):
+        picked = cache.reshape(blocks_dev, BLK, HEAD_SIZE)[local_block]
+        picked = jnp.where(mine, picked, jnp.zeros_like(picked)).reshape(-1, HEAD_SIZE)
+        sink = jnp.where(my_seq == 0, cache[:SINK], jnp.zeros_like(cache[:SINK]))
+        return jnp.concatenate([picked, sink], 0)
+
+    both = jnp.stack([held(prefix_keys), held(prefix_values)], 0)
 
     head_devices = lax.axis_size("head")
     my_head = lax.axis_index("head")

time: 154 us -> 154 us (level)
  waiting for transfers between devices: 65.7 us -> 68.1 us
  Pallas kernels: 18.6 us -> 16.3 us
    gather x2, local copies, waits for them, and re-layouts: 0.76 us -> 3.33 us  [held(): picked = cache.reshape(blocks_dev, BLK, HEAD_SIZE)[local_block]]
    pallas_call x1, Pallas kernels: 18.6 us -> 16.3 us  [attend(): pl.pallas_call(attend_kernel, grid_spec=grid_spec, out_shape=jax.ShapeDty...]
    unnamed x42 -> x44, local copies, waits for them, and re-layouts: 4.84 us -> 3.35 us
  transfers between devices with their start and end apart: 10 -> 10, of which waited for: 2 -> 2; matrix products, arithmetic and copies ran while one was open for 7% -> 6% of each run, Pallas kernels for 0% -> 0%
where the time goes in v12:
time: 154 us; the launch traced here: 152 us
  waiting for transfers between devices  68.1 us (44%)
  starting transfers between devices  46.6 us (30%)
  Pallas kernels  16.3 us (11%)
  local copies, waits for them, and re-layouts  15 us (10%)
  other arithmetic  5.28 us (3%)
    all_to_all x1, waiting for transfers between devices, gather_sums(): lax.all_to_all(jnp.broadcast_to(total, (seq_devices,) + total.shape[1:]),...  39.6 us
    all_to_all x1, waiting for transfers between devices, scatter_sum(): mine = lax.all_to_all(flat, 'seq', 0, 0, tiled=True)  28.5 us
    ppermute x8, starting transfers between devices, shifted(): return lax.ppermute(block, axis, route)  20.9 us
    all_to_all x1, starting transfers between devices, scatter_sum(): mine = lax.all_to_all(flat, 'seq', 0, 0, tiled=True)  18.9 us
    pallas_call x1, Pallas kernels, attend(): pl.pallas_call(attend_kernel, grid_spec=grid_spec, out_shape=jax.ShapeDty...  16.3 us
    all_to_all x1, starting transfers between devices, gather_sums(): lax.all_to_all(jnp.broadcast_to(total, (seq_devices,) + total.shape[1:]),...  6.78 us
    unnamed x44, local copies, waits for them, and re-layouts  3.35 us
    gather x2, local copies, waits for them, and re-layouts, held(): picked = cache.reshape(blocks_dev, BLK, HEAD_SIZE)[local_block]  3.33 us
  transfers between devices with their start and end apart: 10, of which 2 were waited for; matrix products, arithmetic and copies ran while one was open for 6% of the time, Pallas kernels for 0%

profile of v12, /device:TPU:6, one launch (start us, length us, event | category | flops | bytes accessed | tf_op | source)
XLA Modules:
  0.0 151.9 jit_solution(18279063866458116540)
XLA Ops:
  0.0 0.0 copy-start
  0.0 0.7 broadcast_compare_fusion
  0.7 0.2 reduce-window.7
  0.9 0.6 iota_reduce_fusion
  1.5 0.0 copy-done
  1.5 0.6 gather_fusion
  2.1 0.1 reshape.205
  2.2 1.7 %gather_fusion.1 = bf16[24,64,128]{2,1,0:T(8,128)(2,1)S(1)} fusion(bf16[32,64,128]{2,1,0:T(8,128)(2,1)} %bitcast.71, s32[1024]{0:T(1024)S(1)} %get-tuple-element.60), kind=kCustom, calls=%fused_computation.1 | custom fusion | bytes 786528 | tf_op jit(solution)/shard_map/gather | solution.py:154
  3.9 1.7 %gather_fusion.2 = bf16[24,64,128]{2,1,0:T(8,128)(2,1)S(1)} fusion(bf16[32,64,128]{2,1,0:T(8,128)(2,1)} %bitcast.70, s32[1024]{0:T(1024)S(1)} %get-tuple-element.60), kind=kCustom, calls=%fused_computation.2 | custom fusion | bytes 786528 | tf_op jit(solution)/shard_map/gather | solution.py:154
  5.6 0.1 broadcast_in_dim.39
  5.7 0.1 broadcast_in_dim.40
  5.7 0.8 slice_select_fusion
  6.5 0.3 bitcast_select_fusion.1
  6.9 0.1 pad_maximum_fusion
  7.0 1.1 reshape.191
  8.1 18.9 %all-to-all-start = ((bf16[64,52,128]{2,1,0:T(8,128)(2,1)}), bf16[64,52,128]{2,1,0:T(8,128)(2,1)S(1)}, u32[]{:S(2)}, u32[]{:S(2)}) async-start(bf16[64,52,128]{2,1,0:T(8,128)(2,1)} %reshape.191), calls=%async_computation | async-start | bytes 1835008 | tf_op jit(solution)/shard_map/all_to_all | solution.py:128
  27.1 0.0 copy-done.14
  27.1 0.0 copy-done.15
  27.1 0.1 constant_dynamic-slice_fusion
  27.2 0.0 copy-done.1
  27.3 0.1 constant_dynamic-slice_fusion.2
  27.4 5.1 %collective-permute-start.3 = (bf16[64,1280]{1,0:T(8,128)(2,1)S(1)}, bf16[64,1280]{1,0:T(8,128)(2,1)S(1)}, u32[]{:S(2)}, u32[]{:S(2)}) collective-permute-start(bf16[64,1280]{1,0:T(8,128)(2,1)S(1)} %pad_maximum_fusion.6), channel_id=1, source_target_pairs={{4,0},{5,1},{6,2},{7,3},{0,4},{1,5},{2,6},{3,7},{12,8},{13,9},{14,... | collective-permute-start | bytes 491528 | tf_op jit(solution)/shard_map/ppermute | solution.py:25
  32.5 1.9 %collective-permute-start.4 = (bf16[64,1280]{1,0:T(8,128)(2,1)S(1)}, bf16[64,1280]{1,0:T(8,128)(2,1)S(1)}, u32[]{:S(2)}, u32[]{:S(2)}) collective-permute-start(bf16[64,1280]{1,0:T(8,128)(2,1)S(1)} %pad_maximum_fusion.7), channel_id=1, source_target_pairs={{3,0},{4,1},{5,2},{6,3},{7,4},{0,5},{1,6},{2,7},{11,8},{12,9},{13,... | collective-permute-start | bytes 491528 | tf_op jit(solution)/shard_map/ppermute | solution.py:25
  34.5 3.8 %collective-permute-start.5 = (bf16[64,1280]{1,0:T(8,128)(2,1)S(1)}, bf16[64,1280]{1,0:T(8,128)(2,1)S(1)}, u32[]{:S(2)}, u32[]{:S(2)}) collective-permute-start(bf16[64,1280]{1,0:T(8,128)(2,1)S(1)} %pad_maximum_fusion.8), channel_id=1, source_target_pairs={{2,0},{3,1},{4,2},{5,3},{6,4},{7,5},{0,6},{1,7},{10,8},{11,9},{12,... | collective-permute-start | bytes 491528 | tf_op jit(solution)/shard_map/ppermute | solution.py:25
  38.4 0.8 collective-permute-start.6
  39.2 1.9 %collective-permute-start.2 = (bf16[64,1280]{1,0:T(8,128)(2,1)S(1)}, bf16[64,1280]{1,0:T(8,128)(2,1)S(1)}, u32[]{:S(2)}, u32[]{:S(2)}) collective-permute-start(bf16[64,1280]{1,0:T(8,128)(2,1)S(1)} %pad_maximum_fusion.5), channel_id=1, source_target_pairs={{5,0},{6,1},{7,2},{0,3},{1,4},{2,5},{3,6},{4,7},{13,8},{14,9},{15,... | collective-permute-start | bytes 491528 | tf_op jit(solution)/shard_map/ppermute | solution.py:25
  41.1 1.7 %slice_bitcast_fusion.2 = (bf16[1,512,128]{2,1,0:T(8,128)(2,1)}, bf16[1,512,128]{2,1,0:T(8,128)(2,1)}) fusion(bf16[2048,128]{1,0:T(8,128)(2,1)} %param.13, bf16[2048,128]{1,0:T(8,128)(2,1)} %param.12), kind=kLoop, calls=%fused_computation.29 | loop fusion | bytes 524288 | tf_op jit(solution)/shard_map/stack | solution.py:182
  42.9 0.0 collective-permute-done.3
  42.9 2.7 %collective-permute-start.1 = (bf16[64,1280]{1,0:T(8,128)(2,1)S(1)}, bf16[64,1280]{1,0:T(8,128)(2,1)S(1)}, u32[]{:S(2)}, u32[]{:S(2)}) collective-permute-start(bf16[64,1280]{1,0:T(8,128)(2,1)S(1)} %pad_maximum_fusion.4), channel_id=1, source_target_pairs={{6,0},{7,1},{0,2},{1,3},{2,4},{3,5},{4,6},{5,7},{14,8},{15,9},{8,1... | collective-permute-start | bytes 491528 | tf_op jit(solution)/shard_map/ppermute | solution.py:25
  45.5 0.0 collective-permute-done.4
  45.5 0.0 copy-start.3
  45.6 1.3 collective-permute-start
  46.8 0.0 copy-done.3
  46.9 28.5 %all-to-all-done = bf16[64,52,128]{2,1,0:T(8,128)(2,1)S(1)} async-done(((bf16[64,52,128]{2,1,0:T(8,128)(2,1)}), bf16[64,52,128]{2,1,0:T(8,128)(2,1)S(1)}, u32[]{:S(2)}, u32[]{:S(2)}) %all-to-all-start) | async-done | bytes 852000 | tf_op jit(solution)/shard_map/all_to_all | solution.py:128
  75.4 0.2 reduce_sum.12
  75.5 0.0 collective-permute-done.5
  75.5 0.0 copy-start.5
  75.6 0.0 collective-permute-done.6
  75.6 0.0 copy-start.7
  75.6 0.0 collective-permute-done.2
  75.6 0.0 copy-start.9
  75.6 0.0 collective-permute-done.1
  75.6 0.0 collective-permute-done
  75.6 0.7 copy-done.10
  76.4 0.7 copy-done.12
  77.0 0.0 copy-start.13
  77.1 1.0 broadcast_in_dim.43
  78.1 6.8 %all-to-all-start.1 = ((bf16[64,52,128]{2,1,0:T(8,128)(2,1)}), bf16[64,52,128]{2,1,0:T(8,128)(2,1)S(1)}, u32[]{:S(2)}, u32[]{:S(2)}) async-start(bf16[64,52,128]{2,1,0:T(8,128)(2,1)} %broadcast_in_dim.43), calls=%async_computation.1 | async-start | bytes 1835008 | tf_op jit(solution)/shard_map/all_to_all | solution.py:133
  85.0 1.0 bitcast_dynamic-update-slice_fusion.4
  86.1 0.6 gather_fusion.3
  86.8 0.0 copy-start.16
  86.8 0.0 copy-start.17
  86.8 1.7 %pad_maximum_fusion.1 = (bf16[2,512,128]{2,1,0:T(8,128)(2,1)}, bf16[2,512,128]{2,1,0:T(8,128)(2,1)S(1)}) fusion(bf16[1,512,128]{2,1,0:T(8,128)(2,1)S(1)} %get-tuple-element.26, bf16[1,512,128]{2,1,0:T(8,128)(2,1)S(1)} %get-tuple-element.25, bf16[1,512,128]{2,1,0:T(8,128)(2,1)} %get-tuple-element.69, bf16[1,512,128]{2,1,0:T(8,128)(2,1)} %get-tuple-element.70, ...), kind=kLoop, calls=%fused_computation.10 | loop fusion | flops 393216 | bytes 1048577 | tf_op jit(solution)/shard_map/stack | solution.py:181
  88.5 3.4 %collective-permute-start.7 = (bf16[2,512,128]{2,1,0:T(8,128)(2,1)S(1)}, bf16[2,512,128]{2,1,0:T(8,128)(2,1)S(1)}, u32[]{:S(2)}, u32[]{:S(2)}) collective-permute-start(bf16[2,512,128]{2,1,0:T(8,128)(2,1)S(1)} %get-tuple-element.36), channel_id=1, source_target_pairs={{504,0},{0,8},{8,16},{16,24},{24,32},{32,40},{40,48},{48,56},{56,6... | collective-permute-start | bytes 786440 | tf_op jit(solution)/shard_map/ppermute | solution.py:25
  91.9 0.0 copy-done.16
  91.9 0.1 copy.12
  92.0 0.6 reshape.188.diag_ref
  92.6 0.5 broadcast_select_fusion.slot_ref
  93.1 1.1 slice.36.q_ref
  94.3 39.6 %all-to-all-done.1 = bf16[64,52,128]{2,1,0:T(8,128)(2,1)S(1)} async-done(((bf16[64,52,128]{2,1,0:T(8,128)(2,1)}), bf16[64,52,128]{2,1,0:T(8,128)(2,1)S(1)}, u32[]{:S(2)}, u32[]{:S(2)}) %all-to-all-start.1) | async-done | bytes 852000 | tf_op jit(solution)/shard_map/all_to_all | solution.py:133
  133.9 1.1 reshape.193.vk_ref.vv_ref.sk_ref.sv_ref
  134.9 0.0 collective-permute-done.7.prev_ref
  134.9 0.7 copy-done.2
  135.6 16.3 %shard_map.91 = bf16[512,1024]{1,0:T(8,128)(2,1)} custom-call(s32[8]{0:T(128)} %roles_ref.1, s32[8]{0:T(128)} %broadcast_select_fusion.slot_ref, s32[8]{0:T(128)} %count_ref.1, s32[32]{0:T(128)} %reshape.188.diag_ref, bf16[512,1024]{1,0:T(8,128)(2,1)} %slice.36.q_ref, bf16[2,512,128]{2,1,0:T(8,128)(2,1)} %copy-done.2, ...), custom_call_target="tpu_custom_call" | custom-call | tf_op jit(solution)/shard_map/pallas_call | solution.py:119
  (44 shorter events, 0.4 us)
Async XLA Ops:
  0.0 1.5 copy-start
  8.0 19.1 %copy-start.14 = (bf16[64,1024]{1,0:T(8,128)(2,1)S(1)}, bf16[64,1024]{1,0:T(8,128)(2,1)}, u32[]{:S(2)}) copy-start(bf16[64,1024]{1,0:T(8,128)(2,1)} %param.11) | copy-start | bytes 393220
  8.0 19.1 %copy-start.15 = (bf16[64,1024]{1,0:T(8,128)(2,1)S(1)}, bf16[64,1024]{1,0:T(8,128)(2,1)}, u32[]{:S(2)}) copy-start(bf16[64,1024]{1,0:T(8,128)(2,1)} %param.10) | copy-start | bytes 393220
  8.1 19.2 %copy-start.1 = (bf16[64,8192]{1,0:T(8,128)(2,1)S(1)}, bf16[64,8192]{1,0:T(8,128)(2,1)}, u32[]{:S(2)}) copy-start(bf16[64,8192]{1,0:T(8,128)(2,1)} %param.9) | copy-start | bytes 3145732
  8.1 67.3 %all-to-all-start = ((bf16[64,52,128]{2,1,0:T(8,128)(2,1)}), bf16[64,52,128]{2,1,0:T(8,128)(2,1)S(1)}, u32[]{:S(2)}, u32[]{:S(2)}) async-start(bf16[64,52,128]{2,1,0:T(8,128)(2,1)} %reshape.191), calls=%async_computation | async-start | bytes 1835008 | tf_op jit(solution)/shard_map/all_to_all | solution.py:128
  27.4 15.5 %collective-permute-start.3 = (bf16[64,1280]{1,0:T(8,128)(2,1)S(1)}, bf16[64,1280]{1,0:T(8,128)(2,1)S(1)}, u32[]{:S(2)}, u32[]{:S(2)}) collective-permute-start(bf16[64,1280]{1,0:T(8,128)(2,1)S(1)} %pad_maximum_fusion.6), channel_id=1, source_target_pairs={{4,0},{5,1},{6,2},{7,3},{0,4},{1,5},{2,6},{3,7},{12,8},{13,9},{14,... | collective-permute-start | bytes 491528 | tf_op jit(solution)/shard_map/ppermute | solution.py:25
  32.5 13.0 %collective-permute-start.4 = (bf16[64,1280]{1,0:T(8,128)(2,1)S(1)}, bf16[64,1280]{1,0:T(8,128)(2,1)S(1)}, u32[]{:S(2)}, u32[]{:S(2)}) collective-permute-start(bf16[64,1280]{1,0:T(8,128)(2,1)S(1)} %pad_maximum_fusion.7), channel_id=1, source_target_pairs={{3,0},{4,1},{5,2},{6,3},{7,4},{0,5},{1,6},{2,7},{11,8},{12,9},{13,... | collective-permute-start | bytes 491528 | tf_op jit(solution)/shard_map/ppermute | solution.py:25
  34.5 41.1 %collective-permute-start.5 = (bf16[64,1280]{1,0:T(8,128)(2,1)S(1)}, bf16[64,1280]{1,0:T(8,128)(2,1)S(1)}, u32[]{:S(2)}, u32[]{:S(2)}) collective-permute-start(bf16[64,1280]{1,0:T(8,128)(2,1)S(1)} %pad_maximum_fusion.8), channel_id=1, source_target_pairs={{2,0},{3,1},{4,2},{5,3},{6,4},{7,5},{0,6},{1,7},{10,8},{11,9},{12,... | collective-permute-start | bytes 491528 | tf_op jit(solution)/shard_map/ppermute | solution.py:25
  38.4 37.2 %collective-permute-start.6 = (bf16[64,1280]{1,0:T(8,128)(2,1)S(1)}, bf16[64,1280]{1,0:T(8,128)(2,1)S(1)}, u32[]{:S(2)}, u32[]{:S(2)}) collective-permute-start(bf16[64,1280]{1,0:T(8,128)(2,1)S(1)} %pad_maximum_fusion.9), channel_id=1, source_target_pairs={{1,0},{2,1},{3,2},{4,3},{5,4},{6,5},{7,6},{0,7},{9,8},{10,9},{11,1... | collective-permute-start | bytes 491528 | tf_op jit(solution)/shard_map/ppermute | solution.py:25
  39.2 36.4 %collective-permute-start.2 = (bf16[64,1280]{1,0:T(8,128)(2,1)S(1)}, bf16[64,1280]{1,0:T(8,128)(2,1)S(1)}, u32[]{:S(2)}, u32[]{:S(2)}) collective-permute-start(bf16[64,1280]{1,0:T(8,128)(2,1)S(1)} %pad_maximum_fusion.5), channel_id=1, source_target_pairs={{5,0},{6,1},{7,2},{0,3},{1,4},{2,5},{3,6},{4,7},{13,8},{14,9},{15,... | collective-permute-start | bytes 491528 | tf_op jit(solution)/shard_map/ppermute | solution.py:25
  42.9 32.7 %collective-permute-start.1 = (bf16[64,1280]{1,0:T(8,128)(2,1)S(1)}, bf16[64,1280]{1,0:T(8,128)(2,1)S(1)}, u32[]{:S(2)}, u32[]{:S(2)}) collective-permute-start(bf16[64,1280]{1,0:T(8,128)(2,1)S(1)} %pad_maximum_fusion.4), channel_id=1, source_target_pairs={{6,0},{7,1},{0,2},{1,3},{2,4},{3,5},{4,6},{5,7},{14,8},{15,9},{8,1... | collective-permute-start | bytes 491528 | tf_op jit(solution)/shard_map/ppermute | solution.py:25
  45.5 1.3 copy-start.3
  45.6 30.1 %collective-permute-start = (bf16[64,1280]{1,0:T(8,128)(2,1)S(1)}, bf16[64,1280]{1,0:T(8,128)(2,1)S(1)}, u32[]{:S(2)}, u32[]{:S(2)}) collective-permute-start(bf16[64,1280]{1,0:T(8,128)(2,1)S(1)} %pad_maximum_fusion.3), channel_id=1, source_target_pairs={{7,0},{0,1},{1,2},{2,3},{3,4},{4,5},{5,6},{6,7},{15,8},{8,9},{9,10... | collective-permute-start | bytes 491528 | tf_op jit(solution)/shard_map/ppermute | solution.py:25
  75.5 2.6 %copy-start.5 = (bf16[64,1280]{1,0:T(8,128)(2,1)}, bf16[64,1280]{1,0:T(8,128)(2,1)S(1)}, u32[]{:S(2)}) copy-start(bf16[64,1280]{1,0:T(8,128)(2,1)S(1)} %collective-permute-done.5) | copy-start | bytes 491524
  75.6 2.5 %copy-start.7 = (bf16[64,1280]{1,0:T(8,128)(2,1)}, bf16[64,1280]{1,0:T(8,128)(2,1)S(1)}, u32[]{:S(2)}) copy-start(bf16[64,1280]{1,0:T(8,128)(2,1)S(1)} %collective-permute-done.6) | copy-start | bytes 491524
  75.6 2.5 %copy-start.9 = (bf16[64,1280]{1,0:T(8,128)(2,1)}, bf16[64,1280]{1,0:T(8,128)(2,1)S(1)}, u32[]{:S(2)}) copy-start(bf16[64,1280]{1,0:T(8,128)(2,1)S(1)} %collective-permute-done.2) | copy-start | bytes 491524
  75.6 0.8 copy-start.10
  76.4 0.7 copy-start.12
  77.0 7.9 %copy-start.13 = (bf16[64,1280]{1,0:T(8,128)(2,1)S(1)}, bf16[64,1280]{1,0:T(8,128)(2,1)}, u32[]{:S(2)}) copy-start(bf16[64,1280]{1,0:T(8,128)(2,1)} %copy-done.12) | copy-start | bytes 491524
  78.1 6.9 %copy-start.11 = (bf16[64,1280]{1,0:T(8,128)(2,1)S(1)}, bf16[64,1280]{1,0:T(8,128)(2,1)}, u32[]{:S(2)}) copy-start(bf16[64,1280]{1,0:T(8,128)(2,1)} %copy-done.10) | copy-start | bytes 491524
  78.1 7.9 %copy-start.4 = (bf16[64,1280]{1,0:T(8,128)(2,1)S(1)}, bf16[64,1280]{1,0:T(8,128)(2,1)}, u32[]{:S(2)}) copy-start(bf16[64,1280]{1,0:T(8,128)(2,1)} %copy-done.3) | copy-start | bytes 491524
  78.1 55.7 %all-to-all-start.1 = ((bf16[64,52,128]{2,1,0:T(8,128)(2,1)}), bf16[64,52,128]{2,1,0:T(8,128)(2,1)S(1)}, u32[]{:S(2)}, u32[]{:S(2)}) async-start(bf16[64,52,128]{2,1,0:T(8,128)(2,1)} %broadcast_in_dim.43), calls=%async_computation.1 | async-start | bytes 1835008 | tf_op jit(solution)/shard_map/all_to_all | solution.py:133
  84.9 1.1 copy-start.6
  84.9 1.2 copy-start.8
  86.8 5.1 %copy-start.16 = (s32[8,4]{0,1:T(4,128)S(1)}, s32[8,4]{0,1:T(4,128)}, u32[]{:S(2)}) copy-start(s32[8,4]{0,1:T(4,128)} %param.17) | copy-start | bytes 388
  86.8 5.9 %copy-start.17 = (s32[8]{0:T(128)S(1)}, s32[8]{0:T(128)}, u32[]{:S(2)}) copy-start(s32[8]{0:T(128)} %roles_ref.1) | copy-start | bytes 100
  88.5 46.4 %collective-permute-start.7 = (bf16[2,512,128]{2,1,0:T(8,128)(2,1)S(1)}, bf16[2,512,128]{2,1,0:T(8,128)(2,1)S(1)}, u32[]{:S(2)}, u32[]{:S(2)}) collective-permute-start(bf16[2,512,128]{2,1,0:T(8,128)(2,1)S(1)} %get-tuple-element.36), channel_id=1, source_target_pairs={{504,0},{0,8},{8,16},{16,24},{24,32},{32,40},{40,48},{48,56},{56,6... | collective-permute-start | bytes 786440 | tf_op jit(solution)/shard_map/ppermute | solution.py:25
  134.9 0.7 copy-start.2

commit v13 on v10

--- a/solution.py
+++ b/solution.py
@@ -123,14 +123,15 @@
     )(roles_l, slot_l, count_l, diag_l, q_local, prev_kv, own_kv, side, side, side, side)
 
 
-def scatter_sum(block, seq_devices):
+def scatter_parts(block, seq_devices):
     flat = block.reshape(seq_devices, -1, block.shape[-1])
-    mine = lax.all_to_all(flat, "seq", 0, 0, tiled=True)
-    return jnp.sum(mine.astype(jnp.float32), 0, keepdims=True).astype(block.dtype)
-
-
-def gather_sums(total, shape, seq_devices):
-    every = lax.all_to_all(jnp.broadcast_to(total, (seq_devices,) + total.shape[1:]), "seq", 0, 0, tiled=True)
+    return lax.all_to_all(flat, "seq", 0, 0, tiled=True)
+
+
+def gather_sums(mine, shape, seq_devices):
+    ones = jnp.ones((seq_devices, seq_devices), mine.dtype)
+    total = jnp.einsum("ab,bcd->acd", ones, mine, preferred_element_type=jnp.float32).astype(mine.dtype)
+    every = lax.all_to_all(total, "seq", 0, 0, tiled=True)
     return every.reshape(shape)
 
 
@@ -171,8 +172,8 @@
     received = [columns_for(my_head)]
     for k in range(1, head_devices):
         received.append(shifted(columns_for((my_head + k) % head_devices), "head", k))
-    total = scatter_sum(both, seq_devices)
-    total, received = lax.optimization_barrier((total, received))
+    mine = scatter_parts(both, seq_devices)
+    mine, received = lax.optimization_barrier((mine, received))
     by_shift = jnp.stack(received, 0)
     order = (my_head - jnp.arange(head_devices, dtype=jnp.int32)) % head_devices
     tokens = by_shift[order].reshape(-1, q_width + 2 * kv_width)
@@ -181,7 +182,7 @@
     tail_cache = jnp.stack([prefix_keys[cache_rows - WIN:], prefix_values[cache_rows - WIN:]], 0)
     outgoing = jnp.where(my_seq == seq_devices - 1, tail_cache, kv_local)
     prev_kv = shifted(outgoing, "seq", 1)
-    side = gather_sums(total, both.shape, seq_devices)
+    side = gather_sums(mine, both.shape, seq_devices)
 
     slot_l = jnp.where(is_ret, slot, 0).astype(jnp.int32)
     return attend(

time: 154 us -> 153 us (level)
    all_to_all x2, waiting for transfers between devices: 65.7 us -> 60.8 us  [the longest x1 37.7 us: gather_sums(): every = lax.all_to_all(total, 'seq', 0, 0, tiled=True)]
    ppermute x8, waiting for transfers between devices: 0.02 us -> 3.88 us  [shifted(): return lax.ppermute(block, axis, route)]
    unnamed x42 -> x38, local copies, waits for them, and re-layouts: 4.84 us -> 3.47 us
  transfers between devices with their start and end apart: 10 -> 10, of which waited for: 2 -> 4; matrix products, arithmetic and copies ran while one was open for 7% -> 7% of each run, Pallas kernels for 0% -> 0%
where the time goes in v13:
time: 153 us; the launch traced here: 152 us
  waiting for transfers between devices  64.7 us (42%)
  starting transfers between devices  47.4 us (31%)
  Pallas kernels  18.6 us (12%)
  local copies, waits for them, and re-layouts  14.7 us (10%)
  other arithmetic  5.63 us (4%)
    all_to_all x1, waiting for transfers between devices, gather_sums(): every = lax.all_to_all(total, 'seq', 0, 0, tiled=True)  37.7 us
    all_to_all x1, waiting for transfers between devices, scatter_parts(): return lax.all_to_all(flat, 'seq', 0, 0, tiled=True)  23.1 us
    ppermute x8, starting transfers between devices, shifted(): return lax.ppermute(block, axis, route)  21.7 us
    all_to_all x1, starting transfers between devices, scatter_parts(): return lax.all_to_all(flat, 'seq', 0, 0, tiled=True)  18.9 us
    pallas_call x1, Pallas kernels, attend(): pl.pallas_call(attend_kernel, grid_spec=grid_spec, out_shape=jax.ShapeDty...  18.6 us
    all_to_all x1, starting transfers between devices, gather_sums(): every = lax.all_to_all(total, 'seq', 0, 0, tiled=True)  6.78 us
    ppermute x8, waiting for transfers between devices, shifted(): return lax.ppermute(block, axis, route)  3.88 us
    unnamed x38, local copies, waits for them, and re-layouts  3.47 us
  transfers between devices with their start and end apart: 10, of which 4 were waited for; matrix products, arithmetic and copies ran while one was open for 7% of the time, Pallas kernels for 0%

profile of v13, /device:TPU:6, one launch (start us, length us, event | category | flops | bytes accessed | tf_op | source)
XLA Modules:
  0.0 152.0 jit_solution(6611767251605384985)
XLA Ops:
  0.0 0.0 copy-start
  0.0 0.7 broadcast_compare_fusion
  0.7 0.2 reduce-window.7
  0.9 0.6 iota_reduce_fusion
  1.5 0.0 copy-done
  1.5 0.6 gather_fusion
  2.1 0.1 reshape.190
  2.2 0.8 slice_bitcast_fusion.4
  3.0 1.3 pad_maximum_fusion
  4.3 0.7 gather_fusion.1
  5.0 0.1 copy.24
  5.1 0.1 broadcast_in_dim.35
  5.2 0.1 broadcast_in_dim.36
  5.3 0.3 bitcast_select_fusion
  5.6 0.1 pad_maximum_fusion.1
  5.6 1.1 reshape.176
  6.7 18.9 %all-to-all-start = ((bf16[64,52,128]{2,1,0:T(8,128)(2,1)}), bf16[64,52,128]{2,1,0:T(8,128)(2,1)S(1)}, u32[]{:S(2)}, u32[]{:S(2)}) async-start(bf16[64,52,128]{2,1,0:T(8,128)(2,1)} %reshape.176), calls=%async_computation | async-start | bytes 1835008 | tf_op jit(solution)/shard_map/all_to_all | solution.py:128
  25.8 0.0 copy-done.11
  25.8 0.0 copy-done.12
  25.8 0.1 constant_dynamic-slice_fusion
  25.9 0.0 copy-done.1
  25.9 0.1 constant_dynamic-slice_fusion.2
  26.0 0.0 collective-permute-start
  26.1 3.5 %collective-permute-start.1 = (bf16[64,1280]{1,0:T(8,128)(2,1)S(1)}, bf16[64,1280]{1,0:T(8,128)(2,1)S(1)}, u32[]{:S(2)}, u32[]{:S(2)}) collective-permute-start(bf16[64,1280]{1,0:T(8,128)(2,1)S(1)} %pad_maximum_fusion.5), channel_id=1, source_target_pairs={{6,0},{7,1},{0,2},{1,3},{2,4},{3,5},{4,6},{5,7},{14,8},{15,9},{8,1... | collective-permute-start | bytes 491528 | tf_op jit(solution)/shard_map/ppermute | solution.py:25
  29.6 4.2 %collective-permute-start.2 = (bf16[64,1280]{1,0:T(8,128)(2,1)S(1)}, bf16[64,1280]{1,0:T(8,128)(2,1)S(1)}, u32[]{:S(2)}, u32[]{:S(2)}) collective-permute-start(bf16[64,1280]{1,0:T(8,128)(2,1)S(1)} %pad_maximum_fusion.6), channel_id=1, source_target_pairs={{5,0},{6,1},{7,2},{0,3},{1,4},{2,5},{3,6},{4,7},{13,8},{14,9},{15,... | collective-permute-start | bytes 491528 | tf_op jit(solution)/shard_map/ppermute | solution.py:25
  33.8 3.7 %collective-permute-start.3 = (bf16[64,1280]{1,0:T(8,128)(2,1)S(1)}, bf16[64,1280]{1,0:T(8,128)(2,1)S(1)}, u32[]{:S(2)}, u32[]{:S(2)}) collective-permute-start(bf16[64,1280]{1,0:T(8,128)(2,1)S(1)} %pad_maximum_fusion.7), channel_id=1, source_target_pairs={{4,0},{5,1},{6,2},{7,3},{0,4},{1,5},{2,6},{3,7},{12,8},{13,9},{14,... | collective-permute-start | bytes 491528 | tf_op jit(solution)/shard_map/ppermute | solution.py:25
  37.6 3.7 %collective-permute-start.4 = (bf16[64,1280]{1,0:T(8,128)(2,1)S(1)}, bf16[64,1280]{1,0:T(8,128)(2,1)S(1)}, u32[]{:S(2)}, u32[]{:S(2)}) collective-permute-start(bf16[64,1280]{1,0:T(8,128)(2,1)S(1)} %pad_maximum_fusion.8), channel_id=1, source_target_pairs={{3,0},{4,1},{5,2},{6,3},{7,4},{0,5},{1,6},{2,7},{11,8},{12,9},{13,... | collective-permute-start | bytes 491528 | tf_op jit(solution)/shard_map/ppermute | solution.py:25
  41.3 1.7 %slice_bitcast_fusion.2 = (bf16[1,512,128]{2,1,0:T(8,128)(2,1)}, bf16[1,512,128]{2,1,0:T(8,128)(2,1)}) fusion(bf16[2048,128]{1,0:T(8,128)(2,1)} %param.13, bf16[2048,128]{1,0:T(8,128)(2,1)} %param.12), kind=kLoop, calls=%fused_computation.28 | loop fusion | bytes 524288 | tf_op jit(solution)/shard_map/stack | solution.py:182
  43.0 0.0 collective-permute-done
  43.0 3.3 %collective-permute-start.5 = (bf16[64,1280]{1,0:T(8,128)(2,1)S(1)}, bf16[64,1280]{1,0:T(8,128)(2,1)S(1)}, u32[]{:S(2)}, u32[]{:S(2)}) collective-permute-start(bf16[64,1280]{1,0:T(8,128)(2,1)S(1)} %pad_maximum_fusion.9), channel_id=1, source_target_pairs={{2,0},{3,1},{4,2},{5,3},{6,4},{7,5},{0,6},{1,7},{10,8},{11,9},{12,... | collective-permute-start | bytes 491528 | tf_op jit(solution)/shard_map/ppermute | solution.py:25
  46.3 0.0 collective-permute-done.1
  46.3 0.0 copy-start.3
  46.3 0.0 collective-permute-start.6
  46.3 0.6 copy-done.3
  47.0 0.0 collective-permute-done.2
  47.0 0.0 collective-permute-done.3
  47.0 0.0 collective-permute-done.4
  47.0 0.0 copy-start.7
  47.1 3.5 %collective-permute-done.5 = bf16[64,1280]{1,0:T(8,128)(2,1)S(1)} collective-permute-done((bf16[64,1280]{1,0:T(8,128)(2,1)S(1)}, bf16[64,1280]{1,0:T(8,128)(2,1)S(1)}, u32[]{:S(2)}, u32[]{:S(2)}) %collective-permute-start.5) | collective-permute-done | bytes 163872 | tf_op jit(solution)/shard_map/ppermute | solution.py:25
  50.5 0.4 collective-permute-done.6
  50.9 23.1 %all-to-all-done = bf16[64,52,128]{2,1,0:T(8,128)(2,1)S(1)} async-done(((bf16[64,52,128]{2,1,0:T(8,128)(2,1)}), bf16[64,52,128]{2,1,0:T(8,128)(2,1)S(1)}, u32[]{:S(2)}, u32[]{:S(2)}) %all-to-all-start) | async-done | bytes 852000 | tf_op jit(solution)/shard_map/all_to_all | solution.py:128
  74.0 0.4 convolution_convert_fusion
  74.4 1.5 copy.26
  75.9 0.0 copy-done.7
  75.9 6.8 %all-to-all-start.1 = ((bf16[64,52,128]{2,1,0:T(8,128)(2,1)}), bf16[64,52,128]{2,1,0:T(8,128)(2,1)S(1)}, u32[]{:S(2)}, u32[]{:S(2)}) async-start(bf16[64,52,128]{2,1,0:T(8,128)(2,1)} %copy.26), calls=%async_computation.1 | async-start | bytes 1835008 | tf_op jit(solution)/shard_map/all_to_all | solution.py:134
  82.8 1.0 bitcast_dynamic-update-slice_fusion.4
  83.8 0.9 bitcast_dynamic-update-slice_fusion.3
  84.7 0.0 copy-done.10
  84.8 0.9 bitcast_dynamic-update-slice_fusion
  85.7 0.6 gather_fusion.2
  86.3 0.0 copy-start.13
  86.4 0.0 copy-start.14
  86.4 1.7 %pad_maximum_fusion.2 = (bf16[2,512,128]{2,1,0:T(8,128)(2,1)}, bf16[2,512,128]{2,1,0:T(8,128)(2,1)S(1)}) fusion(bf16[1,512,128]{2,1,0:T(8,128)(2,1)S(1)} %get-tuple-element.26, bf16[1,512,128]{2,1,0:T(8,128)(2,1)S(1)} %get-tuple-element.25, bf16[1,512,128]{2,1,0:T(8,128)(2,1)} %get-tuple-element.67, bf16[1,512,128]{2,1,0:T(8,128)(2,1)} %get-tuple-element.68, ...), kind=kLoop, calls=%fused_computation.9 | loop fusion | flops 393216 | bytes 1048577 | tf_op jit(solution)/shard_map/stack | solution.py:181
  88.1 3.4 %collective-permute-start.7 = (bf16[2,512,128]{2,1,0:T(8,128)(2,1)S(1)}, bf16[2,512,128]{2,1,0:T(8,128)(2,1)S(1)}, u32[]{:S(2)}, u32[]{:S(2)}) collective-permute-start(bf16[2,512,128]{2,1,0:T(8,128)(2,1)S(1)} %get-tuple-element.36), channel_id=1, source_target_pairs={{504,0},{0,8},{8,16},{16,24},{24,32},{32,40},{40,48},{48,56},{56,6... | collective-permute-start | bytes 786440 | tf_op jit(solution)/shard_map/ppermute | solution.py:25
  91.5 0.0 copy-done.13
  91.5 0.1 copy.23
  91.6 0.6 reshape.175.diag_ref
  92.2 0.6 broadcast_select_fusion.slot_ref
  92.8 1.1 slice.34.q_ref
  93.9 37.7 %all-to-all-done.1 = bf16[64,52,128]{2,1,0:T(8,128)(2,1)S(1)} async-done(((bf16[64,52,128]{2,1,0:T(8,128)(2,1)}), bf16[64,52,128]{2,1,0:T(8,128)(2,1)S(1)}, u32[]{:S(2)}, u32[]{:S(2)}) %all-to-all-start.1) | async-done | bytes 852000 | tf_op jit(solution)/shard_map/all_to_all | solution.py:134
  131.6 1.1 reshape.178.vk_ref.vv_ref.sk_ref.sv_ref
  132.7 0.0 collective-permute-done.7.prev_ref
  132.7 0.7 copy-done.2
  133.4 18.6 %shard_map.91 = bf16[512,1024]{1,0:T(8,128)(2,1)} custom-call(s32[8]{0:T(128)} %roles_ref.1, s32[8]{0:T(128)} %broadcast_select_fusion.slot_ref, s32[8]{0:T(128)} %count_ref.1, s32[32]{0:T(128)} %reshape.175.diag_ref, bf16[512,1024]{1,0:T(8,128)(2,1)} %slice.34.q_ref, bf16[2,512,128]{2,1,0:T(8,128)(2,1)} %copy-done.2, ...), custom_call_target="tpu_custom_call" | custom-call | tf_op jit(solution)/shard_map/pallas_call | solution.py:119
  (38 shorter events, 0.3 us)
Async XLA Ops:
  0.0 1.5 copy-start
  6.7 19.1 %copy-start.11 = (bf16[64,1024]{1,0:T(8,128)(2,1)S(1)}, bf16[64,1024]{1,0:T(8,128)(2,1)}, u32[]{:S(2)}) copy-start(bf16[64,1024]{1,0:T(8,128)(2,1)} %param.11) | copy-start | bytes 393220
  6.7 19.1 %copy-start.12 = (bf16[64,1024]{1,0:T(8,128)(2,1)S(1)}, bf16[64,1024]{1,0:T(8,128)(2,1)}, u32[]{:S(2)}) copy-start(bf16[64,1024]{1,0:T(8,128)(2,1)} %param.10) | copy-start | bytes 393220
  6.7 19.2 %copy-start.1 = (bf16[64,8192]{1,0:T(8,128)(2,1)S(1)}, bf16[64,8192]{1,0:T(8,128)(2,1)}, u32[]{:S(2)}) copy-start(bf16[64,8192]{1,0:T(8,128)(2,1)} %param.9) | copy-start | bytes 3145732
  6.7 67.3 %all-to-all-start = ((bf16[64,52,128]{2,1,0:T(8,128)(2,1)}), bf16[64,52,128]{2,1,0:T(8,128)(2,1)S(1)}, u32[]{:S(2)}, u32[]{:S(2)}) async-start(bf16[64,52,128]{2,1,0:T(8,128)(2,1)} %reshape.176), calls=%async_computation | async-start | bytes 1835008 | tf_op jit(solution)/shard_map/all_to_all | solution.py:128
  26.0 17.0 %collective-permute-start = (bf16[64,1280]{1,0:T(8,128)(2,1)S(1)}, bf16[64,1280]{1,0:T(8,128)(2,1)S(1)}, u32[]{:S(2)}, u32[]{:S(2)}) collective-permute-start(bf16[64,1280]{1,0:T(8,128)(2,1)S(1)} %pad_maximum_fusion.4), channel_id=1, source_target_pairs={{7,0},{0,1},{1,2},{2,3},{3,4},{4,5},{5,6},{6,7},{15,8},{8,9},{9,10... | collective-permute-start | bytes 491528 | tf_op jit(solution)/shard_map/ppermute | solution.py:25
  26.1 20.2 %collective-permute-start.1 = (bf16[64,1280]{1,0:T(8,128)(2,1)S(1)}, bf16[64,1280]{1,0:T(8,128)(2,1)S(1)}, u32[]{:S(2)}, u32[]{:S(2)}) collective-permute-start(bf16[64,1280]{1,0:T(8,128)(2,1)S(1)} %pad_maximum_fusion.5), channel_id=1, source_target_pairs={{6,0},{7,1},{0,2},{1,3},{2,4},{3,5},{4,6},{5,7},{14,8},{15,9},{8,1... | collective-permute-start | bytes 491528 | tf_op jit(solution)/shard_map/ppermute | solution.py:25
  29.6 17.4 %collective-permute-start.2 = (bf16[64,1280]{1,0:T(8,128)(2,1)S(1)}, bf16[64,1280]{1,0:T(8,128)(2,1)S(1)}, u32[]{:S(2)}, u32[]{:S(2)}) collective-permute-start(bf16[64,1280]{1,0:T(8,128)(2,1)S(1)} %pad_maximum_fusion.6), channel_id=1, source_target_pairs={{5,0},{6,1},{7,2},{0,3},{1,4},{2,5},{3,6},{4,7},{13,8},{14,9},{15,... | collective-permute-start | bytes 491528 | tf_op jit(solution)/shard_map/ppermute | solution.py:25
  33.8 13.2 %collective-permute-start.3 = (bf16[64,1280]{1,0:T(8,128)(2,1)S(1)}, bf16[64,1280]{1,0:T(8,128)(2,1)S(1)}, u32[]{:S(2)}, u32[]{:S(2)}) collective-permute-start(bf16[64,1280]{1,0:T(8,128)(2,1)S(1)} %pad_maximum_fusion.7), channel_id=1, source_target_pairs={{4,0},{5,1},{6,2},{7,3},{0,4},{1,5},{2,6},{3,7},{12,8},{13,9},{14,... | collective-permute-start | bytes 491528 | tf_op jit(solution)/shard_map/ppermute | solution.py:25
  37.6 9.4 %collective-permute-start.4 = (bf16[64,1280]{1,0:T(8,128)(2,1)S(1)}, bf16[64,1280]{1,0:T(8,128)(2,1)S(1)}, u32[]{:S(2)}, u32[]{:S(2)}) collective-permute-start(bf16[64,1280]{1,0:T(8,128)(2,1)S(1)} %pad_maximum_fusion.8), channel_id=1, source_target_pairs={{3,0},{4,1},{5,2},{6,3},{7,4},{0,5},{1,6},{2,7},{11,8},{12,9},{13,... | collective-permute-start | bytes 491528 | tf_op jit(solution)/shard_map/ppermute | solution.py:25
  43.0 7.5 %collective-permute-start.5 = (bf16[64,1280]{1,0:T(8,128)(2,1)S(1)}, bf16[64,1280]{1,0:T(8,128)(2,1)S(1)}, u32[]{:S(2)}, u32[]{:S(2)}) collective-permute-start(bf16[64,1280]{1,0:T(8,128)(2,1)S(1)} %pad_maximum_fusion.9), channel_id=1, source_target_pairs={{2,0},{3,1},{4,2},{5,3},{6,4},{7,5},{0,6},{1,7},{10,8},{11,9},{12,... | collective-permute-start | bytes 491528 | tf_op jit(solution)/shard_map/ppermute | solution.py:25
  46.3 0.7 copy-start.3
  46.3 4.6 %collective-permute-start.6 = (bf16[64,1280]{1,0:T(8,128)(2,1)S(1)}, bf16[64,1280]{1,0:T(8,128)(2,1)}, u32[]{:S(2)}, u32[]{:S(2)}) collective-permute-start(bf16[64,1280]{1,0:T(8,128)(2,1)S(1)} %pad_maximum_fusion.10), channel_id=1, source_target_pairs={{1,0},{2,1},{3,2},{4,3},{5,4},{6,5},{7,6},{0,7},{9,8},{10,9},{11,1... | collective-permute-start | bytes 491528 | tf_op jit(solution)/shard_map/ppermute | solution.py:25
  47.0 28.9 %copy-start.5 = (bf16[64,1280]{1,0:T(8,128)(2,1)}, bf16[64,1280]{1,0:T(8,128)(2,1)S(1)}, u32[]{:S(2)}) copy-start(bf16[64,1280]{1,0:T(8,128)(2,1)S(1)} %collective-permute-done.2) | copy-start | bytes 491524
  47.0 28.9 %copy-start.6 = (bf16[64,1280]{1,0:T(8,128)(2,1)}, bf16[64,1280]{1,0:T(8,128)(2,1)S(1)}, u32[]{:S(2)}) copy-start(bf16[64,1280]{1,0:T(8,128)(2,1)S(1)} %collective-permute-done.3) | copy-start | bytes 491524
  47.0 28.8 %copy-start.7 = (bf16[64,1280]{1,0:T(8,128)(2,1)}, bf16[64,1280]{1,0:T(8,128)(2,1)S(1)}, u32[]{:S(2)}) copy-start(bf16[64,1280]{1,0:T(8,128)(2,1)S(1)} %collective-permute-done.4) | copy-start | bytes 491524
  50.5 25.4 %copy-start.9 = (bf16[64,1280]{1,0:T(8,128)(2,1)}, bf16[64,1280]{1,0:T(8,128)(2,1)S(1)}, u32[]{:S(2)}) copy-start(bf16[64,1280]{1,0:T(8,128)(2,1)S(1)} %collective-permute-done.5) | copy-start | bytes 491524
  75.9 6.8 %copy-start.4 = (bf16[64,1280]{1,0:T(8,128)(2,1)S(1)}, bf16[64,1280]{1,0:T(8,128)(2,1)}, u32[]{:S(2)}) copy-start(bf16[64,1280]{1,0:T(8,128)(2,1)} %copy-done.3) | copy-start | bytes 491524
  75.9 55.7 %all-to-all-start.1 = ((bf16[64,52,128]{2,1,0:T(8,128)(2,1)}), bf16[64,52,128]{2,1,0:T(8,128)(2,1)S(1)}, u32[]{:S(2)}, u32[]{:S(2)}) async-start(bf16[64,52,128]{2,1,0:T(8,128)(2,1)} %copy.26), calls=%async_computation.1 | async-start | bytes 1835008 | tf_op jit(solution)/shard_map/all_to_all | solution.py:134
  82.7 2.0 %copy-start.8 = (bf16[64,1280]{1,0:T(8,128)(2,1)S(1)}, bf16[64,1280]{1,0:T(8,128)(2,1)}, u32[]{:S(2)}) copy-start(bf16[64,1280]{1,0:T(8,128)(2,1)} %copy-done.7) | copy-start | bytes 491524
  82.7 2.0 %copy-start.10 = (bf16[64,1280]{1,0:T(8,128)(2,1)S(1)}, bf16[64,1280]{1,0:T(8,128)(2,1)}, u32[]{:S(2)}) copy-start(bf16[64,1280]{1,0:T(8,128)(2,1)} %copy-done.9) | copy-start | bytes 491524
  86.3 5.1 %copy-start.13 = (s32[8,4]{0,1:T(4,128)S(1)}, s32[8,4]{0,1:T(4,128)}, u32[]{:S(2)}) copy-start(s32[8,4]{0,1:T(4,128)} %param.17) | copy-start | bytes 388
  86.4 5.8 %copy-start.14 = (s32[8]{0:T(128)S(1)}, s32[8]{0:T(128)}, u32[]{:S(2)}) copy-start(s32[8]{0:T(128)} %roles_ref.1) | copy-start | bytes 100
  88.1 44.6 %collective-permute-start.7 = (bf16[2,512,128]{2,1,0:T(8,128)(2,1)S(1)}, bf16[2,512,128]{2,1,0:T(8,128)(2,1)S(1)}, u32[]{:S(2)}, u32[]{:S(2)}) collective-permute-start(bf16[2,512,128]{2,1,0:T(8,128)(2,1)S(1)} %get-tuple-element.36), channel_id=1, source_target_pairs={{504,0},{0,8},{8,16},{16,24},{24,32},{32,40},{40,48},{48,56},{56,6... | collective-permute-start | bytes 786440 | tf_op jit(solution)/shard_map/ppermute | solution.py:25
  132.7 0.7 copy-start.2

commit v14 on v13

--- a/solution.py
+++ b/solution.py
@@ -149,14 +149,20 @@
     cols_s = columns[head_of_slot]
     owner = cols_s // blocks_dev
     local_block = cols_s - owner * blocks_dev
-    mine = (owner == my_seq)[:, :, None, None]
-    kv_blocks = jnp.stack([prefix_keys, prefix_values], 0).reshape(2, blocks_dev, BLK, HEAD_SIZE)
-    pieces = kv_blocks[:, local_block]
-    pieces = jnp.where(mine[None], pieces, jnp.zeros_like(pieces))
-    pieces = pieces.reshape(2, MAX_RETRIEVERS * VB * BLK, HEAD_SIZE)
-    sink = jnp.stack([prefix_keys[:SINK], prefix_values[:SINK]], 0)
-    sink = jnp.where(my_seq == 0, sink, jnp.zeros_like(sink))
-    both = jnp.concatenate([pieces, sink], 1)
+    mine = owner == my_seq
+
+    vrows = MAX_RETRIEVERS * VB * BLK
+    half_rows = vrows + SINK
+    r = jnp.arange(2 * half_rows, dtype=jnp.int32).reshape(seq_devices, -1)
+    which, rr = r // half_rows, r % half_rows
+    blk = jnp.minimum(rr // BLK, MAX_RETRIEVERS * VB - 1)
+    in_vert = rr < vrows
+    src = jnp.where(in_vert, local_block.reshape(-1)[blk] * BLK + rr % BLK, rr - vrows)
+    valid = jnp.where(in_vert, mine.reshape(-1)[blk], my_seq == 0)
+    table = jnp.concatenate([prefix_keys, prefix_values], 0)
+    flat_both = table[which * cache_rows + src]
+    flat_both = jnp.where(valid[:, :, None], flat_both, jnp.zeros_like(flat_both))
+    both_shape = (2, half_rows, HEAD_SIZE)
 
     head_devices = lax.axis_size("head")
     my_head = lax.axis_index("head")
@@ -172,7 +178,7 @@
     received = [columns_for(my_head)]
     for k in range(1, head_devices):
         received.append(shifted(columns_for((my_head + k) % head_devices), "head", k))
-    mine = scatter_parts(both, seq_devices)
+    mine = lax.all_to_all(flat_both, "seq", 0, 0, tiled=True)
     mine, received = lax.optimization_barrier((mine, received))
     by_shift = jnp.stack(received, 0)
     order = (my_head - jnp.arange(head_devices, dtype=jnp.int32)) % head_devices
@@ -182,7 +188,7 @@
     tail_cache = jnp.stack([prefix_keys[cache_rows - WIN:], prefix_values[cache_rows - WIN:]], 0)
     outgoing = jnp.where(my_seq == seq_devices - 1, tail_cache, kv_local)
     prev_kv = shifted(outgoing, "seq", 1)
-    side = gather_sums(mine, both.shape, seq_devices)
+    side = gather_sums(mine, both_shape, seq_devices)
 
     slot_l = jnp.where(is_ret, slot, 0).astype(jnp.int32)
     return attend(

time: 153 us -> 195 us (1.27)
  local copies, waits for them, and re-layouts: 14.7 us -> 56.1 us
    gather x2 -> x5, local copies, waits for them, and re-layouts: 0.76 us -> 44.6 us  [the longest x2 19 us: shards(): valid = jnp.where(in_vert, mine.reshape(-1)[blk], my_seq == 0)]
    ppermute x8, waiting for transfers between devices: 3.88 us -> 7.87 us  [shifted(): return lax.ppermute(block, axis, route)]
    all_to_all x1, waiting for transfers between devices: 23.1 us -> 19.6 us  [shards(): mine = lax.all_to_all(flat_both, 'seq', 0, 0, tiled=True)]
    unnamed x38 -> x42, local copies, waits for them, and re-layouts: 3.47 us -> 4.66 us
  transfers between devices with their start and end apart: 10 -> 10, of which waited for: 4 -> 5; matrix products, arithmetic and copies ran while one was open for 7% -> 6% of each run, Pallas kernels for 0% -> 0%
where the time goes in v14:
time: 195 us; the launch traced here: 193 us
  waiting for transfers between devices  64.4 us (33%)
  local copies, waits for them, and re-layouts  56.1 us (29%)
  starting transfers between devices  47.1 us (24%)
  Pallas kernels  17.4 us (9%)
  other arithmetic  6.86 us (4%)
    all_to_all x1, waiting for transfers between devices, gather_sums(): every = lax.all_to_all(total, 'seq', 0, 0, tiled=True)  36.9 us
    ppermute x8, starting transfers between devices, shifted(): return lax.ppermute(block, axis, route)  21.5 us
    all_to_all x1, waiting for transfers between devices, shards(): mine = lax.all_to_all(flat_both, 'seq', 0, 0, tiled=True)  19.6 us
    gather x2, local copies, waits for them, and re-layouts, shards(): valid = jnp.where(in_vert, mine.reshape(-1)[blk], my_seq == 0)  19 us
    gather x1, local copies, waits for them, and re-layouts, shards(): local_block.reshape(-1)[blk] * BLK + rr % BLK  18.9 us
    all_to_all x1, starting transfers between devices, shards(): mine = lax.all_to_all(flat_both, 'seq', 0, 0, tiled=True)  18.9 us
    pallas_call x1, Pallas kernels, attend(): pl.pallas_call(attend_kernel, grid_spec=grid_spec, out_shape=jax.ShapeDty...  17.4 us
    ppermute x8, waiting for transfers between devices, shifted(): return lax.ppermute(block, axis, route)  7.87 us
  transfers between devices with their start and end apart: 10, of which 5 were waited for; matrix products, arithmetic and copies ran while one was open for 6% of the time, Pallas kernels for 0%

profile of v14, /device:TPU:6, one launch (start us, length us, event | category | flops | bytes accessed | tf_op | source)
XLA Modules:
  0.0 192.9 jit_solution(11781337492308868913)
XLA Ops:
  0.0 0.1 compare_select_fusion.1
  0.1 0.7 broadcast_compare_fusion.1
  0.7 0.2 reduce-window.7
  0.9 0.6 iota_reduce_fusion
  1.6 0.6 gather_fusion
  2.1 0.1 gather.18
  2.2 0.1 reshape.310
  2.4 0.0 copy-start.2
  2.4 0.0 copy-start.3
  2.4 18.9 %gather_fusion.2 = s32[3328]{0:T(1024)S(1)} fusion(s32[24]{0:T(128)S(1)} %multiply_subtract_fusion, s32[4096]{0:T(1024)S(1)} %pad_clamp_fusion.1), kind=kCustom, calls=%fused_computation.2 | custom fusion | bytes 39936 | tf_op jit(solution)/shard_map/gather | solution.py:160
  21.3 0.1 mul.91
  21.4 0.1 compare_select_fusion
  21.5 0.1 reshape.326
  21.7 0.1 pad_maximum_fusion
  21.7 6.5 %gather_fusion.3 = bf16[3328,128]{1,0:T(8,128)(2,1)S(1)} fusion(bf16[4096,128]{1,0:T(8,128)(2,1)S(1)} %pad_maximum_fusion, s32[4096]{0:T(1024)S(1)} %pad_clamp_fusion), kind=kCustom, calls=%fused_computation.3 | custom fusion | bytes 1717248 | tf_op jit(solution)/shard_map/gather | solution.py:163
  28.3 0.1 reshape.325
  28.4 18.9 %gather_fusion.1 = pred[3328]{0:T(1024)(128)(4,1)S(1)} fusion(pred[24]{0:T(512)(128)(4,1)S(1)} %get-tuple-element.25, s32[4096]{0:T(1024)S(1)} %pad_clamp_fusion.1), kind=kCustom, calls=%fused_computation.1 | custom fusion | bytes 19968 | tf_op jit(solution)/shard_map/gather | solution.py:161
  47.3 0.1 reshape.309
  47.5 1.4 broadcast_select_fusion
  48.9 18.9 %all-to-all-start = ((bf16[64,52,128]{2,1,0:T(8,128)(2,1)}), bf16[64,52,128]{2,1,0:T(8,128)(2,1)S(1)}, u32[]{:S(2)}, u32[]{:S(2)}) async-start(bf16[64,52,128]{2,1,0:T(8,128)(2,1)} %broadcast_select_fusion), calls=%async_computation | async-start | bytes 1835008 | tf_op jit(solution)/shard_map/all_to_all | solution.py:181
  68.0 0.1 constant_dynamic-slice_fusion
  68.1 0.0 copy-done.1
  68.1 0.1 constant_dynamic-slice_fusion.2
  68.2 4.0 %collective-permute-start.4 = (bf16[64,1280]{1,0:T(8,128)(2,1)S(1)}, bf16[64,1280]{1,0:T(8,128)(2,1)S(1)}, u32[]{:S(2)}, u32[]{:S(2)}) collective-permute-start(bf16[64,1280]{1,0:T(8,128)(2,1)S(1)} %pad_maximum_fusion.7), channel_id=1, source_target_pairs={{3,0},{4,1},{5,2},{6,3},{7,4},{0,5},{1,6},{2,7},{11,8},{12,9},{13,... | collective-permute-start | bytes 491528 | tf_op jit(solution)/shard_map/ppermute | solution.py:25
  72.2 3.0 %collective-permute-start.5 = (bf16[64,1280]{1,0:T(8,128)(2,1)S(1)}, bf16[64,1280]{1,0:T(8,128)(2,1)S(1)}, u32[]{:S(2)}, u32[]{:S(2)}) collective-permute-start(bf16[64,1280]{1,0:T(8,128)(2,1)S(1)} %pad_maximum_fusion.8), channel_id=1, source_target_pairs={{2,0},{3,1},{4,2},{5,3},{6,4},{7,5},{0,6},{1,7},{10,8},{11,9},{12,... | collective-permute-start | bytes 491528 | tf_op jit(solution)/shard_map/ppermute | solution.py:25
  75.2 0.5 collective-permute-start.6
  75.8 4.8 %collective-permute-start.3 = (bf16[64,1280]{1,0:T(8,128)(2,1)S(1)}, bf16[64,1280]{1,0:T(8,128)(2,1)S(1)}, u32[]{:S(2)}, u32[]{:S(2)}) collective-permute-start(bf16[64,1280]{1,0:T(8,128)(2,1)S(1)} %pad_maximum_fusion.6), channel_id=1, source_target_pairs={{4,0},{5,1},{6,2},{7,3},{0,4},{1,5},{2,6},{3,7},{12,8},{13,9},{14,... | collective-permute-start | bytes 491528 | tf_op jit(solution)/shard_map/ppermute | solution.py:25
  80.6 1.9 collective-permute-start.2
  82.5 0.7 pad_maximum_fusion.4
  83.2 0.7 pad_maximum_fusion.3
  83.9 0.7 slice_bitcast_fusion.2
  84.6 0.0 collective-permute-done.4
  84.6 1.9 collective-permute-start.1
  86.6 0.0 collective-permute-done.5
  86.6 2.0 %collective-permute-start = (bf16[64,1280]{1,0:T(8,128)(2,1)}, bf16[64,1280]{1,0:T(8,128)(2,1)S(1)}, u32[]{:S(2)}, u32[]{:S(2)}) collective-permute-start(bf16[64,1280]{1,0:T(8,128)(2,1)} %pad_maximum_fusion.3), channel_id=1, source_target_pairs={{7,0},{0,1},{1,2},{2,3},{3,4},{4,5},{5,6},{6,7},{15,8},{8,9},{9,10... | collective-permute-start | bytes 491528 | tf_op jit(solution)/shard_map/ppermute | solution.py:25
  88.7 0.0 collective-permute-done.6
  88.7 0.0 collective-permute-done.3
  88.7 0.0 copy-start.9
  88.7 0.7 collective-permute-done.2
  89.4 5.7 %collective-permute-done.1 = bf16[64,1280]{1,0:T(8,128)(2,1)S(1)} collective-permute-done((bf16[64,1280]{1,0:T(8,128)(2,1)}, bf16[64,1280]{1,0:T(8,128)(2,1)S(1)}, u32[]{:S(2)}, u32[]{:S(2)}) %collective-permute-start.1) | collective-permute-done | bytes 163872 | tf_op jit(solution)/shard_map/ppermute | solution.py:25
  95.0 1.5 collective-permute-done
  96.6 19.6 %all-to-all-done = bf16[64,52,128]{2,1,0:T(8,128)(2,1)S(1)} async-done(((bf16[64,52,128]{2,1,0:T(8,128)(2,1)}), bf16[64,52,128]{2,1,0:T(8,128)(2,1)S(1)}, u32[]{:S(2)}, u32[]{:S(2)}) %all-to-all-start) | async-done | bytes 852000 | tf_op jit(solution)/shard_map/all_to_all | solution.py:181
  116.2 0.4 convolution_convert_fusion
  116.6 1.5 copy.21
  118.1 0.0 copy-done.7
  118.1 6.6 %all-to-all-start.1 = ((bf16[64,52,128]{2,1,0:T(8,128)(2,1)}), bf16[64,52,128]{2,1,0:T(8,128)(2,1)S(1)}, u32[]{:S(2)}, u32[]{:S(2)}) async-start(bf16[64,52,128]{2,1,0:T(8,128)(2,1)} %copy.21), calls=%async_computation.1 | async-start | bytes 1835008 | tf_op jit(solution)/shard_map/all_to_all | solution.py:134
  124.8 1.0 bitcast_dynamic-update-slice_fusion.6
  125.8 0.9 bitcast_dynamic-update-slice_fusion.5
  126.7 0.9 bitcast_dynamic-update-slice_fusion.4
  127.6 0.9 bitcast_dynamic-update-slice_fusion.3
  128.6 0.6 gather_fusion.4
  129.3 0.0 copy-start.15
  129.3 0.0 copy-start.16
  129.3 1.7 pad_maximum_fusion.1
  131.0 3.4 %collective-permute-start.7 = (bf16[2,512,128]{2,1,0:T(8,128)(2,1)S(1)}, bf16[2,512,128]{2,1,0:T(8,128)(2,1)S(1)}, u32[]{:S(2)}, u32[]{:S(2)}) collective-permute-start(bf16[2,512,128]{2,1,0:T(8,128)(2,1)S(1)} %get-tuple-element.38), channel_id=1, source_target_pairs={{504,0},{0,8},{8,16},{16,24},{24,32},{32,40},{40,48},{48,56},{56,6... | collective-permute-start | bytes 786440 | tf_op jit(solution)/shard_map/ppermute | solution.py:25
  134.4 0.1 copy.19
  134.5 0.6 reshape.290.diag_ref
  135.1 0.5 broadcast_select_fusion.1.slot_ref
  135.7 1.1 slice.30.q_ref
  136.8 36.9 %all-to-all-done.1 = bf16[64,52,128]{2,1,0:T(8,128)(2,1)S(1)} async-done(((bf16[64,52,128]{2,1,0:T(8,128)(2,1)}), bf16[64,52,128]{2,1,0:T(8,128)(2,1)S(1)}, u32[]{:S(2)}, u32[]{:S(2)}) %all-to-all-start.1) | async-done | bytes 852000 | tf_op jit(solution)/shard_map/all_to_all | solution.py:134
  173.7 1.1 reshape.298.vk_ref.vv_ref.sk_ref.sv_ref
  174.8 0.0 collective-permute-done.7.prev_ref
  174.8 0.7 copy-done.4
  175.5 17.4 %shard_map.91 = bf16[512,1024]{1,0:T(8,128)(2,1)} custom-call(s32[8]{0:T(128)} %roles_ref.1, s32[8]{0:T(128)} %broadcast_select_fusion.1.slot_ref, s32[8]{0:T(128)} %count_ref.1, s32[32]{0:T(128)} %reshape.290.diag_ref, bf16[512,1024]{1,0:T(8,128)(2,1)} %slice.30.q_ref, bf16[2,512,128]{2,1,0:T(8,128)(2,1)} %copy-done.4, ...), custom_call_target="tpu_custom_call" | custom-call | tf_op jit(solution)/shard_map/pallas_call | solution.py:119
  (48 shorter events, 0.3 us)
Async XLA Ops:
  0.0 1.6 copy-start
  2.4 19.3 %copy-start.2 = (bf16[2048,128]{1,0:T(8,128)(2,1)S(1)}, bf16[2048,128]{1,0:T(8,128)(2,1)}, u32[]{:S(2)}) copy-start(bf16[2048,128]{1,0:T(8,128)(2,1)} %param.13) | copy-start | bytes 1572868
  2.4 19.3 %copy-start.3 = (bf16[2048,128]{1,0:T(8,128)(2,1)S(1)}, bf16[2048,128]{1,0:T(8,128)(2,1)}, u32[]{:S(2)}) copy-start(bf16[2048,128]{1,0:T(8,128)(2,1)} %param.12) | copy-start | bytes 1572868
  48.9 19.1 %copy-start.13 = (bf16[64,1024]{1,0:T(8,128)(2,1)S(1)}, bf16[64,1024]{1,0:T(8,128)(2,1)}, u32[]{:S(2)}) copy-start(bf16[64,1024]{1,0:T(8,128)(2,1)} %param.11) | copy-start | bytes 393220
  48.9 19.1 %copy-start.14 = (bf16[64,1024]{1,0:T(8,128)(2,1)S(1)}, bf16[64,1024]{1,0:T(8,128)(2,1)}, u32[]{:S(2)}) copy-start(bf16[64,1024]{1,0:T(8,128)(2,1)} %param.10) | copy-start | bytes 393220
  48.9 19.2 %copy-start.1 = (bf16[64,8192]{1,0:T(8,128)(2,1)S(1)}, bf16[64,8192]{1,0:T(8,128)(2,1)}, u32[]{:S(2)}) copy-start(bf16[64,8192]{1,0:T(8,128)(2,1)} %param.9) | copy-start | bytes 3145732
  48.9 67.3 %all-to-all-start = ((bf16[64,52,128]{2,1,0:T(8,128)(2,1)}), bf16[64,52,128]{2,1,0:T(8,128)(2,1)S(1)}, u32[]{:S(2)}, u32[]{:S(2)}) async-start(bf16[64,52,128]{2,1,0:T(8,128)(2,1)} %broadcast_select_fusion), calls=%async_computation | async-start | bytes 1835008 | tf_op jit(solution)/shard_map/all_to_all | solution.py:181
  68.2 16.4 %collective-permute-start.4 = (bf16[64,1280]{1,0:T(8,128)(2,1)S(1)}, bf16[64,1280]{1,0:T(8,128)(2,1)S(1)}, u32[]{:S(2)}, u32[]{:S(2)}) collective-permute-start(bf16[64,1280]{1,0:T(8,128)(2,1)S(1)} %pad_maximum_fusion.7), channel_id=1, source_target_pairs={{3,0},{4,1},{5,2},{6,3},{7,4},{0,5},{1,6},{2,7},{11,8},{12,9},{13,... | collective-permute-start | bytes 491528 | tf_op jit(solution)/shard_map/ppermute | solution.py:25
  72.2 14.3 %collective-permute-start.5 = (bf16[64,1280]{1,0:T(8,128)(2,1)S(1)}, bf16[64,1280]{1,0:T(8,128)(2,1)S(1)}, u32[]{:S(2)}, u32[]{:S(2)}) collective-permute-start(bf16[64,1280]{1,0:T(8,128)(2,1)S(1)} %pad_maximum_fusion.8), channel_id=1, source_target_pairs={{2,0},{3,1},{4,2},{5,3},{6,4},{7,5},{0,6},{1,7},{10,8},{11,9},{12,... | collective-permute-start | bytes 491528 | tf_op jit(solution)/shard_map/ppermute | solution.py:25
  75.2 13.4 %collective-permute-start.6 = (bf16[64,1280]{1,0:T(8,128)(2,1)S(1)}, bf16[64,1280]{1,0:T(8,128)(2,1)S(1)}, u32[]{:S(2)}, u32[]{:S(2)}) collective-permute-start(bf16[64,1280]{1,0:T(8,128)(2,1)S(1)} %pad_maximum_fusion.9), channel_id=1, source_target_pairs={{1,0},{2,1},{3,2},{4,3},{5,4},{6,5},{7,6},{0,7},{9,8},{10,9},{11,1... | collective-permute-start | bytes 491528 | tf_op jit(solution)/shard_map/ppermute | solution.py:25
  75.8 12.9 %collective-permute-start.3 = (bf16[64,1280]{1,0:T(8,128)(2,1)S(1)}, bf16[64,1280]{1,0:T(8,128)(2,1)S(1)}, u32[]{:S(2)}, u32[]{:S(2)}) collective-permute-start(bf16[64,1280]{1,0:T(8,128)(2,1)S(1)} %pad_maximum_fusion.6), channel_id=1, source_target_pairs={{4,0},{5,1},{6,2},{7,3},{0,4},{1,5},{2,6},{3,7},{12,8},{13,9},{14,... | collective-permute-start | bytes 491528 | tf_op jit(solution)/shard_map/ppermute | solution.py:25
  80.6 8.8 %collective-permute-start.2 = (bf16[64,1280]{1,0:T(8,128)(2,1)S(1)}, bf16[64,1280]{1,0:T(8,128)(2,1)S(1)}, u32[]{:S(2)}, u32[]{:S(2)}) collective-permute-start(bf16[64,1280]{1,0:T(8,128)(2,1)S(1)} %pad_maximum_fusion.5), channel_id=1, source_target_pairs={{5,0},{6,1},{7,2},{0,3},{1,4},{2,5},{3,6},{4,7},{13,8},{14,9},{15,... | collective-permute-start | bytes 491528 | tf_op jit(solution)/shard_map/ppermute | solution.py:25
  84.6 10.4 %collective-permute-start.1 = (bf16[64,1280]{1,0:T(8,128)(2,1)}, bf16[64,1280]{1,0:T(8,128)(2,1)S(1)}, u32[]{:S(2)}, u32[]{:S(2)}) collective-permute-start(bf16[64,1280]{1,0:T(8,128)(2,1)} %pad_maximum_fusion.4), channel_id=1, source_target_pairs={{6,0},{7,1},{0,2},{1,3},{2,4},{3,5},{4,6},{5,7},{14,8},{15,9},{8,1... | collective-permute-start | bytes 491528 | tf_op jit(solution)/shard_map/ppermute | solution.py:25
  86.6 31.5 %copy-start.5 = (bf16[64,1280]{1,0:T(8,128)(2,1)}, bf16[64,1280]{1,0:T(8,128)(2,1)S(1)}, u32[]{:S(2)}) copy-start(bf16[64,1280]{1,0:T(8,128)(2,1)S(1)} %collective-permute-done.5) | copy-start | bytes 491524
  86.6 10.0 %collective-permute-start = (bf16[64,1280]{1,0:T(8,128)(2,1)}, bf16[64,1280]{1,0:T(8,128)(2,1)S(1)}, u32[]{:S(2)}, u32[]{:S(2)}) collective-permute-start(bf16[64,1280]{1,0:T(8,128)(2,1)} %pad_maximum_fusion.3), channel_id=1, source_target_pairs={{7,0},{0,1},{1,2},{2,3},{3,4},{4,5},{5,6},{6,7},{15,8},{8,9},{9,10... | collective-permute-start | bytes 491528 | tf_op jit(solution)/shard_map/ppermute | solution.py:25
  88.7 29.4 %copy-start.7 = (bf16[64,1280]{1,0:T(8,128)(2,1)}, bf16[64,1280]{1,0:T(8,128)(2,1)S(1)}, u32[]{:S(2)}) copy-start(bf16[64,1280]{1,0:T(8,128)(2,1)S(1)} %collective-permute-done.6) | copy-start | bytes 491524
  88.7 29.4 %copy-start.9 = (bf16[64,1280]{1,0:T(8,128)(2,1)}, bf16[64,1280]{1,0:T(8,128)(2,1)S(1)}, u32[]{:S(2)}) copy-start(bf16[64,1280]{1,0:T(8,128)(2,1)S(1)} %collective-permute-done.3) | copy-start | bytes 491524
  89.4 28.7 %copy-start.10 = (bf16[64,1280]{1,0:T(8,128)(2,1)}, bf16[64,1280]{1,0:T(8,128)(2,1)S(1)}, u32[]{:S(2)}) copy-start(bf16[64,1280]{1,0:T(8,128)(2,1)S(1)} %collective-permute-done.2) | copy-start | bytes 491524
  95.0 23.0 %copy-start.11 = (bf16[64,1280]{1,0:T(8,128)(2,1)}, bf16[64,1280]{1,0:T(8,128)(2,1)S(1)}, u32[]{:S(2)}) copy-start(bf16[64,1280]{1,0:T(8,128)(2,1)S(1)} %collective-permute-done.1) | copy-start | bytes 491524
  96.6 21.5 %copy-start.12 = (bf16[64,1280]{1,0:T(8,128)(2,1)}, bf16[64,1280]{1,0:T(8,128)(2,1)S(1)}, u32[]{:S(2)}) copy-start(bf16[64,1280]{1,0:T(8,128)(2,1)S(1)} %collective-permute-done) | copy-start | bytes 491524
  118.1 55.6 %all-to-all-start.1 = ((bf16[64,52,128]{2,1,0:T(8,128)(2,1)}), bf16[64,52,128]{2,1,0:T(8,128)(2,1)S(1)}, u32[]{:S(2)}, u32[]{:S(2)}) async-start(bf16[64,52,128]{2,1,0:T(8,128)(2,1)} %copy.21), calls=%async_computation.1 | async-start | bytes 1835008 | tf_op jit(solution)/shard_map/all_to_all | solution.py:134
  124.8 3.8 %copy-start.6 = (bf16[64,1280]{1,0:T(8,128)(2,1)S(1)}, bf16[64,1280]{1,0:T(8,128)(2,1)}, u32[]{:S(2)}) copy-start(bf16[64,1280]{1,0:T(8,128)(2,1)} %copy-done.5) | copy-start | bytes 491524
  124.8 3.8 %copy-start.8 = (bf16[64,1280]{1,0:T(8,128)(2,1)S(1)}, bf16[64,1280]{1,0:T(8,128)(2,1)}, u32[]{:S(2)}) copy-start(bf16[64,1280]{1,0:T(8,128)(2,1)} %copy-done.7) | copy-start | bytes 491524
  129.3 5.1 %copy-start.15 = (s32[8,4]{0,1:T(4,128)S(1)}, s32[8,4]{0,1:T(4,128)}, u32[]{:S(2)}) copy-start(s32[8,4]{0,1:T(4,128)} %param.17) | copy-start | bytes 388
  129.3 5.9 %copy-start.16 = (s32[8]{0:T(128)S(1)}, s32[8]{0:T(128)}, u32[]{:S(2)}) copy-start(s32[8]{0:T(128)} %roles_ref.1) | copy-start | bytes 100
  131.0 43.7 %collective-permute-start.7 = (bf16[2,512,128]{2,1,0:T(8,128)(2,1)S(1)}, bf16[2,512,128]{2,1,0:T(8,128)(2,1)S(1)}, u32[]{:S(2)}, u32[]{:S(2)}) collective-permute-start(bf16[2,512,128]{2,1,0:T(8,128)(2,1)S(1)} %get-tuple-element.38), channel_id=1, source_target_pairs={{504,0},{0,8},{8,16},{16,24},{24,32},{32,40},{40,48},{48,56},{56,6... | collective-permute-start | bytes 786440 | tf_op jit(solution)/shard_map/ppermute | solution.py:25
  174.8 0.7 copy-start.4

commit v15 on v13

--- a/solution.py
+++ b/solution.py
@@ -149,14 +149,13 @@
     cols_s = columns[head_of_slot]
     owner = cols_s // blocks_dev
     local_block = cols_s - owner * blocks_dev
-    mine = (owner == my_seq)[:, :, None, None]
+    sink_blocks = jnp.arange(SINK // BLK, dtype=jnp.int32)
+    picks = jnp.concatenate([local_block.reshape(-1), sink_blocks])
+    held = jnp.concatenate([(owner == my_seq).reshape(-1), jnp.broadcast_to(my_seq == 0, sink_blocks.shape)])
     kv_blocks = jnp.stack([prefix_keys, prefix_values], 0).reshape(2, blocks_dev, BLK, HEAD_SIZE)
-    pieces = kv_blocks[:, local_block]
-    pieces = jnp.where(mine[None], pieces, jnp.zeros_like(pieces))
-    pieces = pieces.reshape(2, MAX_RETRIEVERS * VB * BLK, HEAD_SIZE)
-    sink = jnp.stack([prefix_keys[:SINK], prefix_values[:SINK]], 0)
-    sink = jnp.where(my_seq == 0, sink, jnp.zeros_like(sink))
-    both = jnp.concatenate([pieces, sink], 1)
+    pieces = kv_blocks[:, picks]
+    pieces = jnp.where(held[None, :, None, None], pieces, jnp.zeros_like(pieces))
+    both = pieces.reshape(2, -1, HEAD_SIZE)
 
     head_devices = lax.axis_size("head")
     my_head = lax.axis_index("head")

time: 153 us -> 152 us (level)
  local copies, waits for them, and re-layouts: 14.7 us -> 11.5 us
  waiting for transfers between devices: 64.7 us -> 66.7 us
    all_to_all x1, waiting for transfers between devices: 23.1 us -> 19.1 us  [scatter_parts(): return lax.all_to_all(flat, 'seq', 0, 0, tiled=True)]
    ppermute x8, waiting for transfers between devices: 3.88 us -> 7.84 us  [shifted(): return lax.ppermute(block, axis, route)]
    all_to_all x1, waiting for transfers between devices: 37.7 us -> 39.7 us  [gather_sums(): every = lax.all_to_all(total, 'seq', 0, 0, tiled=True)]
    unnamed x38 -> x46, local copies, waits for them, and re-layouts: 3.47 us -> 2.92 us
  transfers between devices with their start and end apart: 10 -> 10, of which waited for: 4 -> 5; matrix products, arithmetic and copies ran while one was open for 7% -> 5% of each run, Pallas kernels for 0% -> 0%
where the time goes in v15:
time: 152 us; the launch traced here: 150 us
  waiting for transfers between devices  66.7 us (44%)
  starting transfers between devices  47 us (31%)
  Pallas kernels  17.4 us (11%)
  local copies, waits for them, and re-layouts  11.5 us (8%)
  other arithmetic  6.64 us (4%)
    all_to_all x1, waiting for transfers between devices, gather_sums(): every = lax.all_to_all(total, 'seq', 0, 0, tiled=True)  39.7 us
    ppermute x8, starting transfers between devices, shifted(): return lax.ppermute(block, axis, route)  21.3 us
    all_to_all x1, waiting for transfers between devices, scatter_parts(): return lax.all_to_all(flat, 'seq', 0, 0, tiled=True)  19.1 us
    all_to_all x1, starting transfers between devices, scatter_parts(): return lax.all_to_all(flat, 'seq', 0, 0, tiled=True)  18.9 us
    pallas_call x1, Pallas kernels, attend(): pl.pallas_call(attend_kernel, grid_spec=grid_spec, out_shape=jax.ShapeDty...  17.4 us
    ppermute x8, waiting for transfers between devices, shifted(): return lax.ppermute(block, axis, route)  7.84 us
    all_to_all x1, starting transfers between devices, gather_sums(): every = lax.all_to_all(total, 'seq', 0, 0, tiled=True)  6.78 us
  transfers between devices with their start and end apart: 10, of which 5 were waited for; matrix products, arithmetic and copies ran while one was open for 5% of the time, Pallas kernels for 0%

profile of v15, /device:TPU:6, one launch (start us, length us, event | category | flops | bytes accessed | tf_op | source)
XLA Modules:
  0.0 150.3 jit_solution(6167023791918852570)
XLA Ops:
  0.0 0.0 copy-start
  0.0 0.7 broadcast_compare_fusion.1
  0.7 0.2 reduce-window.7
  0.9 0.6 iota_reduce_fusion
  1.5 0.0 copy-done
  1.5 0.6 gather_fusion
  2.1 0.1 gather.14
  2.2 0.1 fusion.4
  2.3 1.3 pad_maximum_fusion
  3.6 0.7 gather_fusion.1
  4.3 0.1 copy.24
  4.4 0.1 gather.16
  4.6 0.1 broadcast_in_dim.34
  4.6 0.1 broadcast_in_dim.35
  4.8 1.4 broadcast_select_fusion
  6.2 18.9 %all-to-all-start = ((bf16[64,52,128]{2,1,0:T(8,128)(2,1)}), bf16[64,52,128]{2,1,0:T(8,128)(2,1)S(1)}, u32[]{:S(2)}, u32[]{:S(2)}) async-start(bf16[64,52,128]{2,1,0:T(8,128)(2,1)} %broadcast_select_fusion), calls=%async_computation | async-start | bytes 1835008 | tf_op jit(solution)/shard_map/all_to_all | solution.py:128
  25.2 0.0 copy-done.15
  25.3 0.0 copy-done.16
  25.3 0.1 constant_dynamic-slice_fusion
  25.4 0.0 copy-done.1
  25.4 0.1 constant_dynamic-slice_fusion.2
  25.5 2.4 %collective-permute-start.2 = (bf16[64,1280]{1,0:T(8,128)(2,1)S(1)}, bf16[64,1280]{1,0:T(8,128)(2,1)S(1)}, u32[]{:S(2)}, u32[]{:S(2)}) collective-permute-start(bf16[64,1280]{1,0:T(8,128)(2,1)S(1)} %pad_maximum_fusion.5), channel_id=1, source_target_pairs={{5,0},{6,1},{7,2},{0,3},{1,4},{2,5},{3,6},{4,7},{13,8},{14,9},{15,... | collective-permute-start | bytes 491528 | tf_op jit(solution)/shard_map/ppermute | solution.py:25
  27.9 4.8 %collective-permute-start.3 = (bf16[64,1280]{1,0:T(8,128)(2,1)S(1)}, bf16[64,1280]{1,0:T(8,128)(2,1)S(1)}, u32[]{:S(2)}, u32[]{:S(2)}) collective-permute-start(bf16[64,1280]{1,0:T(8,128)(2,1)S(1)} %pad_maximum_fusion.6), channel_id=1, source_target_pairs={{4,0},{5,1},{6,2},{7,3},{0,4},{1,5},{2,6},{3,7},{12,8},{13,9},{14,... | collective-permute-start | bytes 491528 | tf_op jit(solution)/shard_map/ppermute | solution.py:25
  32.7 4.7 %collective-permute-start.4 = (bf16[64,1280]{1,0:T(8,128)(2,1)S(1)}, bf16[64,1280]{1,0:T(8,128)(2,1)S(1)}, u32[]{:S(2)}, u32[]{:S(2)}) collective-permute-start(bf16[64,1280]{1,0:T(8,128)(2,1)S(1)} %pad_maximum_fusion.7), channel_id=1, source_target_pairs={{3,0},{4,1},{5,2},{6,3},{7,4},{0,5},{1,6},{2,7},{11,8},{12,9},{13,... | collective-permute-start | bytes 491528 | tf_op jit(solution)/shard_map/ppermute | solution.py:25
  37.5 3.0 %collective-permute-start.5 = (bf16[64,1280]{1,0:T(8,128)(2,1)S(1)}, bf16[64,1280]{1,0:T(8,128)(2,1)S(1)}, u32[]{:S(2)}, u32[]{:S(2)}) collective-permute-start(bf16[64,1280]{1,0:T(8,128)(2,1)S(1)} %pad_maximum_fusion.8), channel_id=1, source_target_pairs={{2,0},{3,1},{4,2},{5,3},{6,4},{7,5},{0,6},{1,7},{10,8},{11,9},{12,... | collective-permute-start | bytes 491528 | tf_op jit(solution)/shard_map/ppermute | solution.py:25
  40.5 0.0 collective-permute-start.6
  40.5 1.7 %slice_bitcast_fusion.2 = (bf16[1,512,128]{2,1,0:T(8,128)(2,1)}, bf16[1,512,128]{2,1,0:T(8,128)(2,1)}) fusion(bf16[2048,128]{1,0:T(8,128)(2,1)} %param.13, bf16[2048,128]{1,0:T(8,128)(2,1)} %param.12), kind=kLoop, calls=%fused_computation.27 | loop fusion | bytes 524288 | tf_op jit(solution)/shard_map/stack | solution.py:181
  42.2 0.0 collective-permute-done.2
  42.3 2.9 %collective-permute-start.1 = (bf16[64,1280]{1,0:T(8,128)(2,1)S(1)}, bf16[64,1280]{1,0:T(8,128)(2,1)S(1)}, u32[]{:S(2)}, u32[]{:S(2)}) collective-permute-start(bf16[64,1280]{1,0:T(8,128)(2,1)S(1)} %pad_maximum_fusion.4), channel_id=1, source_target_pairs={{6,0},{7,1},{0,2},{1,3},{2,4},{3,5},{4,6},{5,7},{14,8},{15,9},{8,1... | collective-permute-start | bytes 491528 | tf_op jit(solution)/shard_map/ppermute | solution.py:25
  45.1 0.0 collective-permute-done.3
  45.2 0.0 copy-start.3
  45.2 0.2 collective-permute-start
  45.4 0.4 copy-done.3
  45.8 0.0 collective-permute-done.4
  45.8 0.0 copy-start.5
  45.9 0.0 collective-permute-done.5
  45.9 0.0 copy-start.7
  45.9 0.2 collective-permute-done.6
  46.1 6.3 %collective-permute-done.1 = bf16[64,1280]{1,0:T(8,128)(2,1)S(1)} collective-permute-done((bf16[64,1280]{1,0:T(8,128)(2,1)S(1)}, bf16[64,1280]{1,0:T(8,128)(2,1)S(1)}, u32[]{:S(2)}, u32[]{:S(2)}) %collective-permute-start.1) | collective-permute-done | bytes 163872 | tf_op jit(solution)/shard_map/ppermute | solution.py:25
  52.4 1.3 collective-permute-done
  53.7 0.6 copy-done.13
  54.4 19.1 %all-to-all-done = bf16[64,52,128]{2,1,0:T(8,128)(2,1)S(1)} async-done(((bf16[64,52,128]{2,1,0:T(8,128)(2,1)}), bf16[64,52,128]{2,1,0:T(8,128)(2,1)S(1)}, u32[]{:S(2)}, u32[]{:S(2)}) %all-to-all-start) | async-done | bytes 852000 | tf_op jit(solution)/shard_map/all_to_all | solution.py:128
  73.5 0.4 convolution_convert_fusion
  73.9 1.5 copy.26
  75.4 0.0 copy-done.7
  75.4 6.8 %all-to-all-start.1 = ((bf16[64,52,128]{2,1,0:T(8,128)(2,1)}), bf16[64,52,128]{2,1,0:T(8,128)(2,1)S(1)}, u32[]{:S(2)}, u32[]{:S(2)}) async-start(bf16[64,52,128]{2,1,0:T(8,128)(2,1)} %copy.26), calls=%async_computation.1 | async-start | bytes 1835008 | tf_op jit(solution)/shard_map/all_to_all | solution.py:134
  82.3 0.8 copy-done.6
  83.1 0.1 copy-done.8
  83.2 0.1 copy-done.10
  83.3 0.6 gather_fusion.2
  83.9 0.0 copy-start.17
  83.9 0.0 copy-start.18
  84.0 1.7 %pad_maximum_fusion.1 = (bf16[2,512,128]{2,1,0:T(8,128)(2,1)}, bf16[2,512,128]{2,1,0:T(8,128)(2,1)S(1)}) fusion(bf16[1,512,128]{2,1,0:T(8,128)(2,1)S(1)} %get-tuple-element.28, bf16[1,512,128]{2,1,0:T(8,128)(2,1)S(1)} %get-tuple-element.27, bf16[1,512,128]{2,1,0:T(8,128)(2,1)} %get-tuple-element.67, bf16[1,512,128]{2,1,0:T(8,128)(2,1)} %get-tuple-element.68, ...), kind=kLoop, calls=%fused_computation.8 | loop fusion | flops 393216 | bytes 1048577 | tf_op jit(solution)/shard_map/stack | solution.py:180
  85.7 3.4 %collective-permute-start.7 = (bf16[2,512,128]{2,1,0:T(8,128)(2,1)S(1)}, bf16[2,512,128]{2,1,0:T(8,128)(2,1)S(1)}, u32[]{:S(2)}, u32[]{:S(2)}) collective-permute-start(bf16[2,512,128]{2,1,0:T(8,128)(2,1)S(1)} %get-tuple-element.38), channel_id=1, source_target_pairs={{504,0},{0,8},{8,16},{16,24},{24,32},{32,40},{40,48},{48,56},{56,6... | collective-permute-start | bytes 786440 | tf_op jit(solution)/shard_map/ppermute | solution.py:25
  89.1 0.1 copy.23
  89.2 0.6 reshape.153.diag_ref
  89.8 0.0 copy-done.18
  89.8 0.5 broadcast_select_fusion.1.slot_ref
  90.2 1.1 slice.26.q_ref
  91.4 39.7 %all-to-all-done.1 = bf16[64,52,128]{2,1,0:T(8,128)(2,1)S(1)} async-done(((bf16[64,52,128]{2,1,0:T(8,128)(2,1)}), bf16[64,52,128]{2,1,0:T(8,128)(2,1)S(1)}, u32[]{:S(2)}, u32[]{:S(2)}) %all-to-all-start.1) | async-done | bytes 852000 | tf_op jit(solution)/shard_map/all_to_all | solution.py:134
  131.1 1.1 reshape.155.vk_ref.vv_ref.sk_ref.sv_ref
  132.2 0.0 collective-permute-done.7.prev_ref
  132.2 0.7 copy-done.2
  132.9 17.4 %shard_map.91 = bf16[512,1024]{1,0:T(8,128)(2,1)} custom-call(s32[8]{0:T(128)} %roles_ref.1, s32[8]{0:T(128)} %broadcast_select_fusion.1.slot_ref, s32[8]{0:T(128)} %count_ref.1, s32[32]{0:T(128)} %reshape.153.diag_ref, bf16[512,1024]{1,0:T(8,128)(2,1)} %slice.26.q_ref, bf16[2,512,128]{2,1,0:T(8,128)(2,1)} %copy-done.2, ...), custom_call_target="tpu_custom_call" | custom-call | tf_op jit(solution)/shard_map/pallas_call | solution.py:119
  (46 shorter events, 0.3 us)
Async XLA Ops:
  0.0 1.5 %copy-start = (s32[8,6]{1,0:T(8,128)S(1)}, s32[8,6]{1,0:T(8,128)}, u32[]{:S(2)}) copy-start(s32[8,6]{1,0:T(8,128)} %param.15) | copy-start | bytes 580
  6.2 19.1 %copy-start.15 = (bf16[64,1024]{1,0:T(8,128)(2,1)S(1)}, bf16[64,1024]{1,0:T(8,128)(2,1)}, u32[]{:S(2)}) copy-start(bf16[64,1024]{1,0:T(8,128)(2,1)} %param.11) | copy-start | bytes 393220
  6.2 19.1 %copy-start.16 = (bf16[64,1024]{1,0:T(8,128)(2,1)S(1)}, bf16[64,1024]{1,0:T(8,128)(2,1)}, u32[]{:S(2)}) copy-start(bf16[64,1024]{1,0:T(8,128)(2,1)} %param.10) | copy-start | bytes 393220
  6.2 19.2 %copy-start.1 = (bf16[64,8192]{1,0:T(8,128)(2,1)S(1)}, bf16[64,8192]{1,0:T(8,128)(2,1)}, u32[]{:S(2)}) copy-start(bf16[64,8192]{1,0:T(8,128)(2,1)} %param.9) | copy-start | bytes 3145732
  6.2 67.3 %all-to-all-start = ((bf16[64,52,128]{2,1,0:T(8,128)(2,1)}), bf16[64,52,128]{2,1,0:T(8,128)(2,1)S(1)}, u32[]{:S(2)}, u32[]{:S(2)}) async-start(bf16[64,52,128]{2,1,0:T(8,128)(2,1)} %broadcast_select_fusion), calls=%async_computation | async-start | bytes 1835008 | tf_op jit(solution)/shard_map/all_to_all | solution.py:128
  25.5 16.7 %collective-permute-start.2 = (bf16[64,1280]{1,0:T(8,128)(2,1)S(1)}, bf16[64,1280]{1,0:T(8,128)(2,1)S(1)}, u32[]{:S(2)}, u32[]{:S(2)}) collective-permute-start(bf16[64,1280]{1,0:T(8,128)(2,1)S(1)} %pad_maximum_fusion.5), channel_id=1, source_target_pairs={{5,0},{6,1},{7,2},{0,3},{1,4},{2,5},{3,6},{4,7},{13,8},{14,9},{15,... | collective-permute-start | bytes 491528 | tf_op jit(solution)/shard_map/ppermute | solution.py:25
  27.9 17.2 %collective-permute-start.3 = (bf16[64,1280]{1,0:T(8,128)(2,1)S(1)}, bf16[64,1280]{1,0:T(8,128)(2,1)S(1)}, u32[]{:S(2)}, u32[]{:S(2)}) collective-permute-start(bf16[64,1280]{1,0:T(8,128)(2,1)S(1)} %pad_maximum_fusion.6), channel_id=1, source_target_pairs={{4,0},{5,1},{6,2},{7,3},{0,4},{1,5},{2,6},{3,7},{12,8},{13,9},{14,... | collective-permute-start | bytes 491528 | tf_op jit(solution)/shard_map/ppermute | solution.py:25
  32.7 13.1 %collective-permute-start.4 = (bf16[64,1280]{1,0:T(8,128)(2,1)S(1)}, bf16[64,1280]{1,0:T(8,128)(2,1)S(1)}, u32[]{:S(2)}, u32[]{:S(2)}) collective-permute-start(bf16[64,1280]{1,0:T(8,128)(2,1)S(1)} %pad_maximum_fusion.7), channel_id=1, source_target_pairs={{3,0},{4,1},{5,2},{6,3},{7,4},{0,5},{1,6},{2,7},{11,8},{12,9},{13,... | collective-permute-start | bytes 491528 | tf_op jit(solution)/shard_map/ppermute | solution.py:25
  37.5 8.4 %collective-permute-start.5 = (bf16[64,1280]{1,0:T(8,128)(2,1)S(1)}, bf16[64,1280]{1,0:T(8,128)(2,1)S(1)}, u32[]{:S(2)}, u32[]{:S(2)}) collective-permute-start(bf16[64,1280]{1,0:T(8,128)(2,1)S(1)} %pad_maximum_fusion.8), channel_id=1, source_target_pairs={{2,0},{3,1},{4,2},{5,3},{6,4},{7,5},{0,6},{1,7},{10,8},{11,9},{12,... | collective-permute-start | bytes 491528 | tf_op jit(solution)/shard_map/ppermute | solution.py:25
  40.5 5.6 %collective-permute-start.6 = (bf16[64,1280]{1,0:T(8,128)(2,1)S(1)}, bf16[64,1280]{1,0:T(8,128)(2,1)S(1)}, u32[]{:S(2)}, u32[]{:S(2)}) collective-permute-start(bf16[64,1280]{1,0:T(8,128)(2,1)S(1)} %pad_maximum_fusion.9), channel_id=1, source_target_pairs={{1,0},{2,1},{3,2},{4,3},{5,4},{6,5},{7,6},{0,7},{9,8},{10,9},{11,1... | collective-permute-start | bytes 491528 | tf_op jit(solution)/shard_map/ppermute | solution.py:25
  42.3 10.1 %collective-permute-start.1 = (bf16[64,1280]{1,0:T(8,128)(2,1)S(1)}, bf16[64,1280]{1,0:T(8,128)(2,1)S(1)}, u32[]{:S(2)}, u32[]{:S(2)}) collective-permute-start(bf16[64,1280]{1,0:T(8,128)(2,1)S(1)} %pad_maximum_fusion.4), channel_id=1, source_target_pairs={{6,0},{7,1},{0,2},{1,3},{2,4},{3,5},{4,6},{5,7},{14,8},{15,9},{8,1... | collective-permute-start | bytes 491528 | tf_op jit(solution)/shard_map/ppermute | solution.py:25
  45.2 0.7 copy-start.3
  45.2 8.5 %collective-permute-start = (bf16[64,1280]{1,0:T(8,128)(2,1)S(1)}, bf16[64,1280]{1,0:T(8,128)(2,1)S(1)}, u32[]{:S(2)}, u32[]{:S(2)}) collective-permute-start(bf16[64,1280]{1,0:T(8,128)(2,1)S(1)} %pad_maximum_fusion.3), channel_id=1, source_target_pairs={{7,0},{0,1},{1,2},{2,3},{3,4},{4,5},{5,6},{6,7},{15,8},{8,9},{9,10... | collective-permute-start | bytes 491528 | tf_op jit(solution)/shard_map/ppermute | solution.py:25
  45.8 29.5 %copy-start.5 = (bf16[64,1280]{1,0:T(8,128)(2,1)}, bf16[64,1280]{1,0:T(8,128)(2,1)S(1)}, u32[]{:S(2)}) copy-start(bf16[64,1280]{1,0:T(8,128)(2,1)S(1)} %collective-permute-done.4) | copy-start | bytes 491524
  45.9 29.5 %copy-start.7 = (bf16[64,1280]{1,0:T(8,128)(2,1)}, bf16[64,1280]{1,0:T(8,128)(2,1)S(1)}, u32[]{:S(2)}) copy-start(bf16[64,1280]{1,0:T(8,128)(2,1)S(1)} %collective-permute-done.5) | copy-start | bytes 491524
  46.1 29.3 %copy-start.9 = (bf16[64,1280]{1,0:T(8,128)(2,1)}, bf16[64,1280]{1,0:T(8,128)(2,1)S(1)}, u32[]{:S(2)}) copy-start(bf16[64,1280]{1,0:T(8,128)(2,1)S(1)} %collective-permute-done.6) | copy-start | bytes 491524
  52.4 1.4 copy-start.11
  53.7 0.7 copy-start.13
  75.4 6.8 %copy-start.14 = (bf16[64,1280]{1,0:T(8,128)(2,1)S(1)}, bf16[64,1280]{1,0:T(8,128)(2,1)}, u32[]{:S(2)}) copy-start(bf16[64,1280]{1,0:T(8,128)(2,1)} %copy-done.13) | copy-start | bytes 491524
  75.4 6.9 %copy-start.12 = (bf16[64,1280]{1,0:T(8,128)(2,1)S(1)}, bf16[64,1280]{1,0:T(8,128)(2,1)}, u32[]{:S(2)}) copy-start(bf16[64,1280]{1,0:T(8,128)(2,1)} %copy-done.11) | copy-start | bytes 491524
  75.4 6.9 %copy-start.4 = (bf16[64,1280]{1,0:T(8,128)(2,1)S(1)}, bf16[64,1280]{1,0:T(8,128)(2,1)}, u32[]{:S(2)}) copy-start(bf16[64,1280]{1,0:T(8,128)(2,1)} %copy-done.3) | copy-start | bytes 491524
  75.4 55.7 %all-to-all-start.1 = ((bf16[64,52,128]{2,1,0:T(8,128)(2,1)}), bf16[64,52,128]{2,1,0:T(8,128)(2,1)S(1)}, u32[]{:S(2)}, u32[]{:S(2)}) async-start(bf16[64,52,128]{2,1,0:T(8,128)(2,1)} %copy.26), calls=%async_computation.1 | async-start | bytes 1835008 | tf_op jit(solution)/shard_map/all_to_all | solution.py:134
  82.2 0.9 copy-start.6
  82.2 1.0 copy-start.8
  82.2 1.1 copy-start.10
  83.9 5.1 %copy-start.17 = (s32[8,4]{0,1:T(4,128)S(1)}, s32[8,4]{0,1:T(4,128)}, u32[]{:S(2)}) copy-start(s32[8,4]{0,1:T(4,128)} %param.17) | copy-start | bytes 388
  83.9 5.8 %copy-start.18 = (s32[8]{0:T(128)S(1)}, s32[8]{0:T(128)}, u32[]{:S(2)}) copy-start(s32[8]{0:T(128)} %roles_ref.1) | copy-start | bytes 100
  85.7 46.5 %collective-permute-start.7 = (bf16[2,512,128]{2,1,0:T(8,128)(2,1)S(1)}, bf16[2,512,128]{2,1,0:T(8,128)(2,1)S(1)}, u32[]{:S(2)}, u32[]{:S(2)}) collective-permute-start(bf16[2,512,128]{2,1,0:T(8,128)(2,1)S(1)} %get-tuple-element.38), channel_id=1, source_target_pairs={{504,0},{0,8},{8,16},{16,24},{24,32},{32,40},{40,48},{48,56},{56,6... | collective-permute-start | bytes 786440 | tf_op jit(solution)/shard_map/ppermute | solution.py:25
  132.2 0.7 copy-start.2

commit v16 on v15

--- a/solution.py
+++ b/solution.py
@@ -152,8 +152,7 @@
     sink_blocks = jnp.arange(SINK // BLK, dtype=jnp.int32)
     picks = jnp.concatenate([local_block.reshape(-1), sink_blocks])
     held = jnp.concatenate([(owner == my_seq).reshape(-1), jnp.broadcast_to(my_seq == 0, sink_blocks.shape)])
-    kv_blocks = jnp.stack([prefix_keys, prefix_values], 0).reshape(2, blocks_dev, BLK, HEAD_SIZE)
-    pieces = kv_blocks[:, picks]
+    pieces = jnp.stack([c.reshape(blocks_dev, BLK, HEAD_SIZE)[picks] for c in (prefix_keys, prefix_values)], 0)
     pieces = jnp.where(held[None, :, None, None], pieces, jnp.zeros_like(pieces))
     both = pieces.reshape(2, -1, HEAD_SIZE)
 

time: 152 us -> 153 us (level)
  local copies, waits for them, and re-layouts: 11.5 us -> 14.6 us
    gather x3 -> x2, local copies, waits for them, and re-layouts: 0.92 us -> 3.34 us  [shards(): c.reshape(blocks_dev, BLK, HEAD_SIZE)[picks]]
    unnamed x46 -> x42, local copies, waits for them, and re-layouts: 2.92 us -> 3.45 us
  transfers between devices with their start and end apart: 10 -> 10, of which waited for: 5 -> 5; matrix products, arithmetic and copies ran while one was open for 5% -> 6% of each run, Pallas kernels for 0% -> 0%
where the time goes in v16:
time: 153 us
  waiting for transfers between devices  66.7 us (44%)
  starting transfers between devices  46.4 us (30%)
  Pallas kernels  18.6 us (12%)
  local copies, waits for them, and re-layouts  14.6 us (10%)
  other arithmetic  5.49 us (4%)
    all_to_all x1, waiting for transfers between devices, gather_sums(): every = lax.all_to_all(total, 'seq', 0, 0, tiled=True)  38.8 us
    ppermute x8, starting transfers between devices, shifted(): return lax.ppermute(block, axis, route)  20.7 us
    all_to_all x1, waiting for transfers between devices, scatter_parts(): return lax.all_to_all(flat, 'seq', 0, 0, tiled=True)  19.7 us
    all_to_all x1, starting transfers between devices, scatter_parts(): return lax.all_to_all(flat, 'seq', 0, 0, tiled=True)  18.9 us
    pallas_call x1, Pallas kernels, attend(): pl.pallas_call(attend_kernel, grid_spec=grid_spec, out_shape=jax.ShapeDty...  18.6 us
    ppermute x8, waiting for transfers between devices, shifted(): return lax.ppermute(block, axis, route)  8.27 us
    all_to_all x1, starting transfers between devices, gather_sums(): every = lax.all_to_all(total, 'seq', 0, 0, tiled=True)  6.78 us
    unnamed x42, local copies, waits for them, and re-layouts  3.45 us
  transfers between devices with their start and end apart: 10, of which 5 were waited for; matrix products, arithmetic and copies ran while one was open for 6% of the time, Pallas kernels for 0%

profile of v16, /device:TPU:6, one launch (start us, length us, event | category | flops | bytes accessed | tf_op | source)
XLA Modules:
  0.0 152.8 jit_solution(15316265691163654137)
XLA Ops:
  0.0 0.0 copy-start
  0.0 0.7 broadcast_compare_fusion.1
  0.7 0.2 reduce-window.7
  0.9 0.6 iota_reduce_fusion
  1.5 0.0 copy-done
  1.5 0.6 gather_fusion
  2.1 0.1 gather.15
  2.2 0.1 fusion.4
  2.3 1.7 %gather_fusion.1 = bf16[26,64,128]{2,1,0:T(8,128)(2,1)S(1)} fusion(bf16[32,64,128]{2,1,0:T(8,128)(2,1)} %bitcast.48, s32[1024]{0:T(1024)S(1)} %get-tuple-element.58), kind=kCustom, calls=%fused_computation.1 | custom fusion | bytes 852072 | tf_op jit(solution)/shard_map/gather | solution.py:155
  4.0 1.7 %gather_fusion.2 = bf16[26,64,128]{2,1,0:T(8,128)(2,1)S(1)} fusion(bf16[32,64,128]{2,1,0:T(8,128)(2,1)} %bitcast.47, s32[1024]{0:T(1024)S(1)} %get-tuple-element.58), kind=kCustom, calls=%fused_computation.2 | custom fusion | bytes 852072 | tf_op jit(solution)/shard_map/gather | solution.py:155
  5.7 0.1 pad_maximum_fusion
  5.7 0.1 stack.59
  5.9 0.1 broadcast_in_dim.35
  6.0 0.1 broadcast_in_dim.36
  6.1 1.4 broadcast_select_fusion
  7.5 18.9 %all-to-all-start = ((bf16[64,52,128]{2,1,0:T(8,128)(2,1)}), bf16[64,52,128]{2,1,0:T(8,128)(2,1)S(1)}, u32[]{:S(2)}, u32[]{:S(2)}) async-start(bf16[64,52,128]{2,1,0:T(8,128)(2,1)} %broadcast_select_fusion), calls=%async_computation | async-start | bytes 1835008 | tf_op jit(solution)/shard_map/all_to_all | solution.py:128
  26.6 0.0 copy-done.13
  26.6 0.0 copy-done.14
  26.6 0.1 constant_dynamic-slice_fusion
  26.7 0.0 copy-done.1
  26.7 0.1 constant_dynamic-slice_fusion.2
  26.9 1.9 %collective-permute-start.6 = (bf16[64,1280]{1,0:T(8,128)(2,1)S(1)}, bf16[64,1280]{1,0:T(8,128)(2,1)S(1)}, u32[]{:S(2)}, u32[]{:S(2)}) collective-permute-start(bf16[64,1280]{1,0:T(8,128)(2,1)S(1)} %pad_maximum_fusion.9), channel_id=1, source_target_pairs={{1,0},{2,1},{3,2},{4,3},{5,4},{6,5},{7,6},{0,7},{9,8},{10,9},{11,1... | collective-permute-start | bytes 491528 | tf_op jit(solution)/shard_map/ppermute | solution.py:25
  28.8 3.1 %collective-permute-start.5 = (bf16[64,1280]{1,0:T(8,128)(2,1)S(1)}, bf16[64,1280]{1,0:T(8,128)(2,1)S(1)}, u32[]{:S(2)}, u32[]{:S(2)}) collective-permute-start(bf16[64,1280]{1,0:T(8,128)(2,1)S(1)} %pad_maximum_fusion.8), channel_id=1, source_target_pairs={{2,0},{3,1},{4,2},{5,3},{6,4},{7,5},{0,6},{1,7},{10,8},{11,9},{12,... | collective-permute-start | bytes 491528 | tf_op jit(solution)/shard_map/ppermute | solution.py:25
  31.9 2.4 %collective-permute-start.4 = (bf16[64,1280]{1,0:T(8,128)(2,1)S(1)}, bf16[64,1280]{1,0:T(8,128)(2,1)S(1)}, u32[]{:S(2)}, u32[]{:S(2)}) collective-permute-start(bf16[64,1280]{1,0:T(8,128)(2,1)S(1)} %pad_maximum_fusion.7), channel_id=1, source_target_pairs={{3,0},{4,1},{5,2},{6,3},{7,4},{0,5},{1,6},{2,7},{11,8},{12,9},{13,... | collective-permute-start | bytes 491528 | tf_op jit(solution)/shard_map/ppermute | solution.py:25
  34.3 4.8 %collective-permute-start.3 = (bf16[64,1280]{1,0:T(8,128)(2,1)S(1)}, bf16[64,1280]{1,0:T(8,128)(2,1)S(1)}, u32[]{:S(2)}, u32[]{:S(2)}) collective-permute-start(bf16[64,1280]{1,0:T(8,128)(2,1)S(1)} %pad_maximum_fusion.6), channel_id=1, source_target_pairs={{4,0},{5,1},{6,2},{7,3},{0,4},{1,5},{2,6},{3,7},{12,8},{13,9},{14,... | collective-permute-start | bytes 491528 | tf_op jit(solution)/shard_map/ppermute | solution.py:25
  39.1 1.9 %collective-permute-start.2 = (bf16[64,1280]{1,0:T(8,128)(2,1)S(1)}, bf16[64,1280]{1,0:T(8,128)(2,1)S(1)}, u32[]{:S(2)}, u32[]{:S(2)}) collective-permute-start(bf16[64,1280]{1,0:T(8,128)(2,1)S(1)} %pad_maximum_fusion.5), channel_id=1, source_target_pairs={{5,0},{6,1},{7,2},{0,3},{1,4},{2,5},{3,6},{4,7},{13,8},{14,9},{15,... | collective-permute-start | bytes 491528 | tf_op jit(solution)/shard_map/ppermute | solution.py:25
  41.1 1.7 %slice_bitcast_fusion.2 = (bf16[1,512,128]{2,1,0:T(8,128)(2,1)}, bf16[1,512,128]{2,1,0:T(8,128)(2,1)}) fusion(bf16[2048,128]{1,0:T(8,128)(2,1)} %param.13, bf16[2048,128]{1,0:T(8,128)(2,1)} %param.12), kind=kLoop, calls=%fused_computation.28 | loop fusion | bytes 524288 | tf_op jit(solution)/shard_map/stack | solution.py:180
  42.8 0.0 collective-permute-done.6
  42.8 2.2 %collective-permute-start.1 = (bf16[64,1280]{1,0:T(8,128)(2,1)S(1)}, bf16[64,1280]{1,0:T(8,128)(2,1)S(1)}, u32[]{:S(2)}, u32[]{:S(2)}) collective-permute-start(bf16[64,1280]{1,0:T(8,128)(2,1)S(1)} %pad_maximum_fusion.4), channel_id=1, source_target_pairs={{6,0},{7,1},{0,2},{1,3},{2,4},{3,5},{4,6},{5,7},{14,8},{15,9},{8,1... | collective-permute-start | bytes 491528 | tf_op jit(solution)/shard_map/ppermute | solution.py:25
  45.0 0.0 collective-permute-done.5
  45.1 1.1 collective-permute-start
  46.2 0.0 collective-permute-done.4
  46.2 0.0 collective-permute-done.3
  46.2 0.0 copy-start.7
  46.2 2.1 %collective-permute-done.2 = bf16[64,1280]{1,0:T(8,128)(2,1)S(1)} collective-permute-done((bf16[64,1280]{1,0:T(8,128)(2,1)S(1)}, bf16[64,1280]{1,0:T(8,128)(2,1)S(1)}, u32[]{:S(2)}, u32[]{:S(2)}) %collective-permute-start.2) | collective-permute-done | bytes 163872 | tf_op jit(solution)/shard_map/ppermute | solution.py:25
  48.3 4.6 %collective-permute-done.1 = bf16[64,1280]{1,0:T(8,128)(2,1)S(1)} collective-permute-done((bf16[64,1280]{1,0:T(8,128)(2,1)S(1)}, bf16[64,1280]{1,0:T(8,128)(2,1)S(1)}, u32[]{:S(2)}, u32[]{:S(2)}) %collective-permute-start.1) | collective-permute-done | bytes 163872 | tf_op jit(solution)/shard_map/ppermute | solution.py:25
  53.0 1.5 collective-permute-done
  54.5 0.0 copy-done.9
  54.5 0.7 copy-done.11
  55.2 19.7 %all-to-all-done = bf16[64,52,128]{2,1,0:T(8,128)(2,1)S(1)} async-done(((bf16[64,52,128]{2,1,0:T(8,128)(2,1)}), bf16[64,52,128]{2,1,0:T(8,128)(2,1)S(1)}, u32[]{:S(2)}, u32[]{:S(2)}) %all-to-all-start) | async-done | bytes 852000 | tf_op jit(solution)/shard_map/all_to_all | solution.py:128
  74.9 0.4 convolution_convert_fusion
  75.2 1.5 copy.20
  76.7 0.0 copy-done.7
  76.7 0.0 copy-done.8
  76.7 6.8 %all-to-all-start.1 = ((bf16[64,52,128]{2,1,0:T(8,128)(2,1)}), bf16[64,52,128]{2,1,0:T(8,128)(2,1)S(1)}, u32[]{:S(2)}, u32[]{:S(2)}) async-start(bf16[64,52,128]{2,1,0:T(8,128)(2,1)} %copy.20), calls=%async_computation.1 | async-start | bytes 1835008 | tf_op jit(solution)/shard_map/all_to_all | solution.py:134
  83.6 1.0 bitcast_dynamic-update-slice_fusion.4
  84.6 0.9 bitcast_dynamic-update-slice_fusion.3
  85.5 0.0 copy-done.6
  85.6 0.6 gather_fusion.3
  86.2 0.0 copy-start.15
  86.2 0.0 copy-start.16
  86.3 1.7 %pad_maximum_fusion.1 = (bf16[2,512,128]{2,1,0:T(8,128)(2,1)}, bf16[2,512,128]{2,1,0:T(8,128)(2,1)S(1)}) fusion(bf16[1,512,128]{2,1,0:T(8,128)(2,1)S(1)} %get-tuple-element.28, bf16[1,512,128]{2,1,0:T(8,128)(2,1)S(1)} %get-tuple-element.27, bf16[1,512,128]{2,1,0:T(8,128)(2,1)} %get-tuple-element.67, bf16[1,512,128]{2,1,0:T(8,128)(2,1)} %get-tuple-element.68, ...), kind=kLoop, calls=%fused_computation.9 | loop fusion | flops 393216 | bytes 1048577 | tf_op jit(solution)/shard_map/stack | solution.py:179
  88.0 3.4 %collective-permute-start.7 = (bf16[2,512,128]{2,1,0:T(8,128)(2,1)S(1)}, bf16[2,512,128]{2,1,0:T(8,128)(2,1)S(1)}, u32[]{:S(2)}, u32[]{:S(2)}) collective-permute-start(bf16[2,512,128]{2,1,0:T(8,128)(2,1)S(1)} %get-tuple-element.38), channel_id=1, source_target_pairs={{504,0},{0,8},{8,16},{16,24},{24,32},{32,40},{40,48},{48,56},{56,6... | collective-permute-start | bytes 786440 | tf_op jit(solution)/shard_map/ppermute | solution.py:25
  91.4 0.0 copy-done.15
  91.4 0.1 copy.18
  91.5 0.6 reshape.154.diag_ref
  92.0 0.0 copy-done.16
  92.0 0.5 broadcast_select_fusion.1.slot_ref
  92.6 1.1 slice.28.q_ref
  93.7 38.8 %all-to-all-done.1 = bf16[64,52,128]{2,1,0:T(8,128)(2,1)S(1)} async-done(((bf16[64,52,128]{2,1,0:T(8,128)(2,1)}), bf16[64,52,128]{2,1,0:T(8,128)(2,1)S(1)}, u32[]{:S(2)}, u32[]{:S(2)}) %all-to-all-start.1) | async-done | bytes 852000 | tf_op jit(solution)/shard_map/all_to_all | solution.py:134
  132.5 1.1 reshape.158.vk_ref.vv_ref.sk_ref.sv_ref
  133.6 0.0 collective-permute-done.7.prev_ref
  133.6 0.7 copy-done.2
  134.2 18.6 %shard_map.91 = bf16[512,1024]{1,0:T(8,128)(2,1)} custom-call(s32[8]{0:T(128)} %roles_ref.1, s32[8]{0:T(128)} %broadcast_select_fusion.1.slot_ref, s32[8]{0:T(128)} %count_ref.1, s32[32]{0:T(128)} %reshape.154.diag_ref, bf16[512,1024]{1,0:T(8,128)(2,1)} %slice.28.q_ref, bf16[2,512,128]{2,1,0:T(8,128)(2,1)} %copy-done.2, ...), custom_call_target="tpu_custom_call" | custom-call | tf_op jit(solution)/shard_map/pallas_call | solution.py:119
  (42 shorter events, 0.3 us)
Async XLA Ops:
  0.0 1.5 copy-start
  7.5 19.1 %copy-start.13 = (bf16[64,1024]{1,0:T(8,128)(2,1)S(1)}, bf16[64,1024]{1,0:T(8,128)(2,1)}, u32[]{:S(2)}) copy-start(bf16[64,1024]{1,0:T(8,128)(2,1)} %param.11) | copy-start | bytes 393220
  7.5 19.1 %copy-start.14 = (bf16[64,1024]{1,0:T(8,128)(2,1)S(1)}, bf16[64,1024]{1,0:T(8,128)(2,1)}, u32[]{:S(2)}) copy-start(bf16[64,1024]{1,0:T(8,128)(2,1)} %param.10) | copy-start | bytes 393220
  7.5 19.2 %copy-start.1 = (bf16[64,8192]{1,0:T(8,128)(2,1)S(1)}, bf16[64,8192]{1,0:T(8,128)(2,1)}, u32[]{:S(2)}) copy-start(bf16[64,8192]{1,0:T(8,128)(2,1)} %param.9) | copy-start | bytes 3145732
  7.5 67.3 %all-to-all-start = ((bf16[64,52,128]{2,1,0:T(8,128)(2,1)}), bf16[64,52,128]{2,1,0:T(8,128)(2,1)S(1)}, u32[]{:S(2)}, u32[]{:S(2)}) async-start(bf16[64,52,128]{2,1,0:T(8,128)(2,1)} %broadcast_select_fusion), calls=%async_computation | async-start | bytes 1835008 | tf_op jit(solution)/shard_map/all_to_all | solution.py:128
  26.9 15.9 %collective-permute-start.6 = (bf16[64,1280]{1,0:T(8,128)(2,1)S(1)}, bf16[64,1280]{1,0:T(8,128)(2,1)S(1)}, u32[]{:S(2)}, u32[]{:S(2)}) collective-permute-start(bf16[64,1280]{1,0:T(8,128)(2,1)S(1)} %pad_maximum_fusion.9), channel_id=1, source_target_pairs={{1,0},{2,1},{3,2},{4,3},{5,4},{6,5},{7,6},{0,7},{9,8},{10,9},{11,1... | collective-permute-start | bytes 491528 | tf_op jit(solution)/shard_map/ppermute | solution.py:25
  28.8 16.2 %collective-permute-start.5 = (bf16[64,1280]{1,0:T(8,128)(2,1)S(1)}, bf16[64,1280]{1,0:T(8,128)(2,1)S(1)}, u32[]{:S(2)}, u32[]{:S(2)}) collective-permute-start(bf16[64,1280]{1,0:T(8,128)(2,1)S(1)} %pad_maximum_fusion.8), channel_id=1, source_target_pairs={{2,0},{3,1},{4,2},{5,3},{6,4},{7,5},{0,6},{1,7},{10,8},{11,9},{12,... | collective-permute-start | bytes 491528 | tf_op jit(solution)/shard_map/ppermute | solution.py:25
  31.9 14.3 %collective-permute-start.4 = (bf16[64,1280]{1,0:T(8,128)(2,1)S(1)}, bf16[64,1280]{1,0:T(8,128)(2,1)S(1)}, u32[]{:S(2)}, u32[]{:S(2)}) collective-permute-start(bf16[64,1280]{1,0:T(8,128)(2,1)S(1)} %pad_maximum_fusion.7), channel_id=1, source_target_pairs={{3,0},{4,1},{5,2},{6,3},{7,4},{0,5},{1,6},{2,7},{11,8},{12,9},{13,... | collective-permute-start | bytes 491528 | tf_op jit(solution)/shard_map/ppermute | solution.py:25
  34.3 12.0 %collective-permute-start.3 = (bf16[64,1280]{1,0:T(8,128)(2,1)S(1)}, bf16[64,1280]{1,0:T(8,128)(2,1)S(1)}, u32[]{:S(2)}, u32[]{:S(2)}) collective-permute-start(bf16[64,1280]{1,0:T(8,128)(2,1)S(1)} %pad_maximum_fusion.6), channel_id=1, source_target_pairs={{4,0},{5,1},{6,2},{7,3},{0,4},{1,5},{2,6},{3,7},{12,8},{13,9},{14,... | collective-permute-start | bytes 491528 | tf_op jit(solution)/shard_map/ppermute | solution.py:25
  39.1 9.2 %collective-permute-start.2 = (bf16[64,1280]{1,0:T(8,128)(2,1)S(1)}, bf16[64,1280]{1,0:T(8,128)(2,1)S(1)}, u32[]{:S(2)}, u32[]{:S(2)}) collective-permute-start(bf16[64,1280]{1,0:T(8,128)(2,1)S(1)} %pad_maximum_fusion.5), channel_id=1, source_target_pairs={{5,0},{6,1},{7,2},{0,3},{1,4},{2,5},{3,6},{4,7},{13,8},{14,9},{15,... | collective-permute-start | bytes 491528 | tf_op jit(solution)/shard_map/ppermute | solution.py:25
  42.8 10.2 %collective-permute-start.1 = (bf16[64,1280]{1,0:T(8,128)(2,1)S(1)}, bf16[64,1280]{1,0:T(8,128)(2,1)S(1)}, u32[]{:S(2)}, u32[]{:S(2)}) collective-permute-start(bf16[64,1280]{1,0:T(8,128)(2,1)S(1)} %pad_maximum_fusion.4), channel_id=1, source_target_pairs={{6,0},{7,1},{0,2},{1,3},{2,4},{3,5},{4,6},{5,7},{14,8},{15,9},{8,1... | collective-permute-start | bytes 491528 | tf_op jit(solution)/shard_map/ppermute | solution.py:25
  45.0 1.1 copy-start.3
  45.1 9.4 %collective-permute-start = (bf16[64,1280]{1,0:T(8,128)(2,1)S(1)}, bf16[64,1280]{1,0:T(8,128)(2,1)S(1)}, u32[]{:S(2)}, u32[]{:S(2)}) collective-permute-start(bf16[64,1280]{1,0:T(8,128)(2,1)S(1)} %pad_maximum_fusion.3), channel_id=1, source_target_pairs={{7,0},{0,1},{1,2},{2,3},{3,4},{4,5},{5,6},{6,7},{15,8},{8,9},{9,10... | collective-permute-start | bytes 491528 | tf_op jit(solution)/shard_map/ppermute | solution.py:25
  46.2 30.5 %copy-start.5 = (bf16[64,1280]{1,0:T(8,128)(2,1)}, bf16[64,1280]{1,0:T(8,128)(2,1)S(1)}, u32[]{:S(2)}) copy-start(bf16[64,1280]{1,0:T(8,128)(2,1)S(1)} %collective-permute-done.4) | copy-start | bytes 491524
  46.2 30.5 %copy-start.7 = (bf16[64,1280]{1,0:T(8,128)(2,1)}, bf16[64,1280]{1,0:T(8,128)(2,1)S(1)}, u32[]{:S(2)}) copy-start(bf16[64,1280]{1,0:T(8,128)(2,1)S(1)} %collective-permute-done.3) | copy-start | bytes 491524
  48.3 28.4 %copy-start.8 = (bf16[64,1280]{1,0:T(8,128)(2,1)}, bf16[64,1280]{1,0:T(8,128)(2,1)S(1)}, u32[]{:S(2)}) copy-start(bf16[64,1280]{1,0:T(8,128)(2,1)S(1)} %collective-permute-done.2) | copy-start | bytes 491524
  53.0 1.5 copy-start.9
  54.5 0.7 copy-start.11
  76.7 6.8 %copy-start.12 = (bf16[64,1280]{1,0:T(8,128)(2,1)S(1)}, bf16[64,1280]{1,0:T(8,128)(2,1)}, u32[]{:S(2)}) copy-start(bf16[64,1280]{1,0:T(8,128)(2,1)} %copy-done.11) | copy-start | bytes 491524
  76.7 6.9 %copy-start.10 = (bf16[64,1280]{1,0:T(8,128)(2,1)S(1)}, bf16[64,1280]{1,0:T(8,128)(2,1)}, u32[]{:S(2)}) copy-start(bf16[64,1280]{1,0:T(8,128)(2,1)} %copy-done.9) | copy-start | bytes 491524
  76.7 8.8 %copy-start.4 = (bf16[64,1280]{1,0:T(8,128)(2,1)S(1)}, bf16[64,1280]{1,0:T(8,128)(2,1)}, u32[]{:S(2)}) copy-start(bf16[64,1280]{1,0:T(8,128)(2,1)} %copy-done.3) | copy-start | bytes 491524
  76.7 55.7 %all-to-all-start.1 = ((bf16[64,52,128]{2,1,0:T(8,128)(2,1)}), bf16[64,52,128]{2,1,0:T(8,128)(2,1)S(1)}, u32[]{:S(2)}, u32[]{:S(2)}) async-start(bf16[64,52,128]{2,1,0:T(8,128)(2,1)} %copy.20), calls=%async_computation.1 | async-start | bytes 1835008 | tf_op jit(solution)/shard_map/all_to_all | solution.py:134
  83.5 2.0 %copy-start.6 = (bf16[64,1280]{1,0:T(8,128)(2,1)S(1)}, bf16[64,1280]{1,0:T(8,128)(2,1)}, u32[]{:S(2)}) copy-start(bf16[64,1280]{1,0:T(8,128)(2,1)} %copy-done.5) | copy-start | bytes 491524
  86.2 5.1 %copy-start.15 = (s32[8,4]{0,1:T(4,128)S(1)}, s32[8,4]{0,1:T(4,128)}, u32[]{:S(2)}) copy-start(s32[8,4]{0,1:T(4,128)} %param.17) | copy-start | bytes 388
  86.2 5.8 %copy-start.16 = (s32[8]{0:T(128)S(1)}, s32[8]{0:T(128)}, u32[]{:S(2)}) copy-start(s32[8]{0:T(128)} %roles_ref.1) | copy-start | bytes 100
  88.0 45.6 %collective-permute-start.7 = (bf16[2,512,128]{2,1,0:T(8,128)(2,1)S(1)}, bf16[2,512,128]{2,1,0:T(8,128)(2,1)S(1)}, u32[]{:S(2)}, u32[]{:S(2)}) collective-permute-start(bf16[2,512,128]{2,1,0:T(8,128)(2,1)S(1)} %get-tuple-element.38), channel_id=1, source_target_pairs={{504,0},{0,8},{8,16},{16,24},{24,32},{32,40},{40,48},{48,56},{56,6... | collective-permute-start | bytes 786440 | tf_op jit(solution)/shard_map/ppermute | solution.py:25
  133.6 0.7 copy-start.2
